TPU v7x, 32 devices: a whole 2x2x4 slice. The times are simulated.
32 devices in a mesh: dp: 2 (over x), ctx: 4 (over z), tensor: 4 (over y, core).
Axes of the slice: x: 2, y: 2, z: 4, core: 2. Of those that a mesh axis runs over, the one named last changes fastest.
Arguments:
- queries: bfloat16 [2, 1024, 2048], P('dp', 'ctx', 'tensor'), may hold values from -32 to 32
- keyvals: bfloat16 [2, 1024, 2, 512], P('dp', 'ctx', None, 'tensor'), may hold values from -32 to 32
- documents: int32 [2, 1024], P('dp', 'ctx'), may hold values from 0 to 18, as said below
- output_weight: bfloat16 [2048, 4096], P(('dp', 'ctx'), 'tensor'), may hold values from -0.125 to 0.125
Outputs:
- projected: bfloat16 [2, 1024, 4096], P('dp', 'ctx', 'tensor')
Inputs may be any that keep to these rules, and one draw needn't show every extreme that they name: In each window the document numbers start at 0, never fall and rise by at most one from a position to the next; a window holds exactly 19 documents; no document holds more than 512 positions, and one holds exactly 512.
All inputs are finite; a program needn't handle non-finite values.
Results may differ from a plain program's by a relative error of at most 0.0051.
Values may be sent and summed in bfloat16 or wider, within the bound.
No kernel may reach another device: no remote copies, remote signals or barrier semaphores. Data moves between devices by JAX's collectives and lax.ppermute only.
A program may use at most 64 MiB of HBM per device.

v0:
```python
import math

import jax
import jax.numpy as jnp
from jax import lax
from jax.sharding import PartitionSpec as P

HEAD_DIM = 128


FLOOR_SCORE = -1e30


def shifted(block, axis, distance):
    devices = range(lax.axis_size(axis))
    route = [(i - distance, i) for i in devices if i - distance in devices]
    return lax.ppermute(block, axis, route)


def tile_update(
    softmax_state, query_block, query_place, query_labels, pair_block, key_place, key_labels
):
    maxima, totals, accumulated = softmax_state
    key_count = pair_block.shape[0]
    pair_heads = maxima.shape[0]
    head_size = query_block.shape[3]
    key_block = pair_block[:, 0].reshape(key_count, pair_heads, head_size)
    value_block = pair_block[:, 1].reshape(key_count, pair_heads, head_size)
    scores = jnp.einsum(
        "qhgd,khd->hgqk", query_block, key_block, preferred_element_type=jnp.float32
    )
    scores = scores * (1.0 / math.sqrt(head_size))
    allowed = (query_labels[:, None] == key_labels[None, :]) & (
        key_place[None, :] <= query_place[:, None]
    )
    allowed = allowed & (key_place[None, :] >= 0)
    scores = jnp.where(allowed, scores, FLOOR_SCORE)
    new_max = jnp.maximum(maxima, jnp.max(scores, axis=-1))
    fading = jnp.exp(maxima - new_max)
    exp_terms = jnp.where(allowed, jnp.exp(scores - new_max[..., None]), 0.0)
    totals = totals * fading + jnp.sum(exp_terms, axis=-1)
    update = jnp.einsum(
        "hgqk,khd->qhgd",
        exp_terms.astype(jnp.bfloat16),
        value_block,
        preferred_element_type=jnp.float32,
    )
    accumulated = accumulated * jnp.transpose(fading, (2, 0, 1))[..., None] + update
    return (new_max, totals, accumulated)


def guarded(
    softmax_state, query_block, query_place, query_labels, pair_block, key_place, key_labels
):
    nonempty = (jnp.min(key_place) <= jnp.max(query_place)) & (jnp.max(key_place) >= 0)
    nonempty = (
        nonempty
        & (jnp.max(key_labels) >= jnp.min(query_labels))
        & (jnp.min(key_labels) <= jnp.max(query_labels))
    )
    return lax.cond(
        nonempty,
        lambda running: tile_update(
            running, query_block, query_place, query_labels, pair_block, key_place, key_labels
        ),
        lambda running: running,
        softmax_state,
    )


def shards(queries, keyvals, documents, output_weight):
    length = queries.shape[1]
    pair_width = keyvals.shape[3]
    pair_heads = pair_width // HEAD_DIM
    query_group_size = queries.shape[2] // pair_width
    cycle_size = lax.axis_size("ctx")
    position = lax.axis_index("ctx")
    offsets = jnp.arange(length, dtype=jnp.int32)
    query_rows, query_marks = (queries, documents)
    query_place = position * length + offsets
    query_block = query_rows[0].reshape(length, pair_heads, query_group_size, HEAD_DIM)
    query_labels = query_marks[0]
    start_state = (
        jnp.full((pair_heads, query_group_size, length), FLOOR_SCORE, jnp.float32),
        jnp.zeros((pair_heads, query_group_size, length), jnp.float32),
        jnp.zeros((length, pair_heads, query_group_size, HEAD_DIM), jnp.float32),
    )
    own_state = guarded(
        start_state,
        query_block,
        query_place,
        query_labels,
        keyvals[0],
        position * length + offsets,
        documents[0],
    )
    reach_hops = min(cycle_size - 1, (cycle_size * length // 2 - 1 + length - 1) // length)

    def one_hop(hop_index, hop_carry):
        running, pair_buffer, label_buffer = hop_carry
        pair_buffer, label_buffer = shifted((pair_buffer, label_buffer), "ctx", 1)
        key_place = (position - hop_index) * length + offsets
        running = guarded(
            running,
            query_block,
            query_place,
            query_labels,
            pair_buffer[0],
            key_place,
            label_buffer[0],
        )
        return (running, pair_buffer, label_buffer)

    softmax_state = lax.fori_loop(1, reach_hops + 1, one_hop, (own_state, keyvals, documents))[0]
    maxima, totals, accumulated = softmax_state
    head_values = accumulated / jnp.transpose(totals, (2, 0, 1))[..., None]
    head_values = head_values.reshape(length, pair_heads * query_group_size * HEAD_DIM).astype(
        jnp.bfloat16
    )
    all_rows = lax.all_gather(output_weight, ("dp", "ctx"), axis=0, tiled=True)
    result = jnp.dot(
        lax.all_gather(head_values, "tensor", axis=1, tiled=True),
        all_rows,
        preferred_element_type=jnp.float32,
    )
    return result.astype(jnp.bfloat16)[None]


def solution(mesh):
    placed = (
        P("dp", "ctx", "tensor"),
        P("dp", "ctx", None, "tensor"),
        P("dp", "ctx"),
        P(("dp", "ctx"), "tensor"),
    )
    return jax.shard_map(
        shards, mesh=mesh, in_specs=placed, out_specs=P("dp", "ctx", "tensor"), check_vma=False
    )
```

profile of v0, /device:TPU:0, one launch (start us, length us, event | category | flops | bytes accessed | tf_op | source)
XLA Modules:
  0.0 156.2 jit_solution(3463505213601614344)
XLA Ops:
  6.5 0.0 all-gather.3.cloned.1.call-start
  6.5 0.7 iota_add_fusion.1
  7.2 0.6 fusion.35
  7.8 1.4 fusion.37
  11.7 0.7 copy.38
  14.3 1.1 copy.11
  15.4 0.2 copy.15
  15.6 0.9 copy.14
  16.5 4.2 %conditional.2 = (f32[1,4,256]{2,1,0:T(4,128)}, f32[1,4,256]{2,1,0:T(4,128)S(1)}, f32[256,1,4,128]{3,0,2,1:T(8,128)S(1)}) conditional(s32[]{:T(128)} %convert_element_type.27, () %tuple.41, (s32[1,256]{1,0:T(1,128)}, s32[256]{0:T(256)S(1)}, bf16[1,256,2,128]{3,2,1,0:T(2,128)(2,1)}, bf16[256,1,4,128]{0,3,2,1:T(8,128)(2,1)S(1)}) %tuple.90), branch_computations={%region_4.0_spmd, %region_5.8_spmd} | conditional | flops 136975616 | bytes 4644376 | solution.py:61
  16.5 0.9 and_and_fusion
  17.5 0.9 copy.20
  18.4 0.3 fusion.39
  18.7 0.6 fusion.15
  19.3 0.4 fusion.6
  19.8 0.2 fusion.8
  20.0 0.7 bitcast_add_fusion
  20.7 29.7 %while.24 = (s32[]{:T(128)}, f32[1,4,256]{2,1,0:T(4,128)}, f32[1,4,256]{2,1,0:T(4,128)S(1)}, f32[256,1,4,128]{3,0,2,1:T(8,128)S(1)}, bf16[1,256,2,128]{3,1,2,0:T...) while((s32[]{:T(128)}, f32[1,4,256]{2,1,0:T(4,128)}, ...), condition=%wide.region_17.0_spmd.clone, body=%wide.region_8.17_spmd.clone.sunk | while | flops 137106432 | bytes 5718995 | solution.py:114
  20.7 4.9 %collective-permute-start = (s32[1,256]{1,0:T(1,128)S(1)}, s32[1,256]{1,0:T(1,128)S(1)}, u32[]{:S(2)}, u32[]{:S(2)}) collective-permute-start(s32[1,256]{1,0:T(1,128)S(1)} %get-tuple-element.601), channel_id=1, source_target_pairs={{0,4},{4,8},{8,12},{1,5},{5,9},{9,13},{2,6},{6,10},{10,14},{3,7},{... | collective-permute-start | bytes 3080 | tf_op jit(solution)/shard_map/while/body/eval_jaxpr/ppermute | solution.py:17
  25.6 3.5 %collective-permute-start.1 = (bf16[1,256,2,128]{3,1,2,0:T(8,128)(2,1)S(1)}, bf16[1,256,2,128]{3,1,2,0:T(8,128)(2,1)S(1)}, u32[]{:S(2)}, u32[]{:S(2)}) collective-permute-start(bf16[1,256,2,128]{3,1,2,0:T(8,128)(2,1)S(1)} %get-tuple-element.600), channel_id=1, source_target_pairs={{0,4},{4,8},{8,12},{1,5},{5,9},{9,13},{2,6},{6,10},{10,14},{3,7},{... | collective-permute-start | bytes 393224 | tf_op jit(solution)/shard_map/while/body/eval_jaxpr/ppermute | solution.py:17
  29.1 0.7 fusion.45
  31.7 0.0 collective-permute-done
  31.7 0.7 fusion.46
  35.0 0.0 collective-permute-done.1
  35.0 7.4 %collective-permute-start = (s32[1,256]{1,0:T(1,128)S(1)}, s32[1,256]{1,0:T(1,128)S(1)}, u32[]{:S(2)}, u32[]{:S(2)}) collective-permute-start(s32[1,256]{1,0:T(1,128)S(1)} %get-tuple-element.601), channel_id=1, source_target_pairs={{0,4},{4,8},{8,12},{1,5},{5,9},{9,13},{2,6},{6,10},{10,14},{3,7},{... | collective-permute-start | bytes 3080 | tf_op jit(solution)/shard_map/while/body/eval_jaxpr/ppermute | solution.py:17
  42.5 1.9 %collective-permute-start.1 = (bf16[1,256,2,128]{3,1,2,0:T(8,128)(2,1)S(1)}, bf16[1,256,2,128]{3,1,2,0:T(8,128)(2,1)S(1)}, u32[]{:S(2)}, u32[]{:S(2)}) collective-permute-start(bf16[1,256,2,128]{3,1,2,0:T(8,128)(2,1)S(1)} %get-tuple-element.600), channel_id=1, source_target_pairs={{0,4},{4,8},{8,12},{1,5},{5,9},{9,13},{2,6},{6,10},{10,14},{3,7},{... | collective-permute-start | bytes 393224 | tf_op jit(solution)/shard_map/while/body/eval_jaxpr/ppermute | solution.py:17
  44.4 0.7 fusion.45
  47.0 0.0 collective-permute-done
  47.0 0.7 fusion.46
  50.3 0.0 collective-permute-done.1
  50.3 0.2 copy.16
  50.5 0.7 divide_convert_fusion
  51.3 0.0 all-gather.3.cloned.1.call-update
  51.3 0.0 all-gather.5.cloned.1.call-start
  51.4 0.7 all-gather.5.cloned.1.call-update
  52.1 17.2 %all-gather.3.cloned.1.call-done = bf16[256,2048]{0,1:T(8,128)(2,1)} async-done(((bf16[256,512]{0,1:T(8,128)(2,1)}), bf16[256,2048]{0,1:T(8,128)(2,1)}) %all-gather.3.cloned.1.call-update) | async-done | bytes 1048592 | tf_op jit(solution)/shard_map/all_gather | solution.py:122
  69.2 75.6 %all-gather.5.cloned.1.call-done = bf16[2048,1024]{1,0:T(8,128)(2,1)} async-done(((bf16[256,1024]{1,0:T(8,128)(2,1)}), bf16[2048,1024]{1,0:T(8,128)(2,1)}) %all-gather.5.cloned.1.call-update) | async-done | bytes 4194320 | tf_op jit(solution)/shard_map/all_gather | solution.py:120
  144.8 4.6 %fusion.33 = bf16[1,256,1024]{2,1,0:T(8,128)(2,1)} fusion(bf16[256,2048]{0,1:T(8,128)(2,1)} %all-gather.3.cloned.1.call-done, bf16[2048,1024]{1,0:T(8,128)(2,1)} %all-gather.5.cloned.1.call-done), kind=kOutput, calls=%fused_computation.53 | convolution fusion | flops 1074003968 | bytes 5767168 | tf_op jit(solution)/shard_map/dot_general | solution.py:121
  (12 shorter events, 0.1 us)
Async XLA Ops:
  6.5 62.7 %all-gather.3.cloned.1.call-start = ((), (), s32[]{:S(2)}) async-start(), calls=%async_computation | async-start | bytes 1310720 | tf_op jit(solution)/shard_map/all_gather | solution.py:122
  20.7 11.1 %collective-permute-start = (s32[1,256]{1,0:T(1,128)S(1)}, s32[1,256]{1,0:T(1,128)S(1)}, u32[]{:S(2)}, u32[]{:S(2)}) collective-permute-start(s32[1,256]{1,0:T(1,128)S(1)} %get-tuple-element.601), channel_id=1, source_target_pairs={{0,4},{4,8},{8,12},{1,5},{5,9},{9,13},{2,6},{6,10},{10,14},{3,7},{... | collective-permute-start | bytes 3080 | tf_op jit(solution)/shard_map/while/body/eval_jaxpr/ppermute | solution.py:17
  25.6 9.4 %collective-permute-start.1 = (bf16[1,256,2,128]{3,1,2,0:T(8,128)(2,1)S(1)}, bf16[1,256,2,128]{3,1,2,0:T(8,128)(2,1)S(1)}, u32[]{:S(2)}, u32[]{:S(2)}) collective-permute-start(bf16[1,256,2,128]{3,1,2,0:T(8,128)(2,1)S(1)} %get-tuple-element.600), channel_id=1, source_target_pairs={{0,4},{4,8},{8,12},{1,5},{5,9},{9,13},{2,6},{6,10},{10,14},{3,7},{... | collective-permute-start | bytes 393224 | tf_op jit(solution)/shard_map/while/body/eval_jaxpr/ppermute | solution.py:17
  35.0 12.0 %collective-permute-start = (s32[1,256]{1,0:T(1,128)S(1)}, s32[1,256]{1,0:T(1,128)S(1)}, u32[]{:S(2)}, u32[]{:S(2)}) collective-permute-start(s32[1,256]{1,0:T(1,128)S(1)} %get-tuple-element.601), channel_id=1, source_target_pairs={{0,4},{4,8},{8,12},{1,5},{5,9},{9,13},{2,6},{6,10},{10,14},{3,7},{... | collective-permute-start | bytes 3080 | tf_op jit(solution)/shard_map/while/body/eval_jaxpr/ppermute | solution.py:17
  42.5 7.8 %collective-permute-start.1 = (bf16[1,256,2,128]{3,1,2,0:T(8,128)(2,1)S(1)}, bf16[1,256,2,128]{3,1,2,0:T(8,128)(2,1)S(1)}, u32[]{:S(2)}, u32[]{:S(2)}) collective-permute-start(bf16[1,256,2,128]{3,1,2,0:T(8,128)(2,1)S(1)} %get-tuple-element.600), channel_id=1, source_target_pairs={{0,4},{4,8},{8,12},{1,5},{5,9},{9,13},{2,6},{6,10},{10,14},{3,7},{... | collective-permute-start | bytes 393224 | tf_op jit(solution)/shard_map/while/body/eval_jaxpr/ppermute | solution.py:17
  51.3 93.5 %all-gather.5.cloned.1.call-start = ((), (), s32[]{:S(2)}) async-start(), calls=%async_computation.1 | async-start | bytes 4718592 | tf_op jit(solution)/shard_map/all_gather | solution.py:120
Sparse Core Ops, SparseCore 0:
  51.4 17.7 all-gather.2
  71.3 73.3 all-gather.4
where the time goes:
time: 156 us
  waiting for transfers between devices  93.4 us (60%)
  between operations  17.9 us (11%)
  starting transfers between devices  17.8 us (11%)
  loops' own time  9.04 us (6%)
  other arithmetic  8.74 us (6%)
  matrix products  5.32 us (3%)
  local copies, waits for them, and re-layouts  4.02 us (3%)
    all_gather x1, waiting for transfers between devices, shards(): all_rows = lax.all_gather(output_weight, ('dp', 'ctx'), axis=0, tiled=True)  75.6 us
    ppermute x4, starting transfers between devices, shifted(): return lax.ppermute(block, axis, route)  17.7 us
    all_gather x1, waiting for transfers between devices, shards(): lax.all_gather(head_values, 'tensor', axis=1, tiled=True)  17.2 us
    another operation x1, loops' own time, shards(): lax.fori_loop(1, reach_hops + 1, one_hop, (own_state, keyvals, documents))  8.96 us
    dot_general x1, matrix products, shards(): jnp.dot(lax.all_gather(head_values, 'tensor', axis=1, tiled=True), all_ro...  4.59 us
  transfers between devices with their start and end apart: 6, of which 2 were waited for; matrix products, arithmetic and copies ran while one was open for 2% of the time, Pallas kernels for 0%

commit v1 on v0

v1 whole, which is shorter than its diff:
```python
import math

import jax
import jax.numpy as jnp
from jax import lax
from jax.sharding import PartitionSpec as P

HEAD_DIM = 128


FLOOR_SCORE = -1e30


def shifted(block, axis, distance):
    devices = range(lax.axis_size(axis))
    route = [(i - distance, i) for i in devices if i - distance in devices]
    return lax.ppermute(block, axis, route)


def rotated(block, axis, distance):
    count = lax.axis_size(axis)
    route = [(i, (i + distance) % count) for i in range(count)]
    return lax.ppermute(block, axis, route)


def attention(queries, keyvals, documents):
    length = queries.shape[1]
    pair_width = keyvals.shape[3]
    pair_heads = pair_width // HEAD_DIM
    query_group_size = queries.shape[2] // pair_width
    cycle_size = lax.axis_size("ctx")
    position = lax.axis_index("ctx")
    offsets = jnp.arange(length, dtype=jnp.int32)
    reach_hops = min(cycle_size - 1, (cycle_size * length // 2 - 1 + length - 1) // length)

    pair_blocks = [keyvals[0]]
    label_blocks = [documents[0]]
    place_blocks = [position * length + offsets]
    for hop in range(1, reach_hops + 1):
        pair_block, label_block = shifted((keyvals[0], documents[0]), "ctx", hop)
        pair_blocks.append(pair_block)
        label_blocks.append(label_block)
        place_blocks.append((position - hop) * length + offsets)
    pairs = jnp.concatenate(pair_blocks, axis=0)
    key_labels = jnp.concatenate(label_blocks, axis=0)
    key_place = jnp.concatenate(place_blocks, axis=0)
    key_count = pairs.shape[0]

    query_place = position * length + offsets
    query_labels = documents[0]
    query_block = queries[0].reshape(length, pair_heads, query_group_size, HEAD_DIM)
    key_block = pairs[:, 0].reshape(key_count, pair_heads, HEAD_DIM)
    value_block = pairs[:, 1].reshape(key_count, pair_heads, HEAD_DIM)

    scores = jnp.einsum(
        "qhgd,khd->hgqk", query_block, key_block, preferred_element_type=jnp.float32
    )
    scores = scores * (1.0 / math.sqrt(HEAD_DIM))
    allowed = (
        (query_labels[:, None] == key_labels[None, :])
        & (key_place[None, :] <= query_place[:, None])
        & (key_place[None, :] >= 0)
    )
    scores = jnp.where(allowed, scores, FLOOR_SCORE)
    peak = jnp.max(scores, axis=-1, keepdims=True)
    expo = jnp.where(allowed, jnp.exp(scores - peak), 0.0)
    total = jnp.sum(expo, axis=-1)
    summed = jnp.einsum(
        "hgqk,khd->qhgd",
        expo.astype(jnp.bfloat16),
        value_block,
        preferred_element_type=jnp.float32,
    )
    head_values = summed / jnp.transpose(total, (2, 0, 1))[..., None]
    return head_values.reshape(length, pair_heads * query_group_size * HEAD_DIM).astype(
        jnp.bfloat16
    )


def shards(queries, keyvals, documents, output_weight):
    all_rows = lax.all_gather(output_weight, ("dp", "ctx"), axis=0, tiled=True)
    head_values = attention(queries, keyvals, documents)
    width = head_values.shape[1]
    group = lax.axis_size("tensor")
    me = lax.axis_index("tensor")
    result = None
    for distance in range(group):
        held = head_values if distance == 0 else rotated(head_values, "tensor", distance)
        owner = (me - distance) % group
        rows = lax.dynamic_slice_in_dim(all_rows, owner * width, width, 0)
        part = jnp.dot(held, rows, preferred_element_type=jnp.float32)
        result = part if result is None else result + part
    return result.astype(jnp.bfloat16)[None]


def solution(mesh):
    placed = (
        P("dp", "ctx", "tensor"),
        P("dp", "ctx", None, "tensor"),
        P("dp", "ctx"),
        P(("dp", "ctx"), "tensor"),
    )
    return jax.shard_map(
        shards, mesh=mesh, in_specs=placed, out_specs=P("dp", "ctx", "tensor"), check_vma=False
    )
```

time: 156 us -> 103 us (0.66)
  waiting for transfers between devices: 93.4 us -> 61.4 us
  loops' own time: 9.04 us -> 0 us
  other arithmetic: 8.74 us -> 2.93 us
  between operations: 17.9 us -> 13.6 us
  local copies, waits for them, and re-layouts: 4.02 us -> 1.97 us
  starting transfers between devices: 17.8 us -> 15.8 us
    all_gather x1, waiting for transfers between devices: 75.6 us -> 56.5 us  [shards(): all_rows = lax.all_gather(output_weight, ('dp', 'ctx'), axis=0, tiled=True)]
    all_gather x1 -> x0, waiting for transfers between devices: 17.2 us -> none  [shards(): lax.all_gather(head_values, 'tensor', axis=1, tiled=True)]
    another operation x4 -> x0, loops' own time: 9.04 us -> none  [the longest x1 8.96 us: shards(): lax.fori_loop(1, reach_hops + 1, one_hop, (own_state, keyvals, documents))]
    ppermute x4, starting transfers between devices: 17.7 us -> 12.6 us  [shifted(): return lax.ppermute(block, axis, route)]
    ppermute x4, waiting for transfers between devices: 0.01 us -> 4.15 us  [shifted(): return lax.ppermute(block, axis, route)]
    reduce_min x4 -> x0, other arithmetic: 3.45 us -> none  [the longest x2 1.44 us: guarded(): jnp.min(key_labels) <= jnp.max(query_labels)]
    ppermute x0 -> x3, starting transfers between devices: none -> 3.11 us  [rotated(): return lax.ppermute(block, axis, route)]
    unnamed x4 -> x3, local copies, waits for them, and re-layouts: 2.86 us -> 0.93 us
  transfers between devices with their start and end apart: 6 -> 8, of which waited for: 2 -> 2; matrix products, arithmetic and copies ran while one was open for 2% -> 10% of each run, Pallas kernels for 0% -> 0%
where the time goes in v1:
time: 103 us
  waiting for transfers between devices  61.4 us (60%)
  starting transfers between devices  15.8 us (15%)
  between operations  13.6 us (13%)
  matrix products  6.84 us (7%)
  other arithmetic  2.93 us (3%)
  local copies, waits for them, and re-layouts  1.97 us (2%)
    all_gather x1, waiting for transfers between devices, shards(): all_rows = lax.all_gather(output_weight, ('dp', 'ctx'), axis=0, tiled=True)  56.5 us
    ppermute x4, starting transfers between devices, shifted(): return lax.ppermute(block, axis, route)  12.6 us
    dot_general x4, matrix products, shards(): part = jnp.dot(held, rows, preferred_element_type=jnp.float32)  5.26 us
    ppermute x4, waiting for transfers between devices, shifted(): return lax.ppermute(block, axis, route)  4.15 us
    ppermute x3, starting transfers between devices, rotated(): return lax.ppermute(block, axis, route)  3.11 us
  transfers between devices with their start and end apart: 8, of which 2 were waited for; matrix products, arithmetic and copies ran while one was open for 10% of the time, Pallas kernels for 0%

profile of v1, /device:TPU:0, one launch (start us, length us, event | category | flops | bytes accessed | tf_op | source)
XLA Modules:
  0.0 102.5 jit_solution(18023133421103284949)
XLA Ops:
  6.5 0.0 all-gather.2.cloned.1.call-start
  6.5 0.7 all-gather.2.cloned.1.call-update
  7.3 4.9 %collective-permute-start.2 = (s32[256]{0:T(256)}, s32[256]{0:T(256)S(1)}, u32[]{:S(2)}, u32[]{:S(2)}) collective-permute-start(s32[256]{0:T(256)} %bitcast.73), channel_id=1, source_target_pairs={{0,4},{4,8},{8,12},{1,5},{5,9},{9,13},{2,6},{6,10},{10,14},{3,7},{... | collective-permute-start | bytes 3080 | tf_op jit(solution)/shard_map/ppermute | solution.py:17
  12.2 4.5 %collective-permute-start.3 = (s32[256]{0:T(256)}, s32[256]{0:T(256)S(1)}, u32[]{:S(2)}, u32[]{:S(2)}) collective-permute-start(s32[256]{0:T(256)} %bitcast.74), channel_id=1, source_target_pairs={{0,8},{4,12},{1,9},{5,13},{2,10},{6,14},{3,11},{7,15},{16,24},{20,... | collective-permute-start | bytes 3080 | tf_op jit(solution)/shard_map/ppermute | solution.py:17
  16.7 0.9 copy.17
  17.6 1.3 %collective-permute-start = (bf16[256,2,128]{2,0,1:T(8,128)(2,1)S(1)}, bf16[256,2,128]{2,0,1:T(8,128)(2,1)S(1)}, u32[]{:S(2)}, u32[]{:S(2)}) collective-permute-start(bf16[256,2,128]{2,0,1:T(8,128)(2,1)S(1)} %bitcast.65), channel_id=1, source_target_pairs={{0,4},{4,8},{8,12},{1,5},{5,9},{9,13},{2,6},{6,10},{10,14},{3,7},{... | collective-permute-start | bytes 393224 | tf_op jit(solution)/shard_map/ppermute | solution.py:17
  18.9 1.9 %collective-permute-start.1 = (bf16[256,2,128]{2,0,1:T(8,128)(2,1)S(1)}, bf16[256,2,128]{2,0,1:T(8,128)(2,1)S(1)}, u32[]{:S(2)}, u32[]{:S(2)}) collective-permute-start(bf16[256,2,128]{2,0,1:T(8,128)(2,1)S(1)} %bitcast.66), channel_id=1, source_target_pairs={{0,8},{4,12},{1,9},{5,13},{2,10},{6,14},{3,11},{7,15},{16,24},{20,... | collective-permute-start | bytes 393224 | tf_op jit(solution)/shard_map/ppermute | solution.py:17
  20.9 1.0 %reshape.57 = bf16[256,4,128]{2,1,0:T(4,128)(2,1)S(1)} reshape(bf16[1,256,512]{2,1,0:T(8,128)(2,1)} %param.4) | data formatting | bytes 524288 | tf_op jit(solution)/shard_map/reshape.2
  22.0 0.0 collective-permute-done.2
  22.0 0.0 collective-permute-done.3
  22.0 0.7 pad_add_fusion
  22.7 1.4 %and_and_fusion = pred[256,768]{0,1:T(8,128)(4,1)S(1)} fusion(s32[256]{0:T(256)S(1)} %iota_add_fusion.2, s32[256]{0:T(256)} %bitcast.76, s32[768]{0:T(1024)S(1)} %pad_add_fusion.1, s32[768]{0:T(1024)S(1)} %pad_add_fusion, pred[768]{0:T(1024)(128)(4,1)S(1)} %broadcast_compare_fusion), kind=kLoop, calls=%fused_computation.22 | loop fusion | flops 786432 | bytes 205568 | tf_op jit(solution)/shard_map/and | solution.py:60
  24.1 0.0 collective-permute-done
  24.1 4.1 %collective-permute-done.1 = bf16[256,2,128]{2,0,1:T(8,128)(2,1)S(1)} collective-permute-done((bf16[256,2,128]{2,0,1:T(8,128)(2,1)S(1)}, bf16[256,2,128]{2,0,1:T(8,128)(2,1)S(1)}, u32[]{:S(2)}, u32[]{:S(2)}) %collective-permute-start.1) | collective-permute-done | bytes 131104 | tf_op jit(solution)/shard_map/ppermute | solution.py:17
  28.3 0.6 fusion
  28.9 0.8 fusion.1
  29.7 0.9 fusion.22
  30.7 0.1 collective-permute-start.4
  30.8 1.7 %collective-permute-start.6 = (bf16[256,512]{0,1:T(8,128)(2,1)S(1)}, bf16[256,512]{0,1:T(8,128)(2,1)S(1)}, u32[]{:S(2)}, u32[]{:S(2)}) collective-permute-start(bf16[256,512]{0,1:T(8,128)(2,1)S(1)} %bitcast.69), channel_id=1, source_target_pairs={{0,3},{1,0},{2,1},{3,2},{4,7},{5,4},{6,5},{7,6},{8,11},{9,8},{10,9... | collective-permute-start | bytes 786440 | tf_op jit(solution)/shard_map/ppermute | solution.py:23
  32.5 1.4 %collective-permute-start.5 = (bf16[256,512]{0,1:T(8,128)(2,1)S(1)}, bf16[256,512]{0,1:T(8,128)(2,1)S(1)}, u32[]{:S(2)}, u32[]{:S(2)}) collective-permute-start(bf16[256,512]{0,1:T(8,128)(2,1)S(1)} %bitcast.70), channel_id=1, source_target_pairs={{0,2},{1,3},{2,0},{3,1},{4,6},{5,7},{6,4},{7,5},{8,10},{9,11},{10,... | collective-permute-start | bytes 786440 | tf_op jit(solution)/shard_map/ppermute | solution.py:23
  33.8 56.5 %all-gather.2.cloned.1.call-done = bf16[2048,1024]{1,0:T(8,128)(2,1)} async-done(((bf16[256,1024]{1,0:T(8,128)(2,1)}), bf16[2048,1024]{1,0:T(8,128)(2,1)}) %all-gather.2.cloned.1.call-update) | async-done | bytes 4194320 | tf_op jit(solution)/shard_map/all_gather | solution.py:81
  90.4 0.0 copy-start
  90.4 1.8 %fusion.17 = f32[256,1024]{1,0:T(8,128)S(1)} fusion(bf16[256,512]{0,1:T(8,128)(2,1)S(1)} %bitcast.71, bf16[2048,1024]{1,0:T(8,128)(2,1)} %all-gather.2.cloned.1.call-done, s32[]{:T(128)S(6)} %select_n.41), kind=kOutput, calls=%fused_computation.18 | convolution fusion | flops 268435456 | bytes 2359300 | tf_op jit(solution)/shard_map/dot_general | solution.py:91
  92.2 0.0 collective-permute-done.4
  92.2 1.7 %convolution_add_fusion.1 = f32[256,1024]{1,0:T(8,128)S(1)} fusion(f32[256,1024]{1,0:T(8,128)S(1)} %fusion.17, bf16[256,512]{0,1:T(8,128)(2,1)S(1)} %collective-permute-done.4, bf16[2048,1024]{1,0:T(8,128)(2,1)} %all-gather.2.cloned.1.call-done, s32[]{:T(128)S(6)} %select_n.43), kind=kOutput, calls=%fused_computation.10 | convolution fusion | flops 268697600 | bytes 3407876 | tf_op jit(solution)/shard_map/dot_general | solution.py:91
  93.9 0.0 collective-permute-done.6
  94.0 0.0 copy-done
  94.0 0.5 fusion.13
  94.4 0.0 collective-permute-done.5
  94.4 1.3 %fusion.9 = bf16[1,256,1024]{2,1,0:T(8,128)(2,1)} fusion(f32[256,1024]{1,0:T(8,128)S(1)} %fusion.13, f32[256,1024]{1,0:T(8,128)S(1)} %convolution_add_fusion.1, bf16[256,512]{0,1:T(8,128)(2,1)S(1)} %collective-permute-done.5, bf16[2048,1024]{1,0:T(8,128)(2,1)S(1)} %copy-done, s32[]{:T(128)S(6)} %select_n.45), kind=kOutput, calls=%fused_computation.12 | convolution fusion | flops 269221888 | bytes 3932164 | tf_op jit(solution)/shard_map/dot_general | solution.py:91
  (5 shorter events, 0.1 us)
Async XLA Ops:
  6.5 83.8 %all-gather.2.cloned.1.call-start = ((), (), s32[]{:S(2)}) async-start(), calls=%async_computation | async-start | bytes 4718592 | tf_op jit(solution)/shard_map/all_gather | solution.py:81
  7.3 14.7 %collective-permute-start.2 = (s32[256]{0:T(256)}, s32[256]{0:T(256)S(1)}, u32[]{:S(2)}, u32[]{:S(2)}) collective-permute-start(s32[256]{0:T(256)} %bitcast.73), channel_id=1, source_target_pairs={{0,4},{4,8},{8,12},{1,5},{5,9},{9,13},{2,6},{6,10},{10,14},{3,7},{... | collective-permute-start | bytes 3080 | tf_op jit(solution)/shard_map/ppermute | solution.py:17
  12.2 9.8 %collective-permute-start.3 = (s32[256]{0:T(256)}, s32[256]{0:T(256)S(1)}, u32[]{:S(2)}, u32[]{:S(2)}) collective-permute-start(s32[256]{0:T(256)} %bitcast.74), channel_id=1, source_target_pairs={{0,8},{4,12},{1,9},{5,13},{2,10},{6,14},{3,11},{7,15},{16,24},{20,... | collective-permute-start | bytes 3080 | tf_op jit(solution)/shard_map/ppermute | solution.py:17
  17.6 6.5 %collective-permute-start = (bf16[256,2,128]{2,0,1:T(8,128)(2,1)S(1)}, bf16[256,2,128]{2,0,1:T(8,128)(2,1)S(1)}, u32[]{:S(2)}, u32[]{:S(2)}) collective-permute-start(bf16[256,2,128]{2,0,1:T(8,128)(2,1)S(1)} %bitcast.65), channel_id=1, source_target_pairs={{0,4},{4,8},{8,12},{1,5},{5,9},{9,13},{2,6},{6,10},{10,14},{3,7},{... | collective-permute-start | bytes 393224 | tf_op jit(solution)/shard_map/ppermute | solution.py:17
  18.9 9.3 %collective-permute-start.1 = (bf16[256,2,128]{2,0,1:T(8,128)(2,1)S(1)}, bf16[256,2,128]{2,0,1:T(8,128)(2,1)S(1)}, u32[]{:S(2)}, u32[]{:S(2)}) collective-permute-start(bf16[256,2,128]{2,0,1:T(8,128)(2,1)S(1)} %bitcast.66), channel_id=1, source_target_pairs={{0,8},{4,12},{1,9},{5,13},{2,10},{6,14},{3,11},{7,15},{16,24},{20,... | collective-permute-start | bytes 393224 | tf_op jit(solution)/shard_map/ppermute | solution.py:17
  30.7 61.6 %collective-permute-start.4 = (bf16[256,512]{0,1:T(8,128)(2,1)S(1)}, bf16[256,512]{0,1:T(8,128)(2,1)S(1)}, u32[]{:S(2)}, u32[]{:S(2)}) collective-permute-start(bf16[256,512]{0,1:T(8,128)(2,1)S(1)} %bitcast.68), channel_id=1, source_target_pairs={{0,1},{1,2},{2,3},{3,0},{4,5},{5,6},{6,7},{7,4},{8,9},{9,10},{10,1... | collective-permute-start | bytes 786440 | tf_op jit(solution)/shard_map/ppermute | solution.py:23
  30.8 63.1 %collective-permute-start.6 = (bf16[256,512]{0,1:T(8,128)(2,1)S(1)}, bf16[256,512]{0,1:T(8,128)(2,1)S(1)}, u32[]{:S(2)}, u32[]{:S(2)}) collective-permute-start(bf16[256,512]{0,1:T(8,128)(2,1)S(1)} %bitcast.69), channel_id=1, source_target_pairs={{0,3},{1,0},{2,1},{3,2},{4,7},{5,4},{6,5},{7,6},{8,11},{9,8},{10,9... | collective-permute-start | bytes 786440 | tf_op jit(solution)/shard_map/ppermute | solution.py:23
  32.5 62.0 %collective-permute-start.5 = (bf16[256,512]{0,1:T(8,128)(2,1)S(1)}, bf16[256,512]{0,1:T(8,128)(2,1)S(1)}, u32[]{:S(2)}, u32[]{:S(2)}) collective-permute-start(bf16[256,512]{0,1:T(8,128)(2,1)S(1)} %bitcast.70), channel_id=1, source_target_pairs={{0,2},{1,3},{2,0},{3,1},{4,6},{5,7},{6,4},{7,5},{8,10},{9,11},{10,... | collective-permute-start | bytes 786440 | tf_op jit(solution)/shard_map/ppermute | solution.py:23
  90.4 3.6 %copy-start = (bf16[2048,1024]{1,0:T(8,128)(2,1)S(1)}, bf16[2048,1024]{1,0:T(8,128)(2,1)}, u32[]{:S(2)}) copy-start(bf16[2048,1024]{1,0:T(8,128)(2,1)} %all-gather.2.cloned.1.call-done) | copy-start | bytes 12582916
Sparse Core Ops, SparseCore 0:
  9.5 80.8 all-gather.1

commit v2 on v1

--- a/solution.py
+++ b/solution.py
@@ -77,19 +77,69 @@
     )
 
 
+def line_blocks(block, axis):
+    count = lax.axis_size(axis)
+    upward = [(block, 0)]
+    downward = []
+    rising, falling = block, block
+    for step in range(1, count):
+        rising = lax.ppermute(rising, axis, [(i, i + 1) for i in range(step - 1, count - 1)])
+        falling = lax.ppermute(falling, axis, [(i, i - 1) for i in range(1, count - step + 1)])
+        upward.append((rising, -step))
+        downward.append((falling, step))
+    return upward + downward
+
+
+def crossed(block, count, holders):
+    route = [(side * count + c, (1 - side) * count + c) for side in range(2) for c in holders]
+    return lax.ppermute(block, ("dp", "ctx"), route)
+
+
+def forwarded_rows(output_weight):
+    count = lax.axis_size("ctx")
+    side = lax.axis_index("dp")
+    here = lax.axis_index("ctx")
+    pieces = []
+    for block, offset in line_blocks(output_weight, "ctx"):
+        if offset > 0:
+            holders = range(0, count - offset)
+        else:
+            holders = range(-offset, count)
+        pieces.append((block, side * count + here + offset))
+        pieces.append((crossed(block, count, holders), (1 - side) * count + here + offset))
+    return pieces
+
+
 def shards(queries, keyvals, documents, output_weight):
-    all_rows = lax.all_gather(output_weight, ("dp", "ctx"), axis=0, tiled=True)
+    block_rows = output_weight.shape[0]
+    width = queries.shape[2]
+    pipelined = lax.axis_size("dp") == 2 and width % block_rows == 0
+    if pipelined:
+        pieces = forwarded_rows(output_weight)
+    else:
+        all_rows = lax.all_gather(output_weight, ("dp", "ctx"), axis=0, tiled=True)
     head_values = attention(queries, keyvals, documents)
-    width = head_values.shape[1]
     group = lax.axis_size("tensor")
     me = lax.axis_index("tensor")
+    held = [head_values] + [rotated(head_values, "tensor", d) for d in range(1, group)]
     result = None
-    for distance in range(group):
-        held = head_values if distance == 0 else rotated(head_values, "tensor", distance)
-        owner = (me - distance) % group
-        rows = lax.dynamic_slice_in_dim(all_rows, owner * width, width, 0)
-        part = jnp.dot(held, rows, preferred_element_type=jnp.float32)
-        result = part if result is None else result + part
+    if pipelined:
+        heads_rel = jnp.concatenate(held, axis=1)
+        last_block = lax.axis_size("dp") * lax.axis_size("ctx") - 1
+        for block, row_block in pieces:
+            row_block = jnp.clip(row_block, 0, last_block)
+            first_row = row_block * block_rows
+            owner = first_row // width
+            column = ((me - owner) % group) * width + first_row % width
+            columns = lax.dynamic_slice_in_dim(heads_rel, column, block_rows, 1)
+            part = jnp.dot(columns, block, preferred_element_type=jnp.float32)
+            result = part if result is None else result + part
+    else:
+        for distance in range(group):
+            owner = (me - distance) % group
+            rows = lax.dynamic_slice_in_dim(all_rows, owner * width, width, 0)
+            part = jnp.dot(held[distance], rows, preferred_element_type=jnp.float32)
+            result = part if result is None else result + part
     return result.astype(jnp.bfloat16)[None]
 
 

time: 103 us -> 90.5 us (0.88)
  starting transfers between devices: 15.8 us -> 34.6 us
  waiting for transfers between devices: 61.4 us -> 43 us
  between operations: 13.6 us -> 0.39 us
    all_gather x1 -> x0, waiting for transfers between devices: 56.5 us -> none  [shards(): all_rows = lax.all_gather(output_weight, ('dp', 'ctx'), axis=0, tiled=True)]
    ppermute x0 -> x13, waiting for transfers between devices: none -> 34.2 us  [the longest x3 22.7 us: line_blocks(): lax.ppermute(falling, axis, [(i, i - 1) for i in range(1, count - step +...]
    ppermute x0 -> x13, starting transfers between devices: none -> 19 us  [the longest x7 11.8 us: crossed(): return lax.ppermute(block, ('dp', 'ctx'), route)]
    ppermute x3, waiting for transfers between devices: 0.01 us -> 8.79 us  [rotated(): return lax.ppermute(block, axis, route)]
    ppermute x4, waiting for transfers between devices: 4.15 us -> 0.01 us  [shifted(): return lax.ppermute(block, axis, route)]
    dot_general x4 -> x14, matrix products: 5.26 us -> 5.47 us  [shards(): part = jnp.dot(columns, block, preferred_element_type=jnp.float32)]
  transfers between devices with their start and end apart: 8 -> 20, of which waited for: 2 -> 6; matrix products, arithmetic and copies ran while one was open for 10% -> 12% of each run, Pallas kernels for 0% -> 0%
where the time goes in v2:
time: 90.5 us; the launch traced here: 90 us
  waiting for transfers between devices  43 us (48%)
  starting transfers between devices  34.6 us (38%)
  matrix products  7.07 us (8%)
  other arithmetic  3.01 us (3%)
  local copies, waits for them, and re-layouts  1.94 us (2%)
    ppermute x3, waiting for transfers between devices, line_blocks(): lax.ppermute(falling, axis, [(i, i - 1) for i in range(1, count - step +...  22.7 us
    ppermute x4, starting transfers between devices, shifted(): return lax.ppermute(block, axis, route)  12.6 us
    ppermute x7, starting transfers between devices, crossed(): return lax.ppermute(block, ('dp', 'ctx'), route)  11.8 us
    ppermute x7, waiting for transfers between devices, crossed(): return lax.ppermute(block, ('dp', 'ctx'), route)  11.5 us
    ppermute x3, waiting for transfers between devices, rotated(): return lax.ppermute(block, axis, route)  8.79 us
    dot_general x14, matrix products, shards(): part = jnp.dot(columns, block, preferred_element_type=jnp.float32)  5.47 us
    ppermute x3, starting transfers between devices, line_blocks(): lax.ppermute(falling, axis, [(i, i - 1) for i in range(1, count - step +...  3.86 us
    ppermute x3, starting transfers between devices, line_blocks(): lax.ppermute(rising, axis, [(i, i + 1) for i in range(step - 1, count - 1)])  3.26 us
  transfers between devices with their start and end apart: 20, of which 6 were waited for; matrix products, arithmetic and copies ran while one was open for 12% of the time, Pallas kernels for 0%

profile of v2, /device:TPU:0, one launch (start us, length us, event | category | flops | bytes accessed | tf_op | source)
XLA Modules:
  0.0 90.0 jit_solution(3191099826117735799)
XLA Ops:
  0.0 4.9 %collective-permute-start.2 = (s32[256]{0:T(256)}, s32[256]{0:T(256)S(1)}, u32[]{:S(2)}, u32[]{:S(2)}) collective-permute-start(s32[256]{0:T(256)} %bitcast.83), channel_id=1, source_target_pairs={{0,4},{4,8},{8,12},{1,5},{5,9},{9,13},{2,6},{6,10},{10,14},{3,7},{... | collective-permute-start | bytes 3080 | tf_op jit(solution)/shard_map/ppermute | solution.py:17
  4.9 4.5 %collective-permute-start.3 = (s32[256]{0:T(256)}, s32[256]{0:T(256)S(1)}, u32[]{:S(2)}, u32[]{:S(2)}) collective-permute-start(s32[256]{0:T(256)} %bitcast.84), channel_id=1, source_target_pairs={{0,8},{4,12},{1,9},{5,13},{2,10},{6,14},{3,11},{7,15},{16,24},{20,... | collective-permute-start | bytes 3080 | tf_op jit(solution)/shard_map/ppermute | solution.py:17
  9.4 0.9 %copy.17 = bf16[1,256,2,128]{3,1,2,0:T(8,128)(2,1)S(1)} copy(bf16[1,256,2,128]{3,2,1,0:T(2,128)(2,1)} %param.5) | data formatting | bytes 262144 | tf_op args[1]
  10.4 1.3 %collective-permute-start = (bf16[256,2,128]{2,0,1:T(8,128)(2,1)S(1)}, bf16[256,2,128]{2,0,1:T(8,128)(2,1)S(1)}, u32[]{:S(2)}, u32[]{:S(2)}) collective-permute-start(bf16[256,2,128]{2,0,1:T(8,128)(2,1)S(1)} %bitcast.75), channel_id=1, source_target_pairs={{0,4},{4,8},{8,12},{1,5},{5,9},{9,13},{2,6},{6,10},{10,14},{3,7},{... | collective-permute-start | bytes 393224 | tf_op jit(solution)/shard_map/ppermute | solution.py:17
  11.7 1.9 %collective-permute-start.1 = (bf16[256,2,128]{2,0,1:T(8,128)(2,1)S(1)}, bf16[256,2,128]{2,0,1:T(8,128)(2,1)S(1)}, u32[]{:S(2)}, u32[]{:S(2)}) collective-permute-start(bf16[256,2,128]{2,0,1:T(8,128)(2,1)S(1)} %bitcast.76), channel_id=1, source_target_pairs={{0,8},{4,12},{1,9},{5,13},{2,10},{6,14},{3,11},{7,15},{16,24},{20,... | collective-permute-start | bytes 393224 | tf_op jit(solution)/shard_map/ppermute | solution.py:17
  13.6 1.9 %collective-permute-start.8 = (bf16[256,1024]{1,0:T(8,128)(2,1)}, bf16[256,1024]{1,0:T(8,128)(2,1)S(1)}, u32[]{:S(2)}, u32[]{:S(2)}) collective-permute-start(bf16[256,1024]{1,0:T(8,128)(2,1)} %param.7), channel_id=1, source_target_pairs={{0,4},{4,8},{8,12},{1,5},{5,9},{9,13},{2,6},{6,10},{10,14},{3,7},{... | collective-permute-start | bytes 1572872 | tf_op jit(solution)/shard_map/ppermute | solution.py:86
  15.5 1.0 %reshape.57 = bf16[256,4,128]{2,1,0:T(4,128)(2,1)S(1)} reshape(bf16[1,256,512]{2,1,0:T(8,128)(2,1)} %param.4) | data formatting | bytes 524288 | tf_op jit(solution)/shard_map/reshape.2
  16.6 1.3 %collective-permute-start.14 = (bf16[256,1024]{1,0:T(8,128)(2,1)}, bf16[256,1024]{1,0:T(8,128)(2,1)S(1)}, u32[]{:S(2)}, u32[]{:S(2)}) collective-permute-start(bf16[256,1024]{1,0:T(8,128)(2,1)} %param.7), channel_id=1, source_target_pairs={{4,0},{8,4},{12,8},{5,1},{9,5},{13,9},{6,2},{10,6},{14,10},{7,3},{... | collective-permute-start | bytes 1572872 | tf_op jit(solution)/shard_map/ppermute | solution.py:87
  17.9 0.7 pad_add_fusion
  18.6 1.4 %and_and_fusion = pred[256,768]{0,1:T(8,128)(4,1)S(1)} fusion(s32[256]{0:T(256)S(1)} %iota_add_fusion.2, s32[256]{0:T(256)} %bitcast.86, s32[768]{0:T(1024)S(1)} %pad_add_fusion.1, s32[768]{0:T(1024)S(1)} %pad_add_fusion, pred[768]{0:T(1024)(128)(4,1)S(1)} %broadcast_compare_fusion), kind=kLoop, calls=%fused_computation.27 | loop fusion | flops 786432 | bytes 205568 | tf_op jit(solution)/shard_map/and | solution.py:60
  20.0 0.7 fusion
  20.7 0.8 fusion.1
  21.5 1.0 %fusion.21 = bf16[256,1,4,128]{0,3,2,1:T(8,128)(2,1)S(1)} fusion(f32[768,256,4]{1,0,2:T(8,128)S(1)} %get-tuple-element.6, f32[4,256]{1,0:T(4,128)S(1)} %get-tuple-element.5, pred[256,768]{0,1:T(8,128)(4,1)S(1)} %and_and_fusion, f32[256,4]{0,1:T(4,128)S(1)} %bitcast.82, bf16[768,2,128]{2,0,1:T(8,128)(2,1)S(1)} %pad_maximum_fusion.1), kind=kOutput, calls=%fused_computation.26 | convolution fusion | flops 205520896 | bytes 3809280 | tf_op jit(solution)/shard_map/hgqk,khd->qhgd/dot_general | solution.py:68
  22.5 0.1 collective-permute-start.4
  22.5 1.6 %collective-permute-start.5 = (bf16[256,512]{0,1:T(8,128)(2,1)S(1)}, bf16[256,512]{0,1:T(8,128)(2,1)S(1)}, u32[]{:S(2)}, u32[]{:S(2)}) collective-permute-start(bf16[256,512]{0,1:T(8,128)(2,1)S(1)} %bitcast.79), channel_id=1, source_target_pairs={{0,2},{1,3},{2,0},{3,1},{4,6},{5,7},{6,4},{7,5},{8,10},{9,11},{10,... | collective-permute-start | bytes 786440 | tf_op jit(solution)/shard_map/ppermute | solution.py:23
  24.1 1.4 %collective-permute-start.6 = (bf16[256,512]{0,1:T(8,128)(2,1)S(1)}, bf16[256,512]{0,1:T(8,128)(2,1)S(1)}, u32[]{:S(2)}, u32[]{:S(2)}) collective-permute-start(bf16[256,512]{0,1:T(8,128)(2,1)S(1)} %bitcast.80), channel_id=1, source_target_pairs={{0,3},{1,0},{2,1},{3,2},{4,7},{5,4},{6,5},{7,6},{8,11},{9,8},{10,9... | collective-permute-start | bytes 786440 | tf_op jit(solution)/shard_map/ppermute | solution.py:23
  25.5 5.0 %collective-permute-done.4 = bf16[256,512]{0,1:T(8,128)(2,1)S(1)} collective-permute-done((bf16[256,512]{0,1:T(8,128)(2,1)S(1)}, bf16[256,512]{0,1:T(8,128)(2,1)S(1)}, u32[]{:S(2)}, u32[]{:S(2)}) %collective-permute-start.4) | collective-permute-done | bytes 262176 | tf_op jit(solution)/shard_map/ppermute | solution.py:23
  30.5 1.5 %collective-permute-start.7 = (bf16[256,1024]{1,0:T(8,128)(2,1)S(1)}, bf16[256,1024]{1,0:T(8,128)(2,1)S(1)}, u32[]{:S(2)}, u32[]{:S(2)}) collective-permute-start(bf16[256,1024]{1,0:T(8,128)(2,1)S(1)} %copy-done), channel_id=1, source_target_pairs={{0,16},{4,20},{8,24},{12,28},{16,0},{20,4},{24,8},{28,12},{1,17},{... | collective-permute-start | bytes 1572872 | tf_op jit(solution)/shard_map/ppermute | solution.py:95
  32.0 3.8 %collective-permute-done.6 = bf16[256,512]{0,1:T(8,128)(2,1)S(1)} collective-permute-done((bf16[256,512]{0,1:T(8,128)(2,1)S(1)}, bf16[256,512]{0,1:T(8,128)(2,1)S(1)}, u32[]{:S(2)}, u32[]{:S(2)}) %collective-permute-start.6) | collective-permute-done | bytes 262176 | tf_op jit(solution)/shard_map/ppermute | solution.py:23
  35.8 0.1 pad_maximum_fusion
  35.8 0.7 collective-permute-start.10
  36.5 0.7 collective-permute-start.9
  37.3 1.3 %collective-permute-start.16 = (bf16[256,1024]{1,0:T(8,128)(2,1)S(1)}, bf16[256,1024]{1,0:T(8,128)(2,1)S(1)}, u32[]{:S(2)}, u32[]{:S(2)}) collective-permute-start(bf16[256,1024]{1,0:T(8,128)(2,1)S(1)} %collective-permute-done.14), channel_id=1, source_target_pairs={{4,0},{8,4},{5,1},{9,5},{6,2},{10,6},{7,3},{11,7},{20,16},{24,20},... | collective-permute-start | bytes 1572872 | tf_op jit(solution)/shard_map/ppermute | solution.py:87
  38.6 3.4 %collective-permute-start.15 = (bf16[256,1024]{1,0:T(8,128)(2,1)S(1)}, bf16[256,1024]{1,0:T(8,128)(2,1)S(1)}, u32[]{:S(2)}, u32[]{:S(2)}) collective-permute-start(bf16[256,1024]{1,0:T(8,128)(2,1)S(1)} %collective-permute-done.14), channel_id=1, source_target_pairs={{0,16},{4,20},{8,24},{16,0},{20,4},{24,8},{1,17},{5,21},{9,25},{17... | collective-permute-start | bytes 1572872 | tf_op jit(solution)/shard_map/ppermute | solution.py:95
  42.0 0.3 fusion.42
  42.3 1.2 %collective-permute-done.7 = bf16[256,1024]{1,0:T(8,128)(2,1)S(1)} collective-permute-done((bf16[256,1024]{1,0:T(8,128)(2,1)S(1)}, bf16[256,1024]{1,0:T(8,128)(2,1)S(1)}, u32[]{:S(2)}, u32[]{:S(2)}) %collective-permute-start.7) | collective-permute-done | bytes 524320 | tf_op jit(solution)/shard_map/ppermute | solution.py:95
  43.5 0.3 fusion.44
  43.8 0.3 fusion.12
  44.2 0.3 fusion.33
  44.5 0.7 collective-permute-start.12
  45.2 0.7 collective-permute-start.11
  45.9 12.4 %collective-permute-done.16 = bf16[256,1024]{1,0:T(8,128)(2,1)S(1)} collective-permute-done((bf16[256,1024]{1,0:T(8,128)(2,1)S(1)}, bf16[256,1024]{1,0:T(8,128)(2,1)S(1)}, u32[]{:S(2)}, u32[]{:S(2)}) %collective-permute-start.16) | collective-permute-done | bytes 524320 | tf_op jit(solution)/shard_map/ppermute | solution.py:87
  58.3 1.3 %collective-permute-start.18 = (bf16[256,1024]{1,0:T(8,128)(2,1)S(1)}, bf16[256,1024]{1,0:T(8,128)(2,1)S(1)}, u32[]{:S(2)}, u32[]{:S(2)}) collective-permute-start(bf16[256,1024]{1,0:T(8,128)(2,1)S(1)} %collective-permute-done.16), channel_id=1, source_target_pairs={{4,0},{5,1},{6,2},{7,3},{20,16},{21,17},{22,18},{23,19}} | collective-permute-start | bytes 1572872 | tf_op jit(solution)/shard_map/ppermute | solution.py:87
  59.6 0.3 fusion.39
  60.0 2.4 %collective-permute-start.17 = (bf16[256,1024]{1,0:T(8,128)(2,1)S(1)}, bf16[256,1024]{1,0:T(8,128)(2,1)S(1)}, u32[]{:S(2)}, u32[]{:S(2)}) collective-permute-start(bf16[256,1024]{1,0:T(8,128)(2,1)S(1)} %collective-permute-done.16), channel_id=1, source_target_pairs={{0,16},{4,20},{16,0},{20,4},{1,17},{5,21},{17,1},{21,5},{2,18},{6,... | collective-permute-start | bytes 1572872 | tf_op jit(solution)/shard_map/ppermute | solution.py:95
  62.4 0.3 fusion.11
  62.8 0.3 fusion.30
  63.1 0.7 collective-permute-start.13
  63.8 10.2 %collective-permute-done.18 = bf16[256,1024]{1,0:T(8,128)(2,1)S(1)} collective-permute-done((bf16[256,1024]{1,0:T(8,128)(2,1)S(1)}, bf16[256,1024]{1,0:T(8,128)(2,1)S(1)}, u32[]{:S(2)}, u32[]{:S(2)}) %collective-permute-start.18) | collective-permute-done | bytes 524320 | tf_op jit(solution)/shard_map/ppermute | solution.py:87
  74.0 2.4 %collective-permute-start.19 = (bf16[256,1024]{1,0:T(8,128)(2,1)S(1)}, bf16[256,1024]{1,0:T(8,128)(2,1)S(1)}, u32[]{:S(2)}, u32[]{:S(2)}) collective-permute-start(bf16[256,1024]{1,0:T(8,128)(2,1)S(1)} %collective-permute-done.18), channel_id=1, source_target_pairs={{0,16},{16,0},{1,17},{17,1},{2,18},{18,2},{3,19},{19,3}} | collective-permute-start | bytes 1572872 | tf_op jit(solution)/shard_map/ppermute | solution.py:95
  76.5 0.3 fusion.36
  76.8 0.3 fusion.10
  77.2 0.3 fusion.27
  77.5 0.4 fusion.9
  77.9 0.3 fusion.8
  78.2 0.3 fusion.7
  78.6 10.3 %collective-permute-done.19 = bf16[256,1024]{1,0:T(8,128)(2,1)S(1)} collective-permute-done((bf16[256,1024]{1,0:T(8,128)(2,1)S(1)}, bf16[256,1024]{1,0:T(8,128)(2,1)S(1)}, u32[]{:S(2)}, u32[]{:S(2)}) %collective-permute-start.19) | collective-permute-done | bytes 524320 | tf_op jit(solution)/shard_map/ppermute | solution.py:95
  88.9 1.1 %fusion.14 = bf16[1,256,1024]{2,1,0:T(8,128)(2,1)} fusion(f32[256,1024]{1,0:T(8,128)S(1)} %fusion.7, bf16[256,1024]{1,0:T(8,128)(2,1)S(1)} %collective-permute-done.19, bf16[256,2048]{0,1:T(8,128)(2,1)S(1)} %pad_maximum_fusion, s32[]{:T(128)S(6)} %select_n.264), kind=kOutput, calls=%fused_computation.22 | convolution fusion | flops 134742016 | bytes 2228228 | tf_op jit(solution)/shard_map/dot_general | solution.py:135
  (21 shorter events, 0.1 us)
Async XLA Ops:
  0.0 16.6 %collective-permute-start.2 = (s32[256]{0:T(256)}, s32[256]{0:T(256)S(1)}, u32[]{:S(2)}, u32[]{:S(2)}) collective-permute-start(s32[256]{0:T(256)} %bitcast.83), channel_id=1, source_target_pairs={{0,4},{4,8},{8,12},{1,5},{5,9},{9,13},{2,6},{6,10},{10,14},{3,7},{... | collective-permute-start | bytes 3080 | tf_op jit(solution)/shard_map/ppermute | solution.py:17
  4.9 13.0 %collective-permute-start.3 = (s32[256]{0:T(256)}, s32[256]{0:T(256)S(1)}, u32[]{:S(2)}, u32[]{:S(2)}) collective-permute-start(s32[256]{0:T(256)} %bitcast.84), channel_id=1, source_target_pairs={{0,8},{4,12},{1,9},{5,13},{2,10},{6,14},{3,11},{7,15},{16,24},{20,... | collective-permute-start | bytes 3080 | tf_op jit(solution)/shard_map/ppermute | solution.py:17
  10.4 9.6 %collective-permute-start = (bf16[256,2,128]{2,0,1:T(8,128)(2,1)S(1)}, bf16[256,2,128]{2,0,1:T(8,128)(2,1)S(1)}, u32[]{:S(2)}, u32[]{:S(2)}) collective-permute-start(bf16[256,2,128]{2,0,1:T(8,128)(2,1)S(1)} %bitcast.75), channel_id=1, source_target_pairs={{0,4},{4,8},{8,12},{1,5},{5,9},{9,13},{2,6},{6,10},{10,14},{3,7},{... | collective-permute-start | bytes 393224 | tf_op jit(solution)/shard_map/ppermute | solution.py:17
  11.7 8.3 %collective-permute-start.1 = (bf16[256,2,128]{2,0,1:T(8,128)(2,1)S(1)}, bf16[256,2,128]{2,0,1:T(8,128)(2,1)S(1)}, u32[]{:S(2)}, u32[]{:S(2)}) collective-permute-start(bf16[256,2,128]{2,0,1:T(8,128)(2,1)S(1)} %bitcast.76), channel_id=1, source_target_pairs={{0,8},{4,12},{1,9},{5,13},{2,10},{6,14},{3,11},{7,15},{16,24},{20,... | collective-permute-start | bytes 393224 | tf_op jit(solution)/shard_map/ppermute | solution.py:17
  13.6 22.2 %collective-permute-start.8 = (bf16[256,1024]{1,0:T(8,128)(2,1)}, bf16[256,1024]{1,0:T(8,128)(2,1)S(1)}, u32[]{:S(2)}, u32[]{:S(2)}) collective-permute-start(bf16[256,1024]{1,0:T(8,128)(2,1)} %param.7), channel_id=1, source_target_pairs={{0,4},{4,8},{8,12},{1,5},{5,9},{9,13},{2,6},{6,10},{10,14},{3,7},{... | collective-permute-start | bytes 1572872 | tf_op jit(solution)/shard_map/ppermute | solution.py:86
  16.6 20.7 %collective-permute-start.14 = (bf16[256,1024]{1,0:T(8,128)(2,1)}, bf16[256,1024]{1,0:T(8,128)(2,1)S(1)}, u32[]{:S(2)}, u32[]{:S(2)}) collective-permute-start(bf16[256,1024]{1,0:T(8,128)(2,1)} %param.7), channel_id=1, source_target_pairs={{4,0},{8,4},{12,8},{5,1},{9,5},{13,9},{6,2},{10,6},{14,10},{7,3},{... | collective-permute-start | bytes 1572872 | tf_op jit(solution)/shard_map/ppermute | solution.py:87
  21.5 9.0 %copy-start = (bf16[256,1024]{1,0:T(8,128)(2,1)S(1)}, bf16[256,1024]{1,0:T(8,128)(2,1)}, u32[]{:S(2)}) copy-start(bf16[256,1024]{1,0:T(8,128)(2,1)} %param.7) | copy-start | bytes 1572868
  22.5 8.0 %collective-permute-start.4 = (bf16[256,512]{0,1:T(8,128)(2,1)S(1)}, bf16[256,512]{0,1:T(8,128)(2,1)S(1)}, u32[]{:S(2)}, u32[]{:S(2)}) collective-permute-start(bf16[256,512]{0,1:T(8,128)(2,1)S(1)} %bitcast.78), channel_id=1, source_target_pairs={{0,1},{1,2},{2,3},{3,0},{4,5},{5,6},{6,7},{7,4},{8,9},{9,10},{10,1... | collective-permute-start | bytes 786440 | tf_op jit(solution)/shard_map/ppermute | solution.py:23
  22.5 9.5 %collective-permute-start.5 = (bf16[256,512]{0,1:T(8,128)(2,1)S(1)}, bf16[256,512]{0,1:T(8,128)(2,1)S(1)}, u32[]{:S(2)}, u32[]{:S(2)}) collective-permute-start(bf16[256,512]{0,1:T(8,128)(2,1)S(1)} %bitcast.79), channel_id=1, source_target_pairs={{0,2},{1,3},{2,0},{3,1},{4,6},{5,7},{6,4},{7,5},{8,10},{9,11},{10,... | collective-permute-start | bytes 786440 | tf_op jit(solution)/shard_map/ppermute | solution.py:23
  24.1 11.7 %collective-permute-start.6 = (bf16[256,512]{0,1:T(8,128)(2,1)S(1)}, bf16[256,512]{0,1:T(8,128)(2,1)S(1)}, u32[]{:S(2)}, u32[]{:S(2)}) collective-permute-start(bf16[256,512]{0,1:T(8,128)(2,1)S(1)} %bitcast.80), channel_id=1, source_target_pairs={{0,3},{1,0},{2,1},{3,2},{4,7},{5,4},{6,5},{7,6},{8,11},{9,8},{10,9... | collective-permute-start | bytes 786440 | tf_op jit(solution)/shard_map/ppermute | solution.py:23
  30.5 13.0 %collective-permute-start.7 = (bf16[256,1024]{1,0:T(8,128)(2,1)S(1)}, bf16[256,1024]{1,0:T(8,128)(2,1)S(1)}, u32[]{:S(2)}, u32[]{:S(2)}) collective-permute-start(bf16[256,1024]{1,0:T(8,128)(2,1)S(1)} %copy-done), channel_id=1, source_target_pairs={{0,16},{4,20},{8,24},{12,28},{16,0},{20,4},{24,8},{28,12},{1,17},{... | collective-permute-start | bytes 1572872 | tf_op jit(solution)/shard_map/ppermute | solution.py:95
  35.8 8.6 %collective-permute-start.10 = (bf16[256,1024]{1,0:T(8,128)(2,1)S(1)}, bf16[256,1024]{1,0:T(8,128)(2,1)S(1)}, u32[]{:S(2)}, u32[]{:S(2)}) collective-permute-start(bf16[256,1024]{1,0:T(8,128)(2,1)S(1)} %collective-permute-done.8), channel_id=1, source_target_pairs={{4,8},{8,12},{5,9},{9,13},{6,10},{10,14},{7,11},{11,15},{20,24},{2... | collective-permute-start | bytes 1572872 | tf_op jit(solution)/shard_map/ppermute | solution.py:86
  36.5 23.4 %collective-permute-start.9 = (bf16[256,1024]{1,0:T(8,128)(2,1)S(1)}, bf16[256,1024]{1,0:T(8,128)(2,1)S(1)}, u32[]{:S(2)}, u32[]{:S(2)}) collective-permute-start(bf16[256,1024]{1,0:T(8,128)(2,1)S(1)} %collective-permute-done.8), channel_id=1, source_target_pairs={{4,20},{8,24},{12,28},{20,4},{24,8},{28,12},{5,21},{9,25},{13,29},... | collective-permute-start | bytes 1572872 | tf_op jit(solution)/shard_map/ppermute | solution.py:95
  37.3 21.1 %collective-permute-start.16 = (bf16[256,1024]{1,0:T(8,128)(2,1)S(1)}, bf16[256,1024]{1,0:T(8,128)(2,1)S(1)}, u32[]{:S(2)}, u32[]{:S(2)}) collective-permute-start(bf16[256,1024]{1,0:T(8,128)(2,1)S(1)} %collective-permute-done.14), channel_id=1, source_target_pairs={{4,0},{8,4},{5,1},{9,5},{6,2},{10,6},{7,3},{11,7},{20,16},{24,20},... | collective-permute-start | bytes 1572872 | tf_op jit(solution)/shard_map/ppermute | solution.py:87
  38.6 39.3 %collective-permute-start.15 = (bf16[256,1024]{1,0:T(8,128)(2,1)S(1)}, bf16[256,1024]{1,0:T(8,128)(2,1)S(1)}, u32[]{:S(2)}, u32[]{:S(2)}) collective-permute-start(bf16[256,1024]{1,0:T(8,128)(2,1)S(1)} %collective-permute-done.14), channel_id=1, source_target_pairs={{0,16},{4,20},{8,24},{16,0},{20,4},{24,8},{1,17},{5,21},{9,25},{17... | collective-permute-start | bytes 1572872 | tf_op jit(solution)/shard_map/ppermute | solution.py:95
  44.5 18.6 %collective-permute-start.12 = (bf16[256,1024]{1,0:T(8,128)(2,1)S(1)}, bf16[256,1024]{1,0:T(8,128)(2,1)S(1)}, u32[]{:S(2)}, u32[]{:S(2)}) collective-permute-start(bf16[256,1024]{1,0:T(8,128)(2,1)S(1)} %collective-permute-done.10), channel_id=1, source_target_pairs={{8,12},{9,13},{10,14},{11,15},{24,28},{25,29},{26,30},{27,31}} | collective-permute-start | bytes 1572872 | tf_op jit(solution)/shard_map/ppermute | solution.py:86
  45.2 31.6 %collective-permute-start.11 = (bf16[256,1024]{1,0:T(8,128)(2,1)S(1)}, bf16[256,1024]{1,0:T(8,128)(2,1)S(1)}, u32[]{:S(2)}, u32[]{:S(2)}) collective-permute-start(bf16[256,1024]{1,0:T(8,128)(2,1)S(1)} %collective-permute-done.10), channel_id=1, source_target_pairs={{8,24},{12,28},{24,8},{28,12},{9,25},{13,29},{25,9},{29,13},{10,26... | collective-permute-start | bytes 1572872 | tf_op jit(solution)/shard_map/ppermute | solution.py:95
  58.3 15.7 %collective-permute-start.18 = (bf16[256,1024]{1,0:T(8,128)(2,1)S(1)}, bf16[256,1024]{1,0:T(8,128)(2,1)S(1)}, u32[]{:S(2)}, u32[]{:S(2)}) collective-permute-start(bf16[256,1024]{1,0:T(8,128)(2,1)S(1)} %collective-permute-done.16), channel_id=1, source_target_pairs={{4,0},{5,1},{6,2},{7,3},{20,16},{21,17},{22,18},{23,19}} | collective-permute-start | bytes 1572872 | tf_op jit(solution)/shard_map/ppermute | solution.py:87
  60.0 18.2 %collective-permute-start.17 = (bf16[256,1024]{1,0:T(8,128)(2,1)S(1)}, bf16[256,1024]{1,0:T(8,128)(2,1)S(1)}, u32[]{:S(2)}, u32[]{:S(2)}) collective-permute-start(bf16[256,1024]{1,0:T(8,128)(2,1)S(1)} %collective-permute-done.16), channel_id=1, source_target_pairs={{0,16},{4,20},{16,0},{20,4},{1,17},{5,21},{17,1},{21,5},{2,18},{6,... | collective-permute-start | bytes 1572872 | tf_op jit(solution)/shard_map/ppermute | solution.py:95
  63.1 14.4 %collective-permute-start.13 = (bf16[256,1024]{1,0:T(8,128)(2,1)S(1)}, bf16[256,1024]{1,0:T(8,128)(2,1)S(1)}, u32[]{:S(2)}, u32[]{:S(2)}) collective-permute-start(bf16[256,1024]{1,0:T(8,128)(2,1)S(1)} %collective-permute-done.12), channel_id=1, source_target_pairs={{12,28},{28,12},{13,29},{29,13},{14,30},{30,14},{15,31},{31,15}} | collective-permute-start | bytes 1572872 | tf_op jit(solution)/shard_map/ppermute | solution.py:95
  74.0 14.8 %collective-permute-start.19 = (bf16[256,1024]{1,0:T(8,128)(2,1)S(1)}, bf16[256,1024]{1,0:T(8,128)(2,1)S(1)}, u32[]{:S(2)}, u32[]{:S(2)}) collective-permute-start(bf16[256,1024]{1,0:T(8,128)(2,1)S(1)} %collective-permute-done.18), channel_id=1, source_target_pairs={{0,16},{16,0},{1,17},{17,1},{2,18},{18,2},{3,19},{19,3}} | collective-permute-start | bytes 1572872 | tf_op jit(solution)/shard_map/ppermute | solution.py:95

commit v3 on v1

--- a/solution.py
+++ b/solution.py
@@ -77,10 +77,48 @@
     )
 
 
+def swapped(block, axis):
+    return lax.ppermute(block, axis, [(0, 1), (1, 0)])
+
+
+def split_projection(head_values, output_weight):
+    block_rows = output_weight.shape[0]
+    width = head_values.shape[1]
+    group = lax.axis_size("tensor")
+    me = lax.axis_index("tensor")
+    side = lax.axis_index("dp")
+    side_rows = lax.all_gather(output_weight, "ctx", axis=0, tiled=True)
+    side_width = side_rows.shape[0]
+    foreign = swapped(head_values, "dp")
+    both = jnp.concatenate([head_values, foreign], axis=1)
+    held = [both] + [rotated(both, "tensor", d) for d in range(1, group)]
+    mixed = jnp.concatenate(held, axis=1)
+    local = None
+    partner = None
+    for j in range(side_width // width):
+        owner = side * (side_width // width) + j
+        column = ((me - owner) % group) * (2 * width)
+        own_part = lax.dynamic_slice_in_dim(mixed, column, width, 1)
+        their_part = lax.dynamic_slice_in_dim(mixed, column + width, width, 1)
+        rows = side_rows[j * width:(j + 1) * width]
+        mine = jnp.dot(own_part, rows, preferred_element_type=jnp.float32)
+        theirs = jnp.dot(their_part, rows, preferred_element_type=jnp.float32)
+        local = mine if local is None else local + mine
+        partner = theirs if partner is None else partner + theirs
+    returned = swapped(partner.astype(jnp.bfloat16), "dp")
+    return local + returned.astype(jnp.float32)
+
+
 def shards(queries, keyvals, documents, output_weight):
+    block_rows = output_weight.shape[0]
+    width = queries.shape[2]
+    side_width = block_rows * lax.axis_size("ctx")
+    if lax.axis_size("dp") == 2 and side_width % width == 0:
+        head_values = attention(queries, keyvals, documents)
+        result = split_projection(head_values, output_weight)
+        return result.astype(jnp.bfloat16)[None]
     all_rows = lax.all_gather(output_weight, ("dp", "ctx"), axis=0, tiled=True)
     head_values = attention(queries, keyvals, documents)
-    width = head_values.shape[1]
     group = lax.axis_size("tensor")
     me = lax.axis_index("tensor")
     result = None

time: 103 us -> 91 us (0.88)
  waiting for transfers between devices: 61.4 us -> 40.9 us
  local copies, waits for them, and re-layouts: 1.97 us -> 5.92 us
  starting transfers between devices: 15.8 us -> 18.8 us
  matrix products: 6.84 us -> 8.51 us
    all_gather x1, waiting for transfers between devices: 56.5 us -> 5.7 us  [split_projection(): side_rows = lax.all_gather(output_weight, 'ctx', axis=0, tiled=True)]
    ppermute x3, waiting for transfers between devices: 0.01 us -> 18.4 us  [rotated(): return lax.ppermute(block, axis, route)]
    ppermute x0 -> x2, waiting for transfers between devices: none -> 16.7 us  [swapped(): return lax.ppermute(block, axis, [(0, 1), (1, 0)])]
    ppermute x4, waiting for transfers between devices: 4.15 us -> 0.11 us  [shifted(): return lax.ppermute(block, axis, route)]
    unnamed x3 -> x7, local copies, waits for them, and re-layouts: 0.93 us -> 4.08 us
    ppermute x0 -> x2, starting transfers between devices: none -> 3.08 us  [swapped(): return lax.ppermute(block, axis, [(0, 1), (1, 0)])]
    dot_general x4, matrix products: 5.26 us -> 6.93 us  [the longest x2 3.6 us: split_projection(): mine = jnp.dot(own_part, rows, preferred_element_type=jnp.float32)]
  transfers between devices with their start and end apart: 8 -> 10, of which waited for: 2 -> 7; matrix products, arithmetic and copies ran while one was open for 10% -> 13% of each run, Pallas kernels for 0% -> 0%
where the time goes in v3:
time: 91 us; the launch traced here: 90.6 us
  waiting for transfers between devices  40.9 us (45%)
  starting transfers between devices  18.8 us (21%)
  between operations  13.5 us (15%)
  matrix products  8.51 us (9%)
  local copies, waits for them, and re-layouts  5.92 us (7%)
  other arithmetic  2.97 us (3%)
    ppermute x3, waiting for transfers between devices, rotated(): return lax.ppermute(block, axis, route)  18.4 us
    ppermute x2, waiting for transfers between devices, swapped(): return lax.ppermute(block, axis, [(0, 1), (1, 0)])  16.7 us
    ppermute x4, starting transfers between devices, shifted(): return lax.ppermute(block, axis, route)  12.6 us
    all_gather x1, waiting for transfers between devices, split_projection(): side_rows = lax.all_gather(output_weight, 'ctx', axis=0, tiled=True)  5.7 us
    unnamed x7, local copies, waits for them, and re-layouts  4.08 us
    dot_general x2, matrix products, split_projection(): mine = jnp.dot(own_part, rows, preferred_element_type=jnp.float32)  3.6 us
    dot_general x2, matrix products, split_projection(): theirs = jnp.dot(their_part, rows, preferred_element_type=jnp.float32)  3.33 us
    ppermute x2, starting transfers between devices, swapped(): return lax.ppermute(block, axis, [(0, 1), (1, 0)])  3.08 us
  transfers between devices with their start and end apart: 10, of which 7 were waited for; matrix products, arithmetic and copies ran while one was open for 13% of the time, Pallas kernels for 0%

profile of v3, /device:TPU:0, one launch (start us, length us, event | category | flops | bytes accessed | tf_op | source)
XLA Modules:
  0.0 90.6 jit_solution(18194769413044959261)
XLA Ops:
  6.5 0.0 all-gather.2.cloned.1.call-start
  6.5 4.9 %collective-permute-start.2 = (s32[256]{0:T(256)}, s32[256]{0:T(256)S(1)}, u32[]{:S(2)}, u32[]{:S(2)}) collective-permute-start(s32[256]{0:T(256)} %bitcast.68), channel_id=1, source_target_pairs={{0,4},{4,8},{8,12},{1,5},{5,9},{9,13},{2,6},{6,10},{10,14},{3,7},{... | collective-permute-start | bytes 3080 | tf_op jit(solution)/shard_map/ppermute | solution.py:17
  11.5 4.5 %collective-permute-start.3 = (s32[256]{0:T(256)}, s32[256]{0:T(256)S(1)}, u32[]{:S(2)}, u32[]{:S(2)}) collective-permute-start(s32[256]{0:T(256)} %bitcast.69), channel_id=1, source_target_pairs={{0,8},{4,12},{1,9},{5,13},{2,10},{6,14},{3,11},{7,15},{16,24},{20,... | collective-permute-start | bytes 3080 | tf_op jit(solution)/shard_map/ppermute | solution.py:17
  16.0 0.9 %copy.17 = bf16[1,256,2,128]{3,1,2,0:T(8,128)(2,1)S(1)} copy(bf16[1,256,2,128]{3,2,1,0:T(2,128)(2,1)} %param.5) | data formatting | bytes 262144 | tf_op args[1]
  16.9 1.3 %collective-permute-start = (bf16[256,2,128]{2,0,1:T(8,128)(2,1)S(1)}, bf16[256,2,128]{2,0,1:T(8,128)(2,1)S(1)}, u32[]{:S(2)}, u32[]{:S(2)}) collective-permute-start(bf16[256,2,128]{2,0,1:T(8,128)(2,1)S(1)} %bitcast.64), channel_id=1, source_target_pairs={{0,4},{4,8},{8,12},{1,5},{5,9},{9,13},{2,6},{6,10},{10,14},{3,7},{... | collective-permute-start | bytes 393224 | tf_op jit(solution)/shard_map/ppermute | solution.py:17
  18.2 1.9 %collective-permute-start.1 = (bf16[256,2,128]{2,0,1:T(8,128)(2,1)S(1)}, bf16[256,2,128]{2,0,1:T(8,128)(2,1)S(1)}, u32[]{:S(2)}, u32[]{:S(2)}) collective-permute-start(bf16[256,2,128]{2,0,1:T(8,128)(2,1)S(1)} %bitcast.65), channel_id=1, source_target_pairs={{0,8},{4,12},{1,9},{5,13},{2,10},{6,14},{3,11},{7,15},{16,24},{20,... | collective-permute-start | bytes 393224 | tf_op jit(solution)/shard_map/ppermute | solution.py:17
  20.1 0.0 all-gather.2.cloned.1.call-update
  20.2 1.0 %reshape.57 = bf16[256,4,128]{2,1,0:T(4,128)(2,1)S(1)} reshape(bf16[1,256,512]{2,1,0:T(8,128)(2,1)} %param.4) | data formatting | bytes 524288 | tf_op jit(solution)/shard_map/reshape.2
  21.2 0.0 collective-permute-done.2
  21.3 0.0 collective-permute-done.3
  21.3 0.7 pad_add_fusion
  22.0 1.4 %and_and_fusion = pred[256,768]{0,1:T(8,128)(4,1)S(1)} fusion(s32[256]{0:T(256)S(1)} %iota_add_fusion.2, s32[256]{0:T(256)} %bitcast.71, s32[768]{0:T(1024)S(1)} %pad_add_fusion.1, s32[768]{0:T(1024)S(1)} %pad_add_fusion, pred[768]{0:T(1024)(128)(4,1)S(1)} %broadcast_compare_fusion), kind=kLoop, calls=%fused_computation.23 | loop fusion | flops 786432 | bytes 205568 | tf_op jit(solution)/shard_map/and | solution.py:60
  23.4 0.0 collective-permute-done
  23.4 0.1 collective-permute-done.1
  23.5 0.7 fusion
  24.2 0.8 fusion.1
  24.9 0.9 %fusion.17 = bf16[256,1,4,128]{0,3,2,1:T(8,128)(2,1)S(1)} fusion(f32[768,256,4]{1,0,2:T(8,128)S(1)} %get-tuple-element.6, f32[4,256]{1,0:T(4,128)S(1)} %get-tuple-element.5, pred[256,768]{0,1:T(8,128)(4,1)S(1)} %and_and_fusion, f32[256,4]{0,1:T(4,128)S(1)} %bitcast.67, bf16[768,2,128]{2,0,1:T(8,128)(2,1)S(1)} %pad_maximum_fusion.1), kind=kOutput, calls=%fused_computation.16 | convolution fusion | flops 205520896 | bytes 3809280 | tf_op jit(solution)/shard_map/hgqk,khd->qhgd/dot_general | solution.py:68
  25.9 1.6 %collective-permute-start.4 = (bf16[256,512]{0,1:T(8,128)(2,1)S(1)}, bf16[256,512]{0,1:T(8,128)(2,1)S(1)}, u32[]{:S(2)}, u32[]{:S(2)}) collective-permute-start(bf16[256,512]{0,1:T(8,128)(2,1)S(1)} %bitcast.61), channel_id=1, source_target_pairs={{0,16},{16,0},{1,17},{17,1},{2,18},{18,2},{3,19},{19,3},{4,20},{20... | collective-permute-start | bytes 786440 | tf_op jit(solution)/shard_map/ppermute | solution.py:81
  27.4 5.9 %collective-permute-done.4 = bf16[256,512]{0,1:T(8,128)(2,1)S(1)} collective-permute-done((bf16[256,512]{0,1:T(8,128)(2,1)S(1)}, bf16[256,512]{0,1:T(8,128)(2,1)S(1)}, u32[]{:S(2)}, u32[]{:S(2)}) %collective-permute-start.4) | collective-permute-done | bytes 262176 | tf_op jit(solution)/shard_map/ppermute | solution.py:81
  33.4 0.1 collective-permute-start.5
  33.5 1.6 %collective-permute-start.6 = (bf16[256,1024]{0,1:T(8,128)(2,1)S(1)}, bf16[256,1024]{0,1:T(8,128)(2,1)S(1)}, u32[]{:S(2)}, u32[]{:S(2)}) collective-permute-start(bf16[256,1024]{0,1:T(8,128)(2,1)S(1)} %pad_maximum_fusion), channel_id=1, source_target_pairs={{0,2},{1,3},{2,0},{3,1},{4,6},{5,7},{6,4},{7,5},{8,10},{9,11},{10,... | collective-permute-start | bytes 1572872 | tf_op jit(solution)/shard_map/ppermute | solution.py:23
  35.0 1.4 %collective-permute-start.7 = (bf16[256,1024]{0,1:T(8,128)(2,1)S(1)}, bf16[256,1024]{0,1:T(8,128)(2,1)S(1)}, u32[]{:S(2)}, u32[]{:S(2)}) collective-permute-start(bf16[256,1024]{0,1:T(8,128)(2,1)S(1)} %pad_maximum_fusion), channel_id=1, source_target_pairs={{0,3},{1,0},{2,1},{3,2},{4,7},{5,4},{6,5},{7,6},{8,11},{9,8},{10,9... | collective-permute-start | bytes 1572872 | tf_op jit(solution)/shard_map/ppermute | solution.py:23
  36.4 0.7 constant_dynamic-update-slice_fusion.4
  37.1 0.7 constant_dynamic-update-slice_fusion.3
  37.9 9.2 %collective-permute-done.5 = bf16[256,1024]{0,1:T(8,128)(2,1)S(1)} collective-permute-done((bf16[256,1024]{0,1:T(8,128)(2,1)S(1)}, bf16[256,1024]{0,1:T(8,128)(2,1)S(1)}, u32[]{:S(2)}, u32[]{:S(2)}) %collective-permute-start.5) | collective-permute-done | bytes 524320 | tf_op jit(solution)/shard_map/ppermute | solution.py:23
  47.1 0.8 constant_dynamic-update-slice_fusion.2
  47.9 0.4 collective-permute-done.6
  48.3 0.8 constant_dynamic-update-slice_fusion.1
  49.1 8.8 %collective-permute-done.7 = bf16[256,1024]{0,1:T(8,128)(2,1)S(1)} collective-permute-done((bf16[256,1024]{0,1:T(8,128)(2,1)S(1)}, bf16[256,1024]{0,1:T(8,128)(2,1)S(1)}, u32[]{:S(2)}, u32[]{:S(2)}) %collective-permute-start.7) | collective-permute-done | bytes 524320 | tf_op jit(solution)/shard_map/ppermute | solution.py:23
  57.9 0.8 constant_dynamic-update-slice_fusion
  58.8 5.7 %all-gather.2.cloned.1.call-done = bf16[1024,1024]{1,0:T(8,128)(2,1)} async-done(((bf16[256,1024]{1,0:T(8,128)(2,1)}), bf16[1024,1024]{1,0:T(8,128)(2,1)}) %all-gather.2.cloned.1.call-update) | async-done | bytes 2097168 | tf_op jit(solution)/shard_map/all_gather | solution.py:90
  64.5 0.0 copy-start
  64.5 1.9 %fusion.20 = f32[256,1024]{1,0:T(8,128)S(1)} fusion(bf16[1024,1024]{1,0:T(8,128)(2,1)} %all-gather.2.cloned.1.call-done, bf16[256,4096]{0,1:T(8,128)(2,1)} %constant_dynamic-update-slice_fusion, s32[]{:T(128)S(6)} %select_n.37), kind=kOutput, calls=%fused_computation.17 | convolution fusion | flops 268435456 | bytes 2359300 | tf_op jit(solution)/shard_map/dot_general | solution.py:105
  66.4 0.1 copy-done
  66.4 1.4 %fusion.9 = bf16[256,1024]{1,0:T(8,128)(2,1)S(1)} fusion(f32[256,1024]{1,0:T(8,128)S(1)} %fusion.20, bf16[1024,1024]{1,0:T(8,128)(2,1)S(1)} %copy-done, bf16[256,4096]{0,1:T(8,128)(2,1)} %constant_dynamic-update-slice_fusion, s32[]{:T(128)S(6)} %select_n.36), kind=kOutput, calls=%fused_computation.12 | convolution fusion | flops 268959744 | bytes 2883588 | tf_op jit(solution)/shard_map/dot_general | solution.py:105
  67.9 1.5 %collective-permute-start.8 = (bf16[256,1024]{1,0:T(8,128)(2,1)S(1)}, bf16[256,1024]{1,0:T(8,128)(2,1)S(1)}, u32[]{:S(2)}, u32[]{:S(2)}) collective-permute-start(bf16[256,1024]{1,0:T(8,128)(2,1)S(1)} %fusion.9), channel_id=1, source_target_pairs={{0,16},{16,0},{1,17},{17,1},{2,18},{18,2},{3,19},{19,3},{4,20},{20... | collective-permute-start | bytes 1572872 | tf_op jit(solution)/shard_map/ppermute | solution.py:81
  69.4 1.4 %fusion.22 = f32[256,1024]{1,0:T(8,128)S(1)} fusion(bf16[1024,1024]{1,0:T(8,128)(2,1)S(1)} %copy-done, bf16[256,4096]{0,1:T(8,128)(2,1)} %constant_dynamic-update-slice_fusion, s32[]{:T(128)S(6)} %select_n.35), kind=kOutput, calls=%fused_computation.19 | convolution fusion | flops 268435456 | bytes 2359300 | tf_op jit(solution)/shard_map/dot_general | solution.py:104
  70.8 10.8 %collective-permute-done.8 = bf16[256,1024]{1,0:T(8,128)(2,1)S(1)} collective-permute-done((bf16[256,1024]{1,0:T(8,128)(2,1)S(1)}, bf16[256,1024]{1,0:T(8,128)(2,1)S(1)}, u32[]{:S(2)}, u32[]{:S(2)}) %collective-permute-start.8) | collective-permute-done | bytes 524320 | tf_op jit(solution)/shard_map/ppermute | solution.py:81
  81.6 2.2 %fusion.10 = bf16[1,256,1024]{2,1,0:T(8,128)(2,1)} fusion(f32[256,1024]{1,0:T(8,128)S(1)} %fusion.22, bf16[256,1024]{1,0:T(8,128)(2,1)S(1)} %collective-permute-done.8, bf16[1024,1024]{1,0:T(8,128)(2,1)S(1)} %copy-done, bf16[256,4096]{0,1:T(8,128)(2,1)} %constant_dynamic-update-slice_fusion, s32[]{:T(128)S(6)} %select_n.33), kind=kOutput, calls=%fused_computation.13 | convolution fusion | flops 269484032 | bytes 3407876 | tf_op jit(solution)/shard_map/dot_general | solution.py:104
  (6 shorter events, 0.1 us)
Async XLA Ops:
  6.5 57.9 %all-gather.2.cloned.1.call-start = ((), (), s32[]{:S(2)}) async-start(), calls=%async_computation | async-start | bytes 2621440 | tf_op jit(solution)/shard_map/all_gather | solution.py:90
  6.5 14.7 %collective-permute-start.2 = (s32[256]{0:T(256)}, s32[256]{0:T(256)S(1)}, u32[]{:S(2)}, u32[]{:S(2)}) collective-permute-start(s32[256]{0:T(256)} %bitcast.68), channel_id=1, source_target_pairs={{0,4},{4,8},{8,12},{1,5},{5,9},{9,13},{2,6},{6,10},{10,14},{3,7},{... | collective-permute-start | bytes 3080 | tf_op jit(solution)/shard_map/ppermute | solution.py:17
  11.5 9.8 %collective-permute-start.3 = (s32[256]{0:T(256)}, s32[256]{0:T(256)S(1)}, u32[]{:S(2)}, u32[]{:S(2)}) collective-permute-start(s32[256]{0:T(256)} %bitcast.69), channel_id=1, source_target_pairs={{0,8},{4,12},{1,9},{5,13},{2,10},{6,14},{3,11},{7,15},{16,24},{20,... | collective-permute-start | bytes 3080 | tf_op jit(solution)/shard_map/ppermute | solution.py:17
  16.9 6.5 %collective-permute-start = (bf16[256,2,128]{2,0,1:T(8,128)(2,1)S(1)}, bf16[256,2,128]{2,0,1:T(8,128)(2,1)S(1)}, u32[]{:S(2)}, u32[]{:S(2)}) collective-permute-start(bf16[256,2,128]{2,0,1:T(8,128)(2,1)S(1)} %bitcast.64), channel_id=1, source_target_pairs={{0,4},{4,8},{8,12},{1,5},{5,9},{9,13},{2,6},{6,10},{10,14},{3,7},{... | collective-permute-start | bytes 393224 | tf_op jit(solution)/shard_map/ppermute | solution.py:17
  18.2 5.3 %collective-permute-start.1 = (bf16[256,2,128]{2,0,1:T(8,128)(2,1)S(1)}, bf16[256,2,128]{2,0,1:T(8,128)(2,1)S(1)}, u32[]{:S(2)}, u32[]{:S(2)}) collective-permute-start(bf16[256,2,128]{2,0,1:T(8,128)(2,1)S(1)} %bitcast.65), channel_id=1, source_target_pairs={{0,8},{4,12},{1,9},{5,13},{2,10},{6,14},{3,11},{7,15},{16,24},{20,... | collective-permute-start | bytes 393224 | tf_op jit(solution)/shard_map/ppermute | solution.py:17
  25.9 7.5 %collective-permute-start.4 = (bf16[256,512]{0,1:T(8,128)(2,1)S(1)}, bf16[256,512]{0,1:T(8,128)(2,1)S(1)}, u32[]{:S(2)}, u32[]{:S(2)}) collective-permute-start(bf16[256,512]{0,1:T(8,128)(2,1)S(1)} %bitcast.61), channel_id=1, source_target_pairs={{0,16},{16,0},{1,17},{17,1},{2,18},{18,2},{3,19},{19,3},{4,20},{20... | collective-permute-start | bytes 786440 | tf_op jit(solution)/shard_map/ppermute | solution.py:81
  33.4 13.7 %collective-permute-start.5 = (bf16[256,1024]{0,1:T(8,128)(2,1)S(1)}, bf16[256,1024]{0,1:T(8,128)(2,1)S(1)}, u32[]{:S(2)}, u32[]{:S(2)}) collective-permute-start(bf16[256,1024]{0,1:T(8,128)(2,1)S(1)} %pad_maximum_fusion), channel_id=1, source_target_pairs={{0,1},{1,2},{2,3},{3,0},{4,5},{5,6},{6,7},{7,4},{8,9},{9,10},{10,1... | collective-permute-start | bytes 1572872 | tf_op jit(solution)/shard_map/ppermute | solution.py:23
  33.5 14.8 %collective-permute-start.6 = (bf16[256,1024]{0,1:T(8,128)(2,1)S(1)}, bf16[256,1024]{0,1:T(8,128)(2,1)S(1)}, u32[]{:S(2)}, u32[]{:S(2)}) collective-permute-start(bf16[256,1024]{0,1:T(8,128)(2,1)S(1)} %pad_maximum_fusion), channel_id=1, source_target_pairs={{0,2},{1,3},{2,0},{3,1},{4,6},{5,7},{6,4},{7,5},{8,10},{9,11},{10,... | collective-permute-start | bytes 1572872 | tf_op jit(solution)/shard_map/ppermute | solution.py:23
  35.0 22.9 %collective-permute-start.7 = (bf16[256,1024]{0,1:T(8,128)(2,1)S(1)}, bf16[256,1024]{0,1:T(8,128)(2,1)S(1)}, u32[]{:S(2)}, u32[]{:S(2)}) collective-permute-start(bf16[256,1024]{0,1:T(8,128)(2,1)S(1)} %pad_maximum_fusion), channel_id=1, source_target_pairs={{0,3},{1,0},{2,1},{3,2},{4,7},{5,4},{6,5},{7,6},{8,11},{9,8},{10,9... | collective-permute-start | bytes 1572872 | tf_op jit(solution)/shard_map/ppermute | solution.py:23
  64.5 2.0 %copy-start = (bf16[1024,1024]{1,0:T(8,128)(2,1)S(1)}, bf16[1024,1024]{1,0:T(8,128)(2,1)}, u32[]{:S(2)}) copy-start(bf16[1024,1024]{1,0:T(8,128)(2,1)} %all-gather.2.cloned.1.call-done) | copy-start | bytes 6291460
  67.9 13.7 %collective-permute-start.8 = (bf16[256,1024]{1,0:T(8,128)(2,1)S(1)}, bf16[256,1024]{1,0:T(8,128)(2,1)S(1)}, u32[]{:S(2)}, u32[]{:S(2)}) collective-permute-start(bf16[256,1024]{1,0:T(8,128)(2,1)S(1)} %fusion.9), channel_id=1, source_target_pairs={{0,16},{16,0},{1,17},{17,1},{2,18},{18,2},{3,19},{19,3},{4,20},{20... | collective-permute-start | bytes 1572872 | tf_op jit(solution)/shard_map/ppermute | solution.py:81
Sparse Core Ops, SparseCore 0:
  20.3 44.1 all-gather.1

commit v4 on v1

--- a/solution.py
+++ b/solution.py
@@ -36,10 +36,14 @@
     pair_blocks = [keyvals[0]]
     label_blocks = [documents[0]]
     place_blocks = [position * length + offsets]
+    label_slab = jnp.broadcast_to(
+        documents[0].astype(jnp.bfloat16)[:, None, None], (length, 1, pair_width)
+    )
+    packed = jnp.concatenate([keyvals[0], label_slab], axis=1)
     for hop in range(1, reach_hops + 1):
-        pair_block, label_block = shifted((keyvals[0], documents[0]), "ctx", hop)
-        pair_blocks.append(pair_block)
-        label_blocks.append(label_block)
+        arrived = shifted(packed, "ctx", hop)
+        pair_blocks.append(arrived[:, :2])
+        label_blocks.append(arrived[:, 2, 0].astype(jnp.int32))
         place_blocks.append((position - hop) * length + offsets)
     pairs = jnp.concatenate(pair_blocks, axis=0)
     key_labels = jnp.concatenate(label_blocks, axis=0)
@@ -77,10 +81,71 @@
     )
 
 
+def swapped(block, axis):
+    return lax.ppermute(block, axis, [(0, 1), (1, 0)])
+
+
+def sent(block, route):
+    return lax.ppermute(block, ("dp", "tensor"), route)
+
+
+def needed_heads(head_values):
+    group = lax.axis_size("tensor")
+    me = lax.axis_index("tensor")
+    side = lax.axis_index("dp")
+    foreign = swapped(head_values, "dp")
+    mine = jnp.concatenate([head_values, foreign], axis=1)
+    owners = [(s, 2 * s + k) for s in range(2) for k in range(2)]
+    over_y = sent(mine, [(s * group + p, s * group + (p ^ 2)) for s, p in owners])
+    beside = sent(mine, [(s * group + p, s * group + (p ^ 1)) for s, p in owners])
+    relayed = sent(
+        over_y, [(s * group + (p ^ 2), s * group + (p ^ 3)) for s, p in owners]
+    )
+    on_owner = me // 2 == side
+    same_core = jnp.where(on_owner, mine, over_y)
+    other_core = jnp.where(on_owner, beside, relayed)
+    first_core = me % 2 == 0
+    return [
+        jnp.where(first_core, same_core, other_core),
+        jnp.where(first_core, other_core, same_core),
+    ]
+
+
+def split_projection(head_values, output_weight):
+    width = head_values.shape[1]
+    columns = output_weight.shape[1]
+    half = columns // 2
+    side_rows = [
+        lax.all_gather(output_weight[:, :half], "ctx", axis=0, tiled=True),
+        lax.all_gather(output_weight[:, half:], "ctx", axis=0, tiled=True),
+    ]
+    peers = needed_heads(head_values)
+    outputs = []
+    for rows in side_rows:
+        local = None
+        partner = None
+        for j, both in enumerate(peers):
+            block = rows[j * width:(j + 1) * width]
+            mine = jnp.dot(both[:, :width], block, preferred_element_type=jnp.float32)
+            theirs = jnp.dot(both[:, width:], block, preferred_element_type=jnp.float32)
+            local = mine if local is None else local + mine
+            partner = theirs if partner is None else partner + theirs
+        returned = swapped(partner.astype(jnp.bfloat16), "dp")
+        outputs.append(local + returned.astype(jnp.float32))
+    return jnp.concatenate(outputs, axis=1)
+
+
 def shards(queries, keyvals, documents, output_weight):
+    block_rows = output_weight.shape[0]
+    width = queries.shape[2]
+    side_width = block_rows * lax.axis_size("ctx")
+    fits = output_weight.shape[1] % 256 == 0 and lax.axis_size("tensor") == 4
+    if lax.axis_size("dp") == 2 and side_width == 2 * width and fits:
+        head_values = attention(queries, keyvals, documents)
+        result = split_projection(head_values, output_weight)
+        return result.astype(jnp.bfloat16)[None]
     all_rows = lax.all_gather(output_weight, ("dp", "ctx"), axis=0, tiled=True)
     head_values = attention(queries, keyvals, documents)
-    width = head_values.shape[1]
     group = lax.axis_size("tensor")
     me = lax.axis_index("tensor")
     result = None

time: 103 us -> 94.9 us (0.921)
  waiting for transfers between devices: 61.4 us -> 39.6 us
  starting transfers between devices: 15.8 us -> 24.2 us
  local copies, waits for them, and re-layouts: 1.97 us -> 3.92 us
  matrix products: 6.84 us -> 8.48 us
  other arithmetic: 2.93 us -> 4.48 us
    all_gather x1 -> x2, waiting for transfers between devices: 56.5 us -> 18.9 us  [the longest x1 18.8 us: split_projection(): lax.all_gather(output_weight[:, half:], 'ctx', axis=0, tiled=True)]
    ppermute x3 -> x6, waiting for transfers between devices: 0.01 us -> 19 us  [the longest x3 11.3 us: swapped(): return lax.ppermute(block, axis, [(0, 1), (1, 0)])]
    ppermute x3 -> x6, starting transfers between devices: 3.11 us -> 14.7 us  [the longest x3 8.67 us: swapped(): return lax.ppermute(block, axis, [(0, 1), (1, 0)])]
    ppermute x4 -> x2, starting transfers between devices: 12.6 us -> 9.44 us  [shifted(): return lax.ppermute(block, axis, route)]
    ppermute x4 -> x2, waiting for transfers between devices: 4.15 us -> 1.75 us  [shifted(): return lax.ppermute(block, axis, route)]
    slice x0 -> x3, local copies, waits for them, and re-layouts: none -> 1.87 us  [the longest x1 1.85 us: split_projection(): output_weight[:, :half]]
    dot_general x4 -> x8, matrix products: 5.26 us -> 6.89 us  [the longest x4 5.61 us: split_projection(): theirs = jnp.dot(both[:, width:], block, preferred_element_type=jnp.float32)]
  transfers between devices with their start and end apart: 8 -> 10, of which waited for: 2 -> 5; matrix products, arithmetic and copies ran while one was open for 10% -> 15% of each run, Pallas kernels for 0% -> 0%
where the time goes in v4:
time: 94.9 us; the launch traced here: 94.4 us
  waiting for transfers between devices  39.6 us (42%)
  starting transfers between devices  24.2 us (26%)
  between operations  13.7 us (14%)
  matrix products  8.48 us (9%)
  other arithmetic  4.48 us (5%)
  local copies, waits for them, and re-layouts  3.92 us (4%)
    all_gather x1, waiting for transfers between devices, split_projection(): lax.all_gather(output_weight[:, half:], 'ctx', axis=0, tiled=True)  18.8 us
    ppermute x3, waiting for transfers between devices, swapped(): return lax.ppermute(block, axis, [(0, 1), (1, 0)])  11.3 us
    ppermute x2, starting transfers between devices, shifted(): return lax.ppermute(block, axis, route)  9.44 us
    ppermute x3, starting transfers between devices, swapped(): return lax.ppermute(block, axis, [(0, 1), (1, 0)])  8.67 us
    ppermute x3, waiting for transfers between devices, sent(): return lax.ppermute(block, ('dp', 'tensor'), route)  7.68 us
    ppermute x3, starting transfers between devices, sent(): return lax.ppermute(block, ('dp', 'tensor'), route)  6.06 us
    dot_general x4, matrix products, split_projection(): theirs = jnp.dot(both[:, width:], block, preferred_element_type=jnp.float32)  5.61 us
  transfers between devices with their start and end apart: 10, of which 5 were waited for; matrix products, arithmetic and copies ran while one was open for 15% of the time, Pallas kernels for 0%

profile of v4, /device:TPU:0, one launch (start us, length us, event | category | flops | bytes accessed | tf_op | source)
XLA Modules:
  0.0 94.4 jit_solution(13912264379272496641)
XLA Ops:
  6.5 0.0 all-gather.3.cloned.1.call-start
  6.5 0.8 convert_element_type.48
  7.3 0.9 copy.21
  8.2 0.1 broadcast_in_dim.14
  8.3 6.0 %collective-permute-start.1 = (bf16[256,3,128]{2,0,1:T(8,128)(2,1)S(1)}, bf16[256,3,128]{2,0,1:T(8,128)(2,1)S(1)}, u32[]{:S(2)}, u32[]{:S(2)}) collective-permute-start(bf16[256,3,128]{2,0,1:T(8,128)(2,1)S(1)} %pad_maximum_fusion.3), channel_id=1, source_target_pairs={{0,8},{4,12},{1,9},{5,13},{2,10},{6,14},{3,11},{7,15},{16,24},{20,... | collective-permute-start | bytes 589832 | tf_op jit(solution)/shard_map/ppermute | solution.py:17
  14.3 3.5 %collective-permute-start = (bf16[256,3,128]{2,0,1:T(8,128)(2,1)S(1)}, bf16[256,3,128]{2,0,1:T(8,128)(2,1)S(1)}, u32[]{:S(2)}, u32[]{:S(2)}) collective-permute-start(bf16[256,3,128]{2,0,1:T(8,128)(2,1)S(1)} %pad_maximum_fusion.3), channel_id=1, source_target_pairs={{0,4},{4,8},{8,12},{1,5},{5,9},{9,13},{2,6},{6,10},{10,14},{3,7},{... | collective-permute-start | bytes 589832 | tf_op jit(solution)/shard_map/ppermute | solution.py:17
  17.8 1.8 %fusion.49 = (bf16[256,512]{1,0:T(8,128)(2,1)}, bf16[256,512]{1,0:T(8,128)(2,1)}) fusion(bf16[256,1024]{1,0:T(8,128)(2,1)} %param.7), kind=kLoop, calls=%fused_computation.68 | loop fusion | bytes 1048576 | tf_op jit(solution)/shard_map/slice | solution.py:119
  19.7 0.0 all-gather.3.cloned.1.call-update
  19.7 0.0 all-gather.5.cloned.1.call-start
  19.8 1.0 %reshape.99 = bf16[256,4,128]{2,1,0:T(4,128)(2,1)S(1)} reshape(bf16[1,256,512]{2,1,0:T(8,128)(2,1)} %param.4) | data formatting | bytes 524288 | tf_op jit(solution)/shard_map/reshape.3
  20.8 0.0 collective-permute-done.1
  20.8 0.1 convert_reduce_fusion
  20.9 1.8 %collective-permute-done = bf16[256,3,128]{2,0,1:T(8,128)(2,1)S(1)} collective-permute-done((bf16[256,3,128]{2,0,1:T(8,128)(2,1)S(1)}, bf16[256,3,128]{2,0,1:T(8,128)(2,1)S(1)}, u32[]{:S(2)}, u32[]{:S(2)}) %collective-permute-start) | collective-permute-done | bytes 196640 | tf_op jit(solution)/shard_map/ppermute | solution.py:17
  22.7 0.1 convert_reduce_fusion.1
  22.8 0.7 pad_add_fusion
  23.6 0.0 copy-done.2
  23.6 0.7 and_and_fusion
  24.3 0.7 fusion
  25.0 0.8 fusion.1
  25.8 0.9 fusion.21
  26.7 1.6 %collective-permute-start.2 = (bf16[256,512]{0,1:T(8,128)(2,1)S(1)}, bf16[256,512]{0,1:T(8,128)(2,1)S(1)}, u32[]{:S(2)}, u32[]{:S(2)}) collective-permute-start(bf16[256,512]{0,1:T(8,128)(2,1)S(1)} %bitcast.65), channel_id=1, source_target_pairs={{0,16},{16,0},{1,17},{17,1},{2,18},{18,2},{3,19},{19,3},{4,20},{20... | collective-permute-start | bytes 786440 | tf_op jit(solution)/shard_map/ppermute | solution.py:85
  28.3 5.9 %collective-permute-done.2 = bf16[256,512]{0,1:T(8,128)(2,1)S(1)} collective-permute-done((bf16[256,512]{0,1:T(8,128)(2,1)S(1)}, bf16[256,512]{0,1:T(8,128)(2,1)S(1)}, u32[]{:S(2)}, u32[]{:S(2)}) %collective-permute-start.2) | collective-permute-done | bytes 262176 | tf_op jit(solution)/shard_map/ppermute | solution.py:85
  34.2 3.5 %collective-permute-start.3 = (bf16[256,1024]{0,1:T(8,128)(2,1)S(1)}, bf16[256,1024]{0,1:T(8,128)(2,1)S(1)}, u32[]{:S(2)}, u32[]{:S(2)}) collective-permute-start(bf16[256,1024]{0,1:T(8,128)(2,1)S(1)} %pad_maximum_fusion), channel_id=1, source_target_pairs={{0,2},{1,3},{18,16},{19,17},{4,6},{5,7},{22,20},{23,21},{8,10},{9,... | collective-permute-start | bytes 1572872 | tf_op jit(solution)/shard_map/ppermute | solution.py:89
  37.6 0.0 all-gather.5.cloned.1.call-update
  37.7 1.9 %collective-permute-start.4 = (bf16[256,1024]{0,1:T(8,128)(2,1)S(1)}, bf16[256,1024]{0,1:T(8,128)(2,1)S(1)}, u32[]{:S(2)}, u32[]{:S(2)}) collective-permute-start(bf16[256,1024]{0,1:T(8,128)(2,1)S(1)} %pad_maximum_fusion), channel_id=1, source_target_pairs={{0,1},{1,0},{18,19},{19,18},{4,5},{5,4},{22,23},{23,22},{8,9},{9,8... | collective-permute-start | bytes 1572872 | tf_op jit(solution)/shard_map/ppermute | solution.py:89
  39.6 7.7 %collective-permute-done.3 = bf16[256,1024]{0,1:T(8,128)(2,1)S(1)} collective-permute-done((bf16[256,1024]{0,1:T(8,128)(2,1)S(1)}, bf16[256,1024]{0,1:T(8,128)(2,1)S(1)}, u32[]{:S(2)}, u32[]{:S(2)}) %collective-permute-start.3) | collective-permute-done | bytes 524320 | tf_op jit(solution)/shard_map/ppermute | solution.py:89
  47.3 0.7 collective-permute-start.5
  48.0 0.0 collective-permute-done.4
  48.0 0.0 collective-permute-done.5
  48.0 0.3 broadcast_select_fusion.3
  48.3 0.0 all-gather.3.cloned.1.call-done
  48.4 0.0 copy-start
  48.4 1.4 %fusion.30 = f32[256,512]{1,0:T(8,128)S(1)} fusion(bf16[1024,512]{1,0:T(8,128)(2,1)} %all-gather.3.cloned.1.call-done, bf16[256,1024]{0,1:T(8,128)(2,1)S(1)} %get-tuple-element.6), kind=kOutput, calls=%fused_computation.36 | convolution fusion | flops 134217728 | bytes 1310720 | tf_op jit(solution)/shard_map/dot_general | solution.py:130
  49.8 1.4 %fusion.14 = bf16[256,512]{1,0:T(8,128)(2,1)S(1)} fusion(f32[256,512]{1,0:T(8,128)S(1)} %fusion.30, bf16[1024,512]{1,0:T(8,128)(2,1)} %all-gather.3.cloned.1.call-done, bf16[256,1024]{0,1:T(8,128)(2,1)S(1)} %get-tuple-element.5), kind=kOutput, calls=%fused_computation.17 | convolution fusion | flops 134479872 | bytes 1572864 | tf_op jit(solution)/shard_map/dot_general | solution.py:130
  51.2 5.6 %collective-permute-start.6 = (bf16[256,512]{1,0:T(8,128)(2,1)S(1)}, bf16[256,512]{1,0:T(8,128)(2,1)S(1)}, u32[]{:S(2)}, u32[]{:S(2)}) collective-permute-start(bf16[256,512]{1,0:T(8,128)(2,1)S(1)} %fusion.14), channel_id=1, source_target_pairs={{0,16},{16,0},{1,17},{17,1},{2,18},{18,2},{3,19},{19,3},{4,20},{20... | collective-permute-start | bytes 786440 | tf_op jit(solution)/shard_map/ppermute | solution.py:85
  56.8 18.8 %all-gather.5.cloned.1.call-done = bf16[1024,512]{1,0:T(8,128)(2,1)} async-done(((bf16[256,512]{1,0:T(8,128)(2,1)}), bf16[1024,512]{1,0:T(8,128)(2,1)}) %all-gather.5.cloned.1.call-update) | async-done | bytes 1048592 | tf_op jit(solution)/shard_map/all_gather | solution.py:120
  75.6 1.4 %fusion.24 = f32[256,512]{1,0:T(8,128)S(1)} fusion(bf16[1024,512]{1,0:T(8,128)(2,1)} %all-gather.5.cloned.1.call-done, bf16[256,1024]{0,1:T(8,128)(2,1)S(1)} %get-tuple-element.6), kind=kOutput, calls=%fused_computation.30 | convolution fusion | flops 134217728 | bytes 1310720 | tf_op jit(solution)/shard_map/dot_general | solution.py:130
  77.1 1.4 %fusion.15 = bf16[256,512]{1,0:T(8,128)(2,1)S(1)} fusion(f32[256,512]{1,0:T(8,128)S(1)} %fusion.24, bf16[1024,512]{1,0:T(8,128)(2,1)} %all-gather.5.cloned.1.call-done, bf16[256,1024]{0,1:T(8,128)(2,1)S(1)} %get-tuple-element.5), kind=kOutput, calls=%fused_computation.18 | convolution fusion | flops 134479872 | bytes 1572864 | tf_op jit(solution)/shard_map/dot_general | solution.py:130
  78.4 1.5 %collective-permute-start.7 = (bf16[256,512]{1,0:T(8,128)(2,1)S(1)}, bf16[256,512]{1,0:T(8,128)(2,1)S(1)}, u32[]{:S(2)}, u32[]{:S(2)}) collective-permute-start(bf16[256,512]{1,0:T(8,128)(2,1)S(1)} %fusion.15), channel_id=1, source_target_pairs={{0,16},{16,0},{1,17},{17,1},{2,18},{18,2},{3,19},{19,3},{4,20},{20... | collective-permute-start | bytes 786440 | tf_op jit(solution)/shard_map/ppermute | solution.py:85
  80.0 0.0 copy-done
  80.0 0.3 fusion.32
  80.3 0.0 copy-done.1
  80.3 0.3 fusion.26
  80.6 0.0 collective-permute-done.6
  80.6 0.3 fusion.17
  81.0 5.4 %collective-permute-done.7 = bf16[256,512]{1,0:T(8,128)(2,1)S(1)} collective-permute-done((bf16[256,512]{1,0:T(8,128)(2,1)S(1)}, bf16[256,512]{1,0:T(8,128)(2,1)S(1)}, u32[]{:S(2)}, u32[]{:S(2)}) %collective-permute-start.7) | collective-permute-done | bytes 262176 | tf_op jit(solution)/shard_map/ppermute | solution.py:85
  86.4 0.3 fusion.16
  86.7 0.9 pad_maximum_fusion.1
  (11 shorter events, 0.1 us)
Async XLA Ops:
  6.5 17.0 %copy-start.2 = (s32[1,256]{1,0:T(1,128)S(1)}, s32[1,256]{1,0:T(1,128)}, u32[]{:S(2)}) copy-start(s32[1,256]{1,0:T(1,128)} %param.6) | copy-start | bytes 3076
  6.5 41.8 %all-gather.3.cloned.1.call-start = ((), (), s32[]{:S(2)}) async-start(), calls=%async_computation | async-start | bytes 1310720 | tf_op jit(solution)/shard_map/all_gather | solution.py:119
  8.3 12.5 %collective-permute-start.1 = (bf16[256,3,128]{2,0,1:T(8,128)(2,1)S(1)}, bf16[256,3,128]{2,0,1:T(8,128)(2,1)S(1)}, u32[]{:S(2)}, u32[]{:S(2)}) collective-permute-start(bf16[256,3,128]{2,0,1:T(8,128)(2,1)S(1)} %pad_maximum_fusion.3), channel_id=1, source_target_pairs={{0,8},{4,12},{1,9},{5,13},{2,10},{6,14},{3,11},{7,15},{16,24},{20,... | collective-permute-start | bytes 589832 | tf_op jit(solution)/shard_map/ppermute | solution.py:17
  14.3 8.4 %collective-permute-start = (bf16[256,3,128]{2,0,1:T(8,128)(2,1)S(1)}, bf16[256,3,128]{2,0,1:T(8,128)(2,1)S(1)}, u32[]{:S(2)}, u32[]{:S(2)}) collective-permute-start(bf16[256,3,128]{2,0,1:T(8,128)(2,1)S(1)} %pad_maximum_fusion.3), channel_id=1, source_target_pairs={{0,4},{4,8},{8,12},{1,5},{5,9},{9,13},{2,6},{6,10},{10,14},{3,7},{... | collective-permute-start | bytes 589832 | tf_op jit(solution)/shard_map/ppermute | solution.py:17
  19.7 55.9 %all-gather.5.cloned.1.call-start = ((), (), s32[]{:S(2)}) async-start(), calls=%async_computation.1 | async-start | bytes 1310720 | tf_op jit(solution)/shard_map/all_gather | solution.py:120
  26.7 7.4 %collective-permute-start.2 = (bf16[256,512]{0,1:T(8,128)(2,1)S(1)}, bf16[256,512]{0,1:T(8,128)(2,1)S(1)}, u32[]{:S(2)}, u32[]{:S(2)}) collective-permute-start(bf16[256,512]{0,1:T(8,128)(2,1)S(1)} %bitcast.65), channel_id=1, source_target_pairs={{0,16},{16,0},{1,17},{17,1},{2,18},{18,2},{3,19},{19,3},{4,20},{20... | collective-permute-start | bytes 786440 | tf_op jit(solution)/shard_map/ppermute | solution.py:85
  34.2 13.1 %collective-permute-start.3 = (bf16[256,1024]{0,1:T(8,128)(2,1)S(1)}, bf16[256,1024]{0,1:T(8,128)(2,1)S(1)}, u32[]{:S(2)}, u32[]{:S(2)}) collective-permute-start(bf16[256,1024]{0,1:T(8,128)(2,1)S(1)} %pad_maximum_fusion), channel_id=1, source_target_pairs={{0,2},{1,3},{18,16},{19,17},{4,6},{5,7},{22,20},{23,21},{8,10},{9,... | collective-permute-start | bytes 1572872 | tf_op jit(solution)/shard_map/ppermute | solution.py:89
  37.7 10.3 %collective-permute-start.4 = (bf16[256,1024]{0,1:T(8,128)(2,1)S(1)}, bf16[256,1024]{0,1:T(8,128)(2,1)S(1)}, u32[]{:S(2)}, u32[]{:S(2)}) collective-permute-start(bf16[256,1024]{0,1:T(8,128)(2,1)S(1)} %pad_maximum_fusion), channel_id=1, source_target_pairs={{0,1},{1,0},{18,19},{19,18},{4,5},{5,4},{22,23},{23,22},{8,9},{9,8... | collective-permute-start | bytes 1572872 | tf_op jit(solution)/shard_map/ppermute | solution.py:89
  47.3 0.7 collective-permute-start.5
  48.4 31.6 %copy-start = (bf16[1024,512]{1,0:T(8,128)(2,1)S(1)}, bf16[1024,512]{1,0:T(8,128)(2,1)}, u32[]{:S(2)}) copy-start(bf16[1024,512]{1,0:T(8,128)(2,1)} %all-gather.3.cloned.1.call-done) | copy-start | bytes 3145732
  51.2 29.4 %collective-permute-start.6 = (bf16[256,512]{1,0:T(8,128)(2,1)S(1)}, bf16[256,512]{1,0:T(8,128)(2,1)S(1)}, u32[]{:S(2)}, u32[]{:S(2)}) collective-permute-start(bf16[256,512]{1,0:T(8,128)(2,1)S(1)} %fusion.14), channel_id=1, source_target_pairs={{0,16},{16,0},{1,17},{17,1},{2,18},{18,2},{3,19},{19,3},{4,20},{20... | collective-permute-start | bytes 786440 | tf_op jit(solution)/shard_map/ppermute | solution.py:85
  75.6 4.7 %copy-start.1 = (bf16[1024,512]{1,0:T(8,128)(2,1)S(1)}, bf16[1024,512]{1,0:T(8,128)(2,1)}, u32[]{:S(2)}) copy-start(bf16[1024,512]{1,0:T(8,128)(2,1)} %all-gather.5.cloned.1.call-done) | copy-start | bytes 3145732
  78.4 8.0 %collective-permute-start.7 = (bf16[256,512]{1,0:T(8,128)(2,1)S(1)}, bf16[256,512]{1,0:T(8,128)(2,1)S(1)}, u32[]{:S(2)}, u32[]{:S(2)}) collective-permute-start(bf16[256,512]{1,0:T(8,128)(2,1)S(1)} %fusion.15), channel_id=1, source_target_pairs={{0,16},{16,0},{1,17},{17,1},{2,18},{18,2},{3,19},{19,3},{4,20},{20... | collective-permute-start | bytes 786440 | tf_op jit(solution)/shard_map/ppermute | solution.py:85
Sparse Core Ops, SparseCore 0:
  19.8 26.2 all-gather.2
  47.6 27.9 all-gather.4

commit v5 on v4

--- a/solution.py
+++ b/solution.py
@@ -111,38 +111,30 @@
     ]
 
 
-def split_projection(head_values, output_weight):
+def split_projection(head_values, side_rows):
     width = head_values.shape[1]
-    columns = output_weight.shape[1]
-    half = columns // 2
-    side_rows = [
-        lax.all_gather(output_weight[:, :half], "ctx", axis=0, tiled=True),
-        lax.all_gather(output_weight[:, half:], "ctx", axis=0, tiled=True),
-    ]
     peers = needed_heads(head_values)
-    outputs = []
-    for rows in side_rows:
-        local = None
-        partner = None
-        for j, both in enumerate(peers):
-            block = rows[j * width:(j + 1) * width]
-            mine = jnp.dot(both[:, :width], block, preferred_element_type=jnp.float32)
-            theirs = jnp.dot(both[:, width:], block, preferred_element_type=jnp.float32)
-            local = mine if local is None else local + mine
-            partner = theirs if partner is None else partner + theirs
-        returned = swapped(partner.astype(jnp.bfloat16), "dp")
-        outputs.append(local + returned.astype(jnp.float32))
-    return jnp.concatenate(outputs, axis=1)
+    local = None
+    partner = None
+    for j, both in enumerate(peers):
+        block = side_rows[j * width:(j + 1) * width]
+        mine = jnp.dot(both[:, :width], block, preferred_element_type=jnp.float32)
+        theirs = jnp.dot(both[:, width:], block, preferred_element_type=jnp.float32)
+        local = mine if local is None else local + mine
+        partner = theirs if partner is None else partner + theirs
+    returned = swapped(partner.astype(jnp.bfloat16), "dp")
+    return local + returned.astype(jnp.float32)
 
 
 def shards(queries, keyvals, documents, output_weight):
     block_rows = output_weight.shape[0]
     width = queries.shape[2]
     side_width = block_rows * lax.axis_size("ctx")
-    fits = output_weight.shape[1] % 256 == 0 and lax.axis_size("tensor") == 4
+    fits = lax.axis_size("tensor") == 4
     if lax.axis_size("dp") == 2 and side_width == 2 * width and fits:
+        side_rows = lax.all_gather(output_weight, "ctx", axis=0, tiled=True)
         head_values = attention(queries, keyvals, documents)
-        result = split_projection(head_values, output_weight)
+        result = split_projection(head_values, side_rows)
         return result.astype(jnp.bfloat16)[None]
     all_rows = lax.all_gather(output_weight, ("dp", "ctx"), axis=0, tiled=True)
     head_values = attention(queries, keyvals, documents)

time: 94.9 us -> 90.1 us (0.949)
  the two profiles are of different devices: /device:TPU:0 before, /device:TPU:18 now
where the time goes in v5:
time: 90.1 us; the launch traced here: 89.8 us
  waiting for transfers between devices  53.3 us (59%)
  between operations  13.6 us (15%)
  starting transfers between devices  11 us (12%)
  matrix products  6.85 us (8%)
  other arithmetic  2.94 us (3%)
  local copies, waits for them, and re-layouts  2.06 us (2%)
    ppermute x2, waiting for transfers between devices, swapped(): return lax.ppermute(block, axis, [(0, 1), (1, 0)])  19.9 us
    ppermute x2, waiting for transfers between devices, shifted(): return lax.ppermute(block, axis, route)  18.4 us
    ppermute x3, waiting for transfers between devices, sent(): return lax.ppermute(block, ('dp', 'tensor'), route)  15 us
    ppermute x2, starting transfers between devices, shifted(): return lax.ppermute(block, axis, route)  4.78 us
    ppermute x3, starting transfers between devices, sent(): return lax.ppermute(block, ('dp', 'tensor'), route)  3.9 us
    dot_general x2, matrix products, split_projection(): theirs = jnp.dot(both[:, width:], block, preferred_element_type=jnp.float32)  3.53 us
    ppermute x2, starting transfers between devices, swapped(): return lax.ppermute(block, axis, [(0, 1), (1, 0)])  2.28 us
  transfers between devices with their start and end apart: 8, of which 5 were waited for; matrix products, arithmetic and copies ran while one was open for 6% of the time, Pallas kernels for 0%

profile of v5, /device:TPU:18, one launch (start us, length us, event | category | flops | bytes accessed | tf_op | source)
XLA Modules:
  0.0 89.8 jit_solution(5308309339575664610)
XLA Ops:
  6.5 0.0 copy-start.1
  6.5 0.0 all-gather.2.cloned.1.call-start
  6.5 0.8 convert_element_type.37
  7.3 0.9 %copy.21 = bf16[1,256,2,128]{3,1,2,0:T(8,128)(2,1)S(1)} copy(bf16[1,256,2,128]{3,2,1,0:T(2,128)(2,1)} %param.5) | data formatting | bytes 262144 | tf_op args[1]
  8.2 0.1 broadcast_in_dim.27
  8.3 1.3 %collective-permute-start.1 = (bf16[256,3,128]{2,0,1:T(8,128)(2,1)S(1)}, bf16[256,3,128]{2,0,1:T(8,128)(2,1)S(1)}, u32[]{:S(2)}, u32[]{:S(2)}) collective-permute-start(bf16[256,3,128]{2,0,1:T(8,128)(2,1)S(1)} %pad_maximum_fusion.2), channel_id=1, source_target_pairs={{0,8},{4,12},{1,9},{5,13},{2,10},{6,14},{3,11},{7,15},{16,24},{20,... | collective-permute-start | bytes 589832 | tf_op jit(solution)/shard_map/ppermute | solution.py:17
  9.6 3.5 %collective-permute-start = (bf16[256,3,128]{2,0,1:T(8,128)(2,1)S(1)}, bf16[256,3,128]{2,0,1:T(8,128)(2,1)S(1)}, u32[]{:S(2)}, u32[]{:S(2)}) collective-permute-start(bf16[256,3,128]{2,0,1:T(8,128)(2,1)S(1)} %pad_maximum_fusion.2), channel_id=1, source_target_pairs={{0,4},{4,8},{8,12},{1,5},{5,9},{9,13},{2,6},{6,10},{10,14},{3,7},{... | collective-permute-start | bytes 589832 | tf_op jit(solution)/shard_map/ppermute | solution.py:17
  13.1 0.0 all-gather.2.cloned.1.call-update
  13.2 1.0 %reshape.68 = bf16[256,4,128]{2,1,0:T(4,128)(2,1)S(1)} reshape(bf16[1,256,512]{2,1,0:T(8,128)(2,1)} %param.4) | data formatting | bytes 524288 | tf_op jit(solution)/shard_map/reshape.3
  14.3 18.4 %collective-permute-done = bf16[256,3,128]{2,0,1:T(8,128)(2,1)S(1)} collective-permute-done((bf16[256,3,128]{2,0,1:T(8,128)(2,1)S(1)}, bf16[256,3,128]{2,0,1:T(8,128)(2,1)S(1)}, u32[]{:S(2)}, u32[]{:S(2)}) %collective-permute-start) | collective-permute-done | bytes 196640 | tf_op jit(solution)/shard_map/ppermute | solution.py:17
  32.6 0.0 collective-permute-done.1
  32.7 0.1 convert_reduce_fusion
  32.8 0.1 convert_reduce_fusion.1
  32.9 0.0 copy-done.1
  33.0 0.7 and_and_fusion
  33.7 0.6 fusion
  34.4 0.8 fusion.1
  35.2 0.9 %fusion.17 = bf16[256,1,4,128]{0,3,2,1:T(8,128)(2,1)S(1)} fusion(f32[768,256,4]{1,0,2:T(8,128)S(1)} %get-tuple-element.8, f32[4,256]{1,0:T(4,128)S(1)} %get-tuple-element.7, pred[256,768]{0,1:T(8,128)(4,1)S(1)} %and_and_fusion, f32[256,4]{0,1:T(4,128)S(1)} %bitcast.66, bf16[768,2,128]{2,0,1:T(8,128)(2,1)S(1)} %pad_maximum_fusion.1), kind=kOutput, calls=%fused_computation.16 | convolution fusion | flops 205520896 | bytes 3809280 | tf_op jit(solution)/shard_map/hgqk,khd->qhgd/dot_general | solution.py:72
  36.1 2.2 %collective-permute-start.2 = (bf16[256,512]{0,1:T(8,128)(2,1)S(1)}, bf16[256,512]{0,1:T(8,128)(2,1)S(1)}, u32[]{:S(2)}, u32[]{:S(2)}) collective-permute-start(bf16[256,512]{0,1:T(8,128)(2,1)S(1)} %bitcast.63), channel_id=1, source_target_pairs={{0,16},{16,0},{1,17},{17,1},{2,18},{18,2},{3,19},{19,3},{4,20},{20... | collective-permute-start | bytes 786440 | tf_op jit(solution)/shard_map/ppermute | solution.py:85
  38.3 6.4 %collective-permute-done.2 = bf16[256,512]{0,1:T(8,128)(2,1)S(1)} collective-permute-done((bf16[256,512]{0,1:T(8,128)(2,1)S(1)}, bf16[256,512]{0,1:T(8,128)(2,1)S(1)}, u32[]{:S(2)}, u32[]{:S(2)}) %collective-permute-start.2) | collective-permute-done | bytes 262176 | tf_op jit(solution)/shard_map/ppermute | solution.py:85
  44.7 1.3 %collective-permute-start.3 = (bf16[256,1024]{0,1:T(8,128)(2,1)S(1)}, bf16[256,1024]{0,1:T(8,128)(2,1)S(1)}, u32[]{:S(2)}, u32[]{:S(2)}) collective-permute-start(bf16[256,1024]{0,1:T(8,128)(2,1)S(1)} %pad_maximum_fusion), channel_id=1, source_target_pairs={{0,2},{1,3},{18,16},{19,17},{4,6},{5,7},{22,20},{23,21},{8,10},{9,... | collective-permute-start | bytes 1572872 | tf_op jit(solution)/shard_map/ppermute | solution.py:89
  46.0 0.7 collective-permute-start.4
  46.7 13.2 %collective-permute-done.3 = bf16[256,1024]{0,1:T(8,128)(2,1)S(1)} collective-permute-done((bf16[256,1024]{0,1:T(8,128)(2,1)S(1)}, bf16[256,1024]{0,1:T(8,128)(2,1)S(1)}, u32[]{:S(2)}, u32[]{:S(2)}) %collective-permute-start.3) | collective-permute-done | bytes 524320 | tf_op jit(solution)/shard_map/ppermute | solution.py:89
  59.9 1.9 %collective-permute-start.5 = (bf16[256,1024]{0,1:T(8,128)(2,1)S(1)}, bf16[256,1024]{0,1:T(8,128)(2,1)S(1)}, u32[]{:S(2)}, u32[]{:S(2)}) collective-permute-start(bf16[256,1024]{0,1:T(8,128)(2,1)S(1)} %collective-permute-done.3), channel_id=1, source_target_pairs={{2,3},{3,2},{16,17},{17,16},{6,7},{7,6},{20,21},{21,20},{10,11},{1... | collective-permute-start | bytes 1572872 | tf_op jit(solution)/shard_map/ppermute | solution.py:89
  61.9 0.0 collective-permute-done.4
  61.9 1.8 %collective-permute-done.5 = bf16[256,1024]{0,1:T(8,128)(2,1)S(1)} collective-permute-done((bf16[256,1024]{0,1:T(8,128)(2,1)S(1)}, bf16[256,1024]{0,1:T(8,128)(2,1)S(1)}, u32[]{:S(2)}, u32[]{:S(2)}) %collective-permute-start.5) | collective-permute-done | bytes 524320 | tf_op jit(solution)/shard_map/ppermute | solution.py:89
  63.7 0.3 broadcast_select_fusion.3
  64.0 0.0 all-gather.2.cloned.1.call-done
  64.1 0.0 copy-start
  64.1 1.8 %fusion.20 = f32[256,1024]{1,0:T(8,128)S(1)} fusion(bf16[1024,1024]{1,0:T(8,128)(2,1)} %all-gather.2.cloned.1.call-done, bf16[256,1024]{0,1:T(8,128)(2,1)S(1)} %get-tuple-element.6), kind=kOutput, calls=%fused_computation.17 | convolution fusion | flops 268435456 | bytes 2359296 | tf_op jit(solution)/shard_map/dot_general | solution.py:122
  65.9 1.7 %fusion.9 = bf16[256,1024]{1,0:T(8,128)(2,1)S(1)} fusion(f32[256,1024]{1,0:T(8,128)S(1)} %fusion.20, bf16[1024,1024]{1,0:T(8,128)(2,1)} %all-gather.2.cloned.1.call-done, bf16[256,1024]{0,1:T(8,128)(2,1)S(1)} %get-tuple-element.5), kind=kOutput, calls=%fused_computation.12 | convolution fusion | flops 268959744 | bytes 2883584 | tf_op jit(solution)/shard_map/dot_general | solution.py:122
  67.6 0.1 collective-permute-start.6
  67.7 0.0 copy-done
  67.7 0.5 fusion.22
  68.2 13.5 %collective-permute-done.6 = bf16[256,1024]{1,0:T(8,128)(2,1)S(1)} collective-permute-done((bf16[256,1024]{1,0:T(8,128)(2,1)S(1)}, bf16[256,1024]{1,0:T(8,128)(2,1)S(1)}, u32[]{:S(2)}, u32[]{:S(2)}) %collective-permute-start.6) | collective-permute-done | bytes 524320 | tf_op jit(solution)/shard_map/ppermute | solution.py:85
  81.7 1.3 %fusion.10 = bf16[1,256,1024]{2,1,0:T(8,128)(2,1)} fusion(f32[256,1024]{1,0:T(8,128)S(1)} %fusion.22, bf16[256,1024]{1,0:T(8,128)(2,1)S(1)} %collective-permute-done.6, bf16[1024,1024]{1,0:T(8,128)(2,1)S(1)} %copy-done, bf16[256,1024]{0,1:T(8,128)(2,1)S(1)} %get-tuple-element.5), kind=kOutput, calls=%fused_computation.13 | convolution fusion | flops 269484032 | bytes 3407872 | tf_op jit(solution)/shard_map/dot_general | solution.py:121
  (10 shorter events, 0.1 us)
Async XLA Ops:
  6.5 26.4 %copy-start.1 = (s32[1,256]{1,0:T(1,128)S(1)}, s32[1,256]{1,0:T(1,128)}, u32[]{:S(2)}) copy-start(s32[1,256]{1,0:T(1,128)} %param.6) | copy-start | bytes 3076
  6.5 57.5 %all-gather.2.cloned.1.call-start = ((), (), s32[]{:S(2)}) async-start(), calls=%async_computation | async-start | bytes 2621440 | tf_op jit(solution)/shard_map/all_gather | solution.py:135
  8.3 24.3 %collective-permute-start.1 = (bf16[256,3,128]{2,0,1:T(8,128)(2,1)S(1)}, bf16[256,3,128]{2,0,1:T(8,128)(2,1)S(1)}, u32[]{:S(2)}, u32[]{:S(2)}) collective-permute-start(bf16[256,3,128]{2,0,1:T(8,128)(2,1)S(1)} %pad_maximum_fusion.2), channel_id=1, source_target_pairs={{0,8},{4,12},{1,9},{5,13},{2,10},{6,14},{3,11},{7,15},{16,24},{20,... | collective-permute-start | bytes 589832 | tf_op jit(solution)/shard_map/ppermute | solution.py:17
  9.6 23.0 %collective-permute-start = (bf16[256,3,128]{2,0,1:T(8,128)(2,1)S(1)}, bf16[256,3,128]{2,0,1:T(8,128)(2,1)S(1)}, u32[]{:S(2)}, u32[]{:S(2)}) collective-permute-start(bf16[256,3,128]{2,0,1:T(8,128)(2,1)S(1)} %pad_maximum_fusion.2), channel_id=1, source_target_pairs={{0,4},{4,8},{8,12},{1,5},{5,9},{9,13},{2,6},{6,10},{10,14},{3,7},{... | collective-permute-start | bytes 589832 | tf_op jit(solution)/shard_map/ppermute | solution.py:17
  36.1 8.6 %collective-permute-start.2 = (bf16[256,512]{0,1:T(8,128)(2,1)S(1)}, bf16[256,512]{0,1:T(8,128)(2,1)S(1)}, u32[]{:S(2)}, u32[]{:S(2)}) collective-permute-start(bf16[256,512]{0,1:T(8,128)(2,1)S(1)} %bitcast.63), channel_id=1, source_target_pairs={{0,16},{16,0},{1,17},{17,1},{2,18},{18,2},{3,19},{19,3},{4,20},{20... | collective-permute-start | bytes 786440 | tf_op jit(solution)/shard_map/ppermute | solution.py:85
  44.7 15.2 %collective-permute-start.3 = (bf16[256,1024]{0,1:T(8,128)(2,1)S(1)}, bf16[256,1024]{0,1:T(8,128)(2,1)S(1)}, u32[]{:S(2)}, u32[]{:S(2)}) collective-permute-start(bf16[256,1024]{0,1:T(8,128)(2,1)S(1)} %pad_maximum_fusion), channel_id=1, source_target_pairs={{0,2},{1,3},{18,16},{19,17},{4,6},{5,7},{22,20},{23,21},{8,10},{9,... | collective-permute-start | bytes 1572872 | tf_op jit(solution)/shard_map/ppermute | solution.py:89
  46.0 15.8 %collective-permute-start.4 = (bf16[256,1024]{0,1:T(8,128)(2,1)S(1)}, bf16[256,1024]{0,1:T(8,128)(2,1)S(1)}, u32[]{:S(2)}, u32[]{:S(2)}) collective-permute-start(bf16[256,1024]{0,1:T(8,128)(2,1)S(1)} %pad_maximum_fusion), channel_id=1, source_target_pairs={{0,1},{1,0},{18,19},{19,18},{4,5},{5,4},{22,23},{23,22},{8,9},{9,8... | collective-permute-start | bytes 1572872 | tf_op jit(solution)/shard_map/ppermute | solution.py:89
  59.9 3.8 %collective-permute-start.5 = (bf16[256,1024]{0,1:T(8,128)(2,1)S(1)}, bf16[256,1024]{0,1:T(8,128)(2,1)S(1)}, u32[]{:S(2)}, u32[]{:S(2)}) collective-permute-start(bf16[256,1024]{0,1:T(8,128)(2,1)S(1)} %collective-permute-done.3), channel_id=1, source_target_pairs={{2,3},{3,2},{16,17},{17,16},{6,7},{7,6},{20,21},{21,20},{10,11},{1... | collective-permute-start | bytes 1572872 | tf_op jit(solution)/shard_map/ppermute | solution.py:89
  64.1 3.6 %copy-start = (bf16[1024,1024]{1,0:T(8,128)(2,1)S(1)}, bf16[1024,1024]{1,0:T(8,128)(2,1)}, u32[]{:S(2)}) copy-start(bf16[1024,1024]{1,0:T(8,128)(2,1)} %all-gather.2.cloned.1.call-done) | copy-start | bytes 6291460
  67.6 14.0 %collective-permute-start.6 = (bf16[256,1024]{1,0:T(8,128)(2,1)S(1)}, bf16[256,1024]{1,0:T(8,128)(2,1)S(1)}, u32[]{:S(2)}, u32[]{:S(2)}) collective-permute-start(bf16[256,1024]{1,0:T(8,128)(2,1)S(1)} %fusion.9), channel_id=1, source_target_pairs={{0,16},{16,0},{1,17},{17,1},{2,18},{18,2},{3,19},{19,3},{4,20},{20... | collective-permute-start | bytes 1572872 | tf_op jit(solution)/shard_map/ppermute | solution.py:85
Sparse Core Ops, SparseCore 0:
  13.3 45.7 all-gather.1

commit v6 on v5

--- a/solution.py
+++ b/solution.py
@@ -114,15 +114,19 @@
 def split_projection(head_values, side_rows):
     width = head_values.shape[1]
     peers = needed_heads(head_values)
-    local = None
     partner = None
     for j, both in enumerate(peers):
         block = side_rows[j * width:(j + 1) * width]
+        theirs = jnp.dot(both[:, width:], block, preferred_element_type=jnp.float32)
+        partner = theirs if partner is None else partner + theirs
+    outgoing = partner.astype(jnp.bfloat16)
+    returned = swapped(outgoing, "dp")
+    outgoing, peers, side_rows = lax.optimization_barrier((outgoing, peers, side_rows))
+    local = None
+    for j, both in enumerate(peers):
+        block = side_rows[j * width:(j + 1) * width]
         mine = jnp.dot(both[:, :width], block, preferred_element_type=jnp.float32)
-        theirs = jnp.dot(both[:, width:], block, preferred_element_type=jnp.float32)
         local = mine if local is None else local + mine
-        partner = theirs if partner is None else partner + theirs
-    returned = swapped(partner.astype(jnp.bfloat16), "dp")
     return local + returned.astype(jnp.float32)
 
 

time: 90.1 us -> 89.7 us (level)
  other arithmetic: 2.94 us -> 3.88 us
    broadcast_in_dim x0 -> x1, other arithmetic: none -> 0.94 us  [shards(): return result.astype(jnp.bfloat16)[None]]
where the time goes in v6:
time: 89.7 us; the launch traced here: 89.4 us
  waiting for transfers between devices  52.9 us (59%)
  between operations  13.6 us (15%)
  starting transfers between devices  11 us (12%)
  matrix products  6.04 us (7%)
  other arithmetic  3.88 us (4%)
  local copies, waits for them, and re-layouts  2.06 us (2%)
    ppermute x2, waiting for transfers between devices, swapped(): return lax.ppermute(block, axis, [(0, 1), (1, 0)])  19.4 us
    ppermute x2, waiting for transfers between devices, shifted(): return lax.ppermute(block, axis, route)  18.4 us
    ppermute x3, waiting for transfers between devices, sent(): return lax.ppermute(block, ('dp', 'tensor'), route)  15 us
    ppermute x2, starting transfers between devices, shifted(): return lax.ppermute(block, axis, route)  4.78 us
    ppermute x3, starting transfers between devices, sent(): return lax.ppermute(block, ('dp', 'tensor'), route)  3.9 us
    dot_general x2, matrix products, split_projection(): theirs = jnp.dot(both[:, width:], block, preferred_element_type=jnp.float32)  3.53 us
    ppermute x2, starting transfers between devices, swapped(): return lax.ppermute(block, axis, [(0, 1), (1, 0)])  2.28 us
  transfers between devices with their start and end apart: 8, of which 5 were waited for; matrix products, arithmetic and copies ran while one was open for 6% of the time, Pallas kernels for 0%

profile of v6, /device:TPU:18, one launch (start us, length us, event | category | flops | bytes accessed | tf_op | source)
XLA Modules:
  0.0 89.4 jit_solution(8934210943196748434)
XLA Ops:
  6.5 0.0 copy-start.1
  6.5 0.0 all-gather.2.cloned.1.call-start
  6.5 0.8 convert_element_type.37
  7.3 0.9 %copy.21 = bf16[1,256,2,128]{3,1,2,0:T(8,128)(2,1)S(1)} copy(bf16[1,256,2,128]{3,2,1,0:T(2,128)(2,1)} %param.5) | data formatting | bytes 262144 | tf_op args[1]
  8.2 0.1 broadcast_in_dim.27
  8.3 1.3 %collective-permute-start.1 = (bf16[256,3,128]{2,0,1:T(8,128)(2,1)S(1)}, bf16[256,3,128]{2,0,1:T(8,128)(2,1)S(1)}, u32[]{:S(2)}, u32[]{:S(2)}) collective-permute-start(bf16[256,3,128]{2,0,1:T(8,128)(2,1)S(1)} %pad_maximum_fusion.2), channel_id=1, source_target_pairs={{0,8},{4,12},{1,9},{5,13},{2,10},{6,14},{3,11},{7,15},{16,24},{20,... | collective-permute-start | bytes 589832 | tf_op jit(solution)/shard_map/ppermute | solution.py:17
  9.6 3.5 %collective-permute-start = (bf16[256,3,128]{2,0,1:T(8,128)(2,1)S(1)}, bf16[256,3,128]{2,0,1:T(8,128)(2,1)S(1)}, u32[]{:S(2)}, u32[]{:S(2)}) collective-permute-start(bf16[256,3,128]{2,0,1:T(8,128)(2,1)S(1)} %pad_maximum_fusion.2), channel_id=1, source_target_pairs={{0,4},{4,8},{8,12},{1,5},{5,9},{9,13},{2,6},{6,10},{10,14},{3,7},{... | collective-permute-start | bytes 589832 | tf_op jit(solution)/shard_map/ppermute | solution.py:17
  13.1 0.0 all-gather.2.cloned.1.call-update
  13.2 1.0 %reshape.68 = bf16[256,4,128]{2,1,0:T(4,128)(2,1)S(1)} reshape(bf16[1,256,512]{2,1,0:T(8,128)(2,1)} %param.4) | data formatting | bytes 524288 | tf_op jit(solution)/shard_map/reshape.3
  14.3 18.4 %collective-permute-done = bf16[256,3,128]{2,0,1:T(8,128)(2,1)S(1)} collective-permute-done((bf16[256,3,128]{2,0,1:T(8,128)(2,1)S(1)}, bf16[256,3,128]{2,0,1:T(8,128)(2,1)S(1)}, u32[]{:S(2)}, u32[]{:S(2)}) %collective-permute-start) | collective-permute-done | bytes 196640 | tf_op jit(solution)/shard_map/ppermute | solution.py:17
  32.6 0.0 collective-permute-done.1
  32.7 0.1 convert_reduce_fusion
  32.8 0.1 convert_reduce_fusion.1
  32.9 0.0 copy-done.1
  33.0 0.7 and_and_fusion
  33.7 0.6 fusion
  34.4 0.8 fusion.1
  35.2 0.9 %fusion.20 = bf16[256,1,4,128]{0,3,2,1:T(8,128)(2,1)S(1)} fusion(f32[768,256,4]{1,0,2:T(8,128)S(1)} %get-tuple-element.14, f32[4,256]{1,0:T(4,128)S(1)} %get-tuple-element.13, pred[256,768]{0,1:T(8,128)(4,1)S(1)} %and_and_fusion, f32[256,4]{0,1:T(4,128)S(1)} %bitcast.66, bf16[768,2,128]{2,0,1:T(8,128)(2,1)S(1)} %pad_maximum_fusion.1), kind=kOutput, calls=%fused_computation.20 | convolution fusion | flops 205520896 | bytes 3809280 | tf_op jit(solution)/shard_map/hgqk,khd->qhgd/dot_general | solution.py:72
  36.1 2.2 %collective-permute-start.2 = (bf16[256,512]{0,1:T(8,128)(2,1)S(1)}, bf16[256,512]{0,1:T(8,128)(2,1)S(1)}, u32[]{:S(2)}, u32[]{:S(2)}) collective-permute-start(bf16[256,512]{0,1:T(8,128)(2,1)S(1)} %bitcast.63), channel_id=1, source_target_pairs={{0,16},{16,0},{1,17},{17,1},{2,18},{18,2},{3,19},{19,3},{4,20},{20... | collective-permute-start | bytes 786440 | tf_op jit(solution)/shard_map/ppermute | solution.py:85
  38.3 6.4 %collective-permute-done.2 = bf16[256,512]{0,1:T(8,128)(2,1)S(1)} collective-permute-done((bf16[256,512]{0,1:T(8,128)(2,1)S(1)}, bf16[256,512]{0,1:T(8,128)(2,1)S(1)}, u32[]{:S(2)}, u32[]{:S(2)}) %collective-permute-start.2) | collective-permute-done | bytes 262176 | tf_op jit(solution)/shard_map/ppermute | solution.py:85
  44.7 1.3 %collective-permute-start.3 = (bf16[256,1024]{0,1:T(8,128)(2,1)S(1)}, bf16[256,1024]{0,1:T(8,128)(2,1)S(1)}, u32[]{:S(2)}, u32[]{:S(2)}) collective-permute-start(bf16[256,1024]{0,1:T(8,128)(2,1)S(1)} %pad_maximum_fusion), channel_id=1, source_target_pairs={{0,2},{1,3},{18,16},{19,17},{4,6},{5,7},{22,20},{23,21},{8,10},{9,... | collective-permute-start | bytes 1572872 | tf_op jit(solution)/shard_map/ppermute | solution.py:89
  46.0 0.7 collective-permute-start.4
  46.7 13.2 %collective-permute-done.3 = bf16[256,1024]{0,1:T(8,128)(2,1)S(1)} collective-permute-done((bf16[256,1024]{0,1:T(8,128)(2,1)S(1)}, bf16[256,1024]{0,1:T(8,128)(2,1)S(1)}, u32[]{:S(2)}, u32[]{:S(2)}) %collective-permute-start.3) | collective-permute-done | bytes 524320 | tf_op jit(solution)/shard_map/ppermute | solution.py:89
  59.9 1.9 %collective-permute-start.5 = (bf16[256,1024]{0,1:T(8,128)(2,1)S(1)}, bf16[256,1024]{0,1:T(8,128)(2,1)S(1)}, u32[]{:S(2)}, u32[]{:S(2)}) collective-permute-start(bf16[256,1024]{0,1:T(8,128)(2,1)S(1)} %collective-permute-done.3), channel_id=1, source_target_pairs={{2,3},{3,2},{16,17},{17,16},{6,7},{7,6},{20,21},{21,20},{10,11},{1... | collective-permute-start | bytes 1572872 | tf_op jit(solution)/shard_map/ppermute | solution.py:89
  61.9 0.0 collective-permute-done.4
  61.9 1.8 %collective-permute-done.5 = bf16[256,1024]{0,1:T(8,128)(2,1)S(1)} collective-permute-done((bf16[256,1024]{0,1:T(8,128)(2,1)S(1)}, bf16[256,1024]{0,1:T(8,128)(2,1)S(1)}, u32[]{:S(2)}, u32[]{:S(2)}) %collective-permute-start.5) | collective-permute-done | bytes 524320 | tf_op jit(solution)/shard_map/ppermute | solution.py:89
  63.7 0.3 broadcast_select_fusion.3
  64.0 0.0 all-gather.2.cloned.1.call-done
  64.1 0.0 copy-start
  64.1 1.8 %fusion.11 = f32[256,1024]{1,0:T(8,128)S(1)} fusion(bf16[1024,1024]{1,0:T(8,128)(2,1)} %all-gather.2.cloned.1.call-done, bf16[256,1024]{0,1:T(8,128)(2,1)S(1)} %get-tuple-element.10), kind=kOutput, calls=%fused_computation.12 | convolution fusion | flops 268435456 | bytes 2359296 | tf_op jit(solution)/shard_map/dot_general | solution.py:120
  65.9 1.7 %fusion.7 = bf16[256,1024]{1,0:T(8,128)(2,1)S(1)} fusion(f32[256,1024]{1,0:T(8,128)S(1)} %fusion.11, bf16[1024,1024]{1,0:T(8,128)(2,1)} %all-gather.2.cloned.1.call-done, bf16[256,1024]{0,1:T(8,128)(2,1)S(1)} %get-tuple-element.8), kind=kOutput, calls=%fused_computation.10 | convolution fusion | flops 268959744 | bytes 2883584 | tf_op jit(solution)/shard_map/dot_general | solution.py:120
  67.6 0.1 collective-permute-start.6
  67.7 0.0 copy-done
  67.7 0.5 fusion.15
  68.2 0.5 convolution_add_fusion
  68.6 13.0 %collective-permute-done.6 = bf16[256,1024]{1,0:T(8,128)(2,1)S(1)} collective-permute-done((bf16[256,1024]{1,0:T(8,128)(2,1)S(1)}, bf16[256,1024]{1,0:T(8,128)(2,1)S(1)}, u32[]{:S(2)}, u32[]{:S(2)}) %collective-permute-start.6) | collective-permute-done | bytes 524320 | tf_op jit(solution)/shard_map/ppermute | solution.py:85
  81.7 0.9 %fusion.23 = bf16[1,256,1024]{2,1,0:T(8,128)(2,1)} fusion(f32[256,1024]{1,0:T(8,128)S(1)} %convolution_add_fusion, bf16[256,1024]{1,0:T(8,128)(2,1)S(1)} %collective-permute-done.6), kind=kLoop, calls=%fused_computation.22 | loop fusion | flops 786432 | bytes 2097152 | tf_op jit(solution)/shard_map/broadcast_in_dim | solution.py:142
  (10 shorter events, 0.1 us)
Async XLA Ops:
  6.5 26.4 %copy-start.1 = (s32[1,256]{1,0:T(1,128)S(1)}, s32[1,256]{1,0:T(1,128)}, u32[]{:S(2)}) copy-start(s32[1,256]{1,0:T(1,128)} %param.6) | copy-start | bytes 3076
  6.5 57.5 %all-gather.2.cloned.1.call-start = ((), (), s32[]{:S(2)}) async-start(), calls=%async_computation | async-start | bytes 2621440 | tf_op jit(solution)/shard_map/all_gather | solution.py:139
  8.3 24.3 %collective-permute-start.1 = (bf16[256,3,128]{2,0,1:T(8,128)(2,1)S(1)}, bf16[256,3,128]{2,0,1:T(8,128)(2,1)S(1)}, u32[]{:S(2)}, u32[]{:S(2)}) collective-permute-start(bf16[256,3,128]{2,0,1:T(8,128)(2,1)S(1)} %pad_maximum_fusion.2), channel_id=1, source_target_pairs={{0,8},{4,12},{1,9},{5,13},{2,10},{6,14},{3,11},{7,15},{16,24},{20,... | collective-permute-start | bytes 589832 | tf_op jit(solution)/shard_map/ppermute | solution.py:17
  9.6 23.0 %collective-permute-start = (bf16[256,3,128]{2,0,1:T(8,128)(2,1)S(1)}, bf16[256,3,128]{2,0,1:T(8,128)(2,1)S(1)}, u32[]{:S(2)}, u32[]{:S(2)}) collective-permute-start(bf16[256,3,128]{2,0,1:T(8,128)(2,1)S(1)} %pad_maximum_fusion.2), channel_id=1, source_target_pairs={{0,4},{4,8},{8,12},{1,5},{5,9},{9,13},{2,6},{6,10},{10,14},{3,7},{... | collective-permute-start | bytes 589832 | tf_op jit(solution)/shard_map/ppermute | solution.py:17
  36.1 8.6 %collective-permute-start.2 = (bf16[256,512]{0,1:T(8,128)(2,1)S(1)}, bf16[256,512]{0,1:T(8,128)(2,1)S(1)}, u32[]{:S(2)}, u32[]{:S(2)}) collective-permute-start(bf16[256,512]{0,1:T(8,128)(2,1)S(1)} %bitcast.63), channel_id=1, source_target_pairs={{0,16},{16,0},{1,17},{17,1},{2,18},{18,2},{3,19},{19,3},{4,20},{20... | collective-permute-start | bytes 786440 | tf_op jit(solution)/shard_map/ppermute | solution.py:85
  44.7 15.2 %collective-permute-start.3 = (bf16[256,1024]{0,1:T(8,128)(2,1)S(1)}, bf16[256,1024]{0,1:T(8,128)(2,1)S(1)}, u32[]{:S(2)}, u32[]{:S(2)}) collective-permute-start(bf16[256,1024]{0,1:T(8,128)(2,1)S(1)} %pad_maximum_fusion), channel_id=1, source_target_pairs={{0,2},{1,3},{18,16},{19,17},{4,6},{5,7},{22,20},{23,21},{8,10},{9,... | collective-permute-start | bytes 1572872 | tf_op jit(solution)/shard_map/ppermute | solution.py:89
  46.0 15.8 %collective-permute-start.4 = (bf16[256,1024]{0,1:T(8,128)(2,1)S(1)}, bf16[256,1024]{0,1:T(8,128)(2,1)S(1)}, u32[]{:S(2)}, u32[]{:S(2)}) collective-permute-start(bf16[256,1024]{0,1:T(8,128)(2,1)S(1)} %pad_maximum_fusion), channel_id=1, source_target_pairs={{0,1},{1,0},{18,19},{19,18},{4,5},{5,4},{22,23},{23,22},{8,9},{9,8... | collective-permute-start | bytes 1572872 | tf_op jit(solution)/shard_map/ppermute | solution.py:89
  59.9 3.8 %collective-permute-start.5 = (bf16[256,1024]{0,1:T(8,128)(2,1)S(1)}, bf16[256,1024]{0,1:T(8,128)(2,1)S(1)}, u32[]{:S(2)}, u32[]{:S(2)}) collective-permute-start(bf16[256,1024]{0,1:T(8,128)(2,1)S(1)} %collective-permute-done.3), channel_id=1, source_target_pairs={{2,3},{3,2},{16,17},{17,16},{6,7},{7,6},{20,21},{21,20},{10,11},{1... | collective-permute-start | bytes 1572872 | tf_op jit(solution)/shard_map/ppermute | solution.py:89
  64.1 3.6 %copy-start = (bf16[1024,1024]{1,0:T(8,128)(2,1)S(1)}, bf16[1024,1024]{1,0:T(8,128)(2,1)}, u32[]{:S(2)}) copy-start(bf16[1024,1024]{1,0:T(8,128)(2,1)} %all-gather.2.cloned.1.call-done) | copy-start | bytes 6291460
  67.6 14.0 %collective-permute-start.6 = (bf16[256,1024]{1,0:T(8,128)(2,1)S(1)}, bf16[256,1024]{1,0:T(8,128)(2,1)S(1)}, u32[]{:S(2)}, u32[]{:S(2)}) collective-permute-start(bf16[256,1024]{1,0:T(8,128)(2,1)S(1)} %fusion.7), channel_id=1, source_target_pairs={{0,16},{16,0},{1,17},{17,1},{2,18},{18,2},{3,19},{19,3},{4,20},{20... | collective-permute-start | bytes 1572872 | tf_op jit(solution)/shard_map/ppermute | solution.py:85
Sparse Core Ops, SparseCore 0:
  13.3 45.7 all-gather.1

commit v7 on v6

--- a/solution.py
+++ b/solution.py
@@ -105,28 +105,22 @@
     same_core = jnp.where(on_owner, mine, over_y)
     other_core = jnp.where(on_owner, beside, relayed)
     first_core = me % 2 == 0
-    return [
-        jnp.where(first_core, same_core, other_core),
-        jnp.where(first_core, other_core, same_core),
-    ]
+    width = head_values.shape[1]
+    lower = jnp.where(first_core, same_core, other_core)
+    upper = jnp.where(first_core, other_core, same_core)
+    own_full = jnp.concatenate([lower[:, :width], upper[:, :width]], axis=1)
+    foreign_full = jnp.concatenate([lower[:, width:], upper[:, width:]], axis=1)
+    return own_full, foreign_full
 
 
 def split_projection(head_values, side_rows):
-    width = head_values.shape[1]
-    peers = needed_heads(head_values)
-    partner = None
-    for j, both in enumerate(peers):
-        block = side_rows[j * width:(j + 1) * width]
-        theirs = jnp.dot(both[:, width:], block, preferred_element_type=jnp.float32)
-        partner = theirs if partner is None else partner + theirs
+    own_full, foreign_full = needed_heads(head_values)
+    partner = jnp.dot(foreign_full, side_rows, preferred_element_type=jnp.float32)
     outgoing = partner.astype(jnp.bfloat16)
     returned = swapped(outgoing, "dp")
-    outgoing, peers, side_rows = lax.optimization_barrier((outgoing, peers, side_rows))
-    local = None
-    for j, both in enumerate(peers):
-        block = side_rows[j * width:(j + 1) * width]
-        mine = jnp.dot(both[:, :width], block, preferred_element_type=jnp.float32)
-        local = mine if local is None else local + mine
+    outgoing, own_full, side_rows = lax.optimization_barrier((outgoing, own_full, side_rows))
+    local = jnp.dot(own_full, side_rows, preferred_element_type=jnp.float32)
+    local = lax.optimization_barrier(local)
     return local + returned.astype(jnp.float32)
 
 

time: 89.7 us -> 88 us (0.981)
  matrix products: 6.04 us -> 4.77 us
  waiting for transfers between devices: 52.9 us -> 51.9 us
    dot_general x4 -> x2, matrix products: 4.45 us -> 3.19 us  [the longest x1 2.46 us: split_projection(): jnp.dot(foreign_full, side_rows, preferred_element_type=jnp.float32)]
  transfers between devices with their start and end apart: 8 -> 8, of which waited for: 5 -> 6; matrix products, arithmetic and copies ran while one was open for 6% -> 7% of each run, Pallas kernels for 0% -> 0%
where the time goes in v7:
time: 88 us; the launch traced here: 87.7 us
  waiting for transfers between devices  51.9 us (59%)
  between operations  13.6 us (15%)
  starting transfers between devices  10.7 us (12%)
  matrix products  4.77 us (5%)
  other arithmetic  4.59 us (5%)
  local copies, waits for them, and re-layouts  2.14 us (2%)
    ppermute x2, waiting for transfers between devices, swapped(): return lax.ppermute(block, axis, [(0, 1), (1, 0)])  19.1 us
    ppermute x2, waiting for transfers between devices, shifted(): return lax.ppermute(block, axis, route)  18.5 us
    ppermute x3, waiting for transfers between devices, sent(): return lax.ppermute(block, ('dp', 'tensor'), route)  14.2 us
    ppermute x2, starting transfers between devices, shifted(): return lax.ppermute(block, axis, route)  4.78 us
    ppermute x3, starting transfers between devices, sent(): return lax.ppermute(block, ('dp', 'tensor'), route)  3.9 us
    dot_general x1, matrix products, split_projection(): jnp.dot(foreign_full, side_rows, preferred_element_type=jnp.float32)  2.46 us
    ppermute x2, starting transfers between devices, swapped(): return lax.ppermute(block, axis, [(0, 1), (1, 0)])  1.98 us
  transfers between devices with their start and end apart: 8, of which 6 were waited for; matrix products, arithmetic and copies ran while one was open for 7% of the time, Pallas kernels for 0%

profile of v7, /device:TPU:18, one launch (start us, length us, event | category | flops | bytes accessed | tf_op | source)
XLA Modules:
  0.0 87.7 jit_solution(6828483857982734431)
XLA Ops:
  6.5 0.0 copy-start.1
  6.5 0.0 all-gather.2.cloned.1.call-start
  6.5 0.8 convert_element_type.37
  7.3 0.9 %copy.21 = bf16[1,256,2,128]{3,1,2,0:T(8,128)(2,1)S(1)} copy(bf16[1,256,2,128]{3,2,1,0:T(2,128)(2,1)} %param.5) | data formatting | bytes 262144 | tf_op args[1]
  8.2 0.1 broadcast_in_dim.27
  8.3 1.3 %collective-permute-start.1 = (bf16[256,3,128]{2,0,1:T(8,128)(2,1)S(1)}, bf16[256,3,128]{2,0,1:T(8,128)(2,1)S(1)}, u32[]{:S(2)}, u32[]{:S(2)}) collective-permute-start(bf16[256,3,128]{2,0,1:T(8,128)(2,1)S(1)} %pad_maximum_fusion.3), channel_id=1, source_target_pairs={{0,8},{4,12},{1,9},{5,13},{2,10},{6,14},{3,11},{7,15},{16,24},{20,... | collective-permute-start | bytes 589832 | tf_op jit(solution)/shard_map/ppermute | solution.py:17
  9.6 3.5 %collective-permute-start = (bf16[256,3,128]{2,0,1:T(8,128)(2,1)S(1)}, bf16[256,3,128]{2,0,1:T(8,128)(2,1)S(1)}, u32[]{:S(2)}, u32[]{:S(2)}) collective-permute-start(bf16[256,3,128]{2,0,1:T(8,128)(2,1)S(1)} %pad_maximum_fusion.3), channel_id=1, source_target_pairs={{0,4},{4,8},{8,12},{1,5},{5,9},{9,13},{2,6},{6,10},{10,14},{3,7},{... | collective-permute-start | bytes 589832 | tf_op jit(solution)/shard_map/ppermute | solution.py:17
  13.1 0.0 all-gather.2.cloned.1.call-update
  13.2 1.0 %reshape.68 = bf16[256,4,128]{2,1,0:T(4,128)(2,1)S(1)} reshape(bf16[1,256,512]{2,1,0:T(8,128)(2,1)} %param.4) | data formatting | bytes 524288 | tf_op jit(solution)/shard_map/reshape.3
  14.3 4.5 %collective-permute-done.1 = bf16[256,3,128]{2,0,1:T(8,128)(2,1)S(1)} collective-permute-done((bf16[256,3,128]{2,0,1:T(8,128)(2,1)S(1)}, bf16[256,3,128]{2,0,1:T(8,128)(2,1)S(1)}, u32[]{:S(2)}, u32[]{:S(2)}) %collective-permute-start.1) | collective-permute-done | bytes 196640 | tf_op jit(solution)/shard_map/ppermute | solution.py:17
  18.8 0.1 convert_reduce_fusion
  18.9 13.9 %collective-permute-done = bf16[256,3,128]{2,0,1:T(8,128)(2,1)S(1)} collective-permute-done((bf16[256,3,128]{2,0,1:T(8,128)(2,1)S(1)}, bf16[256,3,128]{2,0,1:T(8,128)(2,1)S(1)}, u32[]{:S(2)}, u32[]{:S(2)}) %collective-permute-start) | collective-permute-done | bytes 196640 | tf_op jit(solution)/shard_map/ppermute | solution.py:17
  32.8 0.1 convert_reduce_fusion.1
  33.0 0.7 pad_add_fusion
  33.7 0.0 copy-done.1
  33.7 0.7 and_and_fusion
  34.5 0.6 fusion
  35.1 0.8 fusion.1
  35.9 0.9 %fusion.13 = bf16[256,1,4,128]{0,3,2,1:T(8,128)(2,1)S(1)} fusion(f32[768,256,4]{1,0,2:T(8,128)S(1)} %get-tuple-element.16, f32[4,256]{1,0:T(4,128)S(1)} %get-tuple-element.15, pred[256,768]{0,1:T(8,128)(4,1)S(1)} %and_and_fusion, f32[256,4]{0,1:T(4,128)S(1)} %bitcast.69, bf16[768,2,128]{2,0,1:T(8,128)(2,1)S(1)} %pad_maximum_fusion.2), kind=kOutput, calls=%fused_computation.12 | convolution fusion | flops 205520896 | bytes 3809280 | tf_op jit(solution)/shard_map/hgqk,khd->qhgd/dot_general | solution.py:72
  36.9 1.9 %collective-permute-start.2 = (bf16[256,512]{0,1:T(8,128)(2,1)S(1)}, bf16[256,512]{0,1:T(8,128)(2,1)S(1)}, u32[]{:S(2)}, u32[]{:S(2)}) collective-permute-start(bf16[256,512]{0,1:T(8,128)(2,1)S(1)} %bitcast.66), channel_id=1, source_target_pairs={{0,16},{16,0},{1,17},{17,1},{2,18},{18,2},{3,19},{19,3},{4,20},{20... | collective-permute-start | bytes 786440 | tf_op jit(solution)/shard_map/ppermute | solution.py:85
  38.8 6.0 %collective-permute-done.2 = bf16[256,512]{0,1:T(8,128)(2,1)S(1)} collective-permute-done((bf16[256,512]{0,1:T(8,128)(2,1)S(1)}, bf16[256,512]{0,1:T(8,128)(2,1)S(1)}, u32[]{:S(2)}, u32[]{:S(2)}) %collective-permute-start.2) | collective-permute-done | bytes 262176 | tf_op jit(solution)/shard_map/ppermute | solution.py:85
  44.8 1.3 %collective-permute-start.3 = (bf16[256,1024]{0,1:T(8,128)(2,1)S(1)}, bf16[256,1024]{0,1:T(8,128)(2,1)S(1)}, u32[]{:S(2)}, u32[]{:S(2)}) collective-permute-start(bf16[256,1024]{0,1:T(8,128)(2,1)S(1)} %pad_maximum_fusion), channel_id=1, source_target_pairs={{0,2},{1,3},{18,16},{19,17},{4,6},{5,7},{22,20},{23,21},{8,10},{9,... | collective-permute-start | bytes 1572872 | tf_op jit(solution)/shard_map/ppermute | solution.py:89
  46.1 0.7 collective-permute-start.4
  46.8 12.4 %collective-permute-done.3 = bf16[256,1024]{0,1:T(8,128)(2,1)S(1)} collective-permute-done((bf16[256,1024]{0,1:T(8,128)(2,1)S(1)}, bf16[256,1024]{0,1:T(8,128)(2,1)S(1)}, u32[]{:S(2)}, u32[]{:S(2)}) %collective-permute-start.3) | collective-permute-done | bytes 524320 | tf_op jit(solution)/shard_map/ppermute | solution.py:89
  59.2 1.9 %collective-permute-start.5 = (bf16[256,1024]{0,1:T(8,128)(2,1)S(1)}, bf16[256,1024]{0,1:T(8,128)(2,1)S(1)}, u32[]{:S(2)}, u32[]{:S(2)}) collective-permute-start(bf16[256,1024]{0,1:T(8,128)(2,1)S(1)} %collective-permute-done.3), channel_id=1, source_target_pairs={{2,3},{3,2},{16,17},{17,16},{6,7},{7,6},{20,21},{21,20},{10,11},{1... | collective-permute-start | bytes 1572872 | tf_op jit(solution)/shard_map/ppermute | solution.py:89
  61.1 0.0 collective-permute-done.4
  61.1 1.8 %collective-permute-done.5 = bf16[256,1024]{0,1:T(8,128)(2,1)S(1)} collective-permute-done((bf16[256,1024]{0,1:T(8,128)(2,1)S(1)}, bf16[256,1024]{0,1:T(8,128)(2,1)S(1)}, u32[]{:S(2)}, u32[]{:S(2)}) %collective-permute-start.5) | collective-permute-done | bytes 524320 | tf_op jit(solution)/shard_map/ppermute | solution.py:89
  63.0 0.3 broadcast_select_fusion.3
  63.4 0.0 all-gather.2.cloned.1.call-done
  63.4 0.0 copy-start
  63.4 2.5 %convolution_convert_fusion = bf16[256,1024]{1,0:T(8,128)(2,1)S(1)} fusion(bf16[1024,1024]{1,0:T(8,128)(2,1)} %all-gather.2.cloned.1.call-done, bf16[256,512]{0,1:T(8,128)(2,1)S(1)} %get-tuple-element.14, bf16[256,512]{0,1:T(8,128)(2,1)S(1)} %get-tuple-element.12), kind=kOutput, calls=%fused_computation.8 | convolution fusion | flops 538181632 | bytes 3145728 | tf_op jit(solution)/shard_map/dot_general | solution.py:118
  65.9 0.1 collective-permute-start.6
  66.0 0.0 copy-done
  66.0 0.7 fusion.28
  66.7 13.2 %collective-permute-done.6 = bf16[256,1024]{1,0:T(8,128)(2,1)S(1)} collective-permute-done((bf16[256,1024]{1,0:T(8,128)(2,1)S(1)}, bf16[256,1024]{1,0:T(8,128)(2,1)S(1)}, u32[]{:S(2)}, u32[]{:S(2)}) %collective-permute-start.6) | collective-permute-done | bytes 524320 | tf_op jit(solution)/shard_map/ppermute | solution.py:85
  79.9 0.9 %fusion.16 = bf16[1,256,1024]{2,1,0:T(8,128)(2,1)} fusion(f32[256,1024]{1,0:T(8,128)S(1)} %fusion.28, bf16[256,1024]{1,0:T(8,128)(2,1)S(1)} %collective-permute-done.6), kind=kLoop, calls=%fused_computation.14 | loop fusion | flops 786432 | bytes 2097152 | tf_op jit(solution)/shard_map/broadcast_in_dim | solution.py:136
  (12 shorter events, 0.2 us)
Async XLA Ops:
  6.5 27.2 %copy-start.1 = (s32[1,256]{1,0:T(1,128)S(1)}, s32[1,256]{1,0:T(1,128)}, u32[]{:S(2)}) copy-start(s32[1,256]{1,0:T(1,128)} %param.6) | copy-start | bytes 3076
  6.5 56.8 %all-gather.2.cloned.1.call-start = ((), (), s32[]{:S(2)}) async-start(), calls=%async_computation | async-start | bytes 2621440 | tf_op jit(solution)/shard_map/all_gather | solution.py:133
  8.3 10.4 %collective-permute-start.1 = (bf16[256,3,128]{2,0,1:T(8,128)(2,1)S(1)}, bf16[256,3,128]{2,0,1:T(8,128)(2,1)S(1)}, u32[]{:S(2)}, u32[]{:S(2)}) collective-permute-start(bf16[256,3,128]{2,0,1:T(8,128)(2,1)S(1)} %pad_maximum_fusion.3), channel_id=1, source_target_pairs={{0,8},{4,12},{1,9},{5,13},{2,10},{6,14},{3,11},{7,15},{16,24},{20,... | collective-permute-start | bytes 589832 | tf_op jit(solution)/shard_map/ppermute | solution.py:17
  9.6 23.2 %collective-permute-start = (bf16[256,3,128]{2,0,1:T(8,128)(2,1)S(1)}, bf16[256,3,128]{2,0,1:T(8,128)(2,1)S(1)}, u32[]{:S(2)}, u32[]{:S(2)}) collective-permute-start(bf16[256,3,128]{2,0,1:T(8,128)(2,1)S(1)} %pad_maximum_fusion.3), channel_id=1, source_target_pairs={{0,4},{4,8},{8,12},{1,5},{5,9},{9,13},{2,6},{6,10},{10,14},{3,7},{... | collective-permute-start | bytes 589832 | tf_op jit(solution)/shard_map/ppermute | solution.py:17
  36.9 7.9 %collective-permute-start.2 = (bf16[256,512]{0,1:T(8,128)(2,1)S(1)}, bf16[256,512]{0,1:T(8,128)(2,1)S(1)}, u32[]{:S(2)}, u32[]{:S(2)}) collective-permute-start(bf16[256,512]{0,1:T(8,128)(2,1)S(1)} %bitcast.66), channel_id=1, source_target_pairs={{0,16},{16,0},{1,17},{17,1},{2,18},{18,2},{3,19},{19,3},{4,20},{20... | collective-permute-start | bytes 786440 | tf_op jit(solution)/shard_map/ppermute | solution.py:85
  44.8 14.4 %collective-permute-start.3 = (bf16[256,1024]{0,1:T(8,128)(2,1)S(1)}, bf16[256,1024]{0,1:T(8,128)(2,1)S(1)}, u32[]{:S(2)}, u32[]{:S(2)}) collective-permute-start(bf16[256,1024]{0,1:T(8,128)(2,1)S(1)} %pad_maximum_fusion), channel_id=1, source_target_pairs={{0,2},{1,3},{18,16},{19,17},{4,6},{5,7},{22,20},{23,21},{8,10},{9,... | collective-permute-start | bytes 1572872 | tf_op jit(solution)/shard_map/ppermute | solution.py:89
  46.1 15.0 %collective-permute-start.4 = (bf16[256,1024]{0,1:T(8,128)(2,1)S(1)}, bf16[256,1024]{0,1:T(8,128)(2,1)S(1)}, u32[]{:S(2)}, u32[]{:S(2)}) collective-permute-start(bf16[256,1024]{0,1:T(8,128)(2,1)S(1)} %pad_maximum_fusion), channel_id=1, source_target_pairs={{0,1},{1,0},{18,19},{19,18},{4,5},{5,4},{22,23},{23,22},{8,9},{9,8... | collective-permute-start | bytes 1572872 | tf_op jit(solution)/shard_map/ppermute | solution.py:89
  59.2 3.8 %collective-permute-start.5 = (bf16[256,1024]{0,1:T(8,128)(2,1)S(1)}, bf16[256,1024]{0,1:T(8,128)(2,1)S(1)}, u32[]{:S(2)}, u32[]{:S(2)}) collective-permute-start(bf16[256,1024]{0,1:T(8,128)(2,1)S(1)} %collective-permute-done.3), channel_id=1, source_target_pairs={{2,3},{3,2},{16,17},{17,16},{6,7},{7,6},{20,21},{21,20},{10,11},{1... | collective-permute-start | bytes 1572872 | tf_op jit(solution)/shard_map/ppermute | solution.py:89
  63.4 2.6 %copy-start = (bf16[1024,1024]{1,0:T(8,128)(2,1)S(1)}, bf16[1024,1024]{1,0:T(8,128)(2,1)}, u32[]{:S(2)}) copy-start(bf16[1024,1024]{1,0:T(8,128)(2,1)} %all-gather.2.cloned.1.call-done) | copy-start | bytes 6291460
  65.9 14.0 %collective-permute-start.6 = (bf16[256,1024]{1,0:T(8,128)(2,1)S(1)}, bf16[256,1024]{1,0:T(8,128)(2,1)S(1)}, u32[]{:S(2)}, u32[]{:S(2)}) collective-permute-start(bf16[256,1024]{1,0:T(8,128)(2,1)S(1)} %convolution_convert_fusion), channel_id=1, source_target_pairs={{0,16},{16,0},{1,17},{17,1},{2,18},{18,2},{3,19},{19,3},{4,20},{20... | collective-permute-start | bytes 1572872 | tf_op jit(solution)/shard_map/ppermute | solution.py:85
Sparse Core Ops, SparseCore 0:
  13.3 45.7 all-gather.1

commit v8 on v7

--- a/solution.py
+++ b/solution.py
@@ -113,14 +113,35 @@
     return own_full, foreign_full
 
 
-def split_projection(head_values, side_rows):
+def line_blocks(block, axis):
+    count = lax.axis_size(axis)
+    here = lax.axis_index(axis)
+    blocks = [(block, here)]
+    rising, falling = block, block
+    for step in range(1, count):
+        rising = lax.ppermute(rising, axis, [(i, i + 1) for i in range(step - 1, count - 1)])
+        falling = lax.ppermute(falling, axis, [(i, i - 1) for i in range(1, count - step + 1)])
+        blocks.append((rising, jnp.clip(here - step, 0, count - 1)))
+        blocks.append((falling, jnp.clip(here + step, 0, count - 1)))
+    return blocks
+
+
+def blockwise(heads, blocks, block_rows):
+    total = None
+    for block, row_block in blocks:
+        columns = lax.dynamic_slice_in_dim(heads, row_block * block_rows, block_rows, 1)
+        part = jnp.dot(columns, block, preferred_element_type=jnp.float32)
+        total = part if total is None else total + part
+    return total
+
+
+def split_projection(head_values, chained):
+    block_rows = chained[0][0].shape[0]
     own_full, foreign_full = needed_heads(head_values)
-    partner = jnp.dot(foreign_full, side_rows, preferred_element_type=jnp.float32)
-    outgoing = partner.astype(jnp.bfloat16)
+    outgoing = blockwise(foreign_full, chained, block_rows).astype(jnp.bfloat16)
     returned = swapped(outgoing, "dp")
-    outgoing, own_full, side_rows = lax.optimization_barrier((outgoing, own_full, side_rows))
-    local = jnp.dot(own_full, side_rows, preferred_element_type=jnp.float32)
-    local = lax.optimization_barrier(local)
+    outgoing, own_full, chained = lax.optimization_barrier((outgoing, own_full, chained))
+    local = lax.optimization_barrier(blockwise(own_full, chained, block_rows))
     return local + returned.astype(jnp.float32)
 
 
@@ -130,9 +151,9 @@
     side_width = block_rows * lax.axis_size("ctx")
     fits = lax.axis_size("tensor") == 4
     if lax.axis_size("dp") == 2 and side_width == 2 * width and fits:
-        side_rows = lax.all_gather(output_weight, "ctx", axis=0, tiled=True)
+        chained = line_blocks(output_weight, "ctx")
         head_values = attention(queries, keyvals, documents)
-        result = split_projection(head_values, side_rows)
+        result = split_projection(head_values, chained)
         return result.astype(jnp.bfloat16)[None]
     all_rows = lax.all_gather(output_weight, ("dp", "ctx"), axis=0, tiled=True)
     head_values = attention(queries, keyvals, documents)

time: 88 us -> 91.1 us (1.035)
  the two profiles are of different devices: /device:TPU:18 before, /device:TPU:0 now
where the time goes in v8:
time: 91.1 us; the launch traced here: 90.5 us
  starting transfers between devices  32.1 us (35%)
  waiting for transfers between devices  29.7 us (33%)
  matrix products  17 us (19%)
  other arithmetic  8.22 us (9%)
  local copies, waits for them, and re-layouts  3.03 us (3%)
    ppermute x3, waiting for transfers between devices, line_blocks(): lax.ppermute(falling, axis, [(i, i - 1) for i in range(1, count - step +...  21.3 us
    dot_general x14, matrix products, blockwise(): part = jnp.dot(columns, block, preferred_element_type=jnp.float32)  15.4 us
    ppermute x2, starting transfers between devices, shifted(): return lax.ppermute(block, axis, route)  9.44 us
    ppermute x3, starting transfers between devices, line_blocks(): lax.ppermute(rising, axis, [(i, i + 1) for i in range(step - 1, count - 1)])  8.96 us
    ppermute x3, starting transfers between devices, sent(): return lax.ppermute(block, ('dp', 'tensor'), route)  7.63 us
    ppermute x3, waiting for transfers between devices, line_blocks(): lax.ppermute(rising, axis, [(i, i + 1) for i in range(step - 1, count - 1)])  4.62 us
    ppermute x3, starting transfers between devices, line_blocks(): lax.ppermute(falling, axis, [(i, i - 1) for i in range(1, count - step +...  3.85 us
    ppermute x2, waiting for transfers between devices, shifted(): return lax.ppermute(block, axis, route)  3.79 us
  transfers between devices with their start and end apart: 13, of which 6 were waited for; matrix products, arithmetic and copies ran while one was open for 19% of the time, Pallas kernels for 0%

profile of v8, /device:TPU:0, one launch (start us, length us, event | category | flops | bytes accessed | tf_op | source)
XLA Modules:
  0.0 90.5 jit_solution(14835549700252891227)
XLA Ops:
  0.0 0.7 convert_element_type.37
  0.7 0.9 %copy.21 = bf16[1,256,2,128]{3,1,2,0:T(8,128)(2,1)S(1)} copy(bf16[1,256,2,128]{3,2,1,0:T(2,128)(2,1)} %param.5) | data formatting | bytes 262144 | tf_op args[1]
  1.6 0.1 broadcast_in_dim.27
  1.7 6.0 %collective-permute-start.1 = (bf16[256,3,128]{2,0,1:T(8,128)(2,1)S(1)}, bf16[256,3,128]{2,0,1:T(8,128)(2,1)S(1)}, u32[]{:S(2)}, u32[]{:S(2)}) collective-permute-start(bf16[256,3,128]{2,0,1:T(8,128)(2,1)S(1)} %pad_maximum_fusion.3), channel_id=1, source_target_pairs={{0,8},{4,12},{1,9},{5,13},{2,10},{6,14},{3,11},{7,15},{16,24},{20,... | collective-permute-start | bytes 589832 | tf_op jit(solution)/shard_map/ppermute | solution.py:17
  7.7 3.5 %collective-permute-start = (bf16[256,3,128]{2,0,1:T(8,128)(2,1)S(1)}, bf16[256,3,128]{2,0,1:T(8,128)(2,1)S(1)}, u32[]{:S(2)}, u32[]{:S(2)}) collective-permute-start(bf16[256,3,128]{2,0,1:T(8,128)(2,1)S(1)} %pad_maximum_fusion.3), channel_id=1, source_target_pairs={{0,4},{4,8},{8,12},{1,5},{5,9},{9,13},{2,6},{6,10},{10,14},{3,7},{... | collective-permute-start | bytes 589832 | tf_op jit(solution)/shard_map/ppermute | solution.py:17
  11.2 1.0 %reshape.68 = bf16[256,4,128]{2,1,0:T(4,128)(2,1)S(1)} reshape(bf16[1,256,512]{2,1,0:T(8,128)(2,1)} %param.4) | data formatting | bytes 524288 | tf_op jit(solution)/shard_map/reshape.3
  12.3 0.6 collective-permute-done.1
  12.9 3.2 %collective-permute-done = bf16[256,3,128]{2,0,1:T(8,128)(2,1)S(1)} collective-permute-done((bf16[256,3,128]{2,0,1:T(8,128)(2,1)S(1)}, bf16[256,3,128]{2,0,1:T(8,128)(2,1)S(1)}, u32[]{:S(2)}, u32[]{:S(2)}) %collective-permute-start) | collective-permute-done | bytes 196640 | tf_op jit(solution)/shard_map/ppermute | solution.py:17
  16.1 0.1 convert_reduce_fusion
  16.3 0.1 convert_reduce_fusion.1
  16.4 0.7 pad_add_fusion
  17.1 1.4 %and_and_fusion = pred[256,768]{0,1:T(8,128)(4,1)S(1)} fusion(s32[256]{0:T(256)S(1)} %iota_add_fusion.2, s32[256]{0:T(256)} %bitcast.83, s32[768]{0:T(1024)S(1)} %pad_add_fusion.1, s32[768]{0:T(1024)S(1)} %pad_add_fusion, pred[768]{0:T(1024)(128)(4,1)S(1)} %broadcast_compare_fusion), kind=kLoop, calls=%fused_computation.39 | loop fusion | flops 786432 | bytes 205568 | tf_op jit(solution)/shard_map/and | solution.py:64
  18.5 0.7 fusion
  19.1 0.8 fusion.1
  19.9 1.0 %fusion.21 = bf16[256,1,4,128]{0,3,2,1:T(8,128)(2,1)S(1)} fusion(f32[768,256,4]{1,0,2:T(8,128)S(1)} %get-tuple-element.42, f32[4,256]{1,0:T(4,128)S(1)} %get-tuple-element.41, pred[256,768]{0,1:T(8,128)(4,1)S(1)} %and_and_fusion, f32[256,4]{0,1:T(4,128)S(1)} %bitcast.80, bf16[768,2,128]{2,0,1:T(8,128)(2,1)S(1)} %pad_maximum_fusion.2), kind=kOutput, calls=%fused_computation.24 | convolution fusion | flops 205520896 | bytes 3809280 | tf_op jit(solution)/shard_map/hgqk,khd->qhgd/dot_general | solution.py:72
  20.9 1.6 %collective-permute-start.2 = (bf16[256,512]{0,1:T(8,128)(2,1)S(1)}, bf16[256,512]{0,1:T(8,128)(2,1)S(1)}, u32[]{:S(2)}, u32[]{:S(2)}) collective-permute-start(bf16[256,512]{0,1:T(8,128)(2,1)S(1)} %bitcast.77), channel_id=1, source_target_pairs={{0,16},{16,0},{1,17},{17,1},{2,18},{18,2},{3,19},{19,3},{4,20},{20... | collective-permute-start | bytes 786440 | tf_op jit(solution)/shard_map/ppermute | solution.py:85
  22.5 7.6 %collective-permute-start.6 = (bf16[256,1024]{1,0:T(8,128)(2,1)S(1)}, bf16[256,1024]{1,0:T(8,128)(2,1)S(1)}, u32[]{:S(2)}, u32[]{:S(2)}) collective-permute-start(bf16[256,1024]{1,0:T(8,128)(2,1)S(1)} %copy-done.2), channel_id=1, source_target_pairs={{0,4},{4,8},{8,12},{1,5},{5,9},{9,13},{2,6},{6,10},{10,14},{3,7},{... | collective-permute-start | bytes 1572872 | tf_op jit(solution)/shard_map/ppermute | solution.py:122
  30.1 1.3 %collective-permute-start.7 = (bf16[256,1024]{1,0:T(8,128)(2,1)S(1)}, bf16[256,1024]{1,0:T(8,128)(2,1)S(1)}, u32[]{:S(2)}, u32[]{:S(2)}) collective-permute-start(bf16[256,1024]{1,0:T(8,128)(2,1)S(1)} %copy-done.2), channel_id=1, source_target_pairs={{4,0},{8,4},{12,8},{5,1},{9,5},{13,9},{6,2},{10,6},{14,10},{7,3},{... | collective-permute-start | bytes 1572872 | tf_op jit(solution)/shard_map/ppermute | solution.py:123
  31.4 0.9 pad_maximum_fusion
  32.2 4.2 %collective-permute-start.3 = (bf16[256,1024]{0,1:T(8,128)(2,1)}, bf16[256,1024]{0,1:T(8,128)(2,1)}, u32[]{:S(2)}, u32[]{:S(2)}) collective-permute-start(bf16[256,1024]{0,1:T(8,128)(2,1)} %pad_maximum_fusion), channel_id=1, source_target_pairs={{0,2},{1,3},{18,16},{19,17},{4,6},{5,7},{22,20},{23,21},{8,10},{9,... | collective-permute-start | bytes 1572872 | tf_op jit(solution)/shard_map/ppermute | solution.py:89
  36.5 4.6 %collective-permute-done.6 = bf16[256,1024]{1,0:T(8,128)(2,1)S(1)} collective-permute-done((bf16[256,1024]{1,0:T(8,128)(2,1)S(1)}, bf16[256,1024]{1,0:T(8,128)(2,1)S(1)}, u32[]{:S(2)}, u32[]{:S(2)}) %collective-permute-start.6) | collective-permute-done | bytes 524320 | tf_op jit(solution)/shard_map/ppermute | solution.py:122
  41.1 0.7 collective-permute-start.8
  41.8 4.2 %collective-permute-done.7 = bf16[256,1024]{1,0:T(8,128)(2,1)S(1)} collective-permute-done((bf16[256,1024]{1,0:T(8,128)(2,1)S(1)}, bf16[256,1024]{1,0:T(8,128)(2,1)S(1)}, u32[]{:S(2)}, u32[]{:S(2)}) %collective-permute-start.7) | collective-permute-done | bytes 524320 | tf_op jit(solution)/shard_map/ppermute | solution.py:123
  46.0 1.3 %collective-permute-start.9 = (bf16[256,1024]{1,0:T(8,128)(2,1)S(1)}, bf16[256,1024]{1,0:T(8,128)(2,1)S(1)}, u32[]{:S(2)}, u32[]{:S(2)}) collective-permute-start(bf16[256,1024]{1,0:T(8,128)(2,1)S(1)} %collective-permute-done.7), channel_id=1, source_target_pairs={{4,0},{8,4},{5,1},{9,5},{6,2},{10,6},{7,3},{11,7},{20,16},{24,20},... | collective-permute-start | bytes 1572872 | tf_op jit(solution)/shard_map/ppermute | solution.py:123
  47.3 1.9 %collective-permute-start.4 = (bf16[256,1024]{0,1:T(8,128)(2,1)}, bf16[256,1024]{0,1:T(8,128)(2,1)}, u32[]{:S(2)}, u32[]{:S(2)}) collective-permute-start(bf16[256,1024]{0,1:T(8,128)(2,1)} %pad_maximum_fusion), channel_id=1, source_target_pairs={{0,1},{1,0},{18,19},{19,18},{4,5},{5,4},{22,23},{23,22},{8,9},{9,8... | collective-permute-start | bytes 1572872 | tf_op jit(solution)/shard_map/ppermute | solution.py:89
  49.2 1.5 %collective-permute-start.5 = (bf16[256,1024]{0,1:T(8,128)(2,1)}, bf16[256,1024]{0,1:T(8,128)(2,1)}, u32[]{:S(2)}, u32[]{:S(2)}) collective-permute-start(bf16[256,1024]{0,1:T(8,128)(2,1)} %collective-permute-done.3), channel_id=1, source_target_pairs={{2,3},{3,2},{16,17},{17,16},{6,7},{7,6},{20,21},{21,20},{10,11},{1... | collective-permute-start | bytes 1572872 | tf_op jit(solution)/shard_map/ppermute | solution.py:89
  50.7 0.7 collective-permute-start.10
  51.4 9.2 %collective-permute-done.9 = bf16[256,1024]{1,0:T(8,128)(2,1)S(1)} collective-permute-done((bf16[256,1024]{1,0:T(8,128)(2,1)S(1)}, bf16[256,1024]{1,0:T(8,128)(2,1)S(1)}, u32[]{:S(2)}, u32[]{:S(2)}) %collective-permute-start.9) | collective-permute-done | bytes 524320 | tf_op jit(solution)/shard_map/ppermute | solution.py:123
  60.6 1.3 %collective-permute-start.11 = (bf16[256,1024]{1,0:T(8,128)(2,1)S(1)}, bf16[256,1024]{1,0:T(8,128)(2,1)S(1)}, u32[]{:S(2)}, u32[]{:S(2)}) collective-permute-start(bf16[256,1024]{1,0:T(8,128)(2,1)S(1)} %collective-permute-done.9), channel_id=1, source_target_pairs={{4,0},{5,1},{6,2},{7,3},{20,16},{21,17},{22,18},{23,19}} | collective-permute-start | bytes 1572872 | tf_op jit(solution)/shard_map/ppermute | solution.py:123
  61.9 1.4 %broadcast_select_fusion.2 = (bf16[256,1024]{0,1:T(8,128)(2,1)S(1)}, bf16[256,1024]{0,1:T(8,128)(2,1)S(1)}) fusion(pred[]{:T(512)S(6)} %eq.21, bf16[256,1024]{0,1:T(8,128)(2,1)} %collective-permute-done.3, pred[]{:T(512)S(6)} %eq.22, bf16[256,1024]{0,1:T(8,128)(2,1)} %collective-permute-done.4, bf16[256,1024]{0,1:T(8,128)(2,1)} %collective-permute-done.5, ...), kind=kLoop, calls=%fused_computation.45 | loop fusion | flops 2097152 | bytes 3145730 | tf_op jit(solution)/shard_map/jit(_where)/select_n | solution.py:110
  63.5 0.6 fusion.31
  64.0 0.6 convolution_add_fusion.4
  64.7 0.5 convolution_add_fusion.3
  65.2 0.6 fusion.40
  65.8 0.6 fusion.13
  66.3 7.9 %collective-permute-done.11 = bf16[256,1024]{1,0:T(8,128)(2,1)S(1)} collective-permute-done((bf16[256,1024]{1,0:T(8,128)(2,1)S(1)}, bf16[256,1024]{1,0:T(8,128)(2,1)S(1)}, u32[]{:S(2)}, u32[]{:S(2)}) %collective-permute-start.11) | collective-permute-done | bytes 524320 | tf_op jit(solution)/shard_map/ppermute | solution.py:123
  74.2 0.5 fusion.28
  74.8 0.8 copy-done.9
  75.6 1.3 %fusion.14 = bf16[256,1024]{1,0:T(8,128)(2,1)} fusion(f32[256,1024]{1,0:T(8,128)S(1)} %fusion.28, f32[256,1024]{1,0:T(8,128)S(1)} %fusion.13, bf16[256,1024]{1,0:T(8,128)(2,1)S(1)} %collective-permute-done.10, s32[]{:T(128)S(6)} %select_n.97, bf16[256,512]{0,1:T(8,128)(2,1)S(1)} %get-tuple-element.38, bf16[256,512]{0,1:T(8,128)(2,1)S(1)} %get-tuple-element.40), kind=kOutput, calls=%fused_computation.20 | convolution fusion | flops 135266304 | bytes 3670020 | tf_op jit(solution)/shard_map/dot_general | solution.py:133
  76.9 0.7 collective-permute-start.12
  77.6 0.3 fusion.54
  78.0 1.4 %fusion.52 = f32[256,1024]{1,0:T(8,128)S(1)} fusion(bf16[256,1024]{1,0:T(8,128)(2,1)} %copy-done.7, bf16[256,1024]{0,1:T(8,128)(2,1)S(1)} %pad_maximum_fusion.1, s32[]{:T(128)S(6)} %select_n.101), kind=kOutput, calls=%fused_computation.74 | convolution fusion | flops 134217728 | bytes 1703940 | tf_op jit(solution)/shard_map/dot_general | solution.py:133
  79.4 1.5 %fusion.50 = f32[256,1024]{1,0:T(8,128)S(1)} fusion(bf16[256,1024]{1,0:T(8,128)(2,1)} %copy-done.3, bf16[256,1024]{0,1:T(8,128)(2,1)} %copy-done, s32[]{:T(128)S(6)} %select_n.102), kind=kOutput, calls=%fused_computation.72 | convolution fusion | flops 134217728 | bytes 1703940 | tf_op jit(solution)/shard_map/dot_general | solution.py:133
  80.9 2.4 %fusion.48 = f32[256,1024]{1,0:T(8,128)} fusion(bf16[256,1024]{1,0:T(8,128)(2,1)} %copy-done.4, bf16[256,1024]{0,1:T(8,128)(2,1)} %copy-done, s32[]{:T(128)S(6)} %select_n.103), kind=kOutput, calls=%fused_computation.70 | convolution fusion | flops 134217728 | bytes 1703940 | tf_op jit(solution)/shard_map/dot_general | solution.py:133
  83.3 1.3 %fusion.46 = f32[256,1024]{1,0:T(8,128)} fusion(bf16[256,1024]{1,0:T(8,128)(2,1)S(1)} %copy-done.10, bf16[256,1024]{0,1:T(8,128)(2,1)S(1)} %copy-done.1, s32[]{:T(128)S(6)} %select_n.104), kind=kOutput, calls=%fused_computation.68 | convolution fusion | flops 134217728 | bytes 1703940 | tf_op jit(solution)/shard_map/dot_general | solution.py:133
  84.6 1.3 %fusion.44 = f32[256,1024]{1,0:T(8,128)} fusion(bf16[256,1024]{1,0:T(8,128)(2,1)S(1)} %copy-done.6, bf16[256,1024]{0,1:T(8,128)(2,1)S(1)} %copy-done.1, s32[]{:T(128)S(6)} %select_n.105), kind=kOutput, calls=%fused_computation.66 | convolution fusion | flops 134217728 | bytes 1703940 | tf_op jit(solution)/shard_map/dot_general | solution.py:133
  85.9 2.5 %fusion.11 = f32[256,1024]{1,0:T(8,128)S(1)} fusion(f32[256,1024]{1,0:T(8,128)} %fusion.44, f32[256,1024]{1,0:T(8,128)} %fusion.46, f32[256,1024]{1,0:T(8,128)} %fusion.48, f32[256,1024]{1,0:T(8,128)S(1)} %fusion.50, f32[256,1024]{1,0:T(8,128)S(1)} %fusion.52, f32[256,1024]{1,0:T(8,128)S(1)} %fusion.54, bf16[256,1024]{1,0:T(8,128)(2,1)} %param.7, ...), kind=kOutput, calls=%fused_computation.13 | convolution fusion | flops 135790592 | bytes 7995396 | tf_op jit(solution)/shard_map/dot_general | solution.py:133
  88.5 2.0 %fusion.24 = bf16[1,256,1024]{2,1,0:T(8,128)(2,1)} fusion(f32[256,1024]{1,0:T(8,128)S(1)} %fusion.11, bf16[256,1024]{1,0:T(8,128)(2,1)} %collective-permute-done.12), kind=kLoop, calls=%fused_computation.40 | loop fusion | flops 786432 | bytes 2097152 | tf_op jit(solution)/shard_map/broadcast_in_dim | solution.py:157
  (41 shorter events, 0.3 us)
Async XLA Ops:
  1.7 11.1 %collective-permute-start.1 = (bf16[256,3,128]{2,0,1:T(8,128)(2,1)S(1)}, bf16[256,3,128]{2,0,1:T(8,128)(2,1)S(1)}, u32[]{:S(2)}, u32[]{:S(2)}) collective-permute-start(bf16[256,3,128]{2,0,1:T(8,128)(2,1)S(1)} %pad_maximum_fusion.3), channel_id=1, source_target_pairs={{0,8},{4,12},{1,9},{5,13},{2,10},{6,14},{3,11},{7,15},{16,24},{20,... | collective-permute-start | bytes 589832 | tf_op jit(solution)/shard_map/ppermute | solution.py:17
  7.7 8.4 %collective-permute-start = (bf16[256,3,128]{2,0,1:T(8,128)(2,1)S(1)}, bf16[256,3,128]{2,0,1:T(8,128)(2,1)S(1)}, u32[]{:S(2)}, u32[]{:S(2)}) collective-permute-start(bf16[256,3,128]{2,0,1:T(8,128)(2,1)S(1)} %pad_maximum_fusion.3), channel_id=1, source_target_pairs={{0,4},{4,8},{8,12},{1,5},{5,9},{9,13},{2,6},{6,10},{10,14},{3,7},{... | collective-permute-start | bytes 589832 | tf_op jit(solution)/shard_map/ppermute | solution.py:17
  19.9 2.5 %copy-start.2 = (bf16[256,1024]{1,0:T(8,128)(2,1)S(1)}, bf16[256,1024]{1,0:T(8,128)(2,1)}, u32[]{:S(2)}) copy-start(bf16[256,1024]{1,0:T(8,128)(2,1)} %param.7) | copy-start | bytes 1572868
  20.9 10.5 %collective-permute-start.2 = (bf16[256,512]{0,1:T(8,128)(2,1)S(1)}, bf16[256,512]{0,1:T(8,128)(2,1)S(1)}, u32[]{:S(2)}, u32[]{:S(2)}) collective-permute-start(bf16[256,512]{0,1:T(8,128)(2,1)S(1)} %bitcast.77), channel_id=1, source_target_pairs={{0,16},{16,0},{1,17},{17,1},{2,18},{18,2},{3,19},{19,3},{4,20},{20... | collective-permute-start | bytes 786440 | tf_op jit(solution)/shard_map/ppermute | solution.py:85
  22.5 18.6 %collective-permute-start.6 = (bf16[256,1024]{1,0:T(8,128)(2,1)S(1)}, bf16[256,1024]{1,0:T(8,128)(2,1)S(1)}, u32[]{:S(2)}, u32[]{:S(2)}) collective-permute-start(bf16[256,1024]{1,0:T(8,128)(2,1)S(1)} %copy-done.2), channel_id=1, source_target_pairs={{0,4},{4,8},{8,12},{1,5},{5,9},{9,13},{2,6},{6,10},{10,14},{3,7},{... | collective-permute-start | bytes 1572872 | tf_op jit(solution)/shard_map/ppermute | solution.py:122
  30.1 15.9 %collective-permute-start.7 = (bf16[256,1024]{1,0:T(8,128)(2,1)S(1)}, bf16[256,1024]{1,0:T(8,128)(2,1)S(1)}, u32[]{:S(2)}, u32[]{:S(2)}) collective-permute-start(bf16[256,1024]{1,0:T(8,128)(2,1)S(1)} %copy-done.2), channel_id=1, source_target_pairs={{4,0},{8,4},{12,8},{5,1},{9,5},{13,9},{6,2},{10,6},{14,10},{7,3},{... | collective-permute-start | bytes 1572872 | tf_op jit(solution)/shard_map/ppermute | solution.py:123
  31.4 30.5 %copy-start.11 = (bf16[256,512]{0,1:T(8,128)(2,1)}, bf16[256,512]{0,1:T(8,128)(2,1)S(1)}, u32[]{:S(2)}) copy-start(bf16[256,512]{0,1:T(8,128)(2,1)S(1)} %collective-permute-done.2) | copy-start | bytes 786436
  32.2 16.9 %collective-permute-start.3 = (bf16[256,1024]{0,1:T(8,128)(2,1)}, bf16[256,1024]{0,1:T(8,128)(2,1)}, u32[]{:S(2)}, u32[]{:S(2)}) collective-permute-start(bf16[256,1024]{0,1:T(8,128)(2,1)} %pad_maximum_fusion), channel_id=1, source_target_pairs={{0,2},{1,3},{18,16},{19,17},{4,6},{5,7},{22,20},{23,21},{8,10},{9,... | collective-permute-start | bytes 1572872 | tf_op jit(solution)/shard_map/ppermute | solution.py:89
  41.1 9.6 %collective-permute-start.8 = (bf16[256,1024]{1,0:T(8,128)(2,1)S(1)}, bf16[256,1024]{1,0:T(8,128)(2,1)S(1)}, u32[]{:S(2)}, u32[]{:S(2)}) collective-permute-start(bf16[256,1024]{1,0:T(8,128)(2,1)S(1)} %collective-permute-done.6), channel_id=1, source_target_pairs={{4,8},{8,12},{5,9},{9,13},{6,10},{10,14},{7,11},{11,15},{20,24},{2... | collective-permute-start | bytes 1572872 | tf_op jit(solution)/shard_map/ppermute | solution.py:122
  46.0 5.4 %copy-start.7 = (bf16[256,1024]{1,0:T(8,128)(2,1)}, bf16[256,1024]{1,0:T(8,128)(2,1)S(1)}, u32[]{:S(2)}) copy-start(bf16[256,1024]{1,0:T(8,128)(2,1)S(1)} %collective-permute-done.7) | copy-start | bytes 1572868
  46.0 14.6 %collective-permute-start.9 = (bf16[256,1024]{1,0:T(8,128)(2,1)S(1)}, bf16[256,1024]{1,0:T(8,128)(2,1)S(1)}, u32[]{:S(2)}, u32[]{:S(2)}) collective-permute-start(bf16[256,1024]{1,0:T(8,128)(2,1)S(1)} %collective-permute-done.7), channel_id=1, source_target_pairs={{4,0},{8,4},{5,1},{9,5},{6,2},{10,6},{7,3},{11,7},{20,16},{24,20},... | collective-permute-start | bytes 1572872 | tf_op jit(solution)/shard_map/ppermute | solution.py:123
  47.3 14.6 %collective-permute-start.4 = (bf16[256,1024]{0,1:T(8,128)(2,1)}, bf16[256,1024]{0,1:T(8,128)(2,1)}, u32[]{:S(2)}, u32[]{:S(2)}) collective-permute-start(bf16[256,1024]{0,1:T(8,128)(2,1)} %pad_maximum_fusion), channel_id=1, source_target_pairs={{0,1},{1,0},{18,19},{19,18},{4,5},{5,4},{22,23},{23,22},{8,9},{9,8... | collective-permute-start | bytes 1572872 | tf_op jit(solution)/shard_map/ppermute | solution.py:89
  49.2 12.7 %collective-permute-start.5 = (bf16[256,1024]{0,1:T(8,128)(2,1)}, bf16[256,1024]{0,1:T(8,128)(2,1)}, u32[]{:S(2)}, u32[]{:S(2)}) collective-permute-start(bf16[256,1024]{0,1:T(8,128)(2,1)} %collective-permute-done.3), channel_id=1, source_target_pairs={{2,3},{3,2},{16,17},{17,16},{6,7},{7,6},{20,21},{21,20},{10,11},{1... | collective-permute-start | bytes 1572872 | tf_op jit(solution)/shard_map/ppermute | solution.py:89
  50.7 15.1 %copy-start.3 = (bf16[256,1024]{1,0:T(8,128)(2,1)}, bf16[256,1024]{1,0:T(8,128)(2,1)S(1)}, u32[]{:S(2)}) copy-start(bf16[256,1024]{1,0:T(8,128)(2,1)S(1)} %collective-permute-done.8) | copy-start | bytes 1572868
  50.7 24.1 %collective-permute-start.10 = (bf16[256,1024]{1,0:T(8,128)(2,1)S(1)}, bf16[256,1024]{1,0:T(8,128)(2,1)S(1)}, u32[]{:S(2)}, u32[]{:S(2)}) collective-permute-start(bf16[256,1024]{1,0:T(8,128)(2,1)S(1)} %collective-permute-done.8), channel_id=1, source_target_pairs={{8,12},{9,13},{10,14},{11,15},{24,28},{25,29},{26,30},{27,31}} | collective-permute-start | bytes 1572872 | tf_op jit(solution)/shard_map/ppermute | solution.py:122
  60.6 4.6 %copy-start.4 = (bf16[256,1024]{1,0:T(8,128)(2,1)}, bf16[256,1024]{1,0:T(8,128)(2,1)S(1)}, u32[]{:S(2)}) copy-start(bf16[256,1024]{1,0:T(8,128)(2,1)S(1)} %collective-permute-done.9) | copy-start | bytes 1572868
  60.6 13.6 %collective-permute-start.11 = (bf16[256,1024]{1,0:T(8,128)(2,1)S(1)}, bf16[256,1024]{1,0:T(8,128)(2,1)S(1)}, u32[]{:S(2)}, u32[]{:S(2)}) collective-permute-start(bf16[256,1024]{1,0:T(8,128)(2,1)S(1)} %collective-permute-done.9), channel_id=1, source_target_pairs={{4,0},{5,1},{6,2},{7,3},{20,16},{21,17},{22,18},{23,19}} | collective-permute-start | bytes 1572872 | tf_op jit(solution)/shard_map/ppermute | solution.py:123
  63.4 1.2 %copy-start.8 = (bf16[256,1024]{1,0:T(8,128)(2,1)S(1)}, bf16[256,1024]{1,0:T(8,128)(2,1)}, u32[]{:S(2)}) copy-start(bf16[256,1024]{1,0:T(8,128)(2,1)} %copy-done.7) | copy-start | bytes 1572868
  63.5 14.5 %copy-start = (bf16[256,1024]{0,1:T(8,128)(2,1)}, bf16[256,1024]{0,1:T(8,128)(2,1)S(1)}, u32[]{:S(2)}) copy-start(bf16[256,1024]{0,1:T(8,128)(2,1)S(1)} %pad_maximum_fusion.1) | copy-start | bytes 1572868
  74.2 3.4 %copy-start.5 = (bf16[256,1024]{1,0:T(8,128)(2,1)}, bf16[256,1024]{1,0:T(8,128)(2,1)S(1)}, u32[]{:S(2)}) copy-start(bf16[256,1024]{1,0:T(8,128)(2,1)S(1)} %collective-permute-done.11) | copy-start | bytes 1572868
  74.8 0.8 copy-start.9
  76.9 11.6 %collective-permute-start.12 = (bf16[256,1024]{1,0:T(8,128)(2,1)}, bf16[256,1024]{1,0:T(8,128)(2,1)}, u32[]{:S(2)}, u32[]{:S(2)}) collective-permute-start(bf16[256,1024]{1,0:T(8,128)(2,1)} %fusion.14), channel_id=1, source_target_pairs={{0,16},{16,0},{1,17},{17,1},{2,18},{18,2},{3,19},{19,3},{4,20},{20... | collective-permute-start | bytes 1572872 | tf_op jit(solution)/shard_map/ppermute | solution.py:85
  77.6 5.7 %copy-start.10 = (bf16[256,1024]{1,0:T(8,128)(2,1)S(1)}, bf16[256,1024]{1,0:T(8,128)(2,1)}, u32[]{:S(2)}) copy-start(bf16[256,1024]{1,0:T(8,128)(2,1)} %copy-done.9) | copy-start | bytes 1572868
  77.9 6.7 %copy-start.6 = (bf16[256,1024]{1,0:T(8,128)(2,1)S(1)}, bf16[256,1024]{1,0:T(8,128)(2,1)}, u32[]{:S(2)}) copy-start(bf16[256,1024]{1,0:T(8,128)(2,1)} %copy-done.5) | copy-start | bytes 1572868
  79.4 3.9 %copy-start.1 = (bf16[256,1024]{0,1:T(8,128)(2,1)S(1)}, bf16[256,1024]{0,1:T(8,128)(2,1)}, u32[]{:S(2)}) copy-start(bf16[256,1024]{0,1:T(8,128)(2,1)} %copy-done) | copy-start | bytes 1572868

commit v9 on v7

--- a/solution.py
+++ b/solution.py
@@ -113,6 +113,25 @@
     return own_full, foreign_full
 
 
+def line_rows(block, axis):
+    count = lax.axis_size(axis)
+    here = lax.axis_index(axis)
+    arrivals = [(block, 0)]
+    rising, falling = block, block
+    for step in range(1, count):
+        rising = lax.ppermute(rising, axis, [(i, i + 1) for i in range(step - 1, count - 1)])
+        falling = lax.ppermute(falling, axis, [(i, i - 1) for i in range(1, count - step + 1)])
+        arrivals.append((rising, -step))
+        arrivals.append((falling, step))
+    ordered = []
+    for place in range(count):
+        chosen = jnp.zeros_like(block)
+        for arrived, offset in arrivals:
+            chosen = jnp.where(here + offset == place, arrived, chosen)
+        ordered.append(chosen)
+    return jnp.concatenate(ordered, axis=0)
+
+
 def split_projection(head_values, side_rows):
     own_full, foreign_full = needed_heads(head_values)
     partner = jnp.dot(foreign_full, side_rows, preferred_element_type=jnp.float32)
@@ -130,7 +149,7 @@
     side_width = block_rows * lax.axis_size("ctx")
     fits = lax.axis_size("tensor") == 4
     if lax.axis_size("dp") == 2 and side_width == 2 * width and fits:
-        side_rows = lax.all_gather(output_weight, "ctx", axis=0, tiled=True)
+        side_rows = line_rows(output_weight, "ctx")
         head_values = attention(queries, keyvals, documents)
         result = split_projection(head_values, side_rows)
         return result.astype(jnp.bfloat16)[None]

time: 88 us -> 88.1 us (level)
  the two profiles are of different devices: /device:TPU:18 before, /device:TPU:0 now
where the time goes in v9:
time: 88.1 us; the launch traced here: 87.7 us
  waiting for transfers between devices  42.1 us (48%)
  starting transfers between devices  32.2 us (37%)
  other arithmetic  7.88 us (9%)
  matrix products  3.06 us (3%)
  local copies, waits for them, and re-layouts  2.13 us (2%)
    ppermute x3, waiting for transfers between devices, line_rows(): lax.ppermute(falling, axis, [(i, i - 1) for i in range(1, count - step +...  24.2 us
    ppermute x2, starting transfers between devices, shifted(): return lax.ppermute(block, axis, route)  9.44 us
    ppermute x2, waiting for transfers between devices, swapped(): return lax.ppermute(block, axis, [(0, 1), (1, 0)])  9.38 us
    ppermute x3, starting transfers between devices, line_rows(): lax.ppermute(rising, axis, [(i, i + 1) for i in range(step - 1, count - 1)])  8.96 us
    ppermute x3, starting transfers between devices, sent(): return lax.ppermute(block, ('dp', 'tensor'), route)  7.62 us
    ppermute x3, waiting for transfers between devices, line_rows(): lax.ppermute(rising, axis, [(i, i + 1) for i in range(step - 1, count - 1)])  4.7 us
    ppermute x3, starting transfers between devices, line_rows(): lax.ppermute(falling, axis, [(i, i - 1) for i in range(1, count - step +...  3.85 us
    ppermute x2, waiting for transfers between devices, shifted(): return lax.ppermute(block, axis, route)  3.79 us
  transfers between devices with their start and end apart: 13, of which 7 were waited for; matrix products, arithmetic and copies ran while one was open for 5% of the time, Pallas kernels for 0%

profile of v9, /device:TPU:0, one launch (start us, length us, event | category | flops | bytes accessed | tf_op | source)
XLA Modules:
  0.0 87.7 jit_solution(4689639788961159337)
XLA Ops:
  0.0 0.7 convert_element_type.37
  0.7 0.9 %copy.21 = bf16[1,256,2,128]{3,1,2,0:T(8,128)(2,1)S(1)} copy(bf16[1,256,2,128]{3,2,1,0:T(2,128)(2,1)} %param.5) | data formatting | bytes 262144 | tf_op args[1]
  1.6 0.1 broadcast_in_dim.27
  1.7 6.0 %collective-permute-start.1 = (bf16[256,3,128]{2,0,1:T(8,128)(2,1)S(1)}, bf16[256,3,128]{2,0,1:T(8,128)(2,1)S(1)}, u32[]{:S(2)}, u32[]{:S(2)}) collective-permute-start(bf16[256,3,128]{2,0,1:T(8,128)(2,1)S(1)} %pad_maximum_fusion.4), channel_id=1, source_target_pairs={{0,8},{4,12},{1,9},{5,13},{2,10},{6,14},{3,11},{7,15},{16,24},{20,... | collective-permute-start | bytes 589832 | tf_op jit(solution)/shard_map/ppermute | solution.py:17
  7.7 3.5 %collective-permute-start = (bf16[256,3,128]{2,0,1:T(8,128)(2,1)S(1)}, bf16[256,3,128]{2,0,1:T(8,128)(2,1)S(1)}, u32[]{:S(2)}, u32[]{:S(2)}) collective-permute-start(bf16[256,3,128]{2,0,1:T(8,128)(2,1)S(1)} %pad_maximum_fusion.4), channel_id=1, source_target_pairs={{0,4},{4,8},{8,12},{1,5},{5,9},{9,13},{2,6},{6,10},{10,14},{3,7},{... | collective-permute-start | bytes 589832 | tf_op jit(solution)/shard_map/ppermute | solution.py:17
  11.2 1.0 %reshape.68 = bf16[256,4,128]{2,1,0:T(4,128)(2,1)S(1)} reshape(bf16[1,256,512]{2,1,0:T(8,128)(2,1)} %param.4) | data formatting | bytes 524288 | tf_op jit(solution)/shard_map/reshape.3
  12.3 0.6 collective-permute-done.1
  12.9 3.2 %collective-permute-done = bf16[256,3,128]{2,0,1:T(8,128)(2,1)S(1)} collective-permute-done((bf16[256,3,128]{2,0,1:T(8,128)(2,1)S(1)}, bf16[256,3,128]{2,0,1:T(8,128)(2,1)S(1)}, u32[]{:S(2)}, u32[]{:S(2)}) %collective-permute-start) | collective-permute-done | bytes 196640 | tf_op jit(solution)/shard_map/ppermute | solution.py:17
  16.1 0.1 convert_reduce_fusion
  16.3 0.1 convert_reduce_fusion.1
  16.4 0.7 pad_add_fusion
  17.1 1.4 %and_and_fusion = pred[256,768]{0,1:T(8,128)(4,1)S(1)} fusion(s32[256]{0:T(256)S(1)} %iota_add_fusion.2, s32[256]{0:T(256)} %bitcast.72, s32[768]{0:T(1024)S(1)} %pad_add_fusion.1, s32[768]{0:T(1024)S(1)} %pad_add_fusion, pred[768]{0:T(1024)(128)(4,1)S(1)} %broadcast_compare_fusion), kind=kLoop, calls=%fused_computation.14 | loop fusion | flops 786432 | bytes 205568 | tf_op jit(solution)/shard_map/and | solution.py:64
  18.5 0.7 fusion
  19.1 0.8 fusion.1
  19.9 1.0 %fusion.13 = bf16[256,1,4,128]{0,3,2,1:T(8,128)(2,1)S(1)} fusion(f32[768,256,4]{1,0,2:T(8,128)S(1)} %get-tuple-element.16, f32[4,256]{1,0:T(4,128)S(1)} %get-tuple-element.15, pred[256,768]{0,1:T(8,128)(4,1)S(1)} %and_and_fusion, f32[256,4]{0,1:T(4,128)S(1)} %bitcast.69, bf16[768,2,128]{2,0,1:T(8,128)(2,1)S(1)} %pad_maximum_fusion.3), kind=kOutput, calls=%fused_computation.13 | convolution fusion | flops 205520896 | bytes 3809280 | tf_op jit(solution)/shard_map/hgqk,khd->qhgd/dot_general | solution.py:72
  20.9 1.6 %collective-permute-start.2 = (bf16[256,512]{0,1:T(8,128)(2,1)S(1)}, bf16[256,512]{0,1:T(8,128)(2,1)S(1)}, u32[]{:S(2)}, u32[]{:S(2)}) collective-permute-start(bf16[256,512]{0,1:T(8,128)(2,1)S(1)} %bitcast.66), channel_id=1, source_target_pairs={{0,16},{16,0},{1,17},{17,1},{2,18},{18,2},{3,19},{19,3},{4,20},{20... | collective-permute-start | bytes 786440 | tf_op jit(solution)/shard_map/ppermute | solution.py:85
  22.5 0.0 copy-done
  22.5 7.6 %collective-permute-start.9 = (bf16[256,1024]{1,0:T(8,128)(2,1)S(1)}, bf16[256,1024]{1,0:T(8,128)(2,1)S(1)}, u32[]{:S(2)}, u32[]{:S(2)}) collective-permute-start(bf16[256,1024]{1,0:T(8,128)(2,1)S(1)} %copy-done), channel_id=1, source_target_pairs={{0,4},{4,8},{8,12},{1,5},{5,9},{9,13},{2,6},{6,10},{10,14},{3,7},{... | collective-permute-start | bytes 1572872 | tf_op jit(solution)/shard_map/ppermute | solution.py:122
  30.1 1.3 %collective-permute-start.6 = (bf16[256,1024]{1,0:T(8,128)(2,1)S(1)}, bf16[256,1024]{1,0:T(8,128)(2,1)S(1)}, u32[]{:S(2)}, u32[]{:S(2)}) collective-permute-start(bf16[256,1024]{1,0:T(8,128)(2,1)S(1)} %copy-done), channel_id=1, source_target_pairs={{4,0},{8,4},{12,8},{5,1},{9,5},{13,9},{6,2},{10,6},{14,10},{7,3},{... | collective-permute-start | bytes 1572872 | tf_op jit(solution)/shard_map/ppermute | solution.py:123
  31.4 0.0 collective-permute-done.2
  31.4 0.8 pad_maximum_fusion.1
  32.2 4.2 %collective-permute-start.3 = (bf16[256,1024]{0,1:T(8,128)(2,1)}, bf16[256,1024]{0,1:T(8,128)(2,1)}, u32[]{:S(2)}, u32[]{:S(2)}) collective-permute-start(bf16[256,1024]{0,1:T(8,128)(2,1)} %pad_maximum_fusion.1), channel_id=1, source_target_pairs={{0,2},{1,3},{18,16},{19,17},{4,6},{5,7},{22,20},{23,21},{8,10},{9,... | collective-permute-start | bytes 1572872 | tf_op jit(solution)/shard_map/ppermute | solution.py:89
  36.4 4.7 %collective-permute-done.9 = bf16[256,1024]{1,0:T(8,128)(2,1)S(1)} collective-permute-done((bf16[256,1024]{1,0:T(8,128)(2,1)S(1)}, bf16[256,1024]{1,0:T(8,128)(2,1)S(1)}, u32[]{:S(2)}, u32[]{:S(2)}) %collective-permute-start.9) | collective-permute-done | bytes 524320 | tf_op jit(solution)/shard_map/ppermute | solution.py:122
  41.1 0.7 collective-permute-start.10
  41.8 4.2 %collective-permute-done.6 = bf16[256,1024]{1,0:T(8,128)(2,1)S(1)} collective-permute-done((bf16[256,1024]{1,0:T(8,128)(2,1)S(1)}, bf16[256,1024]{1,0:T(8,128)(2,1)S(1)}, u32[]{:S(2)}, u32[]{:S(2)}) %collective-permute-start.6) | collective-permute-done | bytes 524320 | tf_op jit(solution)/shard_map/ppermute | solution.py:123
  46.0 1.3 %collective-permute-start.7 = (bf16[256,1024]{1,0:T(8,128)(2,1)S(1)}, bf16[256,1024]{1,0:T(8,128)(2,1)S(1)}, u32[]{:S(2)}, u32[]{:S(2)}) collective-permute-start(bf16[256,1024]{1,0:T(8,128)(2,1)S(1)} %collective-permute-done.6), channel_id=1, source_target_pairs={{4,0},{8,4},{5,1},{9,5},{6,2},{10,6},{7,3},{11,7},{20,16},{24,20},... | collective-permute-start | bytes 1572872 | tf_op jit(solution)/shard_map/ppermute | solution.py:123
  47.3 1.9 %collective-permute-start.4 = (bf16[256,1024]{0,1:T(8,128)(2,1)}, bf16[256,1024]{0,1:T(8,128)(2,1)}, u32[]{:S(2)}, u32[]{:S(2)}) collective-permute-start(bf16[256,1024]{0,1:T(8,128)(2,1)} %pad_maximum_fusion.1), channel_id=1, source_target_pairs={{0,1},{1,0},{18,19},{19,18},{4,5},{5,4},{22,23},{23,22},{8,9},{9,8... | collective-permute-start | bytes 1572872 | tf_op jit(solution)/shard_map/ppermute | solution.py:89
  49.2 0.0 collective-permute-done.3
  49.2 1.5 %collective-permute-start.5 = (bf16[256,1024]{0,1:T(8,128)(2,1)}, bf16[256,1024]{0,1:T(8,128)(2,1)}, u32[]{:S(2)}, u32[]{:S(2)}) collective-permute-start(bf16[256,1024]{0,1:T(8,128)(2,1)} %collective-permute-done.3), channel_id=1, source_target_pairs={{2,3},{3,2},{16,17},{17,16},{6,7},{7,6},{20,21},{21,20},{10,11},{1... | collective-permute-start | bytes 1572872 | tf_op jit(solution)/shard_map/ppermute | solution.py:89
  50.7 0.0 collective-permute-done.10
  50.7 0.7 collective-permute-start.11
  51.4 9.2 %collective-permute-done.7 = bf16[256,1024]{1,0:T(8,128)(2,1)S(1)} collective-permute-done((bf16[256,1024]{1,0:T(8,128)(2,1)S(1)}, bf16[256,1024]{1,0:T(8,128)(2,1)S(1)}, u32[]{:S(2)}, u32[]{:S(2)}) %collective-permute-start.7) | collective-permute-done | bytes 524320 | tf_op jit(solution)/shard_map/ppermute | solution.py:123
  60.6 1.3 %collective-permute-start.8 = (bf16[256,1024]{1,0:T(8,128)(2,1)S(1)}, bf16[256,1024]{1,0:T(8,128)(2,1)S(1)}, u32[]{:S(2)}, u32[]{:S(2)}) collective-permute-start(bf16[256,1024]{1,0:T(8,128)(2,1)S(1)} %collective-permute-done.7), channel_id=1, source_target_pairs={{4,0},{5,1},{6,2},{7,3},{20,16},{21,17},{22,18},{23,19}} | collective-permute-start | bytes 1572872 | tf_op jit(solution)/shard_map/ppermute | solution.py:123
  61.9 0.0 collective-permute-done.4
  61.9 0.0 collective-permute-done.5
  61.9 1.4 %broadcast_select_fusion.3 = (bf16[256,1024]{0,1:T(8,128)(2,1)S(1)}, bf16[256,1024]{0,1:T(8,128)(2,1)S(1)}) fusion(pred[]{:T(512)S(6)} %eq.105, bf16[256,1024]{0,1:T(8,128)(2,1)} %collective-permute-done.3, pred[]{:T(512)S(6)} %eq.106, bf16[256,1024]{0,1:T(8,128)(2,1)} %collective-permute-done.4, bf16[256,1024]{0,1:T(8,128)(2,1)} %collective-permute-done.5, ...), kind=kLoop, calls=%fused_computation.28 | loop fusion | flops 2097152 | bytes 3145730 | tf_op jit(solution)/shard_map/jit(_where)/select_n | solution.py:109
  63.3 0.0 collective-permute-done.11
  63.3 10.9 %collective-permute-done.8 = bf16[256,1024]{1,0:T(8,128)(2,1)S(1)} collective-permute-done((bf16[256,1024]{1,0:T(8,128)(2,1)S(1)}, bf16[256,1024]{1,0:T(8,128)(2,1)S(1)}, u32[]{:S(2)}, u32[]{:S(2)}) %collective-permute-start.8) | collective-permute-done | bytes 524320 | tf_op jit(solution)/shard_map/ppermute | solution.py:123
  74.2 0.2 select_select_fusion
  74.4 0.2 select_select_fusion.1
  74.6 0.2 select_select_fusion.2
  74.7 0.2 select_select_fusion.3
  74.9 0.2 pad_maximum_fusion
  75.1 0.7 convolution_convert_fusion
  75.8 0.8 collective-permute-start.12
  76.6 0.7 fusion.28
  77.3 9.4 %collective-permute-done.12 = bf16[256,1024]{1,0:T(8,128)(2,1)S(1)} collective-permute-done((bf16[256,1024]{1,0:T(8,128)(2,1)S(1)}, bf16[256,1024]{1,0:T(8,128)(2,1)S(1)}, u32[]{:S(2)}, u32[]{:S(2)}) %collective-permute-start.12) | collective-permute-done | bytes 524320 | tf_op jit(solution)/shard_map/ppermute | solution.py:85
  86.7 0.9 %fusion.16 = bf16[1,256,1024]{2,1,0:T(8,128)(2,1)} fusion(f32[256,1024]{1,0:T(8,128)S(1)} %fusion.28, bf16[256,1024]{1,0:T(8,128)(2,1)S(1)} %collective-permute-done.12), kind=kLoop, calls=%fused_computation.15 | loop fusion | flops 786432 | bytes 2097152 | tf_op jit(solution)/shard_map/broadcast_in_dim | solution.py:155
  (12 shorter events, 0.2 us)
Async XLA Ops:
  1.7 11.1 %collective-permute-start.1 = (bf16[256,3,128]{2,0,1:T(8,128)(2,1)S(1)}, bf16[256,3,128]{2,0,1:T(8,128)(2,1)S(1)}, u32[]{:S(2)}, u32[]{:S(2)}) collective-permute-start(bf16[256,3,128]{2,0,1:T(8,128)(2,1)S(1)} %pad_maximum_fusion.4), channel_id=1, source_target_pairs={{0,8},{4,12},{1,9},{5,13},{2,10},{6,14},{3,11},{7,15},{16,24},{20,... | collective-permute-start | bytes 589832 | tf_op jit(solution)/shard_map/ppermute | solution.py:17
  7.7 8.4 %collective-permute-start = (bf16[256,3,128]{2,0,1:T(8,128)(2,1)S(1)}, bf16[256,3,128]{2,0,1:T(8,128)(2,1)S(1)}, u32[]{:S(2)}, u32[]{:S(2)}) collective-permute-start(bf16[256,3,128]{2,0,1:T(8,128)(2,1)S(1)} %pad_maximum_fusion.4), channel_id=1, source_target_pairs={{0,4},{4,8},{8,12},{1,5},{5,9},{9,13},{2,6},{6,10},{10,14},{3,7},{... | collective-permute-start | bytes 589832 | tf_op jit(solution)/shard_map/ppermute | solution.py:17
  19.9 2.5 %copy-start = (bf16[256,1024]{1,0:T(8,128)(2,1)S(1)}, bf16[256,1024]{1,0:T(8,128)(2,1)}, u32[]{:S(2)}) copy-start(bf16[256,1024]{1,0:T(8,128)(2,1)} %param.7) | copy-start | bytes 1572868
  20.9 10.5 %collective-permute-start.2 = (bf16[256,512]{0,1:T(8,128)(2,1)S(1)}, bf16[256,512]{0,1:T(8,128)(2,1)S(1)}, u32[]{:S(2)}, u32[]{:S(2)}) collective-permute-start(bf16[256,512]{0,1:T(8,128)(2,1)S(1)} %bitcast.66), channel_id=1, source_target_pairs={{0,16},{16,0},{1,17},{17,1},{2,18},{18,2},{3,19},{19,3},{4,20},{20... | collective-permute-start | bytes 786440 | tf_op jit(solution)/shard_map/ppermute | solution.py:85
  22.5 18.6 %collective-permute-start.9 = (bf16[256,1024]{1,0:T(8,128)(2,1)S(1)}, bf16[256,1024]{1,0:T(8,128)(2,1)S(1)}, u32[]{:S(2)}, u32[]{:S(2)}) collective-permute-start(bf16[256,1024]{1,0:T(8,128)(2,1)S(1)} %copy-done), channel_id=1, source_target_pairs={{0,4},{4,8},{8,12},{1,5},{5,9},{9,13},{2,6},{6,10},{10,14},{3,7},{... | collective-permute-start | bytes 1572872 | tf_op jit(solution)/shard_map/ppermute | solution.py:122
  30.1 15.9 %collective-permute-start.6 = (bf16[256,1024]{1,0:T(8,128)(2,1)S(1)}, bf16[256,1024]{1,0:T(8,128)(2,1)S(1)}, u32[]{:S(2)}, u32[]{:S(2)}) collective-permute-start(bf16[256,1024]{1,0:T(8,128)(2,1)S(1)} %copy-done), channel_id=1, source_target_pairs={{4,0},{8,4},{12,8},{5,1},{9,5},{13,9},{6,2},{10,6},{14,10},{7,3},{... | collective-permute-start | bytes 1572872 | tf_op jit(solution)/shard_map/ppermute | solution.py:123
  32.2 17.0 %collective-permute-start.3 = (bf16[256,1024]{0,1:T(8,128)(2,1)}, bf16[256,1024]{0,1:T(8,128)(2,1)}, u32[]{:S(2)}, u32[]{:S(2)}) collective-permute-start(bf16[256,1024]{0,1:T(8,128)(2,1)} %pad_maximum_fusion.1), channel_id=1, source_target_pairs={{0,2},{1,3},{18,16},{19,17},{4,6},{5,7},{22,20},{23,21},{8,10},{9,... | collective-permute-start | bytes 1572872 | tf_op jit(solution)/shard_map/ppermute | solution.py:89
  41.1 9.6 %collective-permute-start.10 = (bf16[256,1024]{1,0:T(8,128)(2,1)S(1)}, bf16[256,1024]{1,0:T(8,128)(2,1)S(1)}, u32[]{:S(2)}, u32[]{:S(2)}) collective-permute-start(bf16[256,1024]{1,0:T(8,128)(2,1)S(1)} %collective-permute-done.9), channel_id=1, source_target_pairs={{4,8},{8,12},{5,9},{9,13},{6,10},{10,14},{7,11},{11,15},{20,24},{2... | collective-permute-start | bytes 1572872 | tf_op jit(solution)/shard_map/ppermute | solution.py:122
  46.0 14.6 %collective-permute-start.7 = (bf16[256,1024]{1,0:T(8,128)(2,1)S(1)}, bf16[256,1024]{1,0:T(8,128)(2,1)S(1)}, u32[]{:S(2)}, u32[]{:S(2)}) collective-permute-start(bf16[256,1024]{1,0:T(8,128)(2,1)S(1)} %collective-permute-done.6), channel_id=1, source_target_pairs={{4,0},{8,4},{5,1},{9,5},{6,2},{10,6},{7,3},{11,7},{20,16},{24,20},... | collective-permute-start | bytes 1572872 | tf_op jit(solution)/shard_map/ppermute | solution.py:123
  47.3 14.6 %collective-permute-start.4 = (bf16[256,1024]{0,1:T(8,128)(2,1)}, bf16[256,1024]{0,1:T(8,128)(2,1)}, u32[]{:S(2)}, u32[]{:S(2)}) collective-permute-start(bf16[256,1024]{0,1:T(8,128)(2,1)} %pad_maximum_fusion.1), channel_id=1, source_target_pairs={{0,1},{1,0},{18,19},{19,18},{4,5},{5,4},{22,23},{23,22},{8,9},{9,8... | collective-permute-start | bytes 1572872 | tf_op jit(solution)/shard_map/ppermute | solution.py:89
  49.2 12.7 %collective-permute-start.5 = (bf16[256,1024]{0,1:T(8,128)(2,1)}, bf16[256,1024]{0,1:T(8,128)(2,1)}, u32[]{:S(2)}, u32[]{:S(2)}) collective-permute-start(bf16[256,1024]{0,1:T(8,128)(2,1)} %collective-permute-done.3), channel_id=1, source_target_pairs={{2,3},{3,2},{16,17},{17,16},{6,7},{7,6},{20,21},{21,20},{10,11},{1... | collective-permute-start | bytes 1572872 | tf_op jit(solution)/shard_map/ppermute | solution.py:89
  50.7 12.7 %collective-permute-start.11 = (bf16[256,1024]{1,0:T(8,128)(2,1)S(1)}, bf16[256,1024]{1,0:T(8,128)(2,1)S(1)}, u32[]{:S(2)}, u32[]{:S(2)}) collective-permute-start(bf16[256,1024]{1,0:T(8,128)(2,1)S(1)} %collective-permute-done.10), channel_id=1, source_target_pairs={{8,12},{9,13},{10,14},{11,15},{24,28},{25,29},{26,30},{27,31}} | collective-permute-start | bytes 1572872 | tf_op jit(solution)/shard_map/ppermute | solution.py:122
  60.6 13.6 %collective-permute-start.8 = (bf16[256,1024]{1,0:T(8,128)(2,1)S(1)}, bf16[256,1024]{1,0:T(8,128)(2,1)S(1)}, u32[]{:S(2)}, u32[]{:S(2)}) collective-permute-start(bf16[256,1024]{1,0:T(8,128)(2,1)S(1)} %collective-permute-done.7), channel_id=1, source_target_pairs={{4,0},{5,1},{6,2},{7,3},{20,16},{21,17},{22,18},{23,19}} | collective-permute-start | bytes 1572872 | tf_op jit(solution)/shard_map/ppermute | solution.py:123
  75.8 10.9 %collective-permute-start.12 = (bf16[256,1024]{1,0:T(8,128)(2,1)S(1)}, bf16[256,1024]{1,0:T(8,128)(2,1)S(1)}, u32[]{:S(2)}, u32[]{:S(2)}) collective-permute-start(bf16[256,1024]{1,0:T(8,128)(2,1)S(1)} %convolution_convert_fusion), channel_id=1, source_target_pairs={{0,16},{16,0},{1,17},{17,1},{2,18},{18,2},{3,19},{19,3},{4,20},{20... | collective-permute-start | bytes 1572872 | tf_op jit(solution)/shard_map/ppermute | solution.py:85

commit v10 on v9

--- a/solution.py
+++ b/solution.py
@@ -113,12 +113,19 @@
     return own_full, foreign_full
 
 
-def line_rows(block, axis):
+def first_hop(block, axis):
+    count = lax.axis_size(axis)
+    rising = lax.ppermute(block, axis, [(i, i + 1) for i in range(count - 1)])
+    falling = lax.ppermute(block, axis, [(i, i - 1) for i in range(1, count)])
+    return rising, falling
+
+
+def line_rows(block, first, axis):
     count = lax.axis_size(axis)
     here = lax.axis_index(axis)
-    arrivals = [(block, 0)]
-    rising, falling = block, block
-    for step in range(1, count):
+    rising, falling = first
+    arrivals = [(block, 0), (rising, -1), (falling, 1)]
+    for step in range(2, count):
         rising = lax.ppermute(rising, axis, [(i, i + 1) for i in range(step - 1, count - 1)])
         falling = lax.ppermute(falling, axis, [(i, i - 1) for i in range(1, count - step + 1)])
         arrivals.append((rising, -step))
@@ -149,8 +156,10 @@
     side_width = block_rows * lax.axis_size("ctx")
     fits = lax.axis_size("tensor") == 4
     if lax.axis_size("dp") == 2 and side_width == 2 * width and fits:
-        side_rows = line_rows(output_weight, "ctx")
+        first = first_hop(output_weight, "ctx")
         head_values = attention(queries, keyvals, documents)
+        first, head_values = lax.optimization_barrier((first, head_values))
+        side_rows = line_rows(output_weight, first, "ctx")
         result = split_projection(head_values, side_rows)
         return result.astype(jnp.bfloat16)[None]
     all_rows = lax.all_gather(output_weight, ("dp", "ctx"), axis=0, tiled=True)

time: 88.1 us -> 80.7 us (0.916)
  the two profiles are of different devices: /device:TPU:0 before, /device:TPU:12 now
where the time goes in v10:
time: 80.7 us; the launch traced here: 80.3 us
  waiting for transfers between devices  39.2 us (49%)
  starting transfers between devices  27.2 us (34%)
  other arithmetic  6.9 us (9%)
  local copies, waits for them, and re-layouts  3.57 us (4%)
  matrix products  3.03 us (4%)
    ppermute x2, waiting for transfers between devices, swapped(): return lax.ppermute(block, axis, [(0, 1), (1, 0)])  17.7 us
    ppermute x2, waiting for transfers between devices, shifted(): return lax.ppermute(block, axis, route)  12.3 us
    ppermute x3, waiting for transfers between devices, sent(): return lax.ppermute(block, ('dp', 'tensor'), route)  9.15 us
    ppermute x2, starting transfers between devices, shifted(): return lax.ppermute(block, axis, route)  6.43 us
    ppermute x2, starting transfers between devices, line_rows(): lax.ppermute(rising, axis, [(i, i + 1) for i in range(step - 1, count - 1)])  5.44 us
    ppermute x2, starting transfers between devices, line_rows(): lax.ppermute(falling, axis, [(i, i - 1) for i in range(1, count - step +...  4.01 us
    ppermute x3, starting transfers between devices, sent(): return lax.ppermute(block, ('dp', 'tensor'), route)  3.87 us
    ppermute x1, starting transfers between devices, first_hop(): rising = lax.ppermute(block, axis, [(i, i + 1) for i in range(count - 1)])  3.47 us
  transfers between devices with their start and end apart: 13, of which 7 were waited for; matrix products, arithmetic and copies ran while one was open for 13% of the time, Pallas kernels for 0%

profile of v10, /device:TPU:12, one launch (start us, length us, event | category | flops | bytes accessed | tf_op | source)
XLA Modules:
  0.0 80.3 jit_solution(15706148937102130392)
XLA Ops:
  0.0 3.5 %collective-permute-start = (bf16[256,1024]{1,0:T(8,128)(2,1)}, bf16[256,1024]{1,0:T(8,128)(2,1)S(1)}, u32[]{:S(2)}, u32[]{:S(2)}) collective-permute-start(bf16[256,1024]{1,0:T(8,128)(2,1)} %param.7), channel_id=1, source_target_pairs={{0,4},{4,8},{8,12},{1,5},{5,9},{9,13},{2,6},{6,10},{10,14},{3,7},{... | collective-permute-start | bytes 1572872 | tf_op jit(solution)/shard_map/ppermute | solution.py:118
  3.5 2.4 %collective-permute-start.1 = (bf16[256,1024]{1,0:T(8,128)(2,1)}, bf16[256,1024]{1,0:T(8,128)(2,1)S(1)}, u32[]{:S(2)}, u32[]{:S(2)}) collective-permute-start(bf16[256,1024]{1,0:T(8,128)(2,1)} %param.7), channel_id=1, source_target_pairs={{4,0},{8,4},{12,8},{5,1},{9,5},{13,9},{6,2},{10,6},{14,10},{7,3},{... | collective-permute-start | bytes 1572872 | tf_op jit(solution)/shard_map/ppermute | solution.py:119
  5.9 0.7 convert_element_type.37
  6.6 0.9 %copy.21 = bf16[1,256,2,128]{3,1,2,0:T(8,128)(2,1)S(1)} copy(bf16[1,256,2,128]{3,2,1,0:T(2,128)(2,1)} %param.5) | data formatting | bytes 262144 | tf_op args[1]
  7.5 0.1 broadcast_in_dim.27
  7.6 4.5 %collective-permute-start.3 = (bf16[256,3,128]{2,0,1:T(8,128)(2,1)S(1)}, bf16[256,3,128]{2,0,1:T(8,128)(2,1)S(1)}, u32[]{:S(2)}, u32[]{:S(2)}) collective-permute-start(bf16[256,3,128]{2,0,1:T(8,128)(2,1)S(1)} %pad_maximum_fusion.3), channel_id=1, source_target_pairs={{0,8},{4,12},{1,9},{5,13},{2,10},{6,14},{3,11},{7,15},{16,24},{20,... | collective-permute-start | bytes 589832 | tf_op jit(solution)/shard_map/ppermute | solution.py:17
  12.1 1.9 %collective-permute-start.2 = (bf16[256,3,128]{2,0,1:T(8,128)(2,1)S(1)}, bf16[256,3,128]{2,0,1:T(8,128)(2,1)S(1)}, u32[]{:S(2)}, u32[]{:S(2)}) collective-permute-start(bf16[256,3,128]{2,0,1:T(8,128)(2,1)S(1)} %pad_maximum_fusion.3), channel_id=1, source_target_pairs={{0,4},{4,8},{8,12},{1,5},{5,9},{9,13},{2,6},{6,10},{10,14},{3,7},{... | collective-permute-start | bytes 589832 | tf_op jit(solution)/shard_map/ppermute | solution.py:17
  14.1 1.0 %reshape.68 = bf16[256,4,128]{2,1,0:T(4,128)(2,1)S(1)} reshape(bf16[1,256,512]{2,1,0:T(8,128)(2,1)} %param.4) | data formatting | bytes 524288 | tf_op jit(solution)/shard_map/reshape.3
  15.2 9.3 %collective-permute-done.3 = bf16[256,3,128]{2,0,1:T(8,128)(2,1)S(1)} collective-permute-done((bf16[256,3,128]{2,0,1:T(8,128)(2,1)S(1)}, bf16[256,3,128]{2,0,1:T(8,128)(2,1)S(1)}, u32[]{:S(2)}, u32[]{:S(2)}) %collective-permute-start.3) | collective-permute-done | bytes 196640 | tf_op jit(solution)/shard_map/ppermute | solution.py:17
  24.5 0.1 convert_reduce_fusion
  24.6 2.9 %collective-permute-done.2 = bf16[256,3,128]{2,0,1:T(8,128)(2,1)S(1)} collective-permute-done((bf16[256,3,128]{2,0,1:T(8,128)(2,1)S(1)}, bf16[256,3,128]{2,0,1:T(8,128)(2,1)S(1)}, u32[]{:S(2)}, u32[]{:S(2)}) %collective-permute-start.2) | collective-permute-done | bytes 196640 | tf_op jit(solution)/shard_map/ppermute | solution.py:17
  27.5 0.1 convert_reduce_fusion.1
  27.7 0.7 pad_add_fusion
  28.4 1.4 %and_and_fusion = pred[256,768]{0,1:T(8,128)(4,1)S(1)} fusion(s32[256]{0:T(256)S(1)} %iota_add_fusion.2, s32[256]{0:T(256)} %bitcast.71, s32[768]{0:T(1024)S(1)} %pad_add_fusion.1, s32[768]{0:T(1024)S(1)} %pad_add_fusion, pred[768]{0:T(1024)(128)(4,1)S(1)} %broadcast_compare_fusion), kind=kLoop, calls=%fused_computation.14 | loop fusion | flops 786432 | bytes 205568 | tf_op jit(solution)/shard_map/and | solution.py:64
  29.9 0.6 fusion
  30.5 0.8 fusion.1
  31.3 0.0 copy-start
  31.3 0.9 %fusion.13 = bf16[256,1,4,128]{0,3,2,1:T(8,128)(2,1)S(1)} fusion(f32[768,256,4]{1,0,2:T(8,128)S(1)} %get-tuple-element.22, f32[4,256]{1,0:T(4,128)S(1)} %get-tuple-element.21, pred[256,768]{0,1:T(8,128)(4,1)S(1)} %and_and_fusion, f32[256,4]{0,1:T(4,128)S(1)} %bitcast.68, bf16[768,2,128]{2,0,1:T(8,128)(2,1)S(1)} %pad_maximum_fusion.2), kind=kOutput, calls=%fused_computation.13 | convolution fusion | flops 205520896 | bytes 3809280 | tf_op jit(solution)/shard_map/hgqk,khd->qhgd/dot_general | solution.py:72
  32.2 0.0 collective-permute-done
  32.2 0.0 collective-permute-done.1
  32.3 1.9 %collective-permute-start.8 = (bf16[256,1024]{1,0:T(8,128)(2,1)S(1)}, bf16[256,1024]{1,0:T(8,128)(2,1)S(1)}, u32[]{:S(2)}, u32[]{:S(2)}) collective-permute-start(bf16[256,1024]{1,0:T(8,128)(2,1)S(1)} %collective-permute-done.1), channel_id=1, source_target_pairs={{4,0},{8,4},{5,1},{9,5},{6,2},{10,6},{7,3},{11,7},{20,16},{24,20},... | collective-permute-start | bytes 1572872 | tf_op jit(solution)/shard_map/ppermute | solution.py:130
  34.2 4.0 %collective-permute-start.10 = (bf16[256,1024]{1,0:T(8,128)(2,1)S(1)}, bf16[256,1024]{1,0:T(8,128)(2,1)S(1)}, u32[]{:S(2)}, u32[]{:S(2)}) collective-permute-start(bf16[256,1024]{1,0:T(8,128)(2,1)S(1)} %collective-permute-done), channel_id=1, source_target_pairs={{4,8},{8,12},{5,9},{9,13},{6,10},{10,14},{7,11},{11,15},{20,24},{2... | collective-permute-start | bytes 1572872 | tf_op jit(solution)/shard_map/ppermute | solution.py:129
  38.2 1.6 %collective-permute-start.4 = (bf16[256,512]{0,1:T(8,128)(2,1)S(1)}, bf16[256,512]{0,1:T(8,128)(2,1)S(1)}, u32[]{:S(2)}, u32[]{:S(2)}) collective-permute-start(bf16[256,512]{0,1:T(8,128)(2,1)S(1)} %bitcast.66), channel_id=1, source_target_pairs={{0,16},{16,0},{1,17},{17,1},{2,18},{18,2},{3,19},{19,3},{4,20},{20... | collective-permute-start | bytes 786440 | tf_op jit(solution)/shard_map/ppermute | solution.py:85
  39.7 0.7 constant_dynamic-update-slice_fusion.1
  40.5 4.5 %collective-permute-done.4 = bf16[256,512]{0,1:T(8,128)(2,1)S(1)} collective-permute-done((bf16[256,512]{0,1:T(8,128)(2,1)S(1)}, bf16[256,512]{0,1:T(8,128)(2,1)S(1)}, u32[]{:S(2)}, u32[]{:S(2)}) %collective-permute-start.4) | collective-permute-done | bytes 262176 | tf_op jit(solution)/shard_map/ppermute | solution.py:85
  45.0 0.7 constant_dynamic-update-slice_fusion
  45.7 1.3 %collective-permute-start.5 = (bf16[256,1024]{0,1:T(8,128)(2,1)}, bf16[256,1024]{0,1:T(8,128)(2,1)}, u32[]{:S(2)}, u32[]{:S(2)}) collective-permute-start(bf16[256,1024]{0,1:T(8,128)(2,1)} %constant_dynamic-update-slice_fusion), channel_id=1, source_target_pairs={{0,2},{1,3},{18,16},{19,17},{4,6},{5,7},{22,20},{23,21},{8,10},{9,... | collective-permute-start | bytes 1572872 | tf_op jit(solution)/shard_map/ppermute | solution.py:89
  47.0 0.1 collective-permute-done.8
  47.1 2.1 %collective-permute-start.9 = (bf16[256,1024]{1,0:T(8,128)(2,1)S(1)}, bf16[256,1024]{1,0:T(8,128)(2,1)S(1)}, u32[]{:S(2)}, u32[]{:S(2)}) collective-permute-start(bf16[256,1024]{1,0:T(8,128)(2,1)S(1)} %collective-permute-done.8), channel_id=1, source_target_pairs={{4,0},{5,1},{6,2},{7,3},{20,16},{21,17},{22,18},{23,19}} | collective-permute-start | bytes 1572872 | tf_op jit(solution)/shard_map/ppermute | solution.py:130
  49.2 0.0 collective-permute-done.10
  49.2 1.5 %collective-permute-start.11 = (bf16[256,1024]{1,0:T(8,128)(2,1)S(1)}, bf16[256,1024]{1,0:T(8,128)(2,1)}, u32[]{:S(2)}, u32[]{:S(2)}) collective-permute-start(bf16[256,1024]{1,0:T(8,128)(2,1)S(1)} %collective-permute-done.10), channel_id=1, source_target_pairs={{8,12},{9,13},{10,14},{11,15},{24,28},{25,29},{26,30},{27,31}} | collective-permute-start | bytes 1572872 | tf_op jit(solution)/shard_map/ppermute | solution.py:129
  50.6 0.7 collective-permute-start.6
  51.3 8.0 %collective-permute-done.5 = bf16[256,1024]{0,1:T(8,128)(2,1)} collective-permute-done((bf16[256,1024]{0,1:T(8,128)(2,1)}, bf16[256,1024]{0,1:T(8,128)(2,1)}, u32[]{:S(2)}, u32[]{:S(2)}) %collective-permute-start.5) | collective-permute-done | bytes 524320 | tf_op jit(solution)/shard_map/ppermute | solution.py:89
  59.3 1.9 %collective-permute-start.7 = (bf16[256,1024]{0,1:T(8,128)(2,1)}, bf16[256,1024]{0,1:T(8,128)(2,1)S(1)}, u32[]{:S(2)}, u32[]{:S(2)}) collective-permute-start(bf16[256,1024]{0,1:T(8,128)(2,1)} %collective-permute-done.5), channel_id=1, source_target_pairs={{2,3},{3,2},{16,17},{17,16},{6,7},{7,6},{20,21},{21,20},{10,11},{1... | collective-permute-start | bytes 1572872 | tf_op jit(solution)/shard_map/ppermute | solution.py:89
  61.3 0.0 collective-permute-done.9
  61.3 0.2 select_select_fusion
  61.5 0.2 select_select_fusion.1
  61.7 0.2 select_select_fusion.2
  61.8 0.2 select_select_fusion.3
  62.0 0.2 pad_maximum_fusion
  62.2 0.0 collective-permute-done.6
  62.2 1.1 %collective-permute-done.7 = bf16[256,1024]{0,1:T(8,128)(2,1)S(1)} collective-permute-done((bf16[256,1024]{0,1:T(8,128)(2,1)}, bf16[256,1024]{0,1:T(8,128)(2,1)S(1)}, u32[]{:S(2)}, u32[]{:S(2)}) %collective-permute-start.7) | collective-permute-done | bytes 524320 | tf_op jit(solution)/shard_map/ppermute | solution.py:89
  63.4 1.2 %broadcast_select_fusion.3 = (bf16[256,1024]{0,1:T(8,128)(2,1)S(1)}, bf16[256,1024]{0,1:T(8,128)(2,1)S(1)}) fusion(pred[]{:T(512)S(6)} %eq.105, bf16[256,1024]{0,1:T(8,128)(2,1)} %constant_dynamic-update-slice_fusion, bf16[256,1024]{0,1:T(8,128)(2,1)} %collective-permute-done.5, pred[]{:T(512)S(6)} %eq.106, bf16[256,1024]{0,1:T(8,128)(2,1)S(1)} %collective-permute-done.6, ...), kind=kLoop, calls=%fused_computation.27 | loop fusion | flops 1048576 | bytes 3145730 | tf_op jit(solution)/shard_map/jit(_where)/select_n | solution.py:109
  64.6 0.7 convolution_convert_fusion
  65.3 0.1 collective-permute-start.12
  65.5 0.7 fusion.28
  66.2 13.2 %collective-permute-done.12 = bf16[256,1024]{1,0:T(8,128)(2,1)S(1)} collective-permute-done((bf16[256,1024]{1,0:T(8,128)(2,1)S(1)}, bf16[256,1024]{1,0:T(8,128)(2,1)S(1)}, u32[]{:S(2)}, u32[]{:S(2)}) %collective-permute-start.12) | collective-permute-done | bytes 524320 | tf_op jit(solution)/shard_map/ppermute | solution.py:85
  79.4 0.9 %fusion.16 = bf16[1,256,1024]{2,1,0:T(8,128)(2,1)} fusion(f32[256,1024]{1,0:T(8,128)S(1)} %fusion.28, bf16[256,1024]{1,0:T(8,128)(2,1)S(1)} %collective-permute-done.12), kind=kLoop, calls=%fused_computation.15 | loop fusion | flops 786432 | bytes 2097152 | tf_op jit(solution)/shard_map/broadcast_in_dim | solution.py:164
  (13 shorter events, 0.2 us)
Async XLA Ops:
  0.0 32.2 %collective-permute-start = (bf16[256,1024]{1,0:T(8,128)(2,1)}, bf16[256,1024]{1,0:T(8,128)(2,1)S(1)}, u32[]{:S(2)}, u32[]{:S(2)}) collective-permute-start(bf16[256,1024]{1,0:T(8,128)(2,1)} %param.7), channel_id=1, source_target_pairs={{0,4},{4,8},{8,12},{1,5},{5,9},{9,13},{2,6},{6,10},{10,14},{3,7},{... | collective-permute-start | bytes 1572872 | tf_op jit(solution)/shard_map/ppermute | solution.py:118
  3.5 28.8 %collective-permute-start.1 = (bf16[256,1024]{1,0:T(8,128)(2,1)}, bf16[256,1024]{1,0:T(8,128)(2,1)S(1)}, u32[]{:S(2)}, u32[]{:S(2)}) collective-permute-start(bf16[256,1024]{1,0:T(8,128)(2,1)} %param.7), channel_id=1, source_target_pairs={{4,0},{8,4},{12,8},{5,1},{9,5},{13,9},{6,2},{10,6},{14,10},{7,3},{... | collective-permute-start | bytes 1572872 | tf_op jit(solution)/shard_map/ppermute | solution.py:119
  7.6 16.9 %collective-permute-start.3 = (bf16[256,3,128]{2,0,1:T(8,128)(2,1)S(1)}, bf16[256,3,128]{2,0,1:T(8,128)(2,1)S(1)}, u32[]{:S(2)}, u32[]{:S(2)}) collective-permute-start(bf16[256,3,128]{2,0,1:T(8,128)(2,1)S(1)} %pad_maximum_fusion.3), channel_id=1, source_target_pairs={{0,8},{4,12},{1,9},{5,13},{2,10},{6,14},{3,11},{7,15},{16,24},{20,... | collective-permute-start | bytes 589832 | tf_op jit(solution)/shard_map/ppermute | solution.py:17
  12.1 15.4 %collective-permute-start.2 = (bf16[256,3,128]{2,0,1:T(8,128)(2,1)S(1)}, bf16[256,3,128]{2,0,1:T(8,128)(2,1)S(1)}, u32[]{:S(2)}, u32[]{:S(2)}) collective-permute-start(bf16[256,3,128]{2,0,1:T(8,128)(2,1)S(1)} %pad_maximum_fusion.3), channel_id=1, source_target_pairs={{0,4},{4,8},{8,12},{1,5},{5,9},{9,13},{2,6},{6,10},{10,14},{3,7},{... | collective-permute-start | bytes 589832 | tf_op jit(solution)/shard_map/ppermute | solution.py:17
  31.3 30.0 %copy-start = (bf16[256,1024]{1,0:T(8,128)(2,1)S(1)}, bf16[256,1024]{1,0:T(8,128)(2,1)}, u32[]{:S(2)}) copy-start(bf16[256,1024]{1,0:T(8,128)(2,1)} %param.7) | copy-start | bytes 1572868
  32.3 14.8 %collective-permute-start.8 = (bf16[256,1024]{1,0:T(8,128)(2,1)S(1)}, bf16[256,1024]{1,0:T(8,128)(2,1)S(1)}, u32[]{:S(2)}, u32[]{:S(2)}) collective-permute-start(bf16[256,1024]{1,0:T(8,128)(2,1)S(1)} %collective-permute-done.1), channel_id=1, source_target_pairs={{4,0},{8,4},{5,1},{9,5},{6,2},{10,6},{7,3},{11,7},{20,16},{24,20},... | collective-permute-start | bytes 1572872 | tf_op jit(solution)/shard_map/ppermute | solution.py:130
  34.2 15.0 %collective-permute-start.10 = (bf16[256,1024]{1,0:T(8,128)(2,1)S(1)}, bf16[256,1024]{1,0:T(8,128)(2,1)S(1)}, u32[]{:S(2)}, u32[]{:S(2)}) collective-permute-start(bf16[256,1024]{1,0:T(8,128)(2,1)S(1)} %collective-permute-done), channel_id=1, source_target_pairs={{4,8},{8,12},{5,9},{9,13},{6,10},{10,14},{7,11},{11,15},{20,24},{2... | collective-permute-start | bytes 1572872 | tf_op jit(solution)/shard_map/ppermute | solution.py:129
  38.2 6.8 %collective-permute-start.4 = (bf16[256,512]{0,1:T(8,128)(2,1)S(1)}, bf16[256,512]{0,1:T(8,128)(2,1)S(1)}, u32[]{:S(2)}, u32[]{:S(2)}) collective-permute-start(bf16[256,512]{0,1:T(8,128)(2,1)S(1)} %bitcast.66), channel_id=1, source_target_pairs={{0,16},{16,0},{1,17},{17,1},{2,18},{18,2},{3,19},{19,3},{4,20},{20... | collective-permute-start | bytes 786440 | tf_op jit(solution)/shard_map/ppermute | solution.py:85
  45.7 13.6 %collective-permute-start.5 = (bf16[256,1024]{0,1:T(8,128)(2,1)}, bf16[256,1024]{0,1:T(8,128)(2,1)}, u32[]{:S(2)}, u32[]{:S(2)}) collective-permute-start(bf16[256,1024]{0,1:T(8,128)(2,1)} %constant_dynamic-update-slice_fusion), channel_id=1, source_target_pairs={{0,2},{1,3},{18,16},{19,17},{4,6},{5,7},{22,20},{23,21},{8,10},{9,... | collective-permute-start | bytes 1572872 | tf_op jit(solution)/shard_map/ppermute | solution.py:89
  47.1 14.2 %collective-permute-start.9 = (bf16[256,1024]{1,0:T(8,128)(2,1)S(1)}, bf16[256,1024]{1,0:T(8,128)(2,1)S(1)}, u32[]{:S(2)}, u32[]{:S(2)}) collective-permute-start(bf16[256,1024]{1,0:T(8,128)(2,1)S(1)} %collective-permute-done.8), channel_id=1, source_target_pairs={{4,0},{5,1},{6,2},{7,3},{20,16},{21,17},{22,18},{23,19}} | collective-permute-start | bytes 1572872 | tf_op jit(solution)/shard_map/ppermute | solution.py:130
  49.2 12.1 %collective-permute-start.11 = (bf16[256,1024]{1,0:T(8,128)(2,1)S(1)}, bf16[256,1024]{1,0:T(8,128)(2,1)}, u32[]{:S(2)}, u32[]{:S(2)}) collective-permute-start(bf16[256,1024]{1,0:T(8,128)(2,1)S(1)} %collective-permute-done.10), channel_id=1, source_target_pairs={{8,12},{9,13},{10,14},{11,15},{24,28},{25,29},{26,30},{27,31}} | collective-permute-start | bytes 1572872 | tf_op jit(solution)/shard_map/ppermute | solution.py:129
  50.6 11.6 %collective-permute-start.6 = (bf16[256,1024]{0,1:T(8,128)(2,1)}, bf16[256,1024]{0,1:T(8,128)(2,1)S(1)}, u32[]{:S(2)}, u32[]{:S(2)}) collective-permute-start(bf16[256,1024]{0,1:T(8,128)(2,1)} %constant_dynamic-update-slice_fusion), channel_id=1, source_target_pairs={{0,1},{1,0},{18,19},{19,18},{4,5},{5,4},{22,23},{23,22},{8,9},{9,8... | collective-permute-start | bytes 1572872 | tf_op jit(solution)/shard_map/ppermute | solution.py:89
  59.3 4.0 %collective-permute-start.7 = (bf16[256,1024]{0,1:T(8,128)(2,1)}, bf16[256,1024]{0,1:T(8,128)(2,1)S(1)}, u32[]{:S(2)}, u32[]{:S(2)}) collective-permute-start(bf16[256,1024]{0,1:T(8,128)(2,1)} %collective-permute-done.5), channel_id=1, source_target_pairs={{2,3},{3,2},{16,17},{17,16},{6,7},{7,6},{20,21},{21,20},{10,11},{1... | collective-permute-start | bytes 1572872 | tf_op jit(solution)/shard_map/ppermute | solution.py:89
  65.3 14.0 %collective-permute-start.12 = (bf16[256,1024]{1,0:T(8,128)(2,1)S(1)}, bf16[256,1024]{1,0:T(8,128)(2,1)S(1)}, u32[]{:S(2)}, u32[]{:S(2)}) collective-permute-start(bf16[256,1024]{1,0:T(8,128)(2,1)S(1)} %convolution_convert_fusion), channel_id=1, source_target_pairs={{0,16},{16,0},{1,17},{17,1},{2,18},{18,2},{3,19},{19,3},{4,20},{20... | collective-permute-start | bytes 1572872 | tf_op jit(solution)/shard_map/ppermute | solution.py:85

commit v11 on v10

--- a/solution.py
+++ b/solution.py
@@ -23,7 +23,7 @@
     return lax.ppermute(block, axis, route)
 
 
-def attention(queries, keyvals, documents):
+def attention(queries, keyvals, documents, anchor):
     length = queries.shape[1]
     pair_width = keyvals.shape[3]
     pair_heads = pair_width // HEAD_DIM
@@ -46,6 +46,7 @@
         label_blocks.append(arrived[:, 2, 0].astype(jnp.int32))
         place_blocks.append((position - hop) * length + offsets)
     pairs = jnp.concatenate(pair_blocks, axis=0)
+    pairs, anchor = lax.optimization_barrier((pairs, anchor))
     key_labels = jnp.concatenate(label_blocks, axis=0)
     key_place = jnp.concatenate(place_blocks, axis=0)
     key_count = pairs.shape[0]
@@ -76,9 +77,8 @@
         preferred_element_type=jnp.float32,
     )
     head_values = summed / jnp.transpose(total, (2, 0, 1))[..., None]
-    return head_values.reshape(length, pair_heads * query_group_size * HEAD_DIM).astype(
-        jnp.bfloat16
-    )
+    head_values = head_values.reshape(length, pair_heads * query_group_size * HEAD_DIM)
+    return head_values.astype(jnp.bfloat16), anchor
 
 
 def swapped(block, axis):
@@ -157,13 +157,12 @@
     fits = lax.axis_size("tensor") == 4
     if lax.axis_size("dp") == 2 and side_width == 2 * width and fits:
         first = first_hop(output_weight, "ctx")
-        head_values = attention(queries, keyvals, documents)
-        first, head_values = lax.optimization_barrier((first, head_values))
+        head_values, first = attention(queries, keyvals, documents, first)
         side_rows = line_rows(output_weight, first, "ctx")
         result = split_projection(head_values, side_rows)
         return result.astype(jnp.bfloat16)[None]
     all_rows = lax.all_gather(output_weight, ("dp", "ctx"), axis=0, tiled=True)
-    head_values = attention(queries, keyvals, documents)
+    head_values, _ = attention(queries, keyvals, documents, ())
     group = lax.axis_size("tensor")
     me = lax.axis_index("tensor")
     result = None

time: 80.7 us -> 83.2 us (1.031)
  waiting for transfers between devices: 39.2 us -> 42.8 us
  local copies, waits for them, and re-layouts: 3.57 us -> 2.14 us
  other arithmetic: 6.9 us -> 7.98 us
    ppermute x2, waiting for transfers between devices: 12.3 us -> 3.55 us  [shifted(): return lax.ppermute(block, axis, route)]
    ppermute x1, waiting for transfers between devices: 0.01 us -> 6.41 us  [first_hop(): rising = lax.ppermute(block, axis, [(i, i + 1) for i in range(count - 1)])]
    ppermute x1, waiting for transfers between devices: 0.01 us -> 2.54 us  [first_hop(): falling = lax.ppermute(block, axis, [(i, i - 1) for i in range(1, count)])]
    ppermute x3, waiting for transfers between devices: 9.15 us -> 10.9 us  [sent(): return lax.ppermute(block, ('dp', 'tensor'), route)]
    ppermute x2, waiting for transfers between devices: 17.7 us -> 19.4 us  [swapped(): return lax.ppermute(block, axis, [(0, 1), (1, 0)])]
    ppermute x1, starting transfers between devices: 3.47 us -> 1.92 us  [first_hop(): rising = lax.ppermute(block, axis, [(i, i + 1) for i in range(count - 1)])]
    ppermute x1, starting transfers between devices: 2.39 us -> 3.93 us  [first_hop(): falling = lax.ppermute(block, axis, [(i, i - 1) for i in range(1, count)])]
    concatenate x0 -> x1, other arithmetic: none -> 0.88 us  [needed_heads(): mine = jnp.concatenate([head_values, foreign], axis=1)]
  transfers between devices with their start and end apart: 13 -> 13, of which waited for: 7 -> 7; matrix products, arithmetic and copies ran while one was open for 13% -> 10% of each run, Pallas kernels for 0% -> 0%
where the time goes in v11:
time: 83.2 us; the launch traced here: 82.8 us
  waiting for transfers between devices  42.8 us (51%)
  starting transfers between devices  26.4 us (32%)
  other arithmetic  7.98 us (10%)
  matrix products  3.06 us (4%)
  local copies, waits for them, and re-layouts  2.14 us (3%)
    ppermute x2, waiting for transfers between devices, swapped(): return lax.ppermute(block, axis, [(0, 1), (1, 0)])  19.4 us
    ppermute x3, waiting for transfers between devices, sent(): return lax.ppermute(block, ('dp', 'tensor'), route)  10.9 us
    ppermute x2, starting transfers between devices, shifted(): return lax.ppermute(block, axis, route)  6.43 us
    ppermute x1, waiting for transfers between devices, first_hop(): rising = lax.ppermute(block, axis, [(i, i + 1) for i in range(count - 1)])  6.41 us
    ppermute x2, starting transfers between devices, line_rows(): lax.ppermute(rising, axis, [(i, i + 1) for i in range(step - 1, count - 1)])  5.43 us
    ppermute x1, starting transfers between devices, first_hop(): falling = lax.ppermute(block, axis, [(i, i - 1) for i in range(1, count)])  3.93 us
    ppermute x3, starting transfers between devices, sent(): return lax.ppermute(block, ('dp', 'tensor'), route)  3.87 us
    ppermute x2, waiting for transfers between devices, shifted(): return lax.ppermute(block, axis, route)  3.55 us
  transfers between devices with their start and end apart: 13, of which 7 were waited for; matrix products, arithmetic and copies ran while one was open for 10% of the time, Pallas kernels for 0%

profile of v11, /device:TPU:12, one launch (start us, length us, event | category | flops | bytes accessed | tf_op | source)
XLA Modules:
  0.0 82.8 jit_solution(13943626076223445145)
XLA Ops:
  0.0 0.7 convert_element_type.37
  0.7 0.9 %copy.21 = bf16[1,256,2,128]{3,1,2,0:T(8,128)(2,1)S(1)} copy(bf16[1,256,2,128]{3,2,1,0:T(2,128)(2,1)} %param.5) | data formatting | bytes 262144 | tf_op args[1]
  1.6 0.1 broadcast_in_dim.27
  1.7 4.5 %collective-permute-start.1 = (bf16[256,3,128]{2,0,1:T(8,128)(2,1)S(1)}, bf16[256,3,128]{2,0,1:T(8,128)(2,1)S(1)}, u32[]{:S(2)}, u32[]{:S(2)}) collective-permute-start(bf16[256,3,128]{2,0,1:T(8,128)(2,1)S(1)} %pad_maximum_fusion.4), channel_id=1, source_target_pairs={{0,8},{4,12},{1,9},{5,13},{2,10},{6,14},{3,11},{7,15},{16,24},{20,... | collective-permute-start | bytes 589832 | tf_op jit(solution)/shard_map/ppermute | solution.py:17
  6.3 1.9 %collective-permute-start = (bf16[256,3,128]{2,0,1:T(8,128)(2,1)S(1)}, bf16[256,3,128]{2,0,1:T(8,128)(2,1)S(1)}, u32[]{:S(2)}, u32[]{:S(2)}) collective-permute-start(bf16[256,3,128]{2,0,1:T(8,128)(2,1)S(1)} %pad_maximum_fusion.4), channel_id=1, source_target_pairs={{0,4},{4,8},{8,12},{1,5},{5,9},{9,13},{2,6},{6,10},{10,14},{3,7},{... | collective-permute-start | bytes 589832 | tf_op jit(solution)/shard_map/ppermute | solution.py:17
  8.2 3.9 %collective-permute-start.3 = (bf16[256,1024]{1,0:T(8,128)(2,1)}, bf16[256,1024]{1,0:T(8,128)(2,1)S(1)}, u32[]{:S(2)}, u32[]{:S(2)}) collective-permute-start(bf16[256,1024]{1,0:T(8,128)(2,1)} %param.7), channel_id=1, source_target_pairs={{4,0},{8,4},{12,8},{5,1},{9,5},{13,9},{6,2},{10,6},{14,10},{7,3},{... | collective-permute-start | bytes 1572872 | tf_op jit(solution)/shard_map/ppermute | solution.py:119
  12.1 1.9 %collective-permute-start.2 = (bf16[256,1024]{1,0:T(8,128)(2,1)}, bf16[256,1024]{1,0:T(8,128)(2,1)S(1)}, u32[]{:S(2)}, u32[]{:S(2)}) collective-permute-start(bf16[256,1024]{1,0:T(8,128)(2,1)} %param.7), channel_id=1, source_target_pairs={{0,4},{4,8},{8,12},{1,5},{5,9},{9,13},{2,6},{6,10},{10,14},{3,7},{... | collective-permute-start | bytes 1572872 | tf_op jit(solution)/shard_map/ppermute | solution.py:118
  14.1 1.0 %reshape.68 = bf16[256,4,128]{2,1,0:T(4,128)(2,1)S(1)} reshape(bf16[1,256,512]{2,1,0:T(8,128)(2,1)} %param.4) | data formatting | bytes 524288 | tf_op jit(solution)/shard_map/reshape.3
  15.1 0.0 collective-permute-done.1
  15.2 0.1 convert_reduce_fusion
  15.3 3.6 %collective-permute-done = bf16[256,3,128]{2,0,1:T(8,128)(2,1)S(1)} collective-permute-done((bf16[256,3,128]{2,0,1:T(8,128)(2,1)S(1)}, bf16[256,3,128]{2,0,1:T(8,128)(2,1)S(1)}, u32[]{:S(2)}, u32[]{:S(2)}) %collective-permute-start) | collective-permute-done | bytes 196640 | tf_op jit(solution)/shard_map/ppermute | solution.py:17
  18.9 0.1 convert_reduce_fusion.1
  19.0 0.7 pad_add_fusion
  19.7 1.4 %and_and_fusion = pred[256,768]{0,1:T(8,128)(4,1)S(1)} fusion(s32[256]{0:T(256)S(1)} %iota_add_fusion.2, s32[256]{0:T(256)} %bitcast.72, s32[768]{0:T(1024)S(1)} %pad_add_fusion.1, s32[768]{0:T(1024)S(1)} %pad_add_fusion, pred[768]{0:T(1024)(128)(4,1)S(1)} %broadcast_compare_fusion), kind=kLoop, calls=%fused_computation.14 | loop fusion | flops 786432 | bytes 205568 | tf_op jit(solution)/shard_map/and | solution.py:65
  21.1 2.5 %collective-permute-done.3 = bf16[256,1024]{1,0:T(8,128)(2,1)S(1)} collective-permute-done((bf16[256,1024]{1,0:T(8,128)(2,1)}, bf16[256,1024]{1,0:T(8,128)(2,1)S(1)}, u32[]{:S(2)}, u32[]{:S(2)}) %collective-permute-start.3) | collective-permute-done | bytes 524320 | tf_op jit(solution)/shard_map/ppermute | solution.py:119
  23.7 6.4 %collective-permute-done.2 = bf16[256,1024]{1,0:T(8,128)(2,1)S(1)} collective-permute-done((bf16[256,1024]{1,0:T(8,128)(2,1)}, bf16[256,1024]{1,0:T(8,128)(2,1)S(1)}, u32[]{:S(2)}, u32[]{:S(2)}) %collective-permute-start.2) | collective-permute-done | bytes 524320 | tf_op jit(solution)/shard_map/ppermute | solution.py:118
  30.1 1.9 %collective-permute-start.8 = (bf16[256,1024]{1,0:T(8,128)(2,1)S(1)}, bf16[256,1024]{1,0:T(8,128)(2,1)S(1)}, u32[]{:S(2)}, u32[]{:S(2)}) collective-permute-start(bf16[256,1024]{1,0:T(8,128)(2,1)S(1)} %collective-permute-done.3), channel_id=1, source_target_pairs={{4,0},{8,4},{5,1},{9,5},{6,2},{10,6},{7,3},{11,7},{20,16},{24,20},... | collective-permute-start | bytes 1572872 | tf_op jit(solution)/shard_map/ppermute | solution.py:130
  32.0 4.0 %collective-permute-start.10 = (bf16[256,1024]{1,0:T(8,128)(2,1)S(1)}, bf16[256,1024]{1,0:T(8,128)(2,1)S(1)}, u32[]{:S(2)}, u32[]{:S(2)}) collective-permute-start(bf16[256,1024]{1,0:T(8,128)(2,1)S(1)} %collective-permute-done.2), channel_id=1, source_target_pairs={{4,8},{8,12},{5,9},{9,13},{6,10},{10,14},{7,11},{11,15},{20,24},{2... | collective-permute-start | bytes 1572872 | tf_op jit(solution)/shard_map/ppermute | solution.py:129
  36.0 0.6 fusion
  36.6 0.8 fusion.1
  37.4 1.0 %fusion.13 = bf16[256,1,4,128]{0,3,2,1:T(8,128)(2,1)S(1)} fusion(f32[768,256,4]{1,0,2:T(8,128)S(1)} %get-tuple-element.22, f32[4,256]{1,0:T(4,128)S(1)} %get-tuple-element.21, pred[256,768]{0,1:T(8,128)(4,1)S(1)} %and_and_fusion, f32[256,4]{0,1:T(4,128)S(1)} %bitcast.69, bf16[768,2,128]{2,0,1:T(8,128)(2,1)S(1)} %pad_maximum_fusion.3), kind=kOutput, calls=%fused_computation.13 | convolution fusion | flops 205520896 | bytes 3809280 | tf_op jit(solution)/shard_map/hgqk,khd->qhgd/dot_general | solution.py:73
  38.4 1.6 %collective-permute-start.4 = (bf16[256,512]{0,1:T(8,128)(2,1)S(1)}, bf16[256,512]{0,1:T(8,128)(2,1)S(1)}, u32[]{:S(2)}, u32[]{:S(2)}) collective-permute-start(bf16[256,512]{0,1:T(8,128)(2,1)S(1)} %bitcast.66), channel_id=1, source_target_pairs={{0,16},{16,0},{1,17},{17,1},{2,18},{18,2},{3,19},{19,3},{4,20},{20... | collective-permute-start | bytes 786440 | tf_op jit(solution)/shard_map/ppermute | solution.py:85
  40.0 6.2 %collective-permute-done.4 = bf16[256,512]{0,1:T(8,128)(2,1)S(1)} collective-permute-done((bf16[256,512]{0,1:T(8,128)(2,1)S(1)}, bf16[256,512]{0,1:T(8,128)(2,1)S(1)}, u32[]{:S(2)}, u32[]{:S(2)}) %collective-permute-start.4) | collective-permute-done | bytes 262176 | tf_op jit(solution)/shard_map/ppermute | solution.py:85
  46.2 0.9 %pad_maximum_fusion.1 = bf16[256,1024]{0,1:T(8,128)(2,1)} fusion(bf16[256,512]{0,1:T(8,128)(2,1)S(1)} %collective-permute-done.4, bf16[256,512]{0,1:T(8,128)(2,1)S(1)} %bitcast.67), kind=kLoop, calls=%fused_computation.16 | loop fusion | flops 1048576 | bytes 1048576 | tf_op jit(solution)/shard_map/concatenate | solution.py:97
  47.0 1.3 %collective-permute-start.5 = (bf16[256,1024]{0,1:T(8,128)(2,1)}, bf16[256,1024]{0,1:T(8,128)(2,1)}, u32[]{:S(2)}, u32[]{:S(2)}) collective-permute-start(bf16[256,1024]{0,1:T(8,128)(2,1)} %pad_maximum_fusion.1), channel_id=1, source_target_pairs={{0,2},{1,3},{18,16},{19,17},{4,6},{5,7},{22,20},{23,21},{8,10},{9,... | collective-permute-start | bytes 1572872 | tf_op jit(solution)/shard_map/ppermute | solution.py:89
  48.3 0.0 collective-permute-done.8
  48.3 1.3 %collective-permute-start.9 = (bf16[256,1024]{1,0:T(8,128)(2,1)S(1)}, bf16[256,1024]{1,0:T(8,128)(2,1)S(1)}, u32[]{:S(2)}, u32[]{:S(2)}) collective-permute-start(bf16[256,1024]{1,0:T(8,128)(2,1)S(1)} %collective-permute-done.8), channel_id=1, source_target_pairs={{4,0},{5,1},{6,2},{7,3},{20,16},{21,17},{22,18},{23,19}} | collective-permute-start | bytes 1572872 | tf_op jit(solution)/shard_map/ppermute | solution.py:130
  49.7 0.0 collective-permute-done.10
  49.7 1.5 %collective-permute-start.11 = (bf16[256,1024]{1,0:T(8,128)(2,1)S(1)}, bf16[256,1024]{1,0:T(8,128)(2,1)}, u32[]{:S(2)}, u32[]{:S(2)}) collective-permute-start(bf16[256,1024]{1,0:T(8,128)(2,1)S(1)} %collective-permute-done.10), channel_id=1, source_target_pairs={{8,12},{9,13},{10,14},{11,15},{24,28},{25,29},{26,30},{27,31}} | collective-permute-start | bytes 1572872 | tf_op jit(solution)/shard_map/ppermute | solution.py:129
  51.1 0.7 collective-permute-start.6
  51.8 9.8 %collective-permute-done.5 = bf16[256,1024]{0,1:T(8,128)(2,1)} collective-permute-done((bf16[256,1024]{0,1:T(8,128)(2,1)}, bf16[256,1024]{0,1:T(8,128)(2,1)}, u32[]{:S(2)}, u32[]{:S(2)}) %collective-permute-start.5) | collective-permute-done | bytes 524320 | tf_op jit(solution)/shard_map/ppermute | solution.py:89
  61.6 1.9 %collective-permute-start.7 = (bf16[256,1024]{0,1:T(8,128)(2,1)}, bf16[256,1024]{0,1:T(8,128)(2,1)S(1)}, u32[]{:S(2)}, u32[]{:S(2)}) collective-permute-start(bf16[256,1024]{0,1:T(8,128)(2,1)} %collective-permute-done.5), channel_id=1, source_target_pairs={{2,3},{3,2},{16,17},{17,16},{6,7},{7,6},{20,21},{21,20},{10,11},{1... | collective-permute-start | bytes 1572872 | tf_op jit(solution)/shard_map/ppermute | solution.py:89
  63.5 0.0 collective-permute-done.9
  63.5 0.0 collective-permute-done.11
  63.5 0.0 copy-done
  63.5 0.2 select_select_fusion
  63.7 0.2 select_select_fusion.1
  63.9 0.2 select_select_fusion.2
  64.1 0.2 select_select_fusion.3
  64.3 0.2 pad_maximum_fusion
  64.5 0.0 collective-permute-done.6
  64.5 1.1 %collective-permute-done.7 = bf16[256,1024]{0,1:T(8,128)(2,1)S(1)} collective-permute-done((bf16[256,1024]{0,1:T(8,128)(2,1)}, bf16[256,1024]{0,1:T(8,128)(2,1)S(1)}, u32[]{:S(2)}, u32[]{:S(2)}) %collective-permute-start.7) | collective-permute-done | bytes 524320 | tf_op jit(solution)/shard_map/ppermute | solution.py:89
  65.6 1.3 %broadcast_select_fusion.3 = (bf16[256,1024]{0,1:T(8,128)(2,1)S(1)}, bf16[256,1024]{0,1:T(8,128)(2,1)S(1)}) fusion(pred[]{:T(512)S(6)} %eq.105, bf16[256,1024]{0,1:T(8,128)(2,1)} %collective-permute-done.5, pred[]{:T(512)S(6)} %eq.106, bf16[256,1024]{0,1:T(8,128)(2,1)S(1)} %collective-permute-done.6, bf16[256,1024]{0,1:T(8,128)(2,1)S(1)} %collective-permute-done.7, ...), kind=kLoop, calls=%fused_computation.28 | loop fusion | flops 2097152 | bytes 3145730 | tf_op jit(solution)/shard_map/jit(_where)/select_n | solution.py:109
  67.0 0.7 convolution_convert_fusion
  67.8 0.1 collective-permute-start.12
  67.9 0.7 fusion.32
  68.6 13.2 %collective-permute-done.12 = bf16[256,1024]{1,0:T(8,128)(2,1)S(1)} collective-permute-done((bf16[256,1024]{1,0:T(8,128)(2,1)S(1)}, bf16[256,1024]{1,0:T(8,128)(2,1)S(1)}, u32[]{:S(2)}, u32[]{:S(2)}) %collective-permute-start.12) | collective-permute-done | bytes 524320 | tf_op jit(solution)/shard_map/ppermute | solution.py:85
  81.8 0.9 %fusion.16 = bf16[1,256,1024]{2,1,0:T(8,128)(2,1)} fusion(f32[256,1024]{1,0:T(8,128)S(1)} %fusion.32, bf16[256,1024]{1,0:T(8,128)(2,1)S(1)} %collective-permute-done.12), kind=kLoop, calls=%fused_computation.15 | loop fusion | flops 786432 | bytes 2097152 | tf_op jit(solution)/shard_map/broadcast_in_dim | solution.py:163
  (16 shorter events, 0.2 us)
Async XLA Ops:
  1.7 13.4 %collective-permute-start.1 = (bf16[256,3,128]{2,0,1:T(8,128)(2,1)S(1)}, bf16[256,3,128]{2,0,1:T(8,128)(2,1)S(1)}, u32[]{:S(2)}, u32[]{:S(2)}) collective-permute-start(bf16[256,3,128]{2,0,1:T(8,128)(2,1)S(1)} %pad_maximum_fusion.4), channel_id=1, source_target_pairs={{0,8},{4,12},{1,9},{5,13},{2,10},{6,14},{3,11},{7,15},{16,24},{20,... | collective-permute-start | bytes 589832 | tf_op jit(solution)/shard_map/ppermute | solution.py:17
  6.3 12.6 %collective-permute-start = (bf16[256,3,128]{2,0,1:T(8,128)(2,1)S(1)}, bf16[256,3,128]{2,0,1:T(8,128)(2,1)S(1)}, u32[]{:S(2)}, u32[]{:S(2)}) collective-permute-start(bf16[256,3,128]{2,0,1:T(8,128)(2,1)S(1)} %pad_maximum_fusion.4), channel_id=1, source_target_pairs={{0,4},{4,8},{8,12},{1,5},{5,9},{9,13},{2,6},{6,10},{10,14},{3,7},{... | collective-permute-start | bytes 589832 | tf_op jit(solution)/shard_map/ppermute | solution.py:17
  8.2 15.5 %collective-permute-start.3 = (bf16[256,1024]{1,0:T(8,128)(2,1)}, bf16[256,1024]{1,0:T(8,128)(2,1)S(1)}, u32[]{:S(2)}, u32[]{:S(2)}) collective-permute-start(bf16[256,1024]{1,0:T(8,128)(2,1)} %param.7), channel_id=1, source_target_pairs={{4,0},{8,4},{12,8},{5,1},{9,5},{13,9},{6,2},{10,6},{14,10},{7,3},{... | collective-permute-start | bytes 1572872 | tf_op jit(solution)/shard_map/ppermute | solution.py:119
  12.1 18.0 %collective-permute-start.2 = (bf16[256,1024]{1,0:T(8,128)(2,1)}, bf16[256,1024]{1,0:T(8,128)(2,1)S(1)}, u32[]{:S(2)}, u32[]{:S(2)}) collective-permute-start(bf16[256,1024]{1,0:T(8,128)(2,1)} %param.7), channel_id=1, source_target_pairs={{0,4},{4,8},{8,12},{1,5},{5,9},{9,13},{2,6},{6,10},{10,14},{3,7},{... | collective-permute-start | bytes 1572872 | tf_op jit(solution)/shard_map/ppermute | solution.py:118
  30.1 18.2 %collective-permute-start.8 = (bf16[256,1024]{1,0:T(8,128)(2,1)S(1)}, bf16[256,1024]{1,0:T(8,128)(2,1)S(1)}, u32[]{:S(2)}, u32[]{:S(2)}) collective-permute-start(bf16[256,1024]{1,0:T(8,128)(2,1)S(1)} %collective-permute-done.3), channel_id=1, source_target_pairs={{4,0},{8,4},{5,1},{9,5},{6,2},{10,6},{7,3},{11,7},{20,16},{24,20},... | collective-permute-start | bytes 1572872 | tf_op jit(solution)/shard_map/ppermute | solution.py:130
  32.0 17.7 %collective-permute-start.10 = (bf16[256,1024]{1,0:T(8,128)(2,1)S(1)}, bf16[256,1024]{1,0:T(8,128)(2,1)S(1)}, u32[]{:S(2)}, u32[]{:S(2)}) collective-permute-start(bf16[256,1024]{1,0:T(8,128)(2,1)S(1)} %collective-permute-done.2), channel_id=1, source_target_pairs={{4,8},{8,12},{5,9},{9,13},{6,10},{10,14},{7,11},{11,15},{20,24},{2... | collective-permute-start | bytes 1572872 | tf_op jit(solution)/shard_map/ppermute | solution.py:129
  37.4 26.1 %copy-start = (bf16[256,1024]{1,0:T(8,128)(2,1)S(1)}, bf16[256,1024]{1,0:T(8,128)(2,1)}, u32[]{:S(2)}) copy-start(bf16[256,1024]{1,0:T(8,128)(2,1)} %param.7) | copy-start | bytes 1572868
  38.4 7.7 %collective-permute-start.4 = (bf16[256,512]{0,1:T(8,128)(2,1)S(1)}, bf16[256,512]{0,1:T(8,128)(2,1)S(1)}, u32[]{:S(2)}, u32[]{:S(2)}) collective-permute-start(bf16[256,512]{0,1:T(8,128)(2,1)S(1)} %bitcast.66), channel_id=1, source_target_pairs={{0,16},{16,0},{1,17},{17,1},{2,18},{18,2},{3,19},{19,3},{4,20},{20... | collective-permute-start | bytes 786440 | tf_op jit(solution)/shard_map/ppermute | solution.py:85
  46.2 2.2 %copy-start.1 = (bf16[256,512]{0,1:T(8,128)(2,1)}, bf16[256,512]{0,1:T(8,128)(2,1)S(1)}, u32[]{:S(2)}) copy-start(bf16[256,512]{0,1:T(8,128)(2,1)S(1)} %collective-permute-done.4) | copy-start | bytes 786436
  47.0 14.6 %collective-permute-start.5 = (bf16[256,1024]{0,1:T(8,128)(2,1)}, bf16[256,1024]{0,1:T(8,128)(2,1)}, u32[]{:S(2)}, u32[]{:S(2)}) collective-permute-start(bf16[256,1024]{0,1:T(8,128)(2,1)} %pad_maximum_fusion.1), channel_id=1, source_target_pairs={{0,2},{1,3},{18,16},{19,17},{4,6},{5,7},{22,20},{23,21},{8,10},{9,... | collective-permute-start | bytes 1572872 | tf_op jit(solution)/shard_map/ppermute | solution.py:89
  48.3 15.2 %collective-permute-start.9 = (bf16[256,1024]{1,0:T(8,128)(2,1)S(1)}, bf16[256,1024]{1,0:T(8,128)(2,1)S(1)}, u32[]{:S(2)}, u32[]{:S(2)}) collective-permute-start(bf16[256,1024]{1,0:T(8,128)(2,1)S(1)} %collective-permute-done.8), channel_id=1, source_target_pairs={{4,0},{5,1},{6,2},{7,3},{20,16},{21,17},{22,18},{23,19}} | collective-permute-start | bytes 1572872 | tf_op jit(solution)/shard_map/ppermute | solution.py:130
  49.7 13.8 %collective-permute-start.11 = (bf16[256,1024]{1,0:T(8,128)(2,1)S(1)}, bf16[256,1024]{1,0:T(8,128)(2,1)}, u32[]{:S(2)}, u32[]{:S(2)}) collective-permute-start(bf16[256,1024]{1,0:T(8,128)(2,1)S(1)} %collective-permute-done.10), channel_id=1, source_target_pairs={{8,12},{9,13},{10,14},{11,15},{24,28},{25,29},{26,30},{27,31}} | collective-permute-start | bytes 1572872 | tf_op jit(solution)/shard_map/ppermute | solution.py:129
  51.1 13.3 %collective-permute-start.6 = (bf16[256,1024]{0,1:T(8,128)(2,1)}, bf16[256,1024]{0,1:T(8,128)(2,1)S(1)}, u32[]{:S(2)}, u32[]{:S(2)}) collective-permute-start(bf16[256,1024]{0,1:T(8,128)(2,1)} %pad_maximum_fusion.1), channel_id=1, source_target_pairs={{0,1},{1,0},{18,19},{19,18},{4,5},{5,4},{22,23},{23,22},{8,9},{9,8... | collective-permute-start | bytes 1572872 | tf_op jit(solution)/shard_map/ppermute | solution.py:89
  61.6 4.0 %collective-permute-start.7 = (bf16[256,1024]{0,1:T(8,128)(2,1)}, bf16[256,1024]{0,1:T(8,128)(2,1)S(1)}, u32[]{:S(2)}, u32[]{:S(2)}) collective-permute-start(bf16[256,1024]{0,1:T(8,128)(2,1)} %collective-permute-done.5), channel_id=1, source_target_pairs={{2,3},{3,2},{16,17},{17,16},{6,7},{7,6},{20,21},{21,20},{10,11},{1... | collective-permute-start | bytes 1572872 | tf_op jit(solution)/shard_map/ppermute | solution.py:89
  64.3 1.3 %copy-start.2 = (bf16[256,512]{0,1:T(8,128)(2,1)S(1)}, bf16[256,512]{0,1:T(8,128)(2,1)}, u32[]{:S(2)}) copy-start(bf16[256,512]{0,1:T(8,128)(2,1)} %copy-done.1) | copy-start | bytes 786436
  67.8 14.0 %collective-permute-start.12 = (bf16[256,1024]{1,0:T(8,128)(2,1)S(1)}, bf16[256,1024]{1,0:T(8,128)(2,1)S(1)}, u32[]{:S(2)}, u32[]{:S(2)}) collective-permute-start(bf16[256,1024]{1,0:T(8,128)(2,1)S(1)} %convolution_convert_fusion), channel_id=1, source_target_pairs={{0,16},{16,0},{1,17},{17,1},{2,18},{18,2},{3,19},{19,3},{4,20},{20... | collective-permute-start | bytes 1572872 | tf_op jit(solution)/shard_map/ppermute | solution.py:85

commit v12 on v10

--- a/solution.py
+++ b/solution.py
@@ -115,17 +115,23 @@
 
 def first_hop(block, axis):
     count = lax.axis_size(axis)
+    far = count - 1
     rising = lax.ppermute(block, axis, [(i, i + 1) for i in range(count - 1)])
     falling = lax.ppermute(block, axis, [(i, i - 1) for i in range(1, count)])
-    return rising, falling
+    far_rising = lax.ppermute(block, axis, [(i, i + far) for i in range(count - far)])
+    far_falling = lax.ppermute(block, axis, [(i + far, i) for i in range(count - far)])
+    return rising, falling, far_rising, far_falling
 
 
 def line_rows(block, first, axis):
     count = lax.axis_size(axis)
     here = lax.axis_index(axis)
-    rising, falling = first
+    rising, falling, far_rising, far_falling = first
+    far = count - 1
     arrivals = [(block, 0), (rising, -1), (falling, 1)]
-    for step in range(2, count):
+    if far > 1:
+        arrivals += [(far_rising, -far), (far_falling, far)]
+    for step in range(2, far):
         rising = lax.ppermute(rising, axis, [(i, i + 1) for i in range(step - 1, count - 1)])
         falling = lax.ppermute(falling, axis, [(i, i - 1) for i in range(1, count - step + 1)])
         arrivals.append((rising, -step))

time: 80.7 us -> 95.2 us (1.18)
  the two profiles are of different devices: /device:TPU:12 before, /device:TPU:0 now
where the time goes in v12:
time: 95.2 us; the launch traced here: 94.3 us
  waiting for transfers between devices  48.6 us (51%)
  starting transfers between devices  33.4 us (35%)
  other arithmetic  5.87 us (6%)
  local copies, waits for them, and re-layouts  3.12 us (3%)
  matrix products  3.04 us (3%)
    ppermute x2, waiting for transfers between devices, swapped(): return lax.ppermute(block, axis, [(0, 1), (1, 0)])  16.4 us
    ppermute x2, waiting for transfers between devices, shifted(): return lax.ppermute(block, axis, route)  15.1 us
    ppermute x1, waiting for transfers between devices, first_hop(): lax.ppermute(block, axis, [(i + far, i) for i in range(count - far)])  12.3 us
    ppermute x2, starting transfers between devices, swapped(): return lax.ppermute(block, axis, [(0, 1), (1, 0)])  6.72 us
    ppermute x1, starting transfers between devices, first_hop(): lax.ppermute(block, axis, [(i, i + far) for i in range(count - far)])  6.61 us
    ppermute x3, starting transfers between devices, sent(): return lax.ppermute(block, ('dp', 'tensor'), route)  6.06 us
    ppermute x1, starting transfers between devices, first_hop(): rising = lax.ppermute(block, axis, [(i, i + 1) for i in range(count - 1)])  4.95 us
    ppermute x3, waiting for transfers between devices, sent(): return lax.ppermute(block, ('dp', 'tensor'), route)  4.71 us
  transfers between devices with their start and end apart: 13, of which 6 were waited for; matrix products, arithmetic and copies ran while one was open for 11% of the time, Pallas kernels for 0%

profile of v12, /device:TPU:0, one launch (start us, length us, event | category | flops | bytes accessed | tf_op | source)
XLA Modules:
  0.0 94.3 jit_solution(7571376352547466010)
XLA Ops:
  0.0 5.0 %collective-permute-start = (bf16[256,1024]{1,0:T(8,128)(2,1)}, bf16[256,1024]{1,0:T(8,128)(2,1)S(1)}, u32[]{:S(2)}, u32[]{:S(2)}) collective-permute-start(bf16[256,1024]{1,0:T(8,128)(2,1)} %param.7), channel_id=1, source_target_pairs={{0,4},{4,8},{8,12},{1,5},{5,9},{9,13},{2,6},{6,10},{10,14},{3,7},{... | collective-permute-start | bytes 1572872 | tf_op jit(solution)/shard_map/ppermute | solution.py:119
  5.0 1.3 %collective-permute-start.1 = (bf16[256,1024]{1,0:T(8,128)(2,1)}, bf16[256,1024]{1,0:T(8,128)(2,1)S(1)}, u32[]{:S(2)}, u32[]{:S(2)}) collective-permute-start(bf16[256,1024]{1,0:T(8,128)(2,1)} %param.7), channel_id=1, source_target_pairs={{4,0},{8,4},{12,8},{5,1},{9,5},{13,9},{6,2},{10,6},{14,10},{7,3},{... | collective-permute-start | bytes 1572872 | tf_op jit(solution)/shard_map/ppermute | solution.py:120
  6.3 6.6 %collective-permute-start.2 = (bf16[256,1024]{1,0:T(8,128)(2,1)}, bf16[256,1024]{1,0:T(8,128)(2,1)S(1)}, u32[]{:S(2)}, u32[]{:S(2)}) collective-permute-start(bf16[256,1024]{1,0:T(8,128)(2,1)} %param.7), channel_id=1, source_target_pairs={{0,12},{1,13},{2,14},{3,15},{16,28},{17,29},{18,30},{19,31}} | collective-permute-start | bytes 1572872 | tf_op jit(solution)/shard_map/ppermute | solution.py:121
  12.9 0.7 convert_element_type.37
  13.6 0.9 copy.21
  14.5 0.1 broadcast_in_dim.27
  14.6 1.3 %collective-permute-start.5 = (bf16[256,3,128]{2,0,1:T(8,128)(2,1)S(1)}, bf16[256,3,128]{2,0,1:T(8,128)(2,1)S(1)}, u32[]{:S(2)}, u32[]{:S(2)}) collective-permute-start(bf16[256,3,128]{2,0,1:T(8,128)(2,1)S(1)} %pad_maximum_fusion.3), channel_id=1, source_target_pairs={{0,8},{4,12},{1,9},{5,13},{2,10},{6,14},{3,11},{7,15},{16,24},{20,... | collective-permute-start | bytes 589832 | tf_op jit(solution)/shard_map/ppermute | solution.py:17
  15.9 2.4 %collective-permute-start.4 = (bf16[256,3,128]{2,0,1:T(8,128)(2,1)S(1)}, bf16[256,3,128]{2,0,1:T(8,128)(2,1)S(1)}, u32[]{:S(2)}, u32[]{:S(2)}) collective-permute-start(bf16[256,3,128]{2,0,1:T(8,128)(2,1)S(1)} %pad_maximum_fusion.3), channel_id=1, source_target_pairs={{0,4},{4,8},{8,12},{1,5},{5,9},{9,13},{2,6},{6,10},{10,14},{3,7},{... | collective-permute-start | bytes 589832 | tf_op jit(solution)/shard_map/ppermute | solution.py:17
  18.4 1.0 %reshape.68 = bf16[256,4,128]{2,1,0:T(4,128)(2,1)S(1)} reshape(bf16[1,256,512]{2,1,0:T(8,128)(2,1)} %param.4) | data formatting | bytes 524288 | tf_op jit(solution)/shard_map/reshape.3
  19.5 13.5 %collective-permute-done.5 = bf16[256,3,128]{2,0,1:T(8,128)(2,1)S(1)} collective-permute-done((bf16[256,3,128]{2,0,1:T(8,128)(2,1)S(1)}, bf16[256,3,128]{2,0,1:T(8,128)(2,1)S(1)}, u32[]{:S(2)}, u32[]{:S(2)}) %collective-permute-start.5) | collective-permute-done | bytes 196640 | tf_op jit(solution)/shard_map/ppermute | solution.py:17
  32.9 1.3 %collective-permute-start.3 = (bf16[256,1024]{1,0:T(8,128)(2,1)}, bf16[256,1024]{1,0:T(8,128)(2,1)S(1)}, u32[]{:S(2)}, u32[]{:S(2)}) collective-permute-start(bf16[256,1024]{1,0:T(8,128)(2,1)} %param.7), channel_id=1, source_target_pairs={{12,0},{13,1},{14,2},{15,3},{28,16},{29,17},{30,18},{31,19}} | collective-permute-start | bytes 1572872 | tf_op jit(solution)/shard_map/ppermute | solution.py:122
  34.2 0.1 convert_reduce_fusion
  34.3 1.7 %collective-permute-done.4 = bf16[256,3,128]{2,0,1:T(8,128)(2,1)S(1)} collective-permute-done((bf16[256,3,128]{2,0,1:T(8,128)(2,1)S(1)}, bf16[256,3,128]{2,0,1:T(8,128)(2,1)S(1)}, u32[]{:S(2)}, u32[]{:S(2)}) %collective-permute-start.4) | collective-permute-done | bytes 196640 | tf_op jit(solution)/shard_map/ppermute | solution.py:17
  36.0 0.1 convert_reduce_fusion.1
  36.1 0.7 pad_add_fusion
  36.9 1.4 %and_and_fusion = pred[256,768]{0,1:T(8,128)(4,1)S(1)} fusion(s32[256]{0:T(256)S(1)} %iota_add_fusion.2, s32[256]{0:T(256)} %bitcast.71, s32[768]{0:T(1024)S(1)} %pad_add_fusion.1, s32[768]{0:T(1024)S(1)} %pad_add_fusion, pred[768]{0:T(1024)(128)(4,1)S(1)} %broadcast_compare_fusion), kind=kLoop, calls=%fused_computation.14 | loop fusion | flops 786432 | bytes 205568 | tf_op jit(solution)/shard_map/and | solution.py:64
  38.3 0.6 fusion
  39.0 0.8 fusion.1
  39.8 0.0 copy-start
  39.8 0.9 fusion.13
  40.7 0.0 collective-permute-done
  40.7 0.0 collective-permute-done.1
  40.7 0.0 collective-permute-done.2
  40.8 12.3 %collective-permute-done.3 = bf16[256,1024]{1,0:T(8,128)(2,1)S(1)} collective-permute-done((bf16[256,1024]{1,0:T(8,128)(2,1)}, bf16[256,1024]{1,0:T(8,128)(2,1)S(1)}, u32[]{:S(2)}, u32[]{:S(2)}) %collective-permute-start.3) | collective-permute-done | bytes 524320 | tf_op jit(solution)/shard_map/ppermute | solution.py:122
  53.0 1.3 %collective-permute-start.10 = (bf16[256,1024]{1,0:T(8,128)(2,1)S(1)}, bf16[256,1024]{1,0:T(8,128)(2,1)S(1)}, u32[]{:S(2)}, u32[]{:S(2)}) collective-permute-start(bf16[256,1024]{1,0:T(8,128)(2,1)S(1)} %collective-permute-done.1), channel_id=1, source_target_pairs={{4,0},{8,4},{5,1},{9,5},{6,2},{10,6},{7,3},{11,7},{20,16},{24,20},... | collective-permute-start | bytes 1572872 | tf_op jit(solution)/shard_map/ppermute | solution.py:136
  54.3 1.5 %collective-permute-start.11 = (bf16[256,1024]{1,0:T(8,128)(2,1)S(1)}, bf16[256,1024]{1,0:T(8,128)(2,1)}, u32[]{:S(2)}, u32[]{:S(2)}) collective-permute-start(bf16[256,1024]{1,0:T(8,128)(2,1)S(1)} %collective-permute-done), channel_id=1, source_target_pairs={{4,8},{8,12},{5,9},{9,13},{6,10},{10,14},{7,11},{11,15},{20,24},{2... | collective-permute-start | bytes 1572872 | tf_op jit(solution)/shard_map/ppermute | solution.py:135
  55.8 1.5 %collective-permute-start.6 = (bf16[256,512]{0,1:T(8,128)(2,1)S(1)}, bf16[256,512]{0,1:T(8,128)(2,1)}, u32[]{:S(2)}, u32[]{:S(2)}) collective-permute-start(bf16[256,512]{0,1:T(8,128)(2,1)S(1)} %bitcast.66), channel_id=1, source_target_pairs={{0,16},{16,0},{1,17},{17,1},{2,18},{18,2},{3,19},{19,3},{4,20},{20... | collective-permute-start | bytes 786440 | tf_op jit(solution)/shard_map/ppermute | solution.py:85
  57.3 5.0 %collective-permute-done.6 = bf16[256,512]{0,1:T(8,128)(2,1)} collective-permute-done((bf16[256,512]{0,1:T(8,128)(2,1)S(1)}, bf16[256,512]{0,1:T(8,128)(2,1)}, u32[]{:S(2)}, u32[]{:S(2)}) %collective-permute-start.6) | collective-permute-done | bytes 262176 | tf_op jit(solution)/shard_map/ppermute | solution.py:85
  62.3 1.0 %constant_dynamic-update-slice_fusion = bf16[256,1024]{0,1:T(8,128)(2,1)S(1)} fusion(bf16[256,1024]{0,1:T(8,128)(2,1)S(1)} %constant_dynamic-update-slice_fusion.1, bf16[256,512]{0,1:T(8,128)(2,1)} %collective-permute-done.6), kind=kLoop, calls=%fused_computation.37 | loop fusion | bytes 524288 | tf_op jit(solution)/shard_map/concatenate | solution.py:97
  63.2 3.5 %collective-permute-start.7 = (bf16[256,1024]{0,1:T(8,128)(2,1)S(1)}, bf16[256,1024]{0,1:T(8,128)(2,1)S(1)}, u32[]{:S(2)}, u32[]{:S(2)}) collective-permute-start(bf16[256,1024]{0,1:T(8,128)(2,1)S(1)} %constant_dynamic-update-slice_fusion), channel_id=1, source_target_pairs={{0,2},{1,3},{18,16},{19,17},{4,6},{5,7},{22,20},{23,21},{8,10},{9,... | collective-permute-start | bytes 1572872 | tf_op jit(solution)/shard_map/ppermute | solution.py:89
  66.7 1.9 %collective-permute-start.8 = (bf16[256,1024]{0,1:T(8,128)(2,1)S(1)}, bf16[256,1024]{0,1:T(8,128)(2,1)S(1)}, u32[]{:S(2)}, u32[]{:S(2)}) collective-permute-start(bf16[256,1024]{0,1:T(8,128)(2,1)S(1)} %constant_dynamic-update-slice_fusion), channel_id=1, source_target_pairs={{0,1},{1,0},{18,19},{19,18},{4,5},{5,4},{22,23},{23,22},{8,9},{9,8... | collective-permute-start | bytes 1572872 | tf_op jit(solution)/shard_map/ppermute | solution.py:89
  68.6 0.0 collective-permute-done.10
  68.6 0.0 collective-permute-done.11
  68.7 0.2 select_select_fusion
  68.8 0.2 select_select_fusion.1
  69.0 0.2 select_select_fusion.2
  69.2 4.7 %collective-permute-done.7 = bf16[256,1024]{0,1:T(8,128)(2,1)S(1)} collective-permute-done((bf16[256,1024]{0,1:T(8,128)(2,1)S(1)}, bf16[256,1024]{0,1:T(8,128)(2,1)S(1)}, u32[]{:S(2)}, u32[]{:S(2)}) %collective-permute-start.7) | collective-permute-done | bytes 524320 | tf_op jit(solution)/shard_map/ppermute | solution.py:89
  73.9 0.7 collective-permute-start.9
  74.6 0.2 select_select_fusion.3
  74.8 0.2 pad_maximum_fusion
  75.0 0.0 collective-permute-done.8
  75.0 0.0 collective-permute-done.9
  75.0 0.1 broadcast_select_fusion.3
  75.2 0.7 convolution_convert_fusion
  75.9 5.2 %collective-permute-start.12 = (bf16[256,1024]{1,0:T(8,128)(2,1)S(1)}, bf16[256,1024]{1,0:T(8,128)(2,1)S(1)}, u32[]{:S(2)}, u32[]{:S(2)}) collective-permute-start(bf16[256,1024]{1,0:T(8,128)(2,1)S(1)} %convolution_convert_fusion), channel_id=1, source_target_pairs={{0,16},{16,0},{1,17},{17,1},{2,18},{18,2},{3,19},{19,3},{4,20},{20... | collective-permute-start | bytes 1572872 | tf_op jit(solution)/shard_map/ppermute | solution.py:85
  81.2 0.7 fusion.28
  81.9 11.5 %collective-permute-done.12 = bf16[256,1024]{1,0:T(8,128)(2,1)S(1)} collective-permute-done((bf16[256,1024]{1,0:T(8,128)(2,1)S(1)}, bf16[256,1024]{1,0:T(8,128)(2,1)S(1)}, u32[]{:S(2)}, u32[]{:S(2)}) %collective-permute-start.12) | collective-permute-done | bytes 524320 | tf_op jit(solution)/shard_map/ppermute | solution.py:85
  93.4 0.9 fusion.16
  (13 shorter events, 0.2 us)
Async XLA Ops:
  0.0 40.7 %collective-permute-start = (bf16[256,1024]{1,0:T(8,128)(2,1)}, bf16[256,1024]{1,0:T(8,128)(2,1)S(1)}, u32[]{:S(2)}, u32[]{:S(2)}) collective-permute-start(bf16[256,1024]{1,0:T(8,128)(2,1)} %param.7), channel_id=1, source_target_pairs={{0,4},{4,8},{8,12},{1,5},{5,9},{9,13},{2,6},{6,10},{10,14},{3,7},{... | collective-permute-start | bytes 1572872 | tf_op jit(solution)/shard_map/ppermute | solution.py:119
  5.0 35.8 %collective-permute-start.1 = (bf16[256,1024]{1,0:T(8,128)(2,1)}, bf16[256,1024]{1,0:T(8,128)(2,1)S(1)}, u32[]{:S(2)}, u32[]{:S(2)}) collective-permute-start(bf16[256,1024]{1,0:T(8,128)(2,1)} %param.7), channel_id=1, source_target_pairs={{4,0},{8,4},{12,8},{5,1},{9,5},{13,9},{6,2},{10,6},{14,10},{7,3},{... | collective-permute-start | bytes 1572872 | tf_op jit(solution)/shard_map/ppermute | solution.py:120
  6.3 34.5 %collective-permute-start.2 = (bf16[256,1024]{1,0:T(8,128)(2,1)}, bf16[256,1024]{1,0:T(8,128)(2,1)S(1)}, u32[]{:S(2)}, u32[]{:S(2)}) collective-permute-start(bf16[256,1024]{1,0:T(8,128)(2,1)} %param.7), channel_id=1, source_target_pairs={{0,12},{1,13},{2,14},{3,15},{16,28},{17,29},{18,30},{19,31}} | collective-permute-start | bytes 1572872 | tf_op jit(solution)/shard_map/ppermute | solution.py:121
  14.6 18.3 %collective-permute-start.5 = (bf16[256,3,128]{2,0,1:T(8,128)(2,1)S(1)}, bf16[256,3,128]{2,0,1:T(8,128)(2,1)S(1)}, u32[]{:S(2)}, u32[]{:S(2)}) collective-permute-start(bf16[256,3,128]{2,0,1:T(8,128)(2,1)S(1)} %pad_maximum_fusion.3), channel_id=1, source_target_pairs={{0,8},{4,12},{1,9},{5,13},{2,10},{6,14},{3,11},{7,15},{16,24},{20,... | collective-permute-start | bytes 589832 | tf_op jit(solution)/shard_map/ppermute | solution.py:17
  15.9 20.1 %collective-permute-start.4 = (bf16[256,3,128]{2,0,1:T(8,128)(2,1)S(1)}, bf16[256,3,128]{2,0,1:T(8,128)(2,1)S(1)}, u32[]{:S(2)}, u32[]{:S(2)}) collective-permute-start(bf16[256,3,128]{2,0,1:T(8,128)(2,1)S(1)} %pad_maximum_fusion.3), channel_id=1, source_target_pairs={{0,4},{4,8},{8,12},{1,5},{5,9},{9,13},{2,6},{6,10},{10,14},{3,7},{... | collective-permute-start | bytes 589832 | tf_op jit(solution)/shard_map/ppermute | solution.py:17
  32.9 20.1 %collective-permute-start.3 = (bf16[256,1024]{1,0:T(8,128)(2,1)}, bf16[256,1024]{1,0:T(8,128)(2,1)S(1)}, u32[]{:S(2)}, u32[]{:S(2)}) collective-permute-start(bf16[256,1024]{1,0:T(8,128)(2,1)} %param.7), channel_id=1, source_target_pairs={{12,0},{13,1},{14,2},{15,3},{28,16},{29,17},{30,18},{31,19}} | collective-permute-start | bytes 1572872 | tf_op jit(solution)/shard_map/ppermute | solution.py:122
  39.8 28.9 %copy-start = (bf16[256,1024]{1,0:T(8,128)(2,1)S(1)}, bf16[256,1024]{1,0:T(8,128)(2,1)}, u32[]{:S(2)}) copy-start(bf16[256,1024]{1,0:T(8,128)(2,1)} %param.7) | copy-start | bytes 1572868
  53.0 15.6 %collective-permute-start.10 = (bf16[256,1024]{1,0:T(8,128)(2,1)S(1)}, bf16[256,1024]{1,0:T(8,128)(2,1)S(1)}, u32[]{:S(2)}, u32[]{:S(2)}) collective-permute-start(bf16[256,1024]{1,0:T(8,128)(2,1)S(1)} %collective-permute-done.1), channel_id=1, source_target_pairs={{4,0},{8,4},{5,1},{9,5},{6,2},{10,6},{7,3},{11,7},{20,16},{24,20},... | collective-permute-start | bytes 1572872 | tf_op jit(solution)/shard_map/ppermute | solution.py:136
  54.3 14.3 %collective-permute-start.11 = (bf16[256,1024]{1,0:T(8,128)(2,1)S(1)}, bf16[256,1024]{1,0:T(8,128)(2,1)}, u32[]{:S(2)}, u32[]{:S(2)}) collective-permute-start(bf16[256,1024]{1,0:T(8,128)(2,1)S(1)} %collective-permute-done), channel_id=1, source_target_pairs={{4,8},{8,12},{5,9},{9,13},{6,10},{10,14},{7,11},{11,15},{20,24},{2... | collective-permute-start | bytes 1572872 | tf_op jit(solution)/shard_map/ppermute | solution.py:135
  55.8 6.5 %collective-permute-start.6 = (bf16[256,512]{0,1:T(8,128)(2,1)S(1)}, bf16[256,512]{0,1:T(8,128)(2,1)}, u32[]{:S(2)}, u32[]{:S(2)}) collective-permute-start(bf16[256,512]{0,1:T(8,128)(2,1)S(1)} %bitcast.66), channel_id=1, source_target_pairs={{0,16},{16,0},{1,17},{17,1},{2,18},{18,2},{3,19},{19,3},{4,20},{20... | collective-permute-start | bytes 786440 | tf_op jit(solution)/shard_map/ppermute | solution.py:85
  63.2 10.7 %collective-permute-start.7 = (bf16[256,1024]{0,1:T(8,128)(2,1)S(1)}, bf16[256,1024]{0,1:T(8,128)(2,1)S(1)}, u32[]{:S(2)}, u32[]{:S(2)}) collective-permute-start(bf16[256,1024]{0,1:T(8,128)(2,1)S(1)} %constant_dynamic-update-slice_fusion), channel_id=1, source_target_pairs={{0,2},{1,3},{18,16},{19,17},{4,6},{5,7},{22,20},{23,21},{8,10},{9,... | collective-permute-start | bytes 1572872 | tf_op jit(solution)/shard_map/ppermute | solution.py:89
  66.7 8.3 %collective-permute-start.8 = (bf16[256,1024]{0,1:T(8,128)(2,1)S(1)}, bf16[256,1024]{0,1:T(8,128)(2,1)S(1)}, u32[]{:S(2)}, u32[]{:S(2)}) collective-permute-start(bf16[256,1024]{0,1:T(8,128)(2,1)S(1)} %constant_dynamic-update-slice_fusion), channel_id=1, source_target_pairs={{0,1},{1,0},{18,19},{19,18},{4,5},{5,4},{22,23},{23,22},{8,9},{9,8... | collective-permute-start | bytes 1572872 | tf_op jit(solution)/shard_map/ppermute | solution.py:89
  73.9 1.1 %collective-permute-start.9 = (bf16[256,1024]{0,1:T(8,128)(2,1)S(1)}, bf16[256,1024]{0,1:T(8,128)(2,1)S(1)}, u32[]{:S(2)}, u32[]{:S(2)}) collective-permute-start(bf16[256,1024]{0,1:T(8,128)(2,1)S(1)} %collective-permute-done.7), channel_id=1, source_target_pairs={{2,3},{3,2},{16,17},{17,16},{6,7},{7,6},{20,21},{21,20},{10,11},{1... | collective-permute-start | bytes 1572872 | tf_op jit(solution)/shard_map/ppermute | solution.py:89
  75.9 17.5 %collective-permute-start.12 = (bf16[256,1024]{1,0:T(8,128)(2,1)S(1)}, bf16[256,1024]{1,0:T(8,128)(2,1)S(1)}, u32[]{:S(2)}, u32[]{:S(2)}) collective-permute-start(bf16[256,1024]{1,0:T(8,128)(2,1)S(1)} %convolution_convert_fusion), channel_id=1, source_target_pairs={{0,16},{16,0},{1,17},{17,1},{2,18},{18,2},{3,19},{19,3},{4,20},{20... | collective-permute-start | bytes 1572872 | tf_op jit(solution)/shard_map/ppermute | solution.py:85

commit v13 on v10

--- a/solution.py
+++ b/solution.py
@@ -23,27 +23,33 @@
     return lax.ppermute(block, axis, route)
 
 
-def attention(queries, keyvals, documents):
+def packed_keys(keyvals, documents):
+    length = keyvals.shape[1]
+    label_slab = jnp.broadcast_to(
+        documents[0].astype(jnp.bfloat16)[:, None, None], (length, 1, keyvals.shape[3])
+    )
+    return jnp.concatenate([keyvals[0], label_slab], axis=1)
+
+
+def reach_of(length):
+    cycle_size = lax.axis_size("ctx")
+    return min(cycle_size - 1, (cycle_size * length // 2 - 1 + length - 1) // length)
+
+
+def attention(queries, keyvals, documents, arrived):
     length = queries.shape[1]
     pair_width = keyvals.shape[3]
     pair_heads = pair_width // HEAD_DIM
     query_group_size = queries.shape[2] // pair_width
-    cycle_size = lax.axis_size("ctx")
     position = lax.axis_index("ctx")
     offsets = jnp.arange(length, dtype=jnp.int32)
-    reach_hops = min(cycle_size - 1, (cycle_size * length // 2 - 1 + length - 1) // length)
 
     pair_blocks = [keyvals[0]]
     label_blocks = [documents[0]]
     place_blocks = [position * length + offsets]
-    label_slab = jnp.broadcast_to(
-        documents[0].astype(jnp.bfloat16)[:, None, None], (length, 1, pair_width)
-    )
-    packed = jnp.concatenate([keyvals[0], label_slab], axis=1)
-    for hop in range(1, reach_hops + 1):
-        arrived = shifted(packed, "ctx", hop)
-        pair_blocks.append(arrived[:, :2])
-        label_blocks.append(arrived[:, 2, 0].astype(jnp.int32))
+    for hop, block in enumerate(arrived, start=1):
+        pair_blocks.append(block[:, :2])
+        label_blocks.append(block[:, 2, 0].astype(jnp.int32))
         place_blocks.append((position - hop) * length + offsets)
     pairs = jnp.concatenate(pair_blocks, axis=0)
     key_labels = jnp.concatenate(label_blocks, axis=0)
@@ -155,15 +161,26 @@
     width = queries.shape[2]
     side_width = block_rows * lax.axis_size("ctx")
     fits = lax.axis_size("tensor") == 4
+    fits = fits and reach_of(queries.shape[1]) >= 1
     if lax.axis_size("dp") == 2 and side_width == 2 * width and fits:
-        first = first_hop(output_weight, "ctx")
-        head_values = attention(queries, keyvals, documents)
-        first, head_values = lax.optimization_barrier((first, head_values))
-        side_rows = line_rows(output_weight, first, "ctx")
+        count = lax.axis_size("ctx")
+        columns = output_weight.shape[1]
+        packed = packed_keys(keyvals, documents)
+        joined = jnp.concatenate([output_weight, packed.reshape(packed.shape[0], -1)], axis=1)
+        joined = lax.ppermute(joined, "ctx", [(i, i + 1) for i in range(count - 1)])
+        rising = joined[:, :columns]
+        nearest = joined[:, columns:].reshape(packed.shape)
+        falling = lax.ppermute(output_weight, "ctx", [(i, i - 1) for i in range(1, count)])
+        farther = [shifted(packed, "ctx", hop) for hop in range(2, reach_of(queries.shape[1]) + 1)]
+        falling, farther = lax.optimization_barrier((falling, farther))
+        head_values = attention(queries, keyvals, documents, [nearest] + farther)
+        side_rows = line_rows(output_weight, (rising, falling), "ctx")
         result = split_projection(head_values, side_rows)
         return result.astype(jnp.bfloat16)[None]
     all_rows = lax.all_gather(output_weight, ("dp", "ctx"), axis=0, tiled=True)
-    head_values = attention(queries, keyvals, documents)
+    packed = packed_keys(keyvals, documents)
+    arrived = [shifted(packed, "ctx", hop) for hop in range(1, reach_of(queries.shape[1]) + 1)]
+    head_values = attention(queries, keyvals, documents, arrived)
     group = lax.axis_size("tensor")
     me = lax.axis_index("tensor")
     result = None

time: 80.7 us -> 85.6 us (1.061)
  the two profiles are of different devices: /device:TPU:12 before, /device:TPU:10 now
where the time goes in v13:
time: 85.6 us; the launch traced here: 85.1 us
  waiting for transfers between devices  45.3 us (53%)
  starting transfers between devices  23.6 us (28%)
  other arithmetic  7.52 us (9%)
  local copies, waits for them, and re-layouts  4.31 us (5%)
  matrix products  4.07 us (5%)
    ppermute x2, waiting for transfers between devices, swapped(): return lax.ppermute(block, axis, [(0, 1), (1, 0)])  19.3 us
    ppermute x1, waiting for transfers between devices, shifted(): return lax.ppermute(block, axis, route)  16.3 us
    ppermute x3, waiting for transfers between devices, sent(): return lax.ppermute(block, ('dp', 'tensor'), route)  9.7 us
    ppermute x2, starting transfers between devices, line_rows(): lax.ppermute(rising, axis, [(i, i + 1) for i in range(step - 1, count - 1)])  5.44 us
    ppermute x1, starting transfers between devices, shifted(): return lax.ppermute(block, axis, route)  4.49 us
    ppermute x3, starting transfers between devices, sent(): return lax.ppermute(block, ('dp', 'tensor'), route)  3.87 us
    ppermute x1, starting transfers between devices, shards(): joined = lax.ppermute(joined, 'ctx', [(i, i + 1) for i in range(count - 1)])  3.47 us
    ppermute x2, starting transfers between devices, line_rows(): lax.ppermute(falling, axis, [(i, i - 1) for i in range(1, count - step +...  3.23 us
  transfers between devices with their start and end apart: 12, of which 5 were waited for; matrix products, arithmetic and copies ran while one was open for 10% of the time, Pallas kernels for 0%

profile of v13, /device:TPU:10, one launch (start us, length us, event | category | flops | bytes accessed | tf_op | source)
XLA Modules:
  0.0 85.1 jit_solution(16134742433939931436)
XLA Ops:
  0.0 1.3 %copy.11 = bf16[256,1024]{0,1:T(8,128)(2,1)S(1)} copy(bf16[256,1024]{1,0:T(8,128)(2,1)} %param.7) | data formatting | bytes 1048576 | tf_op args[3]
  1.3 0.7 convert_element_type.37
  2.0 0.9 %copy.30 = bf16[1,256,2,128]{3,1,2,0:T(8,128)(2,1)S(1)} copy(bf16[1,256,2,128]{3,2,1,0:T(2,128)(2,1)} %param.5) | data formatting | bytes 262144 | tf_op args[1]
  2.9 0.1 broadcast_in_dim.27
  3.0 0.1 copy.10
  3.2 0.9 %pad_maximum_fusion.1 = bf16[256,1408]{0,1:T(8,128)(2,1)} fusion(bf16[256,384]{0,1:T(8,128)(2,1)S(1)} %bitcast.72, bf16[256,1024]{0,1:T(8,128)(2,1)S(1)} %copy.11), kind=kLoop, calls=%fused_computation.15 | loop fusion | flops 1441792 | bytes 1441792 | tf_op jit(solution)/shard_map/concatenate | solution.py:169
  4.1 3.5 %collective-permute-start = (bf16[256,1408]{0,1:T(8,128)(2,1)}, bf16[256,1408]{0,1:T(8,128)(2,1)S(1)}, u32[]{:S(2)}, u32[]{:S(2)}) collective-permute-start(bf16[256,1408]{0,1:T(8,128)(2,1)} %pad_maximum_fusion.1), channel_id=1, source_target_pairs={{0,4},{4,8},{8,12},{1,5},{5,9},{9,13},{2,6},{6,10},{10,14},{3,7},{... | collective-permute-start | bytes 2162696 | tf_op jit(solution)/shard_map/ppermute | solution.py:170
  7.6 2.4 %collective-permute-start.1 = (bf16[256,1024]{0,1:T(8,128)(2,1)S(1)}, bf16[256,1024]{0,1:T(8,128)(2,1)S(1)}, u32[]{:S(2)}, u32[]{:S(2)}) collective-permute-start(bf16[256,1024]{0,1:T(8,128)(2,1)S(1)} %copy.11), channel_id=1, source_target_pairs={{4,0},{8,4},{12,8},{5,1},{9,5},{13,9},{6,2},{10,6},{14,10},{7,3},{... | collective-permute-start | bytes 1572872 | tf_op jit(solution)/shard_map/ppermute | solution.py:173
  10.0 4.5 %collective-permute-start.2 = (bf16[256,3,128]{2,0,1:T(8,128)(2,1)S(1)}, bf16[256,3,128]{2,0,1:T(8,128)(2,1)S(1)}, u32[]{:S(2)}, u32[]{:S(2)}) collective-permute-start(bf16[256,3,128]{2,0,1:T(8,128)(2,1)S(1)} %pad_maximum_fusion.5), channel_id=1, source_target_pairs={{0,8},{4,12},{1,9},{5,13},{2,10},{6,14},{3,11},{7,15},{16,24},{20,... | collective-permute-start | bytes 589832 | tf_op jit(solution)/shard_map/ppermute | solution.py:17
  14.5 0.8 reshape.76
  15.3 16.3 %collective-permute-done.2 = bf16[256,3,128]{2,0,1:T(8,128)(2,1)S(1)} collective-permute-done((bf16[256,3,128]{2,0,1:T(8,128)(2,1)S(1)}, bf16[256,3,128]{2,0,1:T(8,128)(2,1)S(1)}, u32[]{:S(2)}, u32[]{:S(2)}) %collective-permute-start.2) | collective-permute-done | bytes 196640 | tf_op jit(solution)/shard_map/ppermute | solution.py:17
  31.6 0.0 collective-permute-done.1
  31.6 1.9 %collective-permute-start.7 = (bf16[256,1024]{0,1:T(8,128)(2,1)S(1)}, bf16[256,1024]{0,1:T(8,128)(2,1)S(1)}, u32[]{:S(2)}, u32[]{:S(2)}) collective-permute-start(bf16[256,1024]{0,1:T(8,128)(2,1)S(1)} %collective-permute-done.1), channel_id=1, source_target_pairs={{4,0},{8,4},{5,1},{9,5},{6,2},{10,6},{7,3},{11,7},{20,16},{24,20},... | collective-permute-start | bytes 1572872 | tf_op jit(solution)/shard_map/ppermute | solution.py:136
  33.5 0.1 convert_reduce_fusion
  33.6 0.0 collective-permute-done
  33.7 0.8 slice.55
  34.5 4.0 %collective-permute-start.9 = (bf16[256,1024]{0,1:T(8,128)(2,1)}, bf16[256,1024]{0,1:T(8,128)(2,1)S(1)}, u32[]{:S(2)}, u32[]{:S(2)}) collective-permute-start(bf16[256,1024]{0,1:T(8,128)(2,1)} %slice.55), channel_id=1, source_target_pairs={{4,8},{8,12},{5,9},{9,13},{6,10},{10,14},{7,11},{11,15},{20,24},{2... | collective-permute-start | bytes 1572872 | tf_op jit(solution)/shard_map/ppermute | solution.py:135
  38.5 0.1 copy.24
  38.7 0.7 and_and_fusion
  39.5 1.6 %fusion = (f32[4,256]{1,0:T(4,128)S(1)}, f32[768,256,4]{1,0,2:T(8,128)S(1)}) fusion(pred[256,768]{0,1:T(8,128)(4,1)S(1)} %and_and_fusion, bf16[256,4,128]{2,1,0:T(4,128)(2,1)} %reshape.76, bf16[768,2,128]{2,0,1:T(8,128)(2,1)S(1)} %pad_maximum_fusion.4), kind=kOutput, calls=%fused_computation.2 | convolution fusion | flops 203684864 | bytes 3805184 | tf_op jit(solution)/shard_map/qhgd,khd->hgqk/dot_general | solution.py:65
  41.1 0.8 fusion.1
  41.8 0.9 %fusion.13 = bf16[256,1,4,128]{0,3,2,1:T(8,128)(2,1)S(1)} fusion(f32[768,256,4]{1,0,2:T(8,128)S(1)} %get-tuple-element.20, f32[4,256]{1,0:T(4,128)S(1)} %get-tuple-element.19, pred[256,768]{0,1:T(8,128)(4,1)S(1)} %and_and_fusion, f32[256,4]{0,1:T(4,128)S(1)} %bitcast.75, bf16[768,2,128]{2,0,1:T(8,128)(2,1)S(1)} %pad_maximum_fusion.4), kind=kOutput, calls=%fused_computation.13 | convolution fusion | flops 205520896 | bytes 3809280 | tf_op jit(solution)/shard_map/hgqk,khd->qhgd/dot_general | solution.py:78
  42.8 0.6 collective-permute-start.3
  43.4 6.1 %collective-permute-done.3 = bf16[256,512]{0,1:T(8,128)(2,1)S(1)} collective-permute-done((bf16[256,512]{0,1:T(8,128)(2,1)S(1)}, bf16[256,512]{0,1:T(8,128)(2,1)S(1)}, u32[]{:S(2)}, u32[]{:S(2)}) %collective-permute-start.3) | collective-permute-done | bytes 262176 | tf_op jit(solution)/shard_map/ppermute | solution.py:91
  49.5 0.9 %pad_maximum_fusion.2 = bf16[256,1024]{0,1:T(8,128)(2,1)} fusion(bf16[256,512]{0,1:T(8,128)(2,1)S(1)} %collective-permute-done.3, bf16[256,512]{0,1:T(8,128)(2,1)S(1)} %bitcast.70), kind=kLoop, calls=%fused_computation.17 | loop fusion | flops 1048576 | bytes 1048576 | tf_op jit(solution)/shard_map/concatenate | solution.py:103
  50.4 1.3 %collective-permute-start.4 = (bf16[256,1024]{0,1:T(8,128)(2,1)}, bf16[256,1024]{0,1:T(8,128)(2,1)}, u32[]{:S(2)}, u32[]{:S(2)}) collective-permute-start(bf16[256,1024]{0,1:T(8,128)(2,1)} %pad_maximum_fusion.2), channel_id=1, source_target_pairs={{0,2},{1,3},{18,16},{19,17},{4,6},{5,7},{22,20},{23,21},{8,10},{9,... | collective-permute-start | bytes 1572872 | tf_op jit(solution)/shard_map/ppermute | solution.py:95
  51.6 0.0 collective-permute-done.7
  51.7 1.3 %collective-permute-start.8 = (bf16[256,1024]{0,1:T(8,128)(2,1)S(1)}, bf16[256,1024]{0,1:T(8,128)(2,1)S(1)}, u32[]{:S(2)}, u32[]{:S(2)}) collective-permute-start(bf16[256,1024]{0,1:T(8,128)(2,1)S(1)} %collective-permute-done.7), channel_id=1, source_target_pairs={{4,0},{5,1},{6,2},{7,3},{20,16},{21,17},{22,18},{23,19}} | collective-permute-start | bytes 1572872 | tf_op jit(solution)/shard_map/ppermute | solution.py:136
  53.0 0.0 collective-permute-done.9
  53.0 1.5 %collective-permute-start.10 = (bf16[256,1024]{0,1:T(8,128)(2,1)S(1)}, bf16[256,1024]{0,1:T(8,128)(2,1)}, u32[]{:S(2)}, u32[]{:S(2)}) collective-permute-start(bf16[256,1024]{0,1:T(8,128)(2,1)S(1)} %collective-permute-done.9), channel_id=1, source_target_pairs={{8,12},{9,13},{10,14},{11,15},{24,28},{25,29},{26,30},{27,31}} | collective-permute-start | bytes 1572872 | tf_op jit(solution)/shard_map/ppermute | solution.py:135
  54.5 0.7 collective-permute-start.5
  55.2 8.7 %collective-permute-done.4 = bf16[256,1024]{0,1:T(8,128)(2,1)} collective-permute-done((bf16[256,1024]{0,1:T(8,128)(2,1)}, bf16[256,1024]{0,1:T(8,128)(2,1)}, u32[]{:S(2)}, u32[]{:S(2)}) %collective-permute-start.4) | collective-permute-done | bytes 524320 | tf_op jit(solution)/shard_map/ppermute | solution.py:95
  63.9 1.9 %collective-permute-start.6 = (bf16[256,1024]{0,1:T(8,128)(2,1)}, bf16[256,1024]{0,1:T(8,128)(2,1)S(1)}, u32[]{:S(2)}, u32[]{:S(2)}) collective-permute-start(bf16[256,1024]{0,1:T(8,128)(2,1)} %collective-permute-done.4), channel_id=1, source_target_pairs={{2,3},{3,2},{16,17},{17,16},{6,7},{7,6},{20,21},{21,20},{10,11},{1... | collective-permute-start | bytes 1572872 | tf_op jit(solution)/shard_map/ppermute | solution.py:95
  65.8 0.0 collective-permute-done.8
  65.8 0.0 collective-permute-done.10
  65.8 0.2 select_select_fusion
  66.0 0.2 select_select_fusion.1
  66.2 0.2 select_select_fusion.2
  66.4 0.2 select_select_fusion.3
  66.6 0.3 pad_maximum_fusion
  66.9 0.0 collective-permute-done.5
  66.9 1.0 %collective-permute-done.6 = bf16[256,1024]{0,1:T(8,128)(2,1)S(1)} collective-permute-done((bf16[256,1024]{0,1:T(8,128)(2,1)}, bf16[256,1024]{0,1:T(8,128)(2,1)S(1)}, u32[]{:S(2)}, u32[]{:S(2)}) %collective-permute-start.6) | collective-permute-done | bytes 524320 | tf_op jit(solution)/shard_map/ppermute | solution.py:95
  67.9 1.4 %broadcast_select_fusion.3 = (bf16[256,1024]{0,1:T(8,128)(2,1)S(1)}, bf16[256,1024]{0,1:T(8,128)(2,1)S(1)}) fusion(pred[]{:T(512)S(6)} %eq.105, bf16[256,1024]{0,1:T(8,128)(2,1)} %collective-permute-done.4, pred[]{:T(512)S(6)} %eq.106, bf16[256,1024]{0,1:T(8,128)(2,1)S(1)} %collective-permute-done.5, bf16[256,1024]{0,1:T(8,128)(2,1)S(1)} %collective-permute-done.6, ...), kind=kLoop, calls=%fused_computation.29 | loop fusion | flops 2097152 | bytes 3145730 | tf_op jit(solution)/shard_map/jit(_where)/select_n | solution.py:115
  69.3 0.8 convolution_convert_fusion
  70.1 0.1 collective-permute-start.11
  70.2 0.8 fusion.28
  71.0 13.2 %collective-permute-done.11 = bf16[256,1024]{1,0:T(8,128)(2,1)S(1)} collective-permute-done((bf16[256,1024]{1,0:T(8,128)(2,1)S(1)}, bf16[256,1024]{1,0:T(8,128)(2,1)S(1)}, u32[]{:S(2)}, u32[]{:S(2)}) %collective-permute-start.11) | collective-permute-done | bytes 524320 | tf_op jit(solution)/shard_map/ppermute | solution.py:91
  84.2 0.9 %fusion.16 = bf16[1,256,1024]{2,1,0:T(8,128)(2,1)} fusion(f32[256,1024]{1,0:T(8,128)S(1)} %fusion.28, bf16[256,1024]{1,0:T(8,128)(2,1)S(1)} %collective-permute-done.11), kind=kLoop, calls=%fused_computation.16 | loop fusion | flops 786432 | bytes 2097152 | tf_op jit(solution)/shard_map/broadcast_in_dim | solution.py:179
  (26 shorter events, 0.3 us)
Async XLA Ops:
  0.0 38.6 %copy-start.5 = (s32[1,256]{1,0:T(1,128)S(1)}, s32[1,256]{1,0:T(1,128)}, u32[]{:S(2)}) copy-start(s32[1,256]{1,0:T(1,128)} %param.6) | copy-start | bytes 3076
  0.0 14.5 %copy-start.4 = (bf16[1,256,512]{2,1,0:T(8,128)(2,1)S(1)}, bf16[1,256,512]{2,1,0:T(8,128)(2,1)}, u32[]{:S(2)}) copy-start(bf16[1,256,512]{2,1,0:T(8,128)(2,1)} %param.4) | copy-start | bytes 786436
  4.1 29.6 %collective-permute-start = (bf16[256,1408]{0,1:T(8,128)(2,1)}, bf16[256,1408]{0,1:T(8,128)(2,1)S(1)}, u32[]{:S(2)}, u32[]{:S(2)}) collective-permute-start(bf16[256,1408]{0,1:T(8,128)(2,1)} %pad_maximum_fusion.1), channel_id=1, source_target_pairs={{0,4},{4,8},{8,12},{1,5},{5,9},{9,13},{2,6},{6,10},{10,14},{3,7},{... | collective-permute-start | bytes 2162696 | tf_op jit(solution)/shard_map/ppermute | solution.py:170
  7.6 24.0 %collective-permute-start.1 = (bf16[256,1024]{0,1:T(8,128)(2,1)S(1)}, bf16[256,1024]{0,1:T(8,128)(2,1)S(1)}, u32[]{:S(2)}, u32[]{:S(2)}) collective-permute-start(bf16[256,1024]{0,1:T(8,128)(2,1)S(1)} %copy.11), channel_id=1, source_target_pairs={{4,0},{8,4},{12,8},{5,1},{9,5},{13,9},{6,2},{10,6},{14,10},{7,3},{... | collective-permute-start | bytes 1572872 | tf_op jit(solution)/shard_map/ppermute | solution.py:173
  10.0 21.6 %collective-permute-start.2 = (bf16[256,3,128]{2,0,1:T(8,128)(2,1)S(1)}, bf16[256,3,128]{2,0,1:T(8,128)(2,1)S(1)}, u32[]{:S(2)}, u32[]{:S(2)}) collective-permute-start(bf16[256,3,128]{2,0,1:T(8,128)(2,1)S(1)} %pad_maximum_fusion.5), channel_id=1, source_target_pairs={{0,8},{4,12},{1,9},{5,13},{2,10},{6,14},{3,11},{7,15},{16,24},{20,... | collective-permute-start | bytes 589832 | tf_op jit(solution)/shard_map/ppermute | solution.py:17
  31.6 20.1 %collective-permute-start.7 = (bf16[256,1024]{0,1:T(8,128)(2,1)S(1)}, bf16[256,1024]{0,1:T(8,128)(2,1)S(1)}, u32[]{:S(2)}, u32[]{:S(2)}) collective-permute-start(bf16[256,1024]{0,1:T(8,128)(2,1)S(1)} %collective-permute-done.1), channel_id=1, source_target_pairs={{4,0},{8,4},{5,1},{9,5},{6,2},{10,6},{7,3},{11,7},{20,16},{24,20},... | collective-permute-start | bytes 1572872 | tf_op jit(solution)/shard_map/ppermute | solution.py:136
  34.5 18.4 %collective-permute-start.9 = (bf16[256,1024]{0,1:T(8,128)(2,1)}, bf16[256,1024]{0,1:T(8,128)(2,1)S(1)}, u32[]{:S(2)}, u32[]{:S(2)}) collective-permute-start(bf16[256,1024]{0,1:T(8,128)(2,1)} %slice.55), channel_id=1, source_target_pairs={{4,8},{8,12},{5,9},{9,13},{6,10},{10,14},{7,11},{11,15},{20,24},{2... | collective-permute-start | bytes 1572872 | tf_op jit(solution)/shard_map/ppermute | solution.py:135
  42.8 10.2 %copy-start = (bf16[256,1,4,128]{0,3,2,1:T(8,128)(2,1)}, bf16[256,1,4,128]{0,3,2,1:T(8,128)(2,1)S(1)}, u32[]{:S(2)}) copy-start(bf16[256,1,4,128]{0,3,2,1:T(8,128)(2,1)S(1)} %fusion.13) | copy-start | bytes 786436
  42.8 6.7 %collective-permute-start.3 = (bf16[256,512]{0,1:T(8,128)(2,1)S(1)}, bf16[256,512]{0,1:T(8,128)(2,1)S(1)}, u32[]{:S(2)}, u32[]{:S(2)}) collective-permute-start(bf16[256,512]{0,1:T(8,128)(2,1)S(1)} %bitcast.69), channel_id=1, source_target_pairs={{0,16},{16,0},{1,17},{17,1},{2,18},{18,2},{3,19},{19,3},{4,20},{20... | collective-permute-start | bytes 786440 | tf_op jit(solution)/shard_map/ppermute | solution.py:91
  49.5 3.5 %copy-start.2 = (bf16[256,512]{0,1:T(8,128)(2,1)}, bf16[256,512]{0,1:T(8,128)(2,1)S(1)}, u32[]{:S(2)}) copy-start(bf16[256,512]{0,1:T(8,128)(2,1)S(1)} %collective-permute-done.3) | copy-start | bytes 786436
  50.4 13.5 %collective-permute-start.4 = (bf16[256,1024]{0,1:T(8,128)(2,1)}, bf16[256,1024]{0,1:T(8,128)(2,1)}, u32[]{:S(2)}, u32[]{:S(2)}) collective-permute-start(bf16[256,1024]{0,1:T(8,128)(2,1)} %pad_maximum_fusion.2), channel_id=1, source_target_pairs={{0,2},{1,3},{18,16},{19,17},{4,6},{5,7},{22,20},{23,21},{8,10},{9,... | collective-permute-start | bytes 1572872 | tf_op jit(solution)/shard_map/ppermute | solution.py:95
  51.7 14.1 %collective-permute-start.8 = (bf16[256,1024]{0,1:T(8,128)(2,1)S(1)}, bf16[256,1024]{0,1:T(8,128)(2,1)S(1)}, u32[]{:S(2)}, u32[]{:S(2)}) collective-permute-start(bf16[256,1024]{0,1:T(8,128)(2,1)S(1)} %collective-permute-done.7), channel_id=1, source_target_pairs={{4,0},{5,1},{6,2},{7,3},{20,16},{21,17},{22,18},{23,19}} | collective-permute-start | bytes 1572872 | tf_op jit(solution)/shard_map/ppermute | solution.py:136
  53.0 12.8 %collective-permute-start.10 = (bf16[256,1024]{0,1:T(8,128)(2,1)S(1)}, bf16[256,1024]{0,1:T(8,128)(2,1)}, u32[]{:S(2)}, u32[]{:S(2)}) collective-permute-start(bf16[256,1024]{0,1:T(8,128)(2,1)S(1)} %collective-permute-done.9), channel_id=1, source_target_pairs={{8,12},{9,13},{10,14},{11,15},{24,28},{25,29},{26,30},{27,31}} | collective-permute-start | bytes 1572872 | tf_op jit(solution)/shard_map/ppermute | solution.py:135
  54.5 12.4 %collective-permute-start.5 = (bf16[256,1024]{0,1:T(8,128)(2,1)}, bf16[256,1024]{0,1:T(8,128)(2,1)S(1)}, u32[]{:S(2)}, u32[]{:S(2)}) collective-permute-start(bf16[256,1024]{0,1:T(8,128)(2,1)} %pad_maximum_fusion.2), channel_id=1, source_target_pairs={{0,1},{1,0},{18,19},{19,18},{4,5},{5,4},{22,23},{23,22},{8,9},{9,8... | collective-permute-start | bytes 1572872 | tf_op jit(solution)/shard_map/ppermute | solution.py:95
  63.9 4.0 %collective-permute-start.6 = (bf16[256,1024]{0,1:T(8,128)(2,1)}, bf16[256,1024]{0,1:T(8,128)(2,1)S(1)}, u32[]{:S(2)}, u32[]{:S(2)}) collective-permute-start(bf16[256,1024]{0,1:T(8,128)(2,1)} %collective-permute-done.4), channel_id=1, source_target_pairs={{2,3},{3,2},{16,17},{17,16},{6,7},{7,6},{20,21},{21,20},{10,11},{1... | collective-permute-start | bytes 1572872 | tf_op jit(solution)/shard_map/ppermute | solution.py:95
  66.5 1.3 %copy-start.1 = (bf16[256,1,4,128]{0,3,2,1:T(8,128)(2,1)S(1)}, bf16[256,1,4,128]{0,3,2,1:T(8,128)(2,1)}, u32[]{:S(2)}) copy-start(bf16[256,1,4,128]{0,3,2,1:T(8,128)(2,1)} %copy-done) | copy-start | bytes 786436
  66.6 1.3 %copy-start.3 = (bf16[256,512]{0,1:T(8,128)(2,1)S(1)}, bf16[256,512]{0,1:T(8,128)(2,1)}, u32[]{:S(2)}) copy-start(bf16[256,512]{0,1:T(8,128)(2,1)} %copy-done.2) | copy-start | bytes 786436
  70.1 14.1 %collective-permute-start.11 = (bf16[256,1024]{1,0:T(8,128)(2,1)S(1)}, bf16[256,1024]{1,0:T(8,128)(2,1)S(1)}, u32[]{:S(2)}, u32[]{:S(2)}) collective-permute-start(bf16[256,1024]{1,0:T(8,128)(2,1)S(1)} %convolution_convert_fusion), channel_id=1, source_target_pairs={{0,16},{16,0},{1,17},{17,1},{2,18},{18,2},{3,19},{19,3},{4,20},{20... | collective-permute-start | bytes 1572872 | tf_op jit(solution)/shard_map/ppermute | solution.py:91

commit v14 on v10

--- a/solution.py
+++ b/solution.py
@@ -120,12 +120,17 @@
     return rising, falling
 
 
-def line_rows(block, first, axis):
+def line_rows(block, first, axis, late_block):
     count = lax.axis_size(axis)
     here = lax.axis_index(axis)
     rising, falling = first
     arrivals = [(block, 0), (rising, -1), (falling, 1)]
-    for step in range(2, count):
+    far = count - 1
+    if far > 1:
+        far_rising = lax.ppermute(late_block, axis, [(i, i + far) for i in range(count - far)])
+        far_falling = lax.ppermute(late_block, axis, [(i + far, i) for i in range(count - far)])
+        arrivals += [(far_rising, -far), (far_falling, far)]
+    for step in range(2, far):
         rising = lax.ppermute(rising, axis, [(i, i + 1) for i in range(step - 1, count - 1)])
         falling = lax.ppermute(falling, axis, [(i, i - 1) for i in range(1, count - step + 1)])
         arrivals.append((rising, -step))
@@ -158,8 +163,8 @@
     if lax.axis_size("dp") == 2 and side_width == 2 * width and fits:
         first = first_hop(output_weight, "ctx")
         head_values = attention(queries, keyvals, documents)
-        first, head_values = lax.optimization_barrier((first, head_values))
-        side_rows = line_rows(output_weight, first, "ctx")
+        first, head_values, late_block = lax.optimization_barrier((first, head_values, output_weight))
+        side_rows = line_rows(output_weight, first, "ctx", late_block)
         result = split_projection(head_values, side_rows)
         return result.astype(jnp.bfloat16)[None]
     all_rows = lax.all_gather(output_weight, ("dp", "ctx"), axis=0, tiled=True)

time: 80.7 us -> 81.7 us (1.012)
  the two profiles are of different devices: /device:TPU:12 before, /device:TPU:0 now
where the time goes in v14:
time: 81.7 us; the launch traced here: 80.4 us
  starting transfers between devices  37.6 us (46%)
  waiting for transfers between devices  30.5 us (37%)
  other arithmetic  5.87 us (7%)
  local copies, waits for them, and re-layouts  3.12 us (4%)
  matrix products  3.05 us (4%)
    ppermute x2, waiting for transfers between devices, swapped(): return lax.ppermute(block, axis, [(0, 1), (1, 0)])  16.4 us
    ppermute x2, starting transfers between devices, shifted(): return lax.ppermute(block, axis, route)  9.06 us
    ppermute x1, starting transfers between devices, line_rows(): lax.ppermute(late_block, axis, [(i, i + far) for i in range(count - far)])  8.4 us
    ppermute x1, waiting for transfers between devices, line_rows(): lax.ppermute(falling, axis, [(i, i - 1) for i in range(1, count - step +...  7.35 us
    ppermute x2, waiting for transfers between devices, shifted(): return lax.ppermute(block, axis, route)  6.48 us
    ppermute x3, starting transfers between devices, sent(): return lax.ppermute(block, ('dp', 'tensor'), route)  6.05 us
    ppermute x1, starting transfers between devices, first_hop(): rising = lax.ppermute(block, axis, [(i, i + 1) for i in range(count - 1)])  4.95 us
    ppermute x2, starting transfers between devices, swapped(): return lax.ppermute(block, axis, [(0, 1), (1, 0)])  4.52 us
  transfers between devices with their start and end apart: 13, of which 6 were waited for; matrix products, arithmetic and copies ran while one was open for 13% of the time, Pallas kernels for 0%

profile of v14, /device:TPU:0, one launch (start us, length us, event | category | flops | bytes accessed | tf_op | source)
XLA Modules:
  0.0 80.4 jit_solution(1443057007677035528)
XLA Ops:
  0.0 5.0 %collective-permute-start = (bf16[256,1024]{1,0:T(8,128)(2,1)}, bf16[256,1024]{1,0:T(8,128)(2,1)S(1)}, u32[]{:S(2)}, u32[]{:S(2)}) collective-permute-start(bf16[256,1024]{1,0:T(8,128)(2,1)} %param.7), channel_id=1, source_target_pairs={{0,4},{4,8},{8,12},{1,5},{5,9},{9,13},{2,6},{6,10},{10,14},{3,7},{... | collective-permute-start | bytes 1572872 | tf_op jit(solution)/shard_map/ppermute | solution.py:118
  5.0 1.3 %collective-permute-start.1 = (bf16[256,1024]{1,0:T(8,128)(2,1)}, bf16[256,1024]{1,0:T(8,128)(2,1)S(1)}, u32[]{:S(2)}, u32[]{:S(2)}) collective-permute-start(bf16[256,1024]{1,0:T(8,128)(2,1)} %param.7), channel_id=1, source_target_pairs={{4,0},{8,4},{12,8},{5,1},{9,5},{13,9},{6,2},{10,6},{14,10},{7,3},{... | collective-permute-start | bytes 1572872 | tf_op jit(solution)/shard_map/ppermute | solution.py:119
  6.3 0.7 convert_element_type.37
  6.9 0.9 %copy.21 = bf16[1,256,2,128]{3,1,2,0:T(8,128)(2,1)S(1)} copy(bf16[1,256,2,128]{3,2,1,0:T(2,128)(2,1)} %param.5) | data formatting | bytes 262144 | tf_op args[1]
  7.9 0.1 broadcast_in_dim.27
  8.0 5.5 %collective-permute-start.3 = (bf16[256,3,128]{2,0,1:T(8,128)(2,1)S(1)}, bf16[256,3,128]{2,0,1:T(8,128)(2,1)S(1)}, u32[]{:S(2)}, u32[]{:S(2)}) collective-permute-start(bf16[256,3,128]{2,0,1:T(8,128)(2,1)S(1)} %pad_maximum_fusion.3), channel_id=1, source_target_pairs={{0,8},{4,12},{1,9},{5,13},{2,10},{6,14},{3,11},{7,15},{16,24},{20,... | collective-permute-start | bytes 589832 | tf_op jit(solution)/shard_map/ppermute | solution.py:17
  13.6 3.5 %collective-permute-start.2 = (bf16[256,3,128]{2,0,1:T(8,128)(2,1)S(1)}, bf16[256,3,128]{2,0,1:T(8,128)(2,1)S(1)}, u32[]{:S(2)}, u32[]{:S(2)}) collective-permute-start(bf16[256,3,128]{2,0,1:T(8,128)(2,1)S(1)} %pad_maximum_fusion.3), channel_id=1, source_target_pairs={{0,4},{4,8},{8,12},{1,5},{5,9},{9,13},{2,6},{6,10},{10,14},{3,7},{... | collective-permute-start | bytes 589832 | tf_op jit(solution)/shard_map/ppermute | solution.py:17
  17.1 1.0 %reshape.68 = bf16[256,4,128]{2,1,0:T(4,128)(2,1)S(1)} reshape(bf16[1,256,512]{2,1,0:T(8,128)(2,1)} %param.4) | data formatting | bytes 524288 | tf_op jit(solution)/shard_map/reshape.3
  18.2 3.5 %collective-permute-done.3 = bf16[256,3,128]{2,0,1:T(8,128)(2,1)S(1)} collective-permute-done((bf16[256,3,128]{2,0,1:T(8,128)(2,1)S(1)}, bf16[256,3,128]{2,0,1:T(8,128)(2,1)S(1)}, u32[]{:S(2)}, u32[]{:S(2)}) %collective-permute-start.3) | collective-permute-done | bytes 196640 | tf_op jit(solution)/shard_map/ppermute | solution.py:17
  21.7 0.1 convert_reduce_fusion
  21.8 2.9 %collective-permute-done.2 = bf16[256,3,128]{2,0,1:T(8,128)(2,1)S(1)} collective-permute-done((bf16[256,3,128]{2,0,1:T(8,128)(2,1)S(1)}, bf16[256,3,128]{2,0,1:T(8,128)(2,1)S(1)}, u32[]{:S(2)}, u32[]{:S(2)}) %collective-permute-start.2) | collective-permute-done | bytes 196640 | tf_op jit(solution)/shard_map/ppermute | solution.py:17
  24.8 0.1 convert_reduce_fusion.1
  24.9 0.7 pad_add_fusion
  25.6 1.4 %and_and_fusion = pred[256,768]{0,1:T(8,128)(4,1)S(1)} fusion(s32[256]{0:T(256)S(1)} %iota_add_fusion.2, s32[256]{0:T(256)} %bitcast.71, s32[768]{0:T(1024)S(1)} %pad_add_fusion.1, s32[768]{0:T(1024)S(1)} %pad_add_fusion, pred[768]{0:T(1024)(128)(4,1)S(1)} %broadcast_compare_fusion), kind=kLoop, calls=%fused_computation.14 | loop fusion | flops 786432 | bytes 205568 | tf_op jit(solution)/shard_map/and | solution.py:64
  27.1 0.7 fusion
  27.7 0.8 fusion.1
  28.5 0.9 %fusion.13 = bf16[256,1,4,128]{0,3,2,1:T(8,128)(2,1)S(1)} fusion(f32[768,256,4]{1,0,2:T(8,128)S(1)} %get-tuple-element.24, f32[4,256]{1,0:T(4,128)S(1)} %get-tuple-element.23, pred[256,768]{0,1:T(8,128)(4,1)S(1)} %and_and_fusion, f32[256,4]{0,1:T(4,128)S(1)} %bitcast.68, bf16[768,2,128]{2,0,1:T(8,128)(2,1)S(1)} %pad_maximum_fusion.2), kind=kOutput, calls=%fused_computation.13 | convolution fusion | flops 205520896 | bytes 3809280 | tf_op jit(solution)/shard_map/hgqk,khd->qhgd/dot_general | solution.py:72
  29.5 0.0 collective-permute-done
  29.5 0.0 collective-permute-done.1
  29.5 1.3 %collective-permute-start.8 = (bf16[256,1024]{1,0:T(8,128)(2,1)S(1)}, bf16[256,1024]{1,0:T(8,128)(2,1)S(1)}, u32[]{:S(2)}, u32[]{:S(2)}) collective-permute-start(bf16[256,1024]{1,0:T(8,128)(2,1)S(1)} %collective-permute-done.1), channel_id=1, source_target_pairs={{4,0},{8,4},{5,1},{9,5},{6,2},{10,6},{7,3},{11,7},{20,16},{24,20},... | collective-permute-start | bytes 1572872 | tf_op jit(solution)/shard_map/ppermute | solution.py:135
  30.8 0.7 collective-permute-start.9
  31.5 0.0 copy-done
  31.5 1.3 %collective-permute-start.10 = (bf16[256,1024]{1,0:T(8,128)(2,1)S(1)}, bf16[256,1024]{1,0:T(8,128)(2,1)S(1)}, u32[]{:S(2)}, u32[]{:S(2)}) collective-permute-start(bf16[256,1024]{1,0:T(8,128)(2,1)S(1)} %copy-done), channel_id=1, source_target_pairs={{12,0},{13,1},{14,2},{15,3},{28,16},{29,17},{30,18},{31,19}} | collective-permute-start | bytes 1572872 | tf_op jit(solution)/shard_map/ppermute | solution.py:131
  32.8 8.4 %collective-permute-start.11 = (bf16[256,1024]{1,0:T(8,128)(2,1)S(1)}, bf16[256,1024]{1,0:T(8,128)(2,1)}, u32[]{:S(2)}, u32[]{:S(2)}) collective-permute-start(bf16[256,1024]{1,0:T(8,128)(2,1)S(1)} %copy-done), channel_id=1, source_target_pairs={{0,12},{1,13},{2,14},{3,15},{16,28},{17,29},{18,30},{19,31}} | collective-permute-start | bytes 1572872 | tf_op jit(solution)/shard_map/ppermute | solution.py:130
  41.2 1.5 %collective-permute-start.4 = (bf16[256,512]{0,1:T(8,128)(2,1)S(1)}, bf16[256,512]{0,1:T(8,128)(2,1)}, u32[]{:S(2)}, u32[]{:S(2)}) collective-permute-start(bf16[256,512]{0,1:T(8,128)(2,1)S(1)} %bitcast.66), channel_id=1, source_target_pairs={{0,16},{16,0},{1,17},{17,1},{2,18},{18,2},{3,19},{19,3},{4,20},{20... | collective-permute-start | bytes 786440 | tf_op jit(solution)/shard_map/ppermute | solution.py:85
  42.7 5.0 %collective-permute-done.4 = bf16[256,512]{0,1:T(8,128)(2,1)} collective-permute-done((bf16[256,512]{0,1:T(8,128)(2,1)S(1)}, bf16[256,512]{0,1:T(8,128)(2,1)}, u32[]{:S(2)}, u32[]{:S(2)}) %collective-permute-start.4) | collective-permute-done | bytes 262176 | tf_op jit(solution)/shard_map/ppermute | solution.py:85
  47.7 1.0 %constant_dynamic-update-slice_fusion = bf16[256,1024]{0,1:T(8,128)(2,1)S(1)} fusion(bf16[256,1024]{0,1:T(8,128)(2,1)S(1)} %constant_dynamic-update-slice_fusion.1, bf16[256,512]{0,1:T(8,128)(2,1)} %collective-permute-done.4), kind=kLoop, calls=%fused_computation.37 | loop fusion | bytes 524288 | tf_op jit(solution)/shard_map/concatenate | solution.py:97
  48.7 3.5 %collective-permute-start.5 = (bf16[256,1024]{0,1:T(8,128)(2,1)S(1)}, bf16[256,1024]{0,1:T(8,128)(2,1)S(1)}, u32[]{:S(2)}, u32[]{:S(2)}) collective-permute-start(bf16[256,1024]{0,1:T(8,128)(2,1)S(1)} %constant_dynamic-update-slice_fusion), channel_id=1, source_target_pairs={{0,2},{1,3},{18,16},{19,17},{4,6},{5,7},{22,20},{23,21},{8,10},{9,... | collective-permute-start | bytes 1572872 | tf_op jit(solution)/shard_map/ppermute | solution.py:89
  52.1 7.3 %collective-permute-done.8 = bf16[256,1024]{1,0:T(8,128)(2,1)S(1)} collective-permute-done((bf16[256,1024]{1,0:T(8,128)(2,1)S(1)}, bf16[256,1024]{1,0:T(8,128)(2,1)S(1)}, u32[]{:S(2)}, u32[]{:S(2)}) %collective-permute-start.8) | collective-permute-done | bytes 524320 | tf_op jit(solution)/shard_map/ppermute | solution.py:135
  59.5 1.9 %collective-permute-start.6 = (bf16[256,1024]{0,1:T(8,128)(2,1)S(1)}, bf16[256,1024]{0,1:T(8,128)(2,1)S(1)}, u32[]{:S(2)}, u32[]{:S(2)}) collective-permute-start(bf16[256,1024]{0,1:T(8,128)(2,1)S(1)} %constant_dynamic-update-slice_fusion), channel_id=1, source_target_pairs={{0,1},{1,0},{18,19},{19,18},{4,5},{5,4},{22,23},{23,22},{8,9},{9,8... | collective-permute-start | bytes 1572872 | tf_op jit(solution)/shard_map/ppermute | solution.py:89
  61.4 0.0 collective-permute-done.9
  61.4 0.0 collective-permute-done.10
  61.4 0.0 collective-permute-done.11
  61.4 0.2 select_select_fusion
  61.6 0.2 select_select_fusion.1
  61.8 0.2 select_select_fusion.2
  62.0 0.0 collective-permute-done.5
  62.0 0.7 collective-permute-start.7
  62.7 0.2 select_select_fusion.3
  62.9 0.2 pad_maximum_fusion
  63.1 0.2 collective-permute-done.6
  63.3 0.0 collective-permute-done.7
  63.3 0.1 broadcast_select_fusion.3
  63.5 0.7 convolution_convert_fusion
  64.2 3.0 %collective-permute-start.12 = (bf16[256,1024]{1,0:T(8,128)(2,1)S(1)}, bf16[256,1024]{1,0:T(8,128)(2,1)S(1)}, u32[]{:S(2)}, u32[]{:S(2)}) collective-permute-start(bf16[256,1024]{1,0:T(8,128)(2,1)S(1)} %convolution_convert_fusion), channel_id=1, source_target_pairs={{0,16},{16,0},{1,17},{17,1},{2,18},{18,2},{3,19},{19,3},{4,20},{20... | collective-permute-start | bytes 1572872 | tf_op jit(solution)/shard_map/ppermute | solution.py:85
  67.3 0.7 fusion.28
  68.0 11.5 %collective-permute-done.12 = bf16[256,1024]{1,0:T(8,128)(2,1)S(1)} collective-permute-done((bf16[256,1024]{1,0:T(8,128)(2,1)S(1)}, bf16[256,1024]{1,0:T(8,128)(2,1)S(1)}, u32[]{:S(2)}, u32[]{:S(2)}) %collective-permute-start.12) | collective-permute-done | bytes 524320 | tf_op jit(solution)/shard_map/ppermute | solution.py:85
  79.5 0.9 %fusion.16 = bf16[1,256,1024]{2,1,0:T(8,128)(2,1)} fusion(f32[256,1024]{1,0:T(8,128)S(1)} %fusion.28, bf16[256,1024]{1,0:T(8,128)(2,1)S(1)} %collective-permute-done.12), kind=kLoop, calls=%fused_computation.15 | loop fusion | flops 786432 | bytes 2097152 | tf_op jit(solution)/shard_map/broadcast_in_dim | solution.py:169
  (13 shorter events, 0.2 us)
Async XLA Ops:
  0.0 29.5 %collective-permute-start = (bf16[256,1024]{1,0:T(8,128)(2,1)}, bf16[256,1024]{1,0:T(8,128)(2,1)S(1)}, u32[]{:S(2)}, u32[]{:S(2)}) collective-permute-start(bf16[256,1024]{1,0:T(8,128)(2,1)} %param.7), channel_id=1, source_target_pairs={{0,4},{4,8},{8,12},{1,5},{5,9},{9,13},{2,6},{6,10},{10,14},{3,7},{... | collective-permute-start | bytes 1572872 | tf_op jit(solution)/shard_map/ppermute | solution.py:118
  5.0 24.5 %collective-permute-start.1 = (bf16[256,1024]{1,0:T(8,128)(2,1)}, bf16[256,1024]{1,0:T(8,128)(2,1)S(1)}, u32[]{:S(2)}, u32[]{:S(2)}) collective-permute-start(bf16[256,1024]{1,0:T(8,128)(2,1)} %param.7), channel_id=1, source_target_pairs={{4,0},{8,4},{12,8},{5,1},{9,5},{13,9},{6,2},{10,6},{14,10},{7,3},{... | collective-permute-start | bytes 1572872 | tf_op jit(solution)/shard_map/ppermute | solution.py:119
  8.0 13.7 %collective-permute-start.3 = (bf16[256,3,128]{2,0,1:T(8,128)(2,1)S(1)}, bf16[256,3,128]{2,0,1:T(8,128)(2,1)S(1)}, u32[]{:S(2)}, u32[]{:S(2)}) collective-permute-start(bf16[256,3,128]{2,0,1:T(8,128)(2,1)S(1)} %pad_maximum_fusion.3), channel_id=1, source_target_pairs={{0,8},{4,12},{1,9},{5,13},{2,10},{6,14},{3,11},{7,15},{16,24},{20,... | collective-permute-start | bytes 589832 | tf_op jit(solution)/shard_map/ppermute | solution.py:17
  13.6 11.2 %collective-permute-start.2 = (bf16[256,3,128]{2,0,1:T(8,128)(2,1)S(1)}, bf16[256,3,128]{2,0,1:T(8,128)(2,1)S(1)}, u32[]{:S(2)}, u32[]{:S(2)}) collective-permute-start(bf16[256,3,128]{2,0,1:T(8,128)(2,1)S(1)} %pad_maximum_fusion.3), channel_id=1, source_target_pairs={{0,4},{4,8},{8,12},{1,5},{5,9},{9,13},{2,6},{6,10},{10,14},{3,7},{... | collective-permute-start | bytes 589832 | tf_op jit(solution)/shard_map/ppermute | solution.py:17
  28.5 3.0 %copy-start = (bf16[256,1024]{1,0:T(8,128)(2,1)S(1)}, bf16[256,1024]{1,0:T(8,128)(2,1)}, u32[]{:S(2)}) copy-start(bf16[256,1024]{1,0:T(8,128)(2,1)} %param.7) | copy-start | bytes 1572868
  29.5 30.0 %collective-permute-start.8 = (bf16[256,1024]{1,0:T(8,128)(2,1)S(1)}, bf16[256,1024]{1,0:T(8,128)(2,1)S(1)}, u32[]{:S(2)}, u32[]{:S(2)}) collective-permute-start(bf16[256,1024]{1,0:T(8,128)(2,1)S(1)} %collective-permute-done.1), channel_id=1, source_target_pairs={{4,0},{8,4},{5,1},{9,5},{6,2},{10,6},{7,3},{11,7},{20,16},{24,20},... | collective-permute-start | bytes 1572872 | tf_op jit(solution)/shard_map/ppermute | solution.py:135
  30.8 30.6 %collective-permute-start.9 = (bf16[256,1024]{1,0:T(8,128)(2,1)S(1)}, bf16[256,1024]{1,0:T(8,128)(2,1)S(1)}, u32[]{:S(2)}, u32[]{:S(2)}) collective-permute-start(bf16[256,1024]{1,0:T(8,128)(2,1)S(1)} %collective-permute-done), channel_id=1, source_target_pairs={{4,8},{8,12},{5,9},{9,13},{6,10},{10,14},{7,11},{11,15},{20,24},{2... | collective-permute-start | bytes 1572872 | tf_op jit(solution)/shard_map/ppermute | solution.py:134
  31.5 29.9 %collective-permute-start.10 = (bf16[256,1024]{1,0:T(8,128)(2,1)S(1)}, bf16[256,1024]{1,0:T(8,128)(2,1)S(1)}, u32[]{:S(2)}, u32[]{:S(2)}) collective-permute-start(bf16[256,1024]{1,0:T(8,128)(2,1)S(1)} %copy-done), channel_id=1, source_target_pairs={{12,0},{13,1},{14,2},{15,3},{28,16},{29,17},{30,18},{31,19}} | collective-permute-start | bytes 1572872 | tf_op jit(solution)/shard_map/ppermute | solution.py:131
  32.8 28.6 %collective-permute-start.11 = (bf16[256,1024]{1,0:T(8,128)(2,1)S(1)}, bf16[256,1024]{1,0:T(8,128)(2,1)}, u32[]{:S(2)}, u32[]{:S(2)}) collective-permute-start(bf16[256,1024]{1,0:T(8,128)(2,1)S(1)} %copy-done), channel_id=1, source_target_pairs={{0,12},{1,13},{2,14},{3,15},{16,28},{17,29},{18,30},{19,31}} | collective-permute-start | bytes 1572872 | tf_op jit(solution)/shard_map/ppermute | solution.py:130
  41.2 6.5 %collective-permute-start.4 = (bf16[256,512]{0,1:T(8,128)(2,1)S(1)}, bf16[256,512]{0,1:T(8,128)(2,1)}, u32[]{:S(2)}, u32[]{:S(2)}) collective-permute-start(bf16[256,512]{0,1:T(8,128)(2,1)S(1)} %bitcast.66), channel_id=1, source_target_pairs={{0,16},{16,0},{1,17},{17,1},{2,18},{18,2},{3,19},{19,3},{4,20},{20... | collective-permute-start | bytes 786440 | tf_op jit(solution)/shard_map/ppermute | solution.py:85
  48.7 13.3 %collective-permute-start.5 = (bf16[256,1024]{0,1:T(8,128)(2,1)S(1)}, bf16[256,1024]{0,1:T(8,128)(2,1)S(1)}, u32[]{:S(2)}, u32[]{:S(2)}) collective-permute-start(bf16[256,1024]{0,1:T(8,128)(2,1)S(1)} %constant_dynamic-update-slice_fusion), channel_id=1, source_target_pairs={{0,2},{1,3},{18,16},{19,17},{4,6},{5,7},{22,20},{23,21},{8,10},{9,... | collective-permute-start | bytes 1572872 | tf_op jit(solution)/shard_map/ppermute | solution.py:89
  59.5 3.8 %collective-permute-start.6 = (bf16[256,1024]{0,1:T(8,128)(2,1)S(1)}, bf16[256,1024]{0,1:T(8,128)(2,1)S(1)}, u32[]{:S(2)}, u32[]{:S(2)}) collective-permute-start(bf16[256,1024]{0,1:T(8,128)(2,1)S(1)} %constant_dynamic-update-slice_fusion), channel_id=1, source_target_pairs={{0,1},{1,0},{18,19},{19,18},{4,5},{5,4},{22,23},{23,22},{8,9},{9,8... | collective-permute-start | bytes 1572872 | tf_op jit(solution)/shard_map/ppermute | solution.py:89
  62.0 1.3 %collective-permute-start.7 = (bf16[256,1024]{0,1:T(8,128)(2,1)S(1)}, bf16[256,1024]{0,1:T(8,128)(2,1)S(1)}, u32[]{:S(2)}, u32[]{:S(2)}) collective-permute-start(bf16[256,1024]{0,1:T(8,128)(2,1)S(1)} %collective-permute-done.5), channel_id=1, source_target_pairs={{2,3},{3,2},{16,17},{17,16},{6,7},{7,6},{20,21},{21,20},{10,11},{1... | collective-permute-start | bytes 1572872 | tf_op jit(solution)/shard_map/ppermute | solution.py:89
  64.2 15.3 %collective-permute-start.12 = (bf16[256,1024]{1,0:T(8,128)(2,1)S(1)}, bf16[256,1024]{1,0:T(8,128)(2,1)S(1)}, u32[]{:S(2)}, u32[]{:S(2)}) collective-permute-start(bf16[256,1024]{1,0:T(8,128)(2,1)S(1)} %convolution_convert_fusion), channel_id=1, source_target_pairs={{0,16},{16,0},{1,17},{17,1},{2,18},{18,2},{3,19},{19,3},{4,20},{20... | collective-permute-start | bytes 1572872 | tf_op jit(solution)/shard_map/ppermute | solution.py:85

commit v15 on v14

--- a/solution.py
+++ b/solution.py
@@ -93,21 +93,20 @@
     group = lax.axis_size("tensor")
     me = lax.axis_index("tensor")
     side = lax.axis_index("dp")
+    width = head_values.shape[1]
+    owners = [(s, 2 * s + k) for s in range(2) for k in range(2)]
+    over_y = [(s * group + p, s * group + (p ^ 2)) for s, p in owners]
     foreign = swapped(head_values, "dp")
-    mine = jnp.concatenate([head_values, foreign], axis=1)
-    owners = [(s, 2 * s + k) for s in range(2) for k in range(2)]
-    over_y = sent(mine, [(s * group + p, s * group + (p ^ 2)) for s, p in owners])
-    beside = sent(mine, [(s * group + p, s * group + (p ^ 1)) for s, p in owners])
-    relayed = sent(
-        over_y, [(s * group + (p ^ 2), s * group + (p ^ 3)) for s, p in owners]
-    )
+    own_over = sent(head_values, over_y)
+    foreign_over = sent(foreign, over_y)
     on_owner = me // 2 == side
-    same_core = jnp.where(on_owner, mine, over_y)
-    other_core = jnp.where(on_owner, beside, relayed)
+    own_same = jnp.where(on_owner, head_values, own_over)
+    foreign_same = jnp.where(on_owner, foreign, foreign_over)
+    both_same = jnp.concatenate([own_same, foreign_same], axis=1)
+    both_other = lax.ppermute(both_same, "tensor", [(t, t ^ 1) for t in range(group)])
     first_core = me % 2 == 0
-    width = head_values.shape[1]
-    lower = jnp.where(first_core, same_core, other_core)
-    upper = jnp.where(first_core, other_core, same_core)
+    lower = jnp.where(first_core, both_same, both_other)
+    upper = jnp.where(first_core, both_other, both_same)
     own_full = jnp.concatenate([lower[:, :width], upper[:, :width]], axis=1)
     foreign_full = jnp.concatenate([lower[:, width:], upper[:, width:]], axis=1)
     return own_full, foreign_full

time: 81.7 us -> 84.5 us (1.034)
  waiting for transfers between devices: 30.5 us -> 38 us
  starting transfers between devices: 37.6 us -> 34 us
  local copies, waits for them, and re-layouts: 3.12 us -> 2.13 us
    ppermute x1, waiting for transfers between devices: 7.35 us -> 16.2 us  [line_rows(): lax.ppermute(falling, axis, [(i, i - 1) for i in range(1, count - step +...]
    ppermute x2, starting transfers between devices: 4.52 us -> 1.62 us  [swapped(): return lax.ppermute(block, axis, [(0, 1), (1, 0)])]
    ppermute x1, starting transfers between devices: 8.4 us -> 6.84 us  [line_rows(): lax.ppermute(late_block, axis, [(i, i + far) for i in range(count - far)])]
    ppermute x2, waiting for transfers between devices: 16.4 us -> 15.3 us  [swapped(): return lax.ppermute(block, axis, [(0, 1), (1, 0)])]
    concatenate x1 -> x0, local copies, waits for them, and re-layouts: 0.97 us -> none  [needed_heads(): mine = jnp.concatenate([head_values, foreign], axis=1)]
    ppermute x3 -> x2, starting transfers between devices: 6.05 us -> 6.85 us  [sent(): return lax.ppermute(block, ('dp', 'tensor'), route)]
  transfers between devices with their start and end apart: 13 -> 13, of which waited for: 6 -> 5; matrix products, arithmetic and copies ran while one was open for 13% -> 11% of each run, Pallas kernels for 0% -> 0%
where the time goes in v15:
time: 84.5 us; the launch traced here: 83.6 us
  waiting for transfers between devices  38 us (45%)
  starting transfers between devices  34 us (40%)
  other arithmetic  6 us (7%)
  matrix products  3.04 us (4%)
  local copies, waits for them, and re-layouts  2.13 us (3%)
    ppermute x1, waiting for transfers between devices, line_rows(): lax.ppermute(falling, axis, [(i, i - 1) for i in range(1, count - step +...  16.2 us
    ppermute x2, waiting for transfers between devices, swapped(): return lax.ppermute(block, axis, [(0, 1), (1, 0)])  15.3 us
    ppermute x2, starting transfers between devices, shifted(): return lax.ppermute(block, axis, route)  9.06 us
    ppermute x2, starting transfers between devices, sent(): return lax.ppermute(block, ('dp', 'tensor'), route)  6.85 us
    ppermute x1, starting transfers between devices, line_rows(): lax.ppermute(late_block, axis, [(i, i + far) for i in range(count - far)])  6.84 us
    ppermute x2, waiting for transfers between devices, shifted(): return lax.ppermute(block, axis, route)  6.48 us
    ppermute x1, starting transfers between devices, first_hop(): rising = lax.ppermute(block, axis, [(i, i + 1) for i in range(count - 1)])  4.95 us
  transfers between devices with their start and end apart: 13, of which 5 were waited for; matrix products, arithmetic and copies ran while one was open for 11% of the time, Pallas kernels for 0%

profile of v15, /device:TPU:0, one launch (start us, length us, event | category | flops | bytes accessed | tf_op | source)
XLA Modules:
  0.0 83.6 jit_solution(14387561037834508508)
XLA Ops:
  0.0 5.0 %collective-permute-start = (bf16[256,1024]{1,0:T(8,128)(2,1)}, bf16[256,1024]{1,0:T(8,128)(2,1)S(1)}, u32[]{:S(2)}, u32[]{:S(2)}) collective-permute-start(bf16[256,1024]{1,0:T(8,128)(2,1)} %param.7), channel_id=1, source_target_pairs={{0,4},{4,8},{8,12},{1,5},{5,9},{9,13},{2,6},{6,10},{10,14},{3,7},{... | collective-permute-start | bytes 1572872 | tf_op jit(solution)/shard_map/ppermute | solution.py:117
  5.0 1.3 %collective-permute-start.1 = (bf16[256,1024]{1,0:T(8,128)(2,1)}, bf16[256,1024]{1,0:T(8,128)(2,1)S(1)}, u32[]{:S(2)}, u32[]{:S(2)}) collective-permute-start(bf16[256,1024]{1,0:T(8,128)(2,1)} %param.7), channel_id=1, source_target_pairs={{4,0},{8,4},{12,8},{5,1},{9,5},{13,9},{6,2},{10,6},{14,10},{7,3},{... | collective-permute-start | bytes 1572872 | tf_op jit(solution)/shard_map/ppermute | solution.py:118
  6.3 0.7 convert_element_type.37
  6.9 0.9 %copy.21 = bf16[1,256,2,128]{3,1,2,0:T(8,128)(2,1)S(1)} copy(bf16[1,256,2,128]{3,2,1,0:T(2,128)(2,1)} %param.5) | data formatting | bytes 262144 | tf_op args[1]
  7.9 0.1 broadcast_in_dim.27
  8.0 5.5 %collective-permute-start.3 = (bf16[256,3,128]{2,0,1:T(8,128)(2,1)S(1)}, bf16[256,3,128]{2,0,1:T(8,128)(2,1)S(1)}, u32[]{:S(2)}, u32[]{:S(2)}) collective-permute-start(bf16[256,3,128]{2,0,1:T(8,128)(2,1)S(1)} %pad_maximum_fusion.4), channel_id=1, source_target_pairs={{0,8},{4,12},{1,9},{5,13},{2,10},{6,14},{3,11},{7,15},{16,24},{20,... | collective-permute-start | bytes 589832 | tf_op jit(solution)/shard_map/ppermute | solution.py:17
  13.6 3.5 %collective-permute-start.2 = (bf16[256,3,128]{2,0,1:T(8,128)(2,1)S(1)}, bf16[256,3,128]{2,0,1:T(8,128)(2,1)S(1)}, u32[]{:S(2)}, u32[]{:S(2)}) collective-permute-start(bf16[256,3,128]{2,0,1:T(8,128)(2,1)S(1)} %pad_maximum_fusion.4), channel_id=1, source_target_pairs={{0,4},{4,8},{8,12},{1,5},{5,9},{9,13},{2,6},{6,10},{10,14},{3,7},{... | collective-permute-start | bytes 589832 | tf_op jit(solution)/shard_map/ppermute | solution.py:17
  17.1 1.0 %reshape.68 = bf16[256,4,128]{2,1,0:T(4,128)(2,1)S(1)} reshape(bf16[1,256,512]{2,1,0:T(8,128)(2,1)} %param.4) | data formatting | bytes 524288 | tf_op jit(solution)/shard_map/reshape.3
  18.2 3.5 %collective-permute-done.3 = bf16[256,3,128]{2,0,1:T(8,128)(2,1)S(1)} collective-permute-done((bf16[256,3,128]{2,0,1:T(8,128)(2,1)S(1)}, bf16[256,3,128]{2,0,1:T(8,128)(2,1)S(1)}, u32[]{:S(2)}, u32[]{:S(2)}) %collective-permute-start.3) | collective-permute-done | bytes 196640 | tf_op jit(solution)/shard_map/ppermute | solution.py:17
  21.7 0.1 convert_reduce_fusion
  21.8 2.9 %collective-permute-done.2 = bf16[256,3,128]{2,0,1:T(8,128)(2,1)S(1)} collective-permute-done((bf16[256,3,128]{2,0,1:T(8,128)(2,1)S(1)}, bf16[256,3,128]{2,0,1:T(8,128)(2,1)S(1)}, u32[]{:S(2)}, u32[]{:S(2)}) %collective-permute-start.2) | collective-permute-done | bytes 196640 | tf_op jit(solution)/shard_map/ppermute | solution.py:17
  24.8 0.1 convert_reduce_fusion.1
  24.9 0.7 pad_add_fusion
  25.6 1.4 %and_and_fusion = pred[256,768]{0,1:T(8,128)(4,1)S(1)} fusion(s32[256]{0:T(256)S(1)} %iota_add_fusion.2, s32[256]{0:T(256)} %bitcast.72, s32[768]{0:T(1024)S(1)} %pad_add_fusion.1, s32[768]{0:T(1024)S(1)} %pad_add_fusion, pred[768]{0:T(1024)(128)(4,1)S(1)} %broadcast_compare_fusion), kind=kLoop, calls=%fused_computation.14 | loop fusion | flops 786432 | bytes 205568 | tf_op jit(solution)/shard_map/and | solution.py:64
  27.1 0.7 fusion
  27.7 0.8 fusion.1
  28.5 0.0 copy-start
  28.5 0.9 %fusion.13 = bf16[256,1,4,128]{0,3,2,1:T(8,128)(2,1)S(1)} fusion(f32[768,256,4]{1,0,2:T(8,128)S(1)} %get-tuple-element.24, f32[4,256]{1,0:T(4,128)S(1)} %get-tuple-element.23, pred[256,768]{0,1:T(8,128)(4,1)S(1)} %and_and_fusion, f32[256,4]{0,1:T(4,128)S(1)} %bitcast.69, bf16[768,2,128]{2,0,1:T(8,128)(2,1)S(1)} %pad_maximum_fusion.3), kind=kOutput, calls=%fused_computation.13 | convolution fusion | flops 205520896 | bytes 3809280 | tf_op jit(solution)/shard_map/hgqk,khd->qhgd/dot_general | solution.py:72
  29.5 0.0 collective-permute-done
  29.5 0.0 collective-permute-done.1
  29.5 1.6 %collective-permute-start.5 = (bf16[256,512]{0,1:T(8,128)(2,1)S(1)}, bf16[256,512]{0,1:T(8,128)(2,1)S(1)}, u32[]{:S(2)}, u32[]{:S(2)}) collective-permute-start(bf16[256,512]{0,1:T(8,128)(2,1)S(1)} %bitcast.66), channel_id=1, source_target_pairs={{0,16},{16,0},{1,17},{17,1},{2,18},{18,2},{3,19},{19,3},{4,20},{20... | collective-permute-start | bytes 786440 | tf_op jit(solution)/shard_map/ppermute | solution.py:85
  31.1 3.4 %collective-permute-start.4 = (bf16[256,512]{0,1:T(8,128)(2,1)S(1)}, bf16[256,512]{0,1:T(8,128)(2,1)S(1)}, u32[]{:S(2)}, u32[]{:S(2)}) collective-permute-start(bf16[256,512]{0,1:T(8,128)(2,1)S(1)} %bitcast.67), channel_id=1, source_target_pairs={{0,2},{1,3},{18,16},{19,17},{4,6},{5,7},{22,20},{23,21},{8,10},{9,... | collective-permute-start | bytes 786440 | tf_op jit(solution)/shard_map/ppermute | solution.py:89
  34.5 2.2 %collective-permute-done.5 = bf16[256,512]{0,1:T(8,128)(2,1)S(1)} collective-permute-done((bf16[256,512]{0,1:T(8,128)(2,1)S(1)}, bf16[256,512]{0,1:T(8,128)(2,1)S(1)}, u32[]{:S(2)}, u32[]{:S(2)}) %collective-permute-start.5) | collective-permute-done | bytes 262176 | tf_op jit(solution)/shard_map/ppermute | solution.py:85
  36.7 3.4 %collective-permute-start.6 = (bf16[256,512]{0,1:T(8,128)(2,1)S(1)}, bf16[256,512]{0,1:T(8,128)(2,1)S(1)}, u32[]{:S(2)}, u32[]{:S(2)}) collective-permute-start(bf16[256,512]{0,1:T(8,128)(2,1)S(1)} %collective-permute-done.5), channel_id=1, source_target_pairs={{0,2},{1,3},{18,16},{19,17},{4,6},{5,7},{22,20},{23,21},{8,10},{9,... | collective-permute-start | bytes 786440 | tf_op jit(solution)/shard_map/ppermute | solution.py:89
  40.3 0.0 copy-done
  40.3 1.3 %collective-permute-start.10 = (bf16[256,1024]{1,0:T(8,128)(2,1)S(1)}, bf16[256,1024]{1,0:T(8,128)(2,1)S(1)}, u32[]{:S(2)}, u32[]{:S(2)}) collective-permute-start(bf16[256,1024]{1,0:T(8,128)(2,1)S(1)} %copy-done), channel_id=1, source_target_pairs={{12,0},{13,1},{14,2},{15,3},{28,16},{29,17},{30,18},{31,19}} | collective-permute-start | bytes 1572872 | tf_op jit(solution)/shard_map/ppermute | solution.py:130
  41.6 6.8 %collective-permute-start.11 = (bf16[256,1024]{1,0:T(8,128)(2,1)S(1)}, bf16[256,1024]{1,0:T(8,128)(2,1)S(1)}, u32[]{:S(2)}, u32[]{:S(2)}) collective-permute-start(bf16[256,1024]{1,0:T(8,128)(2,1)S(1)} %copy-done), channel_id=1, source_target_pairs={{0,12},{1,13},{2,14},{3,15},{16,28},{17,29},{18,30},{19,31}} | collective-permute-start | bytes 1572872 | tf_op jit(solution)/shard_map/ppermute | solution.py:129
  48.4 1.3 %collective-permute-start.8 = (bf16[256,1024]{1,0:T(8,128)(2,1)S(1)}, bf16[256,1024]{1,0:T(8,128)(2,1)S(1)}, u32[]{:S(2)}, u32[]{:S(2)}) collective-permute-start(bf16[256,1024]{1,0:T(8,128)(2,1)S(1)} %collective-permute-done.1), channel_id=1, source_target_pairs={{4,0},{8,4},{5,1},{9,5},{6,2},{10,6},{7,3},{11,7},{20,16},{24,20},... | collective-permute-start | bytes 1572872 | tf_op jit(solution)/shard_map/ppermute | solution.py:134
  49.7 0.0 collective-permute-done.4
  49.7 0.7 collective-permute-start.9
  50.5 0.0 collective-permute-done.6
  50.6 0.1 collective-permute-start.7
  50.6 16.2 %collective-permute-done.8 = bf16[256,1024]{1,0:T(8,128)(2,1)S(1)} collective-permute-done((bf16[256,1024]{1,0:T(8,128)(2,1)S(1)}, bf16[256,1024]{1,0:T(8,128)(2,1)S(1)}, u32[]{:S(2)}, u32[]{:S(2)}) %collective-permute-start.8) | collective-permute-done | bytes 524320 | tf_op jit(solution)/shard_map/ppermute | solution.py:134
  66.8 0.0 collective-permute-done.9
  66.8 0.0 collective-permute-done.10
  66.8 0.0 collective-permute-done.11
  66.8 0.2 select_select_fusion
  67.0 0.2 select_select_fusion.1
  67.2 0.2 select_select_fusion.2
  67.4 0.2 select_select_fusion.3
  67.5 0.2 pad_maximum_fusion
  67.7 0.0 collective-permute-done.7
  67.7 0.2 broadcast_select_fusion.1
  68.0 0.7 convolution_convert_fusion
  68.7 0.1 collective-permute-start.12
  68.9 0.7 fusion.28
  69.6 13.0 %collective-permute-done.12 = bf16[256,1024]{1,0:T(8,128)(2,1)S(1)} collective-permute-done((bf16[256,1024]{1,0:T(8,128)(2,1)S(1)}, bf16[256,1024]{1,0:T(8,128)(2,1)S(1)}, u32[]{:S(2)}, u32[]{:S(2)}) %collective-permute-start.12) | collective-permute-done | bytes 524320 | tf_op jit(solution)/shard_map/ppermute | solution.py:85
  82.6 0.9 %fusion.16 = bf16[1,256,1024]{2,1,0:T(8,128)(2,1)} fusion(f32[256,1024]{1,0:T(8,128)S(1)} %fusion.28, bf16[256,1024]{1,0:T(8,128)(2,1)S(1)} %collective-permute-done.12), kind=kLoop, calls=%fused_computation.15 | loop fusion | flops 786432 | bytes 2097152 | tf_op jit(solution)/shard_map/broadcast_in_dim | solution.py:168
  (14 shorter events, 0.3 us)
Async XLA Ops:
  0.0 29.5 %collective-permute-start = (bf16[256,1024]{1,0:T(8,128)(2,1)}, bf16[256,1024]{1,0:T(8,128)(2,1)S(1)}, u32[]{:S(2)}, u32[]{:S(2)}) collective-permute-start(bf16[256,1024]{1,0:T(8,128)(2,1)} %param.7), channel_id=1, source_target_pairs={{0,4},{4,8},{8,12},{1,5},{5,9},{9,13},{2,6},{6,10},{10,14},{3,7},{... | collective-permute-start | bytes 1572872 | tf_op jit(solution)/shard_map/ppermute | solution.py:117
  5.0 24.5 %collective-permute-start.1 = (bf16[256,1024]{1,0:T(8,128)(2,1)}, bf16[256,1024]{1,0:T(8,128)(2,1)S(1)}, u32[]{:S(2)}, u32[]{:S(2)}) collective-permute-start(bf16[256,1024]{1,0:T(8,128)(2,1)} %param.7), channel_id=1, source_target_pairs={{4,0},{8,4},{12,8},{5,1},{9,5},{13,9},{6,2},{10,6},{14,10},{7,3},{... | collective-permute-start | bytes 1572872 | tf_op jit(solution)/shard_map/ppermute | solution.py:118
  8.0 13.7 %collective-permute-start.3 = (bf16[256,3,128]{2,0,1:T(8,128)(2,1)S(1)}, bf16[256,3,128]{2,0,1:T(8,128)(2,1)S(1)}, u32[]{:S(2)}, u32[]{:S(2)}) collective-permute-start(bf16[256,3,128]{2,0,1:T(8,128)(2,1)S(1)} %pad_maximum_fusion.4), channel_id=1, source_target_pairs={{0,8},{4,12},{1,9},{5,13},{2,10},{6,14},{3,11},{7,15},{16,24},{20,... | collective-permute-start | bytes 589832 | tf_op jit(solution)/shard_map/ppermute | solution.py:17
  13.6 11.2 %collective-permute-start.2 = (bf16[256,3,128]{2,0,1:T(8,128)(2,1)S(1)}, bf16[256,3,128]{2,0,1:T(8,128)(2,1)S(1)}, u32[]{:S(2)}, u32[]{:S(2)}) collective-permute-start(bf16[256,3,128]{2,0,1:T(8,128)(2,1)S(1)} %pad_maximum_fusion.4), channel_id=1, source_target_pairs={{0,4},{4,8},{8,12},{1,5},{5,9},{9,13},{2,6},{6,10},{10,14},{3,7},{... | collective-permute-start | bytes 589832 | tf_op jit(solution)/shard_map/ppermute | solution.py:17
  28.5 11.7 %copy-start = (bf16[256,1024]{1,0:T(8,128)(2,1)S(1)}, bf16[256,1024]{1,0:T(8,128)(2,1)}, u32[]{:S(2)}) copy-start(bf16[256,1024]{1,0:T(8,128)(2,1)} %param.7) | copy-start | bytes 1572868
  29.5 7.2 %collective-permute-start.5 = (bf16[256,512]{0,1:T(8,128)(2,1)S(1)}, bf16[256,512]{0,1:T(8,128)(2,1)S(1)}, u32[]{:S(2)}, u32[]{:S(2)}) collective-permute-start(bf16[256,512]{0,1:T(8,128)(2,1)S(1)} %bitcast.66), channel_id=1, source_target_pairs={{0,16},{16,0},{1,17},{17,1},{2,18},{18,2},{3,19},{19,3},{4,20},{20... | collective-permute-start | bytes 786440 | tf_op jit(solution)/shard_map/ppermute | solution.py:85
  31.1 18.7 %collective-permute-start.4 = (bf16[256,512]{0,1:T(8,128)(2,1)S(1)}, bf16[256,512]{0,1:T(8,128)(2,1)S(1)}, u32[]{:S(2)}, u32[]{:S(2)}) collective-permute-start(bf16[256,512]{0,1:T(8,128)(2,1)S(1)} %bitcast.67), channel_id=1, source_target_pairs={{0,2},{1,3},{18,16},{19,17},{4,6},{5,7},{22,20},{23,21},{8,10},{9,... | collective-permute-start | bytes 786440 | tf_op jit(solution)/shard_map/ppermute | solution.py:89
  36.7 13.7 %collective-permute-start.6 = (bf16[256,512]{0,1:T(8,128)(2,1)S(1)}, bf16[256,512]{0,1:T(8,128)(2,1)S(1)}, u32[]{:S(2)}, u32[]{:S(2)}) collective-permute-start(bf16[256,512]{0,1:T(8,128)(2,1)S(1)} %collective-permute-done.5), channel_id=1, source_target_pairs={{0,2},{1,3},{18,16},{19,17},{4,6},{5,7},{22,20},{23,21},{8,10},{9,... | collective-permute-start | bytes 786440 | tf_op jit(solution)/shard_map/ppermute | solution.py:89
  40.3 26.6 %collective-permute-start.10 = (bf16[256,1024]{1,0:T(8,128)(2,1)S(1)}, bf16[256,1024]{1,0:T(8,128)(2,1)S(1)}, u32[]{:S(2)}, u32[]{:S(2)}) collective-permute-start(bf16[256,1024]{1,0:T(8,128)(2,1)S(1)} %copy-done), channel_id=1, source_target_pairs={{12,0},{13,1},{14,2},{15,3},{28,16},{29,17},{30,18},{31,19}} | collective-permute-start | bytes 1572872 | tf_op jit(solution)/shard_map/ppermute | solution.py:130
  41.6 25.3 %collective-permute-start.11 = (bf16[256,1024]{1,0:T(8,128)(2,1)S(1)}, bf16[256,1024]{1,0:T(8,128)(2,1)S(1)}, u32[]{:S(2)}, u32[]{:S(2)}) collective-permute-start(bf16[256,1024]{1,0:T(8,128)(2,1)S(1)} %copy-done), channel_id=1, source_target_pairs={{0,12},{1,13},{2,14},{3,15},{16,28},{17,29},{18,30},{19,31}} | collective-permute-start | bytes 1572872 | tf_op jit(solution)/shard_map/ppermute | solution.py:129
  48.4 18.4 %collective-permute-start.8 = (bf16[256,1024]{1,0:T(8,128)(2,1)S(1)}, bf16[256,1024]{1,0:T(8,128)(2,1)S(1)}, u32[]{:S(2)}, u32[]{:S(2)}) collective-permute-start(bf16[256,1024]{1,0:T(8,128)(2,1)S(1)} %collective-permute-done.1), channel_id=1, source_target_pairs={{4,0},{8,4},{5,1},{9,5},{6,2},{10,6},{7,3},{11,7},{20,16},{24,20},... | collective-permute-start | bytes 1572872 | tf_op jit(solution)/shard_map/ppermute | solution.py:134
  49.7 17.1 %collective-permute-start.9 = (bf16[256,1024]{1,0:T(8,128)(2,1)S(1)}, bf16[256,1024]{1,0:T(8,128)(2,1)S(1)}, u32[]{:S(2)}, u32[]{:S(2)}) collective-permute-start(bf16[256,1024]{1,0:T(8,128)(2,1)S(1)} %collective-permute-done), channel_id=1, source_target_pairs={{4,8},{8,12},{5,9},{9,13},{6,10},{10,14},{7,11},{11,15},{20,24},{2... | collective-permute-start | bytes 1572872 | tf_op jit(solution)/shard_map/ppermute | solution.py:133
  50.6 17.2 %collective-permute-start.7 = (bf16[256,1024]{0,1:T(8,128)(2,1)S(1)}, bf16[256,1024]{0,1:T(8,128)(2,1)S(1)}, u32[]{:S(2)}, u32[]{:S(2)}) collective-permute-start(bf16[256,1024]{0,1:T(8,128)(2,1)S(1)} %pad_maximum_fusion.1), channel_id=1, source_target_pairs={{0,1},{1,0},{2,3},{3,2},{4,5},{5,4},{6,7},{7,6},{8,9},{9,8},{10,11... | collective-permute-start | bytes 1572872 | tf_op jit(solution)/shard_map/ppermute | solution.py:106
  68.7 13.9 %collective-permute-start.12 = (bf16[256,1024]{1,0:T(8,128)(2,1)S(1)}, bf16[256,1024]{1,0:T(8,128)(2,1)S(1)}, u32[]{:S(2)}, u32[]{:S(2)}) collective-permute-start(bf16[256,1024]{1,0:T(8,128)(2,1)S(1)} %convolution_convert_fusion), channel_id=1, source_target_pairs={{0,16},{16,0},{1,17},{17,1},{2,18},{18,2},{3,19},{19,3},{4,20},{20... | collective-permute-start | bytes 1572872 | tf_op jit(solution)/shard_map/ppermute | solution.py:85

commit v16 on v13

--- a/solution.py
+++ b/solution.py
@@ -119,13 +119,6 @@
     return own_full, foreign_full
 
 
-def first_hop(block, axis):
-    count = lax.axis_size(axis)
-    rising = lax.ppermute(block, axis, [(i, i + 1) for i in range(count - 1)])
-    falling = lax.ppermute(block, axis, [(i, i - 1) for i in range(1, count)])
-    return rising, falling
-
-
 def line_rows(block, first, axis):
     count = lax.axis_size(axis)
     here = lax.axis_index(axis)
@@ -172,8 +165,8 @@
         nearest = joined[:, columns:].reshape(packed.shape)
         falling = lax.ppermute(output_weight, "ctx", [(i, i - 1) for i in range(1, count)])
         farther = [shifted(packed, "ctx", hop) for hop in range(2, reach_of(queries.shape[1]) + 1)]
-        falling, farther = lax.optimization_barrier((falling, farther))
         head_values = attention(queries, keyvals, documents, [nearest] + farther)
+        falling, head_values = lax.optimization_barrier((falling, head_values))
         side_rows = line_rows(output_weight, (rising, falling), "ctx")
         result = split_projection(head_values, side_rows)
         return result.astype(jnp.bfloat16)[None]

time: 85.6 us -> 82.4 us (0.963)
  other arithmetic: 7.52 us -> 5.61 us
  waiting for transfers between devices: 45.3 us -> 44.1 us
  matrix products: 4.07 us -> 3.12 us
  starting transfers between devices: 23.6 us -> 24.5 us
    dot_general x1, matrix products: 1.6 us -> 0.64 us  [attention(): jnp.einsum('qhgd,khd->hgqk', query_block, key_block, preferred_element_ty...]
    ppermute x2, starting transfers between devices: 3.23 us -> 4.14 us  [line_rows(): lax.ppermute(falling, axis, [(i, i - 1) for i in range(1, count - step +...]
    concatenate x1 -> x0, other arithmetic: 0.88 us -> none  [needed_heads(): mine = jnp.concatenate([head_values, foreign], axis=1)]
    concatenate x1, other arithmetic: 0.91 us -> 0.05 us  [shards(): jnp.concatenate([output_weight, packed.reshape(packed.shape[0], -1)], axi...]
    unnamed x15 -> x8, local copies, waits for them, and re-layouts: 2.35 us -> 3.06 us
  transfers between devices with their start and end apart: 12 -> 12, of which waited for: 5 -> 5; matrix products, arithmetic and copies ran while one was open for 10% -> 8% of each run, Pallas kernels for 0% -> 0%
where the time goes in v16:
time: 82.4 us; the launch traced here: 82 us
  waiting for transfers between devices  44.1 us (54%)
  starting transfers between devices  24.5 us (30%)
  other arithmetic  5.61 us (7%)
  local copies, waits for them, and re-layouts  4.23 us (5%)
  matrix products  3.12 us (4%)
    ppermute x2, waiting for transfers between devices, swapped(): return lax.ppermute(block, axis, [(0, 1), (1, 0)])  18.5 us
    ppermute x1, waiting for transfers between devices, shifted(): return lax.ppermute(block, axis, route)  16.7 us
    ppermute x3, waiting for transfers between devices, sent(): return lax.ppermute(block, ('dp', 'tensor'), route)  8.85 us
    ppermute x2, starting transfers between devices, line_rows(): lax.ppermute(rising, axis, [(i, i + 1) for i in range(step - 1, count - 1)])  5.43 us
    ppermute x1, starting transfers between devices, shifted(): return lax.ppermute(block, axis, route)  4.49 us
    ppermute x2, starting transfers between devices, line_rows(): lax.ppermute(falling, axis, [(i, i - 1) for i in range(1, count - step +...  4.14 us
    ppermute x3, starting transfers between devices, sent(): return lax.ppermute(block, ('dp', 'tensor'), route)  3.87 us
    ppermute x1, starting transfers between devices, shards(): joined = lax.ppermute(joined, 'ctx', [(i, i + 1) for i in range(count - 1)])  3.48 us
  transfers between devices with their start and end apart: 12, of which 5 were waited for; matrix products, arithmetic and copies ran while one was open for 8% of the time, Pallas kernels for 0%

profile of v16, /device:TPU:10, one launch (start us, length us, event | category | flops | bytes accessed | tf_op | source)
XLA Modules:
  0.0 82.0 jit_solution(18200184948763902670)
XLA Ops:
  0.0 1.3 %copy.9 = bf16[256,1024]{0,1:T(8,128)(2,1)S(1)} copy(bf16[256,1024]{1,0:T(8,128)(2,1)} %param.7) | data formatting | bytes 1048576 | tf_op args[3]
  1.3 0.7 convert_element_type.37
  2.0 0.9 %copy.30 = bf16[1,256,2,128]{3,1,2,0:T(8,128)(2,1)S(1)} copy(bf16[1,256,2,128]{3,2,1,0:T(2,128)(2,1)} %param.5) | data formatting | bytes 262144 | tf_op args[1]
  2.9 0.1 broadcast_in_dim.27
  3.0 0.1 copy.11
  3.2 3.5 %collective-permute-start.1 = (bf16[256,1408]{0,1:T(8,128)(2,1)S(1)}, bf16[256,1408]{0,1:T(8,128)(2,1)S(1)}, u32[]{:S(2)}, u32[]{:S(2)}) collective-permute-start(bf16[256,1408]{0,1:T(8,128)(2,1)S(1)} %pad_maximum_fusion.1), channel_id=1, source_target_pairs={{0,4},{4,8},{8,12},{1,5},{5,9},{9,13},{2,6},{6,10},{10,14},{3,7},{... | collective-permute-start | bytes 2162696 | tf_op jit(solution)/shard_map/ppermute | solution.py:163
  6.7 2.4 %collective-permute-start = (bf16[256,1024]{0,1:T(8,128)(2,1)S(1)}, bf16[256,1024]{0,1:T(8,128)(2,1)S(1)}, u32[]{:S(2)}, u32[]{:S(2)}) collective-permute-start(bf16[256,1024]{0,1:T(8,128)(2,1)S(1)} %copy.9), channel_id=1, source_target_pairs={{4,0},{8,4},{12,8},{5,1},{9,5},{13,9},{6,2},{10,6},{14,10},{7,3},{... | collective-permute-start | bytes 1572872 | tf_op jit(solution)/shard_map/ppermute | solution.py:166
  9.1 4.5 %collective-permute-start.2 = (bf16[256,3,128]{2,0,1:T(8,128)(2,1)S(1)}, bf16[256,3,128]{2,0,1:T(8,128)(2,1)S(1)}, u32[]{:S(2)}, u32[]{:S(2)}) collective-permute-start(bf16[256,3,128]{2,0,1:T(8,128)(2,1)S(1)} %pad_maximum_fusion.4), channel_id=1, source_target_pairs={{0,8},{4,12},{1,9},{5,13},{2,10},{6,14},{3,11},{7,15},{16,24},{20,... | collective-permute-start | bytes 589832 | tf_op jit(solution)/shard_map/ppermute | solution.py:17
  13.7 0.0 copy-done
  13.7 0.1 reshape.76
  13.8 16.7 %collective-permute-done.2 = bf16[256,3,128]{2,0,1:T(8,128)(2,1)S(1)} collective-permute-done((bf16[256,3,128]{2,0,1:T(8,128)(2,1)S(1)}, bf16[256,3,128]{2,0,1:T(8,128)(2,1)S(1)}, u32[]{:S(2)}, u32[]{:S(2)}) %collective-permute-start.2) | collective-permute-done | bytes 196640 | tf_op jit(solution)/shard_map/ppermute | solution.py:17
  30.6 0.1 convert_reduce_fusion
  30.7 0.0 collective-permute-done.1
  30.7 0.1 copy.24
  30.9 0.7 and_and_fusion
  31.7 0.6 fusion
  32.3 0.8 fusion.1
  33.1 0.9 %fusion.13 = bf16[256,1,4,128]{0,3,2,1:T(8,128)(2,1)S(1)} fusion(f32[768,256,4]{1,0,2:T(8,128)S(1)} %get-tuple-element.20, f32[4,256]{1,0:T(4,128)S(1)} %get-tuple-element.19, pred[256,768]{0,1:T(8,128)(4,1)S(1)} %and_and_fusion, f32[256,4]{0,1:T(4,128)S(1)} %bitcast.74, bf16[768,2,128]{2,0,1:T(8,128)(2,1)S(1)} %pad_maximum_fusion.3), kind=kOutput, calls=%fused_computation.13 | convolution fusion | flops 205520896 | bytes 3809280 | tf_op jit(solution)/shard_map/hgqk,khd->qhgd/dot_general | solution.py:78
  34.1 0.0 collective-permute-done
  34.1 1.9 %collective-permute-start.7 = (bf16[256,1024]{0,1:T(8,128)(2,1)S(1)}, bf16[256,1024]{0,1:T(8,128)(2,1)S(1)}, u32[]{:S(2)}, u32[]{:S(2)}) collective-permute-start(bf16[256,1024]{0,1:T(8,128)(2,1)S(1)} %collective-permute-done), channel_id=1, source_target_pairs={{4,0},{8,4},{5,1},{9,5},{6,2},{10,6},{7,3},{11,7},{20,16},{24,20},... | collective-permute-start | bytes 1572872 | tf_op jit(solution)/shard_map/ppermute | solution.py:129
  36.0 4.0 %collective-permute-start.9 = (bf16[256,1024]{0,1:T(8,128)(2,1)S(1)}, bf16[256,1024]{0,1:T(8,128)(2,1)S(1)}, u32[]{:S(2)}, u32[]{:S(2)}) collective-permute-start(bf16[256,1024]{0,1:T(8,128)(2,1)S(1)} %slice.57), channel_id=1, source_target_pairs={{4,8},{8,12},{5,9},{9,13},{6,10},{10,14},{7,11},{11,15},{20,24},{2... | collective-permute-start | bytes 1572872 | tf_op jit(solution)/shard_map/ppermute | solution.py:128
  40.0 0.6 collective-permute-start.3
  40.6 0.7 constant_dynamic-update-slice_fusion.1
  41.4 5.4 %collective-permute-done.3 = bf16[256,512]{0,1:T(8,128)(2,1)S(1)} collective-permute-done((bf16[256,512]{0,1:T(8,128)(2,1)S(1)}, bf16[256,512]{0,1:T(8,128)(2,1)S(1)}, u32[]{:S(2)}, u32[]{:S(2)}) %collective-permute-start.3) | collective-permute-done | bytes 262176 | tf_op jit(solution)/shard_map/ppermute | solution.py:91
  46.7 0.7 constant_dynamic-update-slice_fusion
  47.4 1.3 %collective-permute-start.4 = (bf16[256,1024]{0,1:T(8,128)(2,1)}, bf16[256,1024]{0,1:T(8,128)(2,1)}, u32[]{:S(2)}, u32[]{:S(2)}) collective-permute-start(bf16[256,1024]{0,1:T(8,128)(2,1)} %constant_dynamic-update-slice_fusion), channel_id=1, source_target_pairs={{0,2},{1,3},{18,16},{19,17},{4,6},{5,7},{22,20},{23,21},{8,10},{9,... | collective-permute-start | bytes 1572872 | tf_op jit(solution)/shard_map/ppermute | solution.py:95
  48.7 0.0 collective-permute-done.7
  48.8 2.2 %collective-permute-start.8 = (bf16[256,1024]{0,1:T(8,128)(2,1)S(1)}, bf16[256,1024]{0,1:T(8,128)(2,1)S(1)}, u32[]{:S(2)}, u32[]{:S(2)}) collective-permute-start(bf16[256,1024]{0,1:T(8,128)(2,1)S(1)} %collective-permute-done.7), channel_id=1, source_target_pairs={{4,0},{5,1},{6,2},{7,3},{20,16},{21,17},{22,18},{23,19}} | collective-permute-start | bytes 1572872 | tf_op jit(solution)/shard_map/ppermute | solution.py:129
  51.0 0.0 collective-permute-done.9
  51.0 1.4 %collective-permute-start.10 = (bf16[256,1024]{0,1:T(8,128)(2,1)S(1)}, bf16[256,1024]{0,1:T(8,128)(2,1)}, u32[]{:S(2)}, u32[]{:S(2)}) collective-permute-start(bf16[256,1024]{0,1:T(8,128)(2,1)S(1)} %collective-permute-done.9), channel_id=1, source_target_pairs={{8,12},{9,13},{10,14},{11,15},{24,28},{25,29},{26,30},{27,31}} | collective-permute-start | bytes 1572872 | tf_op jit(solution)/shard_map/ppermute | solution.py:128
  52.5 0.7 collective-permute-start.5
  53.1 7.8 %collective-permute-done.4 = bf16[256,1024]{0,1:T(8,128)(2,1)} collective-permute-done((bf16[256,1024]{0,1:T(8,128)(2,1)}, bf16[256,1024]{0,1:T(8,128)(2,1)}, u32[]{:S(2)}, u32[]{:S(2)}) %collective-permute-start.4) | collective-permute-done | bytes 524320 | tf_op jit(solution)/shard_map/ppermute | solution.py:95
  61.0 1.9 %collective-permute-start.6 = (bf16[256,1024]{0,1:T(8,128)(2,1)}, bf16[256,1024]{0,1:T(8,128)(2,1)S(1)}, u32[]{:S(2)}, u32[]{:S(2)}) collective-permute-start(bf16[256,1024]{0,1:T(8,128)(2,1)} %collective-permute-done.4), channel_id=1, source_target_pairs={{2,3},{3,2},{16,17},{17,16},{6,7},{7,6},{20,21},{21,20},{10,11},{1... | collective-permute-start | bytes 1572872 | tf_op jit(solution)/shard_map/ppermute | solution.py:95
  62.9 0.0 collective-permute-done.8
  62.9 0.0 collective-permute-done.10
  62.9 0.2 select_select_fusion
  63.1 0.2 select_select_fusion.1
  63.3 0.2 select_select_fusion.2
  63.4 0.2 select_select_fusion.3
  63.6 0.3 pad_maximum_fusion
  63.9 0.0 collective-permute-done.5
  63.9 1.0 %collective-permute-done.6 = bf16[256,1024]{0,1:T(8,128)(2,1)S(1)} collective-permute-done((bf16[256,1024]{0,1:T(8,128)(2,1)}, bf16[256,1024]{0,1:T(8,128)(2,1)S(1)}, u32[]{:S(2)}, u32[]{:S(2)}) %collective-permute-start.6) | collective-permute-done | bytes 524320 | tf_op jit(solution)/shard_map/ppermute | solution.py:95
  65.0 1.2 %broadcast_select_fusion.3 = (bf16[256,1024]{0,1:T(8,128)(2,1)S(1)}, bf16[256,1024]{0,1:T(8,128)(2,1)S(1)}) fusion(pred[]{:T(512)S(6)} %eq.105, bf16[256,1024]{0,1:T(8,128)(2,1)} %constant_dynamic-update-slice_fusion, bf16[256,1024]{0,1:T(8,128)(2,1)} %collective-permute-done.4, pred[]{:T(512)S(6)} %eq.106, bf16[256,1024]{0,1:T(8,128)(2,1)S(1)} %collective-permute-done.5, ...), kind=kLoop, calls=%fused_computation.28 | loop fusion | flops 1048576 | bytes 3145730 | tf_op jit(solution)/shard_map/jit(_where)/select_n | solution.py:115
  66.2 0.8 convolution_convert_fusion
  67.0 0.1 collective-permute-start.11
  67.1 0.8 fusion.28
  67.9 13.1 %collective-permute-done.11 = bf16[256,1024]{1,0:T(8,128)(2,1)S(1)} collective-permute-done((bf16[256,1024]{1,0:T(8,128)(2,1)S(1)}, bf16[256,1024]{1,0:T(8,128)(2,1)S(1)}, u32[]{:S(2)}, u32[]{:S(2)}) %collective-permute-start.11) | collective-permute-done | bytes 524320 | tf_op jit(solution)/shard_map/ppermute | solution.py:91
  81.0 0.9 %fusion.16 = bf16[1,256,1024]{2,1,0:T(8,128)(2,1)} fusion(f32[256,1024]{1,0:T(8,128)S(1)} %fusion.28, bf16[256,1024]{1,0:T(8,128)(2,1)S(1)} %collective-permute-done.11), kind=kLoop, calls=%fused_computation.16 | loop fusion | flops 786432 | bytes 2097152 | tf_op jit(solution)/shard_map/broadcast_in_dim | solution.py:172
  (19 shorter events, 0.3 us)
Async XLA Ops:
  0.0 30.9 %copy-start.1 = (s32[1,256]{1,0:T(1,128)S(1)}, s32[1,256]{1,0:T(1,128)}, u32[]{:S(2)}) copy-start(s32[1,256]{1,0:T(1,128)} %param.6) | copy-start | bytes 3076
  0.0 13.7 %copy-start = (bf16[1,256,512]{2,1,0:T(8,128)(2,1)S(1)}, bf16[1,256,512]{2,1,0:T(8,128)(2,1)}, u32[]{:S(2)}) copy-start(bf16[1,256,512]{2,1,0:T(8,128)(2,1)} %param.4) | copy-start | bytes 786436
  3.2 27.4 %collective-permute-start.1 = (bf16[256,1408]{0,1:T(8,128)(2,1)S(1)}, bf16[256,1408]{0,1:T(8,128)(2,1)S(1)}, u32[]{:S(2)}, u32[]{:S(2)}) collective-permute-start(bf16[256,1408]{0,1:T(8,128)(2,1)S(1)} %pad_maximum_fusion.1), channel_id=1, source_target_pairs={{0,4},{4,8},{8,12},{1,5},{5,9},{9,13},{2,6},{6,10},{10,14},{3,7},{... | collective-permute-start | bytes 2162696 | tf_op jit(solution)/shard_map/ppermute | solution.py:163
  6.7 27.3 %collective-permute-start = (bf16[256,1024]{0,1:T(8,128)(2,1)S(1)}, bf16[256,1024]{0,1:T(8,128)(2,1)S(1)}, u32[]{:S(2)}, u32[]{:S(2)}) collective-permute-start(bf16[256,1024]{0,1:T(8,128)(2,1)S(1)} %copy.9), channel_id=1, source_target_pairs={{4,0},{8,4},{12,8},{5,1},{9,5},{13,9},{6,2},{10,6},{14,10},{7,3},{... | collective-permute-start | bytes 1572872 | tf_op jit(solution)/shard_map/ppermute | solution.py:166
  9.1 21.4 %collective-permute-start.2 = (bf16[256,3,128]{2,0,1:T(8,128)(2,1)S(1)}, bf16[256,3,128]{2,0,1:T(8,128)(2,1)S(1)}, u32[]{:S(2)}, u32[]{:S(2)}) collective-permute-start(bf16[256,3,128]{2,0,1:T(8,128)(2,1)S(1)} %pad_maximum_fusion.4), channel_id=1, source_target_pairs={{0,8},{4,12},{1,9},{5,13},{2,10},{6,14},{3,11},{7,15},{16,24},{20,... | collective-permute-start | bytes 589832 | tf_op jit(solution)/shard_map/ppermute | solution.py:17
  34.1 14.7 %collective-permute-start.7 = (bf16[256,1024]{0,1:T(8,128)(2,1)S(1)}, bf16[256,1024]{0,1:T(8,128)(2,1)S(1)}, u32[]{:S(2)}, u32[]{:S(2)}) collective-permute-start(bf16[256,1024]{0,1:T(8,128)(2,1)S(1)} %collective-permute-done), channel_id=1, source_target_pairs={{4,0},{8,4},{5,1},{9,5},{6,2},{10,6},{7,3},{11,7},{20,16},{24,20},... | collective-permute-start | bytes 1572872 | tf_op jit(solution)/shard_map/ppermute | solution.py:129
  36.0 15.0 %collective-permute-start.9 = (bf16[256,1024]{0,1:T(8,128)(2,1)S(1)}, bf16[256,1024]{0,1:T(8,128)(2,1)S(1)}, u32[]{:S(2)}, u32[]{:S(2)}) collective-permute-start(bf16[256,1024]{0,1:T(8,128)(2,1)S(1)} %slice.57), channel_id=1, source_target_pairs={{4,8},{8,12},{5,9},{9,13},{6,10},{10,14},{7,11},{11,15},{20,24},{2... | collective-permute-start | bytes 1572872 | tf_op jit(solution)/shard_map/ppermute | solution.py:128
  40.0 6.7 %collective-permute-start.3 = (bf16[256,512]{0,1:T(8,128)(2,1)S(1)}, bf16[256,512]{0,1:T(8,128)(2,1)S(1)}, u32[]{:S(2)}, u32[]{:S(2)}) collective-permute-start(bf16[256,512]{0,1:T(8,128)(2,1)S(1)} %bitcast.72), channel_id=1, source_target_pairs={{0,16},{16,0},{1,17},{17,1},{2,18},{18,2},{3,19},{19,3},{4,20},{20... | collective-permute-start | bytes 786440 | tf_op jit(solution)/shard_map/ppermute | solution.py:91
  47.4 13.5 %collective-permute-start.4 = (bf16[256,1024]{0,1:T(8,128)(2,1)}, bf16[256,1024]{0,1:T(8,128)(2,1)}, u32[]{:S(2)}, u32[]{:S(2)}) collective-permute-start(bf16[256,1024]{0,1:T(8,128)(2,1)} %constant_dynamic-update-slice_fusion), channel_id=1, source_target_pairs={{0,2},{1,3},{18,16},{19,17},{4,6},{5,7},{22,20},{23,21},{8,10},{9,... | collective-permute-start | bytes 1572872 | tf_op jit(solution)/shard_map/ppermute | solution.py:95
  48.8 14.1 %collective-permute-start.8 = (bf16[256,1024]{0,1:T(8,128)(2,1)S(1)}, bf16[256,1024]{0,1:T(8,128)(2,1)S(1)}, u32[]{:S(2)}, u32[]{:S(2)}) collective-permute-start(bf16[256,1024]{0,1:T(8,128)(2,1)S(1)} %collective-permute-done.7), channel_id=1, source_target_pairs={{4,0},{5,1},{6,2},{7,3},{20,16},{21,17},{22,18},{23,19}} | collective-permute-start | bytes 1572872 | tf_op jit(solution)/shard_map/ppermute | solution.py:129
  51.0 11.9 %collective-permute-start.10 = (bf16[256,1024]{0,1:T(8,128)(2,1)S(1)}, bf16[256,1024]{0,1:T(8,128)(2,1)}, u32[]{:S(2)}, u32[]{:S(2)}) collective-permute-start(bf16[256,1024]{0,1:T(8,128)(2,1)S(1)} %collective-permute-done.9), channel_id=1, source_target_pairs={{8,12},{9,13},{10,14},{11,15},{24,28},{25,29},{26,30},{27,31}} | collective-permute-start | bytes 1572872 | tf_op jit(solution)/shard_map/ppermute | solution.py:128
  52.5 11.5 %collective-permute-start.5 = (bf16[256,1024]{0,1:T(8,128)(2,1)}, bf16[256,1024]{0,1:T(8,128)(2,1)S(1)}, u32[]{:S(2)}, u32[]{:S(2)}) collective-permute-start(bf16[256,1024]{0,1:T(8,128)(2,1)} %constant_dynamic-update-slice_fusion), channel_id=1, source_target_pairs={{0,1},{1,0},{18,19},{19,18},{4,5},{5,4},{22,23},{23,22},{8,9},{9,8... | collective-permute-start | bytes 1572872 | tf_op jit(solution)/shard_map/ppermute | solution.py:95
  61.0 4.0 %collective-permute-start.6 = (bf16[256,1024]{0,1:T(8,128)(2,1)}, bf16[256,1024]{0,1:T(8,128)(2,1)S(1)}, u32[]{:S(2)}, u32[]{:S(2)}) collective-permute-start(bf16[256,1024]{0,1:T(8,128)(2,1)} %collective-permute-done.4), channel_id=1, source_target_pairs={{2,3},{3,2},{16,17},{17,16},{6,7},{7,6},{20,21},{21,20},{10,11},{1... | collective-permute-start | bytes 1572872 | tf_op jit(solution)/shard_map/ppermute | solution.py:95
  67.0 14.0 %collective-permute-start.11 = (bf16[256,1024]{1,0:T(8,128)(2,1)S(1)}, bf16[256,1024]{1,0:T(8,128)(2,1)S(1)}, u32[]{:S(2)}, u32[]{:S(2)}) collective-permute-start(bf16[256,1024]{1,0:T(8,128)(2,1)S(1)} %convolution_convert_fusion), channel_id=1, source_target_pairs={{0,16},{16,0},{1,17},{17,1},{2,18},{18,2},{3,19},{19,3},{4,20},{20... | collective-permute-start | bytes 1572872 | tf_op jit(solution)/shard_map/ppermute | solution.py:91

commit v17 on v10

--- a/solution.py
+++ b/solution.py
@@ -141,25 +141,31 @@
 
 def split_projection(head_values, side_rows):
     own_full, foreign_full = needed_heads(head_values)
-    partner = jnp.dot(foreign_full, side_rows, preferred_element_type=jnp.float32)
-    outgoing = partner.astype(jnp.bfloat16)
-    returned = swapped(outgoing, "dp")
-    outgoing, own_full, side_rows = lax.optimization_barrier((outgoing, own_full, side_rows))
-    local = jnp.dot(own_full, side_rows, preferred_element_type=jnp.float32)
-    local = lax.optimization_barrier(local)
-    return local + returned.astype(jnp.float32)
+    returned = []
+    for rows in side_rows:
+        partner = jnp.dot(foreign_full, rows, preferred_element_type=jnp.float32)
+        returned.append(swapped(partner.astype(jnp.bfloat16), "dp"))
+    own_full, side_rows = lax.optimization_barrier((own_full, side_rows))
+    outputs = []
+    for rows, back in zip(side_rows, returned):
+        local = jnp.dot(own_full, rows, preferred_element_type=jnp.float32)
+        local = lax.optimization_barrier(local)
+        outputs.append(local + back.astype(jnp.float32))
+    return jnp.concatenate(outputs, axis=1)
 
 
 def shards(queries, keyvals, documents, output_weight):
     block_rows = output_weight.shape[0]
     width = queries.shape[2]
     side_width = block_rows * lax.axis_size("ctx")
-    fits = lax.axis_size("tensor") == 4
+    fits = lax.axis_size("tensor") == 4 and output_weight.shape[1] % 256 == 0
     if lax.axis_size("dp") == 2 and side_width == 2 * width and fits:
-        first = first_hop(output_weight, "ctx")
+        half = output_weight.shape[1] // 2
+        halves = [output_weight[:, :half], output_weight[:, half:]]
+        firsts = [first_hop(piece, "ctx") for piece in halves]
         head_values = attention(queries, keyvals, documents)
-        first, head_values = lax.optimization_barrier((first, head_values))
-        side_rows = line_rows(output_weight, first, "ctx")
+        firsts, head_values = lax.optimization_barrier((firsts, head_values))
+        side_rows = [line_rows(piece, f, "ctx") for piece, f in zip(halves, firsts)]
         result = split_projection(head_values, side_rows)
         return result.astype(jnp.bfloat16)[None]
     all_rows = lax.all_gather(output_weight, ("dp", "ctx"), axis=0, tiled=True)

time: 80.7 us -> 83.6 us (1.036)
  the two profiles are of different devices: /device:TPU:12 before, /device:TPU:18 now
where the time goes in v17:
time: 83.6 us; the launch traced here: 83 us
  starting transfers between devices  39.9 us (48%)
  waiting for transfers between devices  30.3 us (36%)
  other arithmetic  4.7 us (6%)
  local copies, waits for them, and re-layouts  4.19 us (5%)
  matrix products  3.4 us (4%)
    ppermute x3, waiting for transfers between devices, swapped(): return lax.ppermute(block, axis, [(0, 1), (1, 0)])  11 us
    ppermute x4, starting transfers between devices, line_rows(): lax.ppermute(rising, axis, [(i, i + 1) for i in range(step - 1, count - 1)])  9.99 us
    ppermute x2, starting transfers between devices, first_hop(): falling = lax.ppermute(block, axis, [(i, i - 1) for i in range(1, count)])  7.94 us
    ppermute x3, waiting for transfers between devices, sent(): return lax.ppermute(block, ('dp', 'tensor'), route)  6.99 us
    ppermute x2, waiting for transfers between devices, first_hop(): rising = lax.ppermute(block, axis, [(i, i + 1) for i in range(count - 1)])  6.85 us
    ppermute x4, starting transfers between devices, line_rows(): lax.ppermute(falling, axis, [(i, i - 1) for i in range(1, count - step +...  6.73 us
    ppermute x4, waiting for transfers between devices, line_rows(): lax.ppermute(rising, axis, [(i, i + 1) for i in range(step - 1, count - 1)])  5.48 us
    ppermute x2, starting transfers between devices, shifted(): return lax.ppermute(block, axis, route)  4.78 us
  transfers between devices with their start and end apart: 20, of which 10 were waited for; matrix products, arithmetic and copies ran while one was open for 10% of the time, Pallas kernels for 0%

profile of v17, /device:TPU:18, one launch (start us, length us, event | category | flops | bytes accessed | tf_op | source)
XLA Modules:
  0.0 83.0 jit_solution(17967084681722970504)
XLA Ops:
  0.0 0.8 convert_element_type.48
  0.8 0.9 %copy.21 = bf16[1,256,2,128]{3,1,2,0:T(8,128)(2,1)S(1)} copy(bf16[1,256,2,128]{3,2,1,0:T(2,128)(2,1)} %param.5) | data formatting | bytes 262144 | tf_op args[1]
  1.7 0.1 broadcast_in_dim.14
  1.8 1.3 %collective-permute-start.5 = (bf16[256,3,128]{2,0,1:T(8,128)(2,1)S(1)}, bf16[256,3,128]{2,0,1:T(8,128)(2,1)S(1)}, u32[]{:S(2)}, u32[]{:S(2)}) collective-permute-start(bf16[256,3,128]{2,0,1:T(8,128)(2,1)S(1)} %pad_maximum_fusion.8), channel_id=1, source_target_pairs={{0,8},{4,12},{1,9},{5,13},{2,10},{6,14},{3,11},{7,15},{16,24},{20,... | collective-permute-start | bytes 589832 | tf_op jit(solution)/shard_map/ppermute | solution.py:17
  3.1 3.5 %collective-permute-start.4 = (bf16[256,3,128]{2,0,1:T(8,128)(2,1)S(1)}, bf16[256,3,128]{2,0,1:T(8,128)(2,1)S(1)}, u32[]{:S(2)}, u32[]{:S(2)}) collective-permute-start(bf16[256,3,128]{2,0,1:T(8,128)(2,1)S(1)} %pad_maximum_fusion.8), channel_id=1, source_target_pairs={{0,4},{4,8},{8,12},{1,5},{5,9},{9,13},{2,6},{6,10},{10,14},{3,7},{... | collective-permute-start | bytes 589832 | tf_op jit(solution)/shard_map/ppermute | solution.py:17
  6.6 1.1 %fusion.27 = (bf16[256,512]{1,0:T(8,128)(2,1)S(1)}, bf16[256,512]{1,0:T(8,128)(2,1)S(1)}) fusion(bf16[256,1024]{1,0:T(8,128)(2,1)} %param.7), kind=kLoop, calls=%fused_computation.59 | loop fusion | bytes 1048576 | tf_op jit(solution)/shard_map/slice | solution.py:164
  7.7 4.0 %collective-permute-start.3 = (bf16[256,512]{1,0:T(8,128)(2,1)S(1)}, bf16[256,512]{1,0:T(8,128)(2,1)S(1)}, u32[]{:S(2)}, u32[]{:S(2)}) collective-permute-start(bf16[256,512]{1,0:T(8,128)(2,1)S(1)} %get-tuple-element.27), channel_id=1, source_target_pairs={{4,0},{8,4},{12,8},{5,1},{9,5},{13,9},{6,2},{10,6},{14,10},{7,3},{... | collective-permute-start | bytes 786440 | tf_op jit(solution)/shard_map/ppermute | solution.py:119
  11.7 1.9 %collective-permute-start.2 = (bf16[256,512]{1,0:T(8,128)(2,1)S(1)}, bf16[256,512]{1,0:T(8,128)(2,1)S(1)}, u32[]{:S(2)}, u32[]{:S(2)}) collective-permute-start(bf16[256,512]{1,0:T(8,128)(2,1)S(1)} %get-tuple-element.27), channel_id=1, source_target_pairs={{0,4},{4,8},{8,12},{1,5},{5,9},{9,13},{2,6},{6,10},{10,14},{3,7},{... | collective-permute-start | bytes 786440 | tf_op jit(solution)/shard_map/ppermute | solution.py:118
  13.6 3.9 %collective-permute-start.1 = (bf16[256,512]{1,0:T(8,128)(2,1)S(1)}, bf16[256,512]{1,0:T(8,128)(2,1)S(1)}, u32[]{:S(2)}, u32[]{:S(2)}) collective-permute-start(bf16[256,512]{1,0:T(8,128)(2,1)S(1)} %get-tuple-element.28), channel_id=1, source_target_pairs={{4,0},{8,4},{12,8},{5,1},{9,5},{13,9},{6,2},{10,6},{14,10},{7,3},{... | collective-permute-start | bytes 786440 | tf_op jit(solution)/shard_map/ppermute | solution.py:119
  17.6 1.0 %reshape.99 = bf16[256,4,128]{2,1,0:T(4,128)(2,1)S(1)} reshape(bf16[1,256,512]{2,1,0:T(8,128)(2,1)} %param.4) | data formatting | bytes 524288 | tf_op jit(solution)/shard_map/reshape.3
  18.7 1.9 %collective-permute-start = (bf16[256,512]{1,0:T(8,128)(2,1)S(1)}, bf16[256,512]{1,0:T(8,128)(2,1)S(1)}, u32[]{:S(2)}, u32[]{:S(2)}) collective-permute-start(bf16[256,512]{1,0:T(8,128)(2,1)S(1)} %get-tuple-element.28), channel_id=1, source_target_pairs={{0,4},{4,8},{8,12},{1,5},{5,9},{9,13},{2,6},{6,10},{10,14},{3,7},{... | collective-permute-start | bytes 786440 | tf_op jit(solution)/shard_map/ppermute | solution.py:118
  20.7 0.1 convert_reduce_fusion
  20.8 0.1 convert_reduce_fusion.1
  20.9 0.7 and_and_fusion
  21.7 0.7 fusion
  22.3 0.8 fusion.1
  23.1 0.9 %fusion.13 = bf16[256,1,4,128]{0,3,2,1:T(8,128)(2,1)S(1)} fusion(f32[768,256,4]{1,0,2:T(8,128)S(1)} %get-tuple-element.30, f32[4,256]{1,0:T(4,128)S(1)} %get-tuple-element.29, pred[256,768]{0,1:T(8,128)(4,1)S(1)} %and_and_fusion, f32[256,4]{0,1:T(4,128)S(1)} %bitcast.71, bf16[768,2,128]{2,0,1:T(8,128)(2,1)S(1)} %pad_maximum_fusion.5), kind=kOutput, calls=%fused_computation.14 | convolution fusion | flops 205520896 | bytes 3809280 | tf_op jit(solution)/shard_map/hgqk,khd->qhgd/dot_general | solution.py:72
  24.1 1.3 %collective-permute-done.2 = bf16[256,512]{1,0:T(8,128)(2,1)S(1)} collective-permute-done((bf16[256,512]{1,0:T(8,128)(2,1)S(1)}, bf16[256,512]{1,0:T(8,128)(2,1)S(1)}, u32[]{:S(2)}, u32[]{:S(2)}) %collective-permute-start.2) | collective-permute-done | bytes 262176 | tf_op jit(solution)/shard_map/ppermute | solution.py:118
  25.4 5.5 %collective-permute-done = bf16[256,512]{1,0:T(8,128)(2,1)S(1)} collective-permute-done((bf16[256,512]{1,0:T(8,128)(2,1)S(1)}, bf16[256,512]{1,0:T(8,128)(2,1)S(1)}, u32[]{:S(2)}, u32[]{:S(2)}) %collective-permute-start) | collective-permute-done | bytes 262176 | tf_op jit(solution)/shard_map/ppermute | solution.py:118
  31.0 1.5 %collective-permute-start.10 = (bf16[256,512]{1,0:T(8,128)(2,1)S(1)}, bf16[256,512]{1,0:T(8,128)(2,1)S(1)}, u32[]{:S(2)}, u32[]{:S(2)}) collective-permute-start(bf16[256,512]{1,0:T(8,128)(2,1)S(1)} %collective-permute-done.1), channel_id=1, source_target_pairs={{4,0},{8,4},{5,1},{9,5},{6,2},{10,6},{7,3},{11,7},{20,16},{24,20},... | collective-permute-start | bytes 786440 | tf_op jit(solution)/shard_map/ppermute | solution.py:130
  32.4 1.9 %collective-permute-start.12 = (bf16[256,512]{1,0:T(8,128)(2,1)S(1)}, bf16[256,512]{1,0:T(8,128)(2,1)S(1)}, u32[]{:S(2)}, u32[]{:S(2)}) collective-permute-start(bf16[256,512]{1,0:T(8,128)(2,1)S(1)} %collective-permute-done), channel_id=1, source_target_pairs={{4,8},{8,12},{5,9},{9,13},{6,10},{10,14},{7,11},{11,15},{20,24},{2... | collective-permute-start | bytes 786440 | tf_op jit(solution)/shard_map/ppermute | solution.py:129
  34.3 0.6 collective-permute-start.6
  34.9 3.9 %collective-permute-start.14 = (bf16[256,512]{1,0:T(8,128)(2,1)S(1)}, bf16[256,512]{1,0:T(8,128)(2,1)S(1)}, u32[]{:S(2)}, u32[]{:S(2)}) collective-permute-start(bf16[256,512]{1,0:T(8,128)(2,1)S(1)} %collective-permute-done.3), channel_id=1, source_target_pairs={{4,0},{8,4},{5,1},{9,5},{6,2},{10,6},{7,3},{11,7},{20,16},{24,20},... | collective-permute-start | bytes 786440 | tf_op jit(solution)/shard_map/ppermute | solution.py:130
  38.9 1.9 %collective-permute-start.16 = (bf16[256,512]{1,0:T(8,128)(2,1)S(1)}, bf16[256,512]{1,0:T(8,128)(2,1)S(1)}, u32[]{:S(2)}, u32[]{:S(2)}) collective-permute-start(bf16[256,512]{1,0:T(8,128)(2,1)S(1)} %collective-permute-done.2), channel_id=1, source_target_pairs={{4,8},{8,12},{5,9},{9,13},{6,10},{10,14},{7,11},{11,15},{20,24},{2... | collective-permute-start | bytes 786440 | tf_op jit(solution)/shard_map/ppermute | solution.py:129
  40.8 0.7 collective-permute-start.11
  41.5 0.9 %collective-permute-done.12 = bf16[256,512]{1,0:T(8,128)(2,1)S(1)} collective-permute-done((bf16[256,512]{1,0:T(8,128)(2,1)S(1)}, bf16[256,512]{1,0:T(8,128)(2,1)S(1)}, u32[]{:S(2)}, u32[]{:S(2)}) %collective-permute-start.12) | collective-permute-done | bytes 262176 | tf_op jit(solution)/shard_map/ppermute | solution.py:129
  42.4 2.2 %collective-permute-start.13 = (bf16[256,512]{1,0:T(8,128)(2,1)S(1)}, bf16[256,512]{1,0:T(8,128)(2,1)S(1)}, u32[]{:S(2)}, u32[]{:S(2)}) collective-permute-start(bf16[256,512]{1,0:T(8,128)(2,1)S(1)} %collective-permute-done.12), channel_id=1, source_target_pairs={{8,12},{9,13},{10,14},{11,15},{24,28},{25,29},{26,30},{27,31}} | collective-permute-start | bytes 786440 | tf_op jit(solution)/shard_map/ppermute | solution.py:129
  44.7 1.0 %constant_dynamic-update-slice_fusion = bf16[256,1024]{0,1:T(8,128)(2,1)S(1)} fusion(bf16[256,1024]{0,1:T(8,128)(2,1)S(1)} %constant_dynamic-update-slice_fusion.1, bf16[256,512]{0,1:T(8,128)(2,1)} %collective-permute-done.6), kind=kLoop, calls=%fused_computation.44 | loop fusion | bytes 524288 | tf_op jit(solution)/shard_map/concatenate | solution.py:97
  45.7 0.7 collective-permute-start.8
  46.4 1.3 %collective-permute-start.7 = (bf16[256,1024]{0,1:T(8,128)(2,1)S(1)}, bf16[256,1024]{0,1:T(8,128)(2,1)S(1)}, u32[]{:S(2)}, u32[]{:S(2)}) collective-permute-start(bf16[256,1024]{0,1:T(8,128)(2,1)S(1)} %constant_dynamic-update-slice_fusion), channel_id=1, source_target_pairs={{0,2},{1,3},{18,16},{19,17},{4,6},{5,7},{22,20},{23,21},{8,10},{9,... | collective-permute-start | bytes 1572872 | tf_op jit(solution)/shard_map/ppermute | solution.py:89
  47.7 0.3 collective-permute-done.16
  48.0 0.7 collective-permute-start.15
  48.7 3.9 %collective-permute-start.17 = (bf16[256,512]{1,0:T(8,128)(2,1)S(1)}, bf16[256,512]{1,0:T(8,128)(2,1)S(1)}, u32[]{:S(2)}, u32[]{:S(2)}) collective-permute-start(bf16[256,512]{1,0:T(8,128)(2,1)S(1)} %collective-permute-done.16), channel_id=1, source_target_pairs={{8,12},{9,13},{10,14},{11,15},{24,28},{25,29},{26,30},{27,31}} | collective-permute-start | bytes 786440 | tf_op jit(solution)/shard_map/ppermute | solution.py:129
  52.7 0.5 collective-permute-done.13
  53.3 3.8 %collective-permute-done.17 = bf16[256,512]{1,0:T(8,128)(2,1)S(1)} collective-permute-done((bf16[256,512]{1,0:T(8,128)(2,1)S(1)}, bf16[256,512]{1,0:T(8,128)(2,1)S(1)}, u32[]{:S(2)}, u32[]{:S(2)}) %collective-permute-start.17) | collective-permute-done | bytes 262176 | tf_op jit(solution)/shard_map/ppermute | solution.py:129
  57.2 0.1 select_select_fusion.1
  57.6 5.4 %collective-permute-done.7 = bf16[256,1024]{0,1:T(8,128)(2,1)S(1)} collective-permute-done((bf16[256,1024]{0,1:T(8,128)(2,1)S(1)}, bf16[256,1024]{0,1:T(8,128)(2,1)S(1)}, u32[]{:S(2)}, u32[]{:S(2)}) %collective-permute-start.7) | collective-permute-done | bytes 524320 | tf_op jit(solution)/shard_map/ppermute | solution.py:89
  63.0 1.9 %collective-permute-start.9 = (bf16[256,1024]{0,1:T(8,128)(2,1)S(1)}, bf16[256,1024]{0,1:T(8,128)(2,1)S(1)}, u32[]{:S(2)}, u32[]{:S(2)}) collective-permute-start(bf16[256,1024]{0,1:T(8,128)(2,1)S(1)} %collective-permute-done.7), channel_id=1, source_target_pairs={{2,3},{3,2},{16,17},{17,16},{6,7},{7,6},{20,21},{21,20},{10,11},{1... | collective-permute-start | bytes 1572872 | tf_op jit(solution)/shard_map/ppermute | solution.py:89
  65.2 1.6 %collective-permute-done.9 = bf16[256,1024]{0,1:T(8,128)(2,1)S(1)} collective-permute-done((bf16[256,1024]{0,1:T(8,128)(2,1)S(1)}, bf16[256,1024]{0,1:T(8,128)(2,1)S(1)}, u32[]{:S(2)}, u32[]{:S(2)}) %collective-permute-start.9) | collective-permute-done | bytes 524320 | tf_op jit(solution)/shard_map/ppermute | solution.py:89
  66.8 0.2 broadcast_select_fusion.3
  67.1 0.5 convolution_convert_fusion
  67.5 0.5 convolution_convert_fusion.1
  68.1 2.0 %collective-permute-start.19 = (bf16[256,512]{1,0:T(8,128)(2,1)S(1)}, bf16[256,512]{1,0:T(8,128)(2,1)S(1)}, u32[]{:S(2)}, u32[]{:S(2)}) collective-permute-start(bf16[256,512]{1,0:T(8,128)(2,1)S(1)} %convolution_convert_fusion), channel_id=1, source_target_pairs={{0,16},{16,0},{1,17},{17,1},{2,18},{18,2},{3,19},{19,3},{4,20},{20... | collective-permute-start | bytes 786440 | tf_op jit(solution)/shard_map/ppermute | solution.py:85
  70.1 0.4 fusion.28
  70.6 0.5 fusion.29
  71.0 6.2 %collective-permute-done.18 = bf16[256,512]{1,0:T(8,128)(2,1)S(1)} collective-permute-done((bf16[256,512]{1,0:T(8,128)(2,1)S(1)}, bf16[256,512]{1,0:T(8,128)(2,1)S(1)}, u32[]{:S(2)}, u32[]{:S(2)}) %collective-permute-start.18) | collective-permute-done | bytes 262176 | tf_op jit(solution)/shard_map/ppermute | solution.py:85
  77.3 4.7 %collective-permute-done.19 = bf16[256,512]{1,0:T(8,128)(2,1)S(1)} collective-permute-done((bf16[256,512]{1,0:T(8,128)(2,1)S(1)}, bf16[256,512]{1,0:T(8,128)(2,1)S(1)}, u32[]{:S(2)}, u32[]{:S(2)}) %collective-permute-start.19) | collective-permute-done | bytes 262176 | tf_op jit(solution)/shard_map/ppermute | solution.py:85
  82.1 0.9 %pad_maximum_fusion.4 = bf16[1,256,1024]{2,1,0:T(8,128)(2,1)} fusion(bf16[1,256,512]{2,1,0:T(8,128)(2,1)S(1)} %fusion.17, bf16[1,256,512]{2,1,0:T(8,128)(2,1)S(1)} %fusion.16), kind=kLoop, calls=%fused_computation.18 | loop fusion | flops 1048576 | bytes 1048576 | tf_op jit(solution)/shard_map/concatenate | solution.py:154
  (39 shorter events, 1.3 us)
Async XLA Ops:
  0.0 20.9 %copy-start.1 = (s32[1,256]{1,0:T(1,128)S(1)}, s32[1,256]{1,0:T(1,128)}, u32[]{:S(2)}) copy-start(s32[1,256]{1,0:T(1,128)} %param.6) | copy-start | bytes 3076
  1.8 16.8 %collective-permute-start.5 = (bf16[256,3,128]{2,0,1:T(8,128)(2,1)S(1)}, bf16[256,3,128]{2,0,1:T(8,128)(2,1)S(1)}, u32[]{:S(2)}, u32[]{:S(2)}) collective-permute-start(bf16[256,3,128]{2,0,1:T(8,128)(2,1)S(1)} %pad_maximum_fusion.8), channel_id=1, source_target_pairs={{0,8},{4,12},{1,9},{5,13},{2,10},{6,14},{3,11},{7,15},{16,24},{20,... | collective-permute-start | bytes 589832 | tf_op jit(solution)/shard_map/ppermute | solution.py:17
  3.1 17.5 %collective-permute-start.4 = (bf16[256,3,128]{2,0,1:T(8,128)(2,1)S(1)}, bf16[256,3,128]{2,0,1:T(8,128)(2,1)S(1)}, u32[]{:S(2)}, u32[]{:S(2)}) collective-permute-start(bf16[256,3,128]{2,0,1:T(8,128)(2,1)S(1)} %pad_maximum_fusion.8), channel_id=1, source_target_pairs={{0,4},{4,8},{8,12},{1,5},{5,9},{9,13},{2,6},{6,10},{10,14},{3,7},{... | collective-permute-start | bytes 589832 | tf_op jit(solution)/shard_map/ppermute | solution.py:17
  7.7 16.4 %collective-permute-start.3 = (bf16[256,512]{1,0:T(8,128)(2,1)S(1)}, bf16[256,512]{1,0:T(8,128)(2,1)S(1)}, u32[]{:S(2)}, u32[]{:S(2)}) collective-permute-start(bf16[256,512]{1,0:T(8,128)(2,1)S(1)} %get-tuple-element.27), channel_id=1, source_target_pairs={{4,0},{8,4},{12,8},{5,1},{9,5},{13,9},{6,2},{10,6},{14,10},{7,3},{... | collective-permute-start | bytes 786440 | tf_op jit(solution)/shard_map/ppermute | solution.py:119
  11.7 13.7 %collective-permute-start.2 = (bf16[256,512]{1,0:T(8,128)(2,1)S(1)}, bf16[256,512]{1,0:T(8,128)(2,1)S(1)}, u32[]{:S(2)}, u32[]{:S(2)}) collective-permute-start(bf16[256,512]{1,0:T(8,128)(2,1)S(1)} %get-tuple-element.27), channel_id=1, source_target_pairs={{0,4},{4,8},{8,12},{1,5},{5,9},{9,13},{2,6},{6,10},{10,14},{3,7},{... | collective-permute-start | bytes 786440 | tf_op jit(solution)/shard_map/ppermute | solution.py:118
  13.6 11.8 %collective-permute-start.1 = (bf16[256,512]{1,0:T(8,128)(2,1)S(1)}, bf16[256,512]{1,0:T(8,128)(2,1)S(1)}, u32[]{:S(2)}, u32[]{:S(2)}) collective-permute-start(bf16[256,512]{1,0:T(8,128)(2,1)S(1)} %get-tuple-element.28), channel_id=1, source_target_pairs={{4,0},{8,4},{12,8},{5,1},{9,5},{13,9},{6,2},{10,6},{14,10},{7,3},{... | collective-permute-start | bytes 786440 | tf_op jit(solution)/shard_map/ppermute | solution.py:119
  18.7 12.3 %collective-permute-start = (bf16[256,512]{1,0:T(8,128)(2,1)S(1)}, bf16[256,512]{1,0:T(8,128)(2,1)S(1)}, u32[]{:S(2)}, u32[]{:S(2)}) collective-permute-start(bf16[256,512]{1,0:T(8,128)(2,1)S(1)} %get-tuple-element.28), channel_id=1, source_target_pairs={{0,4},{4,8},{8,12},{1,5},{5,9},{9,13},{2,6},{6,10},{10,14},{3,7},{... | collective-permute-start | bytes 786440 | tf_op jit(solution)/shard_map/ppermute | solution.py:118
  23.1 30.0 %copy-start = (bf16[256,1024]{1,0:T(8,128)(2,1)S(1)}, bf16[256,1024]{1,0:T(8,128)(2,1)}, u32[]{:S(2)}) copy-start(bf16[256,1024]{1,0:T(8,128)(2,1)} %param.7) | copy-start | bytes 1572868
  31.0 9.9 %collective-permute-start.10 = (bf16[256,512]{1,0:T(8,128)(2,1)S(1)}, bf16[256,512]{1,0:T(8,128)(2,1)S(1)}, u32[]{:S(2)}, u32[]{:S(2)}) collective-permute-start(bf16[256,512]{1,0:T(8,128)(2,1)S(1)} %collective-permute-done.1), channel_id=1, source_target_pairs={{4,0},{8,4},{5,1},{9,5},{6,2},{10,6},{7,3},{11,7},{20,16},{24,20},... | collective-permute-start | bytes 786440 | tf_op jit(solution)/shard_map/ppermute | solution.py:130
  32.4 10.0 %collective-permute-start.12 = (bf16[256,512]{1,0:T(8,128)(2,1)S(1)}, bf16[256,512]{1,0:T(8,128)(2,1)S(1)}, u32[]{:S(2)}, u32[]{:S(2)}) collective-permute-start(bf16[256,512]{1,0:T(8,128)(2,1)S(1)} %collective-permute-done), channel_id=1, source_target_pairs={{4,8},{8,12},{5,9},{9,13},{6,10},{10,14},{7,11},{11,15},{20,24},{2... | collective-permute-start | bytes 786440 | tf_op jit(solution)/shard_map/ppermute | solution.py:129
  34.3 10.4 %collective-permute-start.6 = (bf16[256,512]{0,1:T(8,128)(2,1)S(1)}, bf16[256,512]{0,1:T(8,128)(2,1)}, u32[]{:S(2)}, u32[]{:S(2)}) collective-permute-start(bf16[256,512]{0,1:T(8,128)(2,1)S(1)} %bitcast.69), channel_id=1, source_target_pairs={{0,16},{16,0},{1,17},{17,1},{2,18},{18,2},{3,19},{19,3},{4,20},{20... | collective-permute-start | bytes 786440 | tf_op jit(solution)/shard_map/ppermute | solution.py:85
  34.9 11.5 %collective-permute-start.14 = (bf16[256,512]{1,0:T(8,128)(2,1)S(1)}, bf16[256,512]{1,0:T(8,128)(2,1)S(1)}, u32[]{:S(2)}, u32[]{:S(2)}) collective-permute-start(bf16[256,512]{1,0:T(8,128)(2,1)S(1)} %collective-permute-done.3), channel_id=1, source_target_pairs={{4,0},{8,4},{5,1},{9,5},{6,2},{10,6},{7,3},{11,7},{20,16},{24,20},... | collective-permute-start | bytes 786440 | tf_op jit(solution)/shard_map/ppermute | solution.py:130
  38.9 9.1 %collective-permute-start.16 = (bf16[256,512]{1,0:T(8,128)(2,1)S(1)}, bf16[256,512]{1,0:T(8,128)(2,1)S(1)}, u32[]{:S(2)}, u32[]{:S(2)}) collective-permute-start(bf16[256,512]{1,0:T(8,128)(2,1)S(1)} %collective-permute-done.2), channel_id=1, source_target_pairs={{4,8},{8,12},{5,9},{9,13},{6,10},{10,14},{7,11},{11,15},{20,24},{2... | collective-permute-start | bytes 786440 | tf_op jit(solution)/shard_map/ppermute | solution.py:129
  40.8 7.9 %collective-permute-start.11 = (bf16[256,512]{1,0:T(8,128)(2,1)S(1)}, bf16[256,512]{1,0:T(8,128)(2,1)S(1)}, u32[]{:S(2)}, u32[]{:S(2)}) collective-permute-start(bf16[256,512]{1,0:T(8,128)(2,1)S(1)} %collective-permute-done.10), channel_id=1, source_target_pairs={{4,0},{5,1},{6,2},{7,3},{20,16},{21,17},{22,18},{23,19}} | collective-permute-start | bytes 786440 | tf_op jit(solution)/shard_map/ppermute | solution.py:130
  42.4 10.8 %collective-permute-start.13 = (bf16[256,512]{1,0:T(8,128)(2,1)S(1)}, bf16[256,512]{1,0:T(8,128)(2,1)S(1)}, u32[]{:S(2)}, u32[]{:S(2)}) collective-permute-start(bf16[256,512]{1,0:T(8,128)(2,1)S(1)} %collective-permute-done.12), channel_id=1, source_target_pairs={{8,12},{9,13},{10,14},{11,15},{24,28},{25,29},{26,30},{27,31}} | collective-permute-start | bytes 786440 | tf_op jit(solution)/shard_map/ppermute | solution.py:129
  45.7 19.5 %collective-permute-start.8 = (bf16[256,1024]{0,1:T(8,128)(2,1)S(1)}, bf16[256,1024]{0,1:T(8,128)(2,1)S(1)}, u32[]{:S(2)}, u32[]{:S(2)}) collective-permute-start(bf16[256,1024]{0,1:T(8,128)(2,1)S(1)} %constant_dynamic-update-slice_fusion), channel_id=1, source_target_pairs={{0,1},{1,0},{18,19},{19,18},{4,5},{5,4},{22,23},{23,22},{8,9},{9,8... | collective-permute-start | bytes 1572872 | tf_op jit(solution)/shard_map/ppermute | solution.py:89
  46.4 16.6 %collective-permute-start.7 = (bf16[256,1024]{0,1:T(8,128)(2,1)S(1)}, bf16[256,1024]{0,1:T(8,128)(2,1)S(1)}, u32[]{:S(2)}, u32[]{:S(2)}) collective-permute-start(bf16[256,1024]{0,1:T(8,128)(2,1)S(1)} %constant_dynamic-update-slice_fusion), channel_id=1, source_target_pairs={{0,2},{1,3},{18,16},{19,17},{4,6},{5,7},{22,20},{23,21},{8,10},{9,... | collective-permute-start | bytes 1572872 | tf_op jit(solution)/shard_map/ppermute | solution.py:89
  48.0 5.3 %collective-permute-start.15 = (bf16[256,512]{1,0:T(8,128)(2,1)S(1)}, bf16[256,512]{1,0:T(8,128)(2,1)S(1)}, u32[]{:S(2)}, u32[]{:S(2)}) collective-permute-start(bf16[256,512]{1,0:T(8,128)(2,1)S(1)} %collective-permute-done.14), channel_id=1, source_target_pairs={{4,0},{5,1},{6,2},{7,3},{20,16},{21,17},{22,18},{23,19}} | collective-permute-start | bytes 786440 | tf_op jit(solution)/shard_map/ppermute | solution.py:130
  48.7 8.4 %collective-permute-start.17 = (bf16[256,512]{1,0:T(8,128)(2,1)S(1)}, bf16[256,512]{1,0:T(8,128)(2,1)S(1)}, u32[]{:S(2)}, u32[]{:S(2)}) collective-permute-start(bf16[256,512]{1,0:T(8,128)(2,1)S(1)} %collective-permute-done.16), channel_id=1, source_target_pairs={{8,12},{9,13},{10,14},{11,15},{24,28},{25,29},{26,30},{27,31}} | collective-permute-start | bytes 786440 | tf_op jit(solution)/shard_map/ppermute | solution.py:129
  63.0 3.8 %collective-permute-start.9 = (bf16[256,1024]{0,1:T(8,128)(2,1)S(1)}, bf16[256,1024]{0,1:T(8,128)(2,1)S(1)}, u32[]{:S(2)}, u32[]{:S(2)}) collective-permute-start(bf16[256,1024]{0,1:T(8,128)(2,1)S(1)} %collective-permute-done.7), channel_id=1, source_target_pairs={{2,3},{3,2},{16,17},{17,16},{6,7},{7,6},{20,21},{21,20},{10,11},{1... | collective-permute-start | bytes 1572872 | tf_op jit(solution)/shard_map/ppermute | solution.py:89
  68.0 9.2 %collective-permute-start.18 = (bf16[256,512]{1,0:T(8,128)(2,1)S(1)}, bf16[256,512]{1,0:T(8,128)(2,1)S(1)}, u32[]{:S(2)}, u32[]{:S(2)}) collective-permute-start(bf16[256,512]{1,0:T(8,128)(2,1)S(1)} %convolution_convert_fusion.1), channel_id=1, source_target_pairs={{0,16},{16,0},{1,17},{17,1},{2,18},{18,2},{3,19},{19,3},{4,20},{20... | collective-permute-start | bytes 786440 | tf_op jit(solution)/shard_map/ppermute | solution.py:85
  68.1 14.0 %collective-permute-start.19 = (bf16[256,512]{1,0:T(8,128)(2,1)S(1)}, bf16[256,512]{1,0:T(8,128)(2,1)S(1)}, u32[]{:S(2)}, u32[]{:S(2)}) collective-permute-start(bf16[256,512]{1,0:T(8,128)(2,1)S(1)} %convolution_convert_fusion), channel_id=1, source_target_pairs={{0,16},{16,0},{1,17},{17,1},{2,18},{18,2},{3,19},{19,3},{4,20},{20... | collective-permute-start | bytes 786440 | tf_op jit(solution)/shard_map/ppermute | solution.py:85

commit v18 on v10

--- a/solution.py
+++ b/solution.py
@@ -113,28 +113,24 @@
     return own_full, foreign_full
 
 
-def first_hop(block, axis):
+def ring_step(block, axis):
     count = lax.axis_size(axis)
-    rising = lax.ppermute(block, axis, [(i, i + 1) for i in range(count - 1)])
-    falling = lax.ppermute(block, axis, [(i, i - 1) for i in range(1, count)])
-    return rising, falling
+    return lax.ppermute(block, axis, [(i, (i + 1) % count) for i in range(count)])
 
 
 def line_rows(block, first, axis):
     count = lax.axis_size(axis)
     here = lax.axis_index(axis)
-    rising, falling = first
-    arrivals = [(block, 0), (rising, -1), (falling, 1)]
+    arrivals = [(block, 0), (first, 1)]
+    carried = first
     for step in range(2, count):
-        rising = lax.ppermute(rising, axis, [(i, i + 1) for i in range(step - 1, count - 1)])
-        falling = lax.ppermute(falling, axis, [(i, i - 1) for i in range(1, count - step + 1)])
-        arrivals.append((rising, -step))
-        arrivals.append((falling, step))
+        carried = ring_step(carried, axis)
+        arrivals.append((carried, step))
     ordered = []
     for place in range(count):
         chosen = jnp.zeros_like(block)
-        for arrived, offset in arrivals:
-            chosen = jnp.where(here + offset == place, arrived, chosen)
+        for arrived, back in arrivals:
+            chosen = jnp.where((here - back) % count == place, arrived, chosen)
         ordered.append(chosen)
     return jnp.concatenate(ordered, axis=0)
 
@@ -156,7 +152,7 @@
     side_width = block_rows * lax.axis_size("ctx")
     fits = lax.axis_size("tensor") == 4
     if lax.axis_size("dp") == 2 and side_width == 2 * width and fits:
-        first = first_hop(output_weight, "ctx")
+        first = ring_step(output_weight, "ctx")
         head_values = attention(queries, keyvals, documents)
         first, head_values = lax.optimization_barrier((first, head_values))
         side_rows = line_rows(output_weight, first, "ctx")

time: 80.7 us -> 75.6 us (0.937)
  the two profiles are of different devices: /device:TPU:12 before, /device:TPU:0 now
where the time goes in v18:
time: 75.6 us; the launch traced here: 75.3 us
  waiting for transfers between devices  37.6 us (50%)
  starting transfers between devices  26.7 us (35%)
  other arithmetic  5.45 us (7%)
  matrix products  3.04 us (4%)
  local copies, waits for them, and re-layouts  2.17 us (3%)
    ppermute x2, waiting for transfers between devices, swapped(): return lax.ppermute(block, axis, [(0, 1), (1, 0)])  16.9 us
    ppermute x3, waiting for transfers between devices, ring_step(): lax.ppermute(block, axis, [(i, (i + 1) % count) for i in range(count)])  10.3 us
    ppermute x2, starting transfers between devices, shifted(): return lax.ppermute(block, axis, route)  9.44 us
    ppermute x3, starting transfers between devices, ring_step(): lax.ppermute(block, axis, [(i, (i + 1) % count) for i in range(count)])  8.17 us
    ppermute x3, starting transfers between devices, sent(): return lax.ppermute(block, ('dp', 'tensor'), route)  6.05 us
    ppermute x3, waiting for transfers between devices, sent(): return lax.ppermute(block, ('dp', 'tensor'), route)  5.8 us
    ppermute x2, waiting for transfers between devices, shifted(): return lax.ppermute(block, axis, route)  4.68 us
    ppermute x2, starting transfers between devices, swapped(): return lax.ppermute(block, axis, [(0, 1), (1, 0)])  3.05 us
  transfers between devices with their start and end apart: 10, of which 7 were waited for; matrix products, arithmetic and copies ran while one was open for 9% of the time, Pallas kernels for 0%

profile of v18, /device:TPU:0, one launch (start us, length us, event | category | flops | bytes accessed | tf_op | source)
XLA Modules:
  0.0 75.3 jit_solution(8814866725381127283)
XLA Ops:
  0.0 0.7 convert_element_type.37
  0.7 0.9 %copy.21 = bf16[1,256,2,128]{3,1,2,0:T(8,128)(2,1)S(1)} copy(bf16[1,256,2,128]{3,2,1,0:T(2,128)(2,1)} %param.5) | data formatting | bytes 262144 | tf_op args[1]
  1.6 0.1 broadcast_in_dim.27
  1.7 6.0 %collective-permute-start.2 = (bf16[256,3,128]{2,0,1:T(8,128)(2,1)S(1)}, bf16[256,3,128]{2,0,1:T(8,128)(2,1)S(1)}, u32[]{:S(2)}, u32[]{:S(2)}) collective-permute-start(bf16[256,3,128]{2,0,1:T(8,128)(2,1)S(1)} %pad_maximum_fusion.3), channel_id=1, source_target_pairs={{0,8},{4,12},{1,9},{5,13},{2,10},{6,14},{3,11},{7,15},{16,24},{20,... | collective-permute-start | bytes 589832 | tf_op jit(solution)/shard_map/ppermute | solution.py:17
  7.7 3.5 %collective-permute-start.1 = (bf16[256,3,128]{2,0,1:T(8,128)(2,1)S(1)}, bf16[256,3,128]{2,0,1:T(8,128)(2,1)S(1)}, u32[]{:S(2)}, u32[]{:S(2)}) collective-permute-start(bf16[256,3,128]{2,0,1:T(8,128)(2,1)S(1)} %pad_maximum_fusion.3), channel_id=1, source_target_pairs={{0,4},{4,8},{8,12},{1,5},{5,9},{9,13},{2,6},{6,10},{10,14},{3,7},{... | collective-permute-start | bytes 589832 | tf_op jit(solution)/shard_map/ppermute | solution.py:17
  11.2 0.1 collective-permute-start
  11.3 1.0 %reshape.68 = bf16[256,4,128]{2,1,0:T(4,128)(2,1)S(1)} reshape(bf16[1,256,512]{2,1,0:T(8,128)(2,1)} %param.4) | data formatting | bytes 524288 | tf_op jit(solution)/shard_map/reshape.3
  12.4 0.5 collective-permute-done.2
  12.9 4.2 %collective-permute-done.1 = bf16[256,3,128]{2,0,1:T(8,128)(2,1)S(1)} collective-permute-done((bf16[256,3,128]{2,0,1:T(8,128)(2,1)S(1)}, bf16[256,3,128]{2,0,1:T(8,128)(2,1)S(1)}, u32[]{:S(2)}, u32[]{:S(2)}) %collective-permute-start.1) | collective-permute-done | bytes 196640 | tf_op jit(solution)/shard_map/ppermute | solution.py:17
  17.1 0.1 convert_reduce_fusion
  17.2 0.1 convert_reduce_fusion.1
  17.3 0.7 pad_add_fusion
  18.0 1.4 %and_and_fusion = pred[256,768]{0,1:T(8,128)(4,1)S(1)} fusion(s32[256]{0:T(256)S(1)} %iota_add_fusion.2, s32[256]{0:T(256)} %bitcast.71, s32[768]{0:T(1024)S(1)} %pad_add_fusion.1, s32[768]{0:T(1024)S(1)} %pad_add_fusion, pred[768]{0:T(1024)(128)(4,1)S(1)} %broadcast_compare_fusion), kind=kLoop, calls=%fused_computation.14 | loop fusion | flops 786432 | bytes 205568 | tf_op jit(solution)/shard_map/and | solution.py:64
  19.4 0.6 fusion
  20.1 0.8 %fusion.1 = f32[4,256]{1,0:T(4,128)S(1)} fusion(f32[768,256,4]{1,0,2:T(8,128)S(1)} %get-tuple-element.23, f32[4,256]{1,0:T(4,128)S(1)} %get-tuple-element.22, pred[256,768]{0,1:T(8,128)(4,1)S(1)} %and_and_fusion), kind=kLoop, calls=%fused_computation.3 | loop fusion | flops 3931136 | bytes 3350528 | tf_op jit(solution)/shard_map/reduce_sum | solution.py:71
  20.9 0.0 copy-start
  20.9 0.9 %fusion.13 = bf16[256,1,4,128]{0,3,2,1:T(8,128)(2,1)S(1)} fusion(f32[768,256,4]{1,0,2:T(8,128)S(1)} %get-tuple-element.23, f32[4,256]{1,0:T(4,128)S(1)} %get-tuple-element.22, pred[256,768]{0,1:T(8,128)(4,1)S(1)} %and_and_fusion, f32[256,4]{0,1:T(4,128)S(1)} %bitcast.68, bf16[768,2,128]{2,0,1:T(8,128)(2,1)S(1)} %pad_maximum_fusion.2), kind=kOutput, calls=%fused_computation.13 | convolution fusion | flops 205520896 | bytes 3809280 | tf_op jit(solution)/shard_map/hgqk,khd->qhgd/dot_general | solution.py:72
  21.8 5.6 %collective-permute-done = bf16[256,1024]{1,0:T(8,128)(2,1)S(1)} collective-permute-done((bf16[256,1024]{1,0:T(8,128)(2,1)}, bf16[256,1024]{1,0:T(8,128)(2,1)S(1)}, u32[]{:S(2)}, u32[]{:S(2)}) %collective-permute-start) | collective-permute-done | bytes 524320 | tf_op jit(solution)/shard_map/ppermute | solution.py:118
  27.4 5.7 %collective-permute-start.7 = (bf16[256,1024]{1,0:T(8,128)(2,1)S(1)}, bf16[256,1024]{1,0:T(8,128)(2,1)S(1)}, u32[]{:S(2)}, u32[]{:S(2)}) collective-permute-start(bf16[256,1024]{1,0:T(8,128)(2,1)S(1)} %collective-permute-done), channel_id=1, source_target_pairs={{0,4},{4,8},{8,12},{12,0},{1,5},{5,9},{9,13},{13,1},{2,6},{6,10},{... | collective-permute-start | bytes 1572872 | tf_op jit(solution)/shard_map/ppermute | solution.py:118
  33.1 1.5 %collective-permute-start.3 = (bf16[256,512]{0,1:T(8,128)(2,1)S(1)}, bf16[256,512]{0,1:T(8,128)(2,1)S(1)}, u32[]{:S(2)}, u32[]{:S(2)}) collective-permute-start(bf16[256,512]{0,1:T(8,128)(2,1)S(1)} %bitcast.66), channel_id=1, source_target_pairs={{0,16},{16,0},{1,17},{17,1},{2,18},{18,2},{3,19},{19,3},{4,20},{20... | collective-permute-start | bytes 786440 | tf_op jit(solution)/shard_map/ppermute | solution.py:85
  34.6 6.4 %collective-permute-done.3 = bf16[256,512]{0,1:T(8,128)(2,1)S(1)} collective-permute-done((bf16[256,512]{0,1:T(8,128)(2,1)S(1)}, bf16[256,512]{0,1:T(8,128)(2,1)S(1)}, u32[]{:S(2)}, u32[]{:S(2)}) %collective-permute-start.3) | collective-permute-done | bytes 262176 | tf_op jit(solution)/shard_map/ppermute | solution.py:85
  41.1 3.5 %collective-permute-start.4 = (bf16[256,1024]{0,1:T(8,128)(2,1)S(1)}, bf16[256,1024]{0,1:T(8,128)(2,1)S(1)}, u32[]{:S(2)}, u32[]{:S(2)}) collective-permute-start(bf16[256,1024]{0,1:T(8,128)(2,1)S(1)} %constant_dynamic-update-slice_fusion), channel_id=1, source_target_pairs={{0,2},{1,3},{18,16},{19,17},{4,6},{5,7},{22,20},{23,21},{8,10},{9,... | collective-permute-start | bytes 1572872 | tf_op jit(solution)/shard_map/ppermute | solution.py:89
  44.5 0.0 collective-permute-done.7
  44.6 2.4 %collective-permute-start.8 = (bf16[256,1024]{1,0:T(8,128)(2,1)S(1)}, bf16[256,1024]{1,0:T(8,128)(2,1)S(1)}, u32[]{:S(2)}, u32[]{:S(2)}) collective-permute-start(bf16[256,1024]{1,0:T(8,128)(2,1)S(1)} %collective-permute-done.7), channel_id=1, source_target_pairs={{0,4},{4,8},{8,12},{12,0},{1,5},{5,9},{9,13},{13,1},{2,6},{6,10},{... | collective-permute-start | bytes 1572872 | tf_op jit(solution)/shard_map/ppermute | solution.py:118
  47.0 1.9 %collective-permute-start.5 = (bf16[256,1024]{0,1:T(8,128)(2,1)S(1)}, bf16[256,1024]{0,1:T(8,128)(2,1)S(1)}, u32[]{:S(2)}, u32[]{:S(2)}) collective-permute-start(bf16[256,1024]{0,1:T(8,128)(2,1)S(1)} %constant_dynamic-update-slice_fusion), channel_id=1, source_target_pairs={{0,1},{1,0},{18,19},{19,18},{4,5},{5,4},{22,23},{23,22},{8,9},{9,8... | collective-permute-start | bytes 1572872 | tf_op jit(solution)/shard_map/ppermute | solution.py:89
  48.9 5.8 %collective-permute-done.4 = bf16[256,1024]{0,1:T(8,128)(2,1)S(1)} collective-permute-done((bf16[256,1024]{0,1:T(8,128)(2,1)S(1)}, bf16[256,1024]{0,1:T(8,128)(2,1)S(1)}, u32[]{:S(2)}, u32[]{:S(2)}) %collective-permute-start.4) | collective-permute-done | bytes 524320 | tf_op jit(solution)/shard_map/ppermute | solution.py:89
  54.7 0.7 collective-permute-start.6
  55.4 4.7 %collective-permute-done.8 = bf16[256,1024]{1,0:T(8,128)(2,1)S(1)} collective-permute-done((bf16[256,1024]{1,0:T(8,128)(2,1)S(1)}, bf16[256,1024]{1,0:T(8,128)(2,1)S(1)}, u32[]{:S(2)}, u32[]{:S(2)}) %collective-permute-start.8) | collective-permute-done | bytes 524320 | tf_op jit(solution)/shard_map/ppermute | solution.py:118
  60.1 0.0 copy-done
  60.1 0.1 select_select_fusion.2
  60.2 0.2 select_select_fusion.3
  60.4 0.2 pad_maximum_fusion
  60.6 0.0 collective-permute-done.5
  60.6 0.0 collective-permute-done.6
  60.6 0.1 broadcast_select_fusion.3
  60.8 0.7 convolution_convert_fusion
  61.5 1.6 %collective-permute-start.9 = (bf16[256,1024]{1,0:T(8,128)(2,1)S(1)}, bf16[256,1024]{1,0:T(8,128)(2,1)S(1)}, u32[]{:S(2)}, u32[]{:S(2)}) collective-permute-start(bf16[256,1024]{1,0:T(8,128)(2,1)S(1)} %convolution_convert_fusion), channel_id=1, source_target_pairs={{0,16},{16,0},{1,17},{17,1},{2,18},{18,2},{3,19},{19,3},{4,20},{20... | collective-permute-start | bytes 1572872 | tf_op jit(solution)/shard_map/ppermute | solution.py:85
  63.1 0.7 fusion.28
  63.9 10.5 %collective-permute-done.9 = bf16[256,1024]{1,0:T(8,128)(2,1)S(1)} collective-permute-done((bf16[256,1024]{1,0:T(8,128)(2,1)S(1)}, bf16[256,1024]{1,0:T(8,128)(2,1)S(1)}, u32[]{:S(2)}, u32[]{:S(2)}) %collective-permute-start.9) | collective-permute-done | bytes 524320 | tf_op jit(solution)/shard_map/ppermute | solution.py:85
  74.3 0.9 %fusion.16 = bf16[1,256,1024]{2,1,0:T(8,128)(2,1)} fusion(f32[256,1024]{1,0:T(8,128)S(1)} %fusion.28, bf16[256,1024]{1,0:T(8,128)(2,1)S(1)} %collective-permute-done.9), kind=kLoop, calls=%fused_computation.15 | loop fusion | flops 786432 | bytes 2097152 | tf_op jit(solution)/shard_map/broadcast_in_dim | solution.py:160
  (13 shorter events, 0.2 us)
Async XLA Ops:
  1.7 11.1 %collective-permute-start.2 = (bf16[256,3,128]{2,0,1:T(8,128)(2,1)S(1)}, bf16[256,3,128]{2,0,1:T(8,128)(2,1)S(1)}, u32[]{:S(2)}, u32[]{:S(2)}) collective-permute-start(bf16[256,3,128]{2,0,1:T(8,128)(2,1)S(1)} %pad_maximum_fusion.3), channel_id=1, source_target_pairs={{0,8},{4,12},{1,9},{5,13},{2,10},{6,14},{3,11},{7,15},{16,24},{20,... | collective-permute-start | bytes 589832 | tf_op jit(solution)/shard_map/ppermute | solution.py:17
  7.7 9.4 %collective-permute-start.1 = (bf16[256,3,128]{2,0,1:T(8,128)(2,1)S(1)}, bf16[256,3,128]{2,0,1:T(8,128)(2,1)S(1)}, u32[]{:S(2)}, u32[]{:S(2)}) collective-permute-start(bf16[256,3,128]{2,0,1:T(8,128)(2,1)S(1)} %pad_maximum_fusion.3), channel_id=1, source_target_pairs={{0,4},{4,8},{8,12},{1,5},{5,9},{9,13},{2,6},{6,10},{10,14},{3,7},{... | collective-permute-start | bytes 589832 | tf_op jit(solution)/shard_map/ppermute | solution.py:17
  11.2 16.2 %collective-permute-start = (bf16[256,1024]{1,0:T(8,128)(2,1)}, bf16[256,1024]{1,0:T(8,128)(2,1)S(1)}, u32[]{:S(2)}, u32[]{:S(2)}) collective-permute-start(bf16[256,1024]{1,0:T(8,128)(2,1)} %param.7), channel_id=1, source_target_pairs={{0,4},{4,8},{8,12},{12,0},{1,5},{5,9},{9,13},{13,1},{2,6},{6,10},{... | collective-permute-start | bytes 1572872 | tf_op jit(solution)/shard_map/ppermute | solution.py:118
  20.9 39.2 %copy-start = (bf16[256,1024]{1,0:T(8,128)(2,1)S(1)}, bf16[256,1024]{1,0:T(8,128)(2,1)}, u32[]{:S(2)}) copy-start(bf16[256,1024]{1,0:T(8,128)(2,1)} %param.7) | copy-start | bytes 1572868
  27.4 17.1 %collective-permute-start.7 = (bf16[256,1024]{1,0:T(8,128)(2,1)S(1)}, bf16[256,1024]{1,0:T(8,128)(2,1)S(1)}, u32[]{:S(2)}, u32[]{:S(2)}) collective-permute-start(bf16[256,1024]{1,0:T(8,128)(2,1)S(1)} %collective-permute-done), channel_id=1, source_target_pairs={{0,4},{4,8},{8,12},{12,0},{1,5},{5,9},{9,13},{13,1},{2,6},{6,10},{... | collective-permute-start | bytes 1572872 | tf_op jit(solution)/shard_map/ppermute | solution.py:118
  33.1 7.9 %collective-permute-start.3 = (bf16[256,512]{0,1:T(8,128)(2,1)S(1)}, bf16[256,512]{0,1:T(8,128)(2,1)S(1)}, u32[]{:S(2)}, u32[]{:S(2)}) collective-permute-start(bf16[256,512]{0,1:T(8,128)(2,1)S(1)} %bitcast.66), channel_id=1, source_target_pairs={{0,16},{16,0},{1,17},{17,1},{2,18},{18,2},{3,19},{19,3},{4,20},{20... | collective-permute-start | bytes 786440 | tf_op jit(solution)/shard_map/ppermute | solution.py:85
  41.1 13.6 %collective-permute-start.4 = (bf16[256,1024]{0,1:T(8,128)(2,1)S(1)}, bf16[256,1024]{0,1:T(8,128)(2,1)S(1)}, u32[]{:S(2)}, u32[]{:S(2)}) collective-permute-start(bf16[256,1024]{0,1:T(8,128)(2,1)S(1)} %constant_dynamic-update-slice_fusion), channel_id=1, source_target_pairs={{0,2},{1,3},{18,16},{19,17},{4,6},{5,7},{22,20},{23,21},{8,10},{9,... | collective-permute-start | bytes 1572872 | tf_op jit(solution)/shard_map/ppermute | solution.py:89
  44.6 15.5 %collective-permute-start.8 = (bf16[256,1024]{1,0:T(8,128)(2,1)S(1)}, bf16[256,1024]{1,0:T(8,128)(2,1)S(1)}, u32[]{:S(2)}, u32[]{:S(2)}) collective-permute-start(bf16[256,1024]{1,0:T(8,128)(2,1)S(1)} %collective-permute-done.7), channel_id=1, source_target_pairs={{0,4},{4,8},{8,12},{12,0},{1,5},{5,9},{9,13},{13,1},{2,6},{6,10},{... | collective-permute-start | bytes 1572872 | tf_op jit(solution)/shard_map/ppermute | solution.py:118
  47.0 13.6 %collective-permute-start.5 = (bf16[256,1024]{0,1:T(8,128)(2,1)S(1)}, bf16[256,1024]{0,1:T(8,128)(2,1)S(1)}, u32[]{:S(2)}, u32[]{:S(2)}) collective-permute-start(bf16[256,1024]{0,1:T(8,128)(2,1)S(1)} %constant_dynamic-update-slice_fusion), channel_id=1, source_target_pairs={{0,1},{1,0},{18,19},{19,18},{4,5},{5,4},{22,23},{23,22},{8,9},{9,8... | collective-permute-start | bytes 1572872 | tf_op jit(solution)/shard_map/ppermute | solution.py:89
  54.7 5.9 %collective-permute-start.6 = (bf16[256,1024]{0,1:T(8,128)(2,1)S(1)}, bf16[256,1024]{0,1:T(8,128)(2,1)S(1)}, u32[]{:S(2)}, u32[]{:S(2)}) collective-permute-start(bf16[256,1024]{0,1:T(8,128)(2,1)S(1)} %collective-permute-done.4), channel_id=1, source_target_pairs={{2,3},{3,2},{16,17},{17,16},{6,7},{7,6},{20,21},{21,20},{10,11},{1... | collective-permute-start | bytes 1572872 | tf_op jit(solution)/shard_map/ppermute | solution.py:89
  61.5 12.8 %collective-permute-start.9 = (bf16[256,1024]{1,0:T(8,128)(2,1)S(1)}, bf16[256,1024]{1,0:T(8,128)(2,1)S(1)}, u32[]{:S(2)}, u32[]{:S(2)}) collective-permute-start(bf16[256,1024]{1,0:T(8,128)(2,1)S(1)} %convolution_convert_fusion), channel_id=1, source_target_pairs={{0,16},{16,0},{1,17},{17,1},{2,18},{18,2},{3,19},{19,3},{4,20},{20... | collective-permute-start | bytes 1572872 | tf_op jit(solution)/shard_map/ppermute | solution.py:85

commit v19 on v18

--- a/solution.py
+++ b/solution.py
@@ -97,13 +97,9 @@
     mine = jnp.concatenate([head_values, foreign], axis=1)
     owners = [(s, 2 * s + k) for s in range(2) for k in range(2)]
     over_y = sent(mine, [(s * group + p, s * group + (p ^ 2)) for s, p in owners])
-    beside = sent(mine, [(s * group + p, s * group + (p ^ 1)) for s, p in owners])
-    relayed = sent(
-        over_y, [(s * group + (p ^ 2), s * group + (p ^ 3)) for s, p in owners]
-    )
     on_owner = me // 2 == side
     same_core = jnp.where(on_owner, mine, over_y)
-    other_core = jnp.where(on_owner, beside, relayed)
+    other_core = lax.ppermute(same_core, "tensor", [(t, t ^ 1) for t in range(group)])
     first_core = me % 2 == 0
     width = head_values.shape[1]
     lower = jnp.where(first_core, same_core, other_core)

time: 75.6 us -> 76 us (level)
  waiting for transfers between devices: 37.6 us -> 41.5 us
  starting transfers between devices: 26.7 us -> 23.3 us
    ppermute x3, waiting for transfers between devices: 10.3 us -> 25 us  [ring_step(): lax.ppermute(block, axis, [(i, (i + 1) % count) for i in range(count)])]
    ppermute x2, waiting for transfers between devices: 16.9 us -> 11.2 us  [swapped(): return lax.ppermute(block, axis, [(0, 1), (1, 0)])]
    ppermute x3 -> x1, waiting for transfers between devices: 5.8 us -> 0.71 us  [sent(): return lax.ppermute(block, ('dp', 'tensor'), route)]
    ppermute x3 -> x1, starting transfers between devices: 6.05 us -> 3.46 us  [sent(): return lax.ppermute(block, ('dp', 'tensor'), route)]
    ppermute x2, starting transfers between devices: 3.05 us -> 2.09 us  [swapped(): return lax.ppermute(block, axis, [(0, 1), (1, 0)])]
  transfers between devices with their start and end apart: 10 -> 9, of which waited for: 7 -> 8; matrix products, arithmetic and copies ran while one was open for 9% -> 9% of each run, Pallas kernels for 0% -> 0%
where the time goes in v19:
time: 76 us; the launch traced here: 75.7 us
  waiting for transfers between devices  41.5 us (55%)
  starting transfers between devices  23.3 us (31%)
  other arithmetic  5.49 us (7%)
  matrix products  3.05 us (4%)
  local copies, waits for them, and re-layouts  2.17 us (3%)
    ppermute x3, waiting for transfers between devices, ring_step(): lax.ppermute(block, axis, [(i, (i + 1) % count) for i in range(count)])  25 us
    ppermute x2, waiting for transfers between devices, swapped(): return lax.ppermute(block, axis, [(0, 1), (1, 0)])  11.2 us
    ppermute x2, starting transfers between devices, shifted(): return lax.ppermute(block, axis, route)  9.44 us
    ppermute x3, starting transfers between devices, ring_step(): lax.ppermute(block, axis, [(i, (i + 1) % count) for i in range(count)])  8.22 us
    ppermute x2, waiting for transfers between devices, shifted(): return lax.ppermute(block, axis, route)  4.58 us
    ppermute x1, starting transfers between devices, sent(): return lax.ppermute(block, ('dp', 'tensor'), route)  3.46 us
    ppermute x2, starting transfers between devices, swapped(): return lax.ppermute(block, axis, [(0, 1), (1, 0)])  2.09 us
  transfers between devices with their start and end apart: 9, of which 8 were waited for; matrix products, arithmetic and copies ran while one was open for 9% of the time, Pallas kernels for 0%

profile of v19, /device:TPU:0, one launch (start us, length us, event | category | flops | bytes accessed | tf_op | source)
XLA Modules:
  0.0 75.7 jit_solution(10960523967678605394)
XLA Ops:
  0.0 0.7 convert_element_type.37
  0.7 0.9 %copy.21 = bf16[1,256,2,128]{3,1,2,0:T(8,128)(2,1)S(1)} copy(bf16[1,256,2,128]{3,2,1,0:T(2,128)(2,1)} %param.5) | data formatting | bytes 262144 | tf_op args[1]
  1.6 0.1 broadcast_in_dim.27
  1.7 6.0 %collective-permute-start.2 = (bf16[256,3,128]{2,0,1:T(8,128)(2,1)S(1)}, bf16[256,3,128]{2,0,1:T(8,128)(2,1)S(1)}, u32[]{:S(2)}, u32[]{:S(2)}) collective-permute-start(bf16[256,3,128]{2,0,1:T(8,128)(2,1)S(1)} %pad_maximum_fusion.3), channel_id=1, source_target_pairs={{0,8},{4,12},{1,9},{5,13},{2,10},{6,14},{3,11},{7,15},{16,24},{20,... | collective-permute-start | bytes 589832 | tf_op jit(solution)/shard_map/ppermute | solution.py:17
  7.7 3.5 %collective-permute-start.1 = (bf16[256,3,128]{2,0,1:T(8,128)(2,1)S(1)}, bf16[256,3,128]{2,0,1:T(8,128)(2,1)S(1)}, u32[]{:S(2)}, u32[]{:S(2)}) collective-permute-start(bf16[256,3,128]{2,0,1:T(8,128)(2,1)S(1)} %pad_maximum_fusion.3), channel_id=1, source_target_pairs={{0,4},{4,8},{8,12},{1,5},{5,9},{9,13},{2,6},{6,10},{10,14},{3,7},{... | collective-permute-start | bytes 589832 | tf_op jit(solution)/shard_map/ppermute | solution.py:17
  11.2 0.1 collective-permute-start
  11.3 1.0 %reshape.68 = bf16[256,4,128]{2,1,0:T(4,128)(2,1)S(1)} reshape(bf16[1,256,512]{2,1,0:T(8,128)(2,1)} %param.4) | data formatting | bytes 524288 | tf_op jit(solution)/shard_map/reshape.3
  12.4 0.5 collective-permute-done.2
  12.8 0.1 convert_reduce_fusion
  13.0 4.1 %collective-permute-done.1 = bf16[256,3,128]{2,0,1:T(8,128)(2,1)S(1)} collective-permute-done((bf16[256,3,128]{2,0,1:T(8,128)(2,1)S(1)}, bf16[256,3,128]{2,0,1:T(8,128)(2,1)S(1)}, u32[]{:S(2)}, u32[]{:S(2)}) %collective-permute-start.1) | collective-permute-done | bytes 196640 | tf_op jit(solution)/shard_map/ppermute | solution.py:17
  17.1 0.1 convert_reduce_fusion.1
  17.2 0.7 pad_add_fusion
  17.9 1.4 %and_and_fusion = pred[256,768]{0,1:T(8,128)(4,1)S(1)} fusion(s32[256]{0:T(256)S(1)} %iota_add_fusion.2, s32[256]{0:T(256)} %bitcast.71, s32[768]{0:T(1024)S(1)} %pad_add_fusion.1, s32[768]{0:T(1024)S(1)} %pad_add_fusion, pred[768]{0:T(1024)(128)(4,1)S(1)} %broadcast_compare_fusion), kind=kLoop, calls=%fused_computation.14 | loop fusion | flops 786432 | bytes 205568 | tf_op jit(solution)/shard_map/and | solution.py:64
  19.4 0.7 fusion
  20.0 0.8 %fusion.1 = f32[4,256]{1,0:T(4,128)S(1)} fusion(f32[768,256,4]{1,0,2:T(8,128)S(1)} %get-tuple-element.23, f32[4,256]{1,0:T(4,128)S(1)} %get-tuple-element.22, pred[256,768]{0,1:T(8,128)(4,1)S(1)} %and_and_fusion), kind=kLoop, calls=%fused_computation.3 | loop fusion | flops 3931136 | bytes 3350528 | tf_op jit(solution)/shard_map/reduce_sum | solution.py:71
  20.8 0.9 %fusion.13 = bf16[256,1,4,128]{0,3,2,1:T(8,128)(2,1)S(1)} fusion(f32[768,256,4]{1,0,2:T(8,128)S(1)} %get-tuple-element.23, f32[4,256]{1,0:T(4,128)S(1)} %get-tuple-element.22, pred[256,768]{0,1:T(8,128)(4,1)S(1)} %and_and_fusion, f32[256,4]{0,1:T(4,128)S(1)} %bitcast.68, bf16[768,2,128]{2,0,1:T(8,128)(2,1)S(1)} %pad_maximum_fusion.2), kind=kOutput, calls=%fused_computation.13 | convolution fusion | flops 205520896 | bytes 3809280 | tf_op jit(solution)/shard_map/hgqk,khd->qhgd/dot_general | solution.py:72
  21.8 0.0 copy-start
  21.8 5.7 %collective-permute-done = bf16[256,1024]{1,0:T(8,128)(2,1)S(1)} collective-permute-done((bf16[256,1024]{1,0:T(8,128)(2,1)}, bf16[256,1024]{1,0:T(8,128)(2,1)S(1)}, u32[]{:S(2)}, u32[]{:S(2)}) %collective-permute-start) | collective-permute-done | bytes 524320 | tf_op jit(solution)/shard_map/ppermute | solution.py:114
  27.4 1.5 %collective-permute-start.3 = (bf16[256,512]{0,1:T(8,128)(2,1)S(1)}, bf16[256,512]{0,1:T(8,128)(2,1)S(1)}, u32[]{:S(2)}, u32[]{:S(2)}) collective-permute-start(bf16[256,512]{0,1:T(8,128)(2,1)S(1)} %bitcast.66), channel_id=1, source_target_pairs={{0,16},{16,0},{1,17},{17,1},{2,18},{18,2},{3,19},{19,3},{4,20},{20... | collective-permute-start | bytes 786440 | tf_op jit(solution)/shard_map/ppermute | solution.py:85
  28.9 5.7 %collective-permute-start.6 = (bf16[256,1024]{1,0:T(8,128)(2,1)S(1)}, bf16[256,1024]{1,0:T(8,128)(2,1)S(1)}, u32[]{:S(2)}, u32[]{:S(2)}) collective-permute-start(bf16[256,1024]{1,0:T(8,128)(2,1)S(1)} %collective-permute-done), channel_id=1, source_target_pairs={{0,4},{4,8},{8,12},{12,0},{1,5},{5,9},{9,13},{13,1},{2,6},{6,10},{... | collective-permute-start | bytes 1572872 | tf_op jit(solution)/shard_map/ppermute | solution.py:114
  34.6 0.2 collective-permute-done.3
  34.8 3.5 %collective-permute-start.4 = (bf16[256,1024]{0,1:T(8,128)(2,1)S(1)}, bf16[256,1024]{0,1:T(8,128)(2,1)S(1)}, u32[]{:S(2)}, u32[]{:S(2)}) collective-permute-start(bf16[256,1024]{0,1:T(8,128)(2,1)S(1)} %constant_dynamic-update-slice_fusion), channel_id=1, source_target_pairs={{0,2},{1,3},{18,16},{19,17},{4,6},{5,7},{22,20},{23,21},{8,10},{9,... | collective-permute-start | bytes 1572872 | tf_op jit(solution)/shard_map/ppermute | solution.py:89
  38.3 7.4 %collective-permute-done.6 = bf16[256,1024]{1,0:T(8,128)(2,1)S(1)} collective-permute-done((bf16[256,1024]{1,0:T(8,128)(2,1)S(1)}, bf16[256,1024]{1,0:T(8,128)(2,1)S(1)}, u32[]{:S(2)}, u32[]{:S(2)}) %collective-permute-start.6) | collective-permute-done | bytes 524320 | tf_op jit(solution)/shard_map/ppermute | solution.py:114
  45.7 2.5 %collective-permute-start.7 = (bf16[256,1024]{1,0:T(8,128)(2,1)S(1)}, bf16[256,1024]{1,0:T(8,128)(2,1)S(1)}, u32[]{:S(2)}, u32[]{:S(2)}) collective-permute-start(bf16[256,1024]{1,0:T(8,128)(2,1)S(1)} %collective-permute-done.6), channel_id=1, source_target_pairs={{0,4},{4,8},{8,12},{12,0},{1,5},{5,9},{9,13},{13,1},{2,6},{6,10},{... | collective-permute-start | bytes 1572872 | tf_op jit(solution)/shard_map/ppermute | solution.py:114
  48.2 0.7 collective-permute-done.4
  48.9 0.1 broadcast_select_fusion
  48.9 0.1 collective-permute-start.5
  49.0 11.9 %collective-permute-done.7 = bf16[256,1024]{1,0:T(8,128)(2,1)S(1)} collective-permute-done((bf16[256,1024]{1,0:T(8,128)(2,1)S(1)}, bf16[256,1024]{1,0:T(8,128)(2,1)S(1)}, u32[]{:S(2)}, u32[]{:S(2)}) %collective-permute-start.7) | collective-permute-done | bytes 524320 | tf_op jit(solution)/shard_map/ppermute | solution.py:114
  61.0 0.0 copy-done
  61.0 0.1 select_select_fusion.2
  61.1 0.2 select_select_fusion.3
  61.3 0.2 pad_maximum_fusion
  61.5 0.0 collective-permute-done.5
  61.5 0.1 broadcast_select_fusion.2
  61.6 0.7 convolution_convert_fusion
  62.4 0.6 collective-permute-start.8
  63.0 0.7 fusion.28
  63.7 11.1 %collective-permute-done.8 = bf16[256,1024]{1,0:T(8,128)(2,1)S(1)} collective-permute-done((bf16[256,1024]{1,0:T(8,128)(2,1)S(1)}, bf16[256,1024]{1,0:T(8,128)(2,1)S(1)}, u32[]{:S(2)}, u32[]{:S(2)}) %collective-permute-start.8) | collective-permute-done | bytes 524320 | tf_op jit(solution)/shard_map/ppermute | solution.py:85
  74.8 0.9 %fusion.16 = bf16[1,256,1024]{2,1,0:T(8,128)(2,1)} fusion(f32[256,1024]{1,0:T(8,128)S(1)} %fusion.28, bf16[256,1024]{1,0:T(8,128)(2,1)S(1)} %collective-permute-done.8), kind=kLoop, calls=%fused_computation.15 | loop fusion | flops 786432 | bytes 2097152 | tf_op jit(solution)/shard_map/broadcast_in_dim | solution.py:156
  (13 shorter events, 0.2 us)
Async XLA Ops:
  1.7 11.1 %collective-permute-start.2 = (bf16[256,3,128]{2,0,1:T(8,128)(2,1)S(1)}, bf16[256,3,128]{2,0,1:T(8,128)(2,1)S(1)}, u32[]{:S(2)}, u32[]{:S(2)}) collective-permute-start(bf16[256,3,128]{2,0,1:T(8,128)(2,1)S(1)} %pad_maximum_fusion.3), channel_id=1, source_target_pairs={{0,8},{4,12},{1,9},{5,13},{2,10},{6,14},{3,11},{7,15},{16,24},{20,... | collective-permute-start | bytes 589832 | tf_op jit(solution)/shard_map/ppermute | solution.py:17
  7.7 9.4 %collective-permute-start.1 = (bf16[256,3,128]{2,0,1:T(8,128)(2,1)S(1)}, bf16[256,3,128]{2,0,1:T(8,128)(2,1)S(1)}, u32[]{:S(2)}, u32[]{:S(2)}) collective-permute-start(bf16[256,3,128]{2,0,1:T(8,128)(2,1)S(1)} %pad_maximum_fusion.3), channel_id=1, source_target_pairs={{0,4},{4,8},{8,12},{1,5},{5,9},{9,13},{2,6},{6,10},{10,14},{3,7},{... | collective-permute-start | bytes 589832 | tf_op jit(solution)/shard_map/ppermute | solution.py:17
  11.2 16.2 %collective-permute-start = (bf16[256,1024]{1,0:T(8,128)(2,1)}, bf16[256,1024]{1,0:T(8,128)(2,1)S(1)}, u32[]{:S(2)}, u32[]{:S(2)}) collective-permute-start(bf16[256,1024]{1,0:T(8,128)(2,1)} %param.7), channel_id=1, source_target_pairs={{0,4},{4,8},{8,12},{12,0},{1,5},{5,9},{9,13},{13,1},{2,6},{6,10},{... | collective-permute-start | bytes 1572872 | tf_op jit(solution)/shard_map/ppermute | solution.py:114
  21.8 39.2 %copy-start = (bf16[256,1024]{1,0:T(8,128)(2,1)S(1)}, bf16[256,1024]{1,0:T(8,128)(2,1)}, u32[]{:S(2)}) copy-start(bf16[256,1024]{1,0:T(8,128)(2,1)} %param.7) | copy-start | bytes 1572868
  27.4 7.4 %collective-permute-start.3 = (bf16[256,512]{0,1:T(8,128)(2,1)S(1)}, bf16[256,512]{0,1:T(8,128)(2,1)S(1)}, u32[]{:S(2)}, u32[]{:S(2)}) collective-permute-start(bf16[256,512]{0,1:T(8,128)(2,1)S(1)} %bitcast.66), channel_id=1, source_target_pairs={{0,16},{16,0},{1,17},{17,1},{2,18},{18,2},{3,19},{19,3},{4,20},{20... | collective-permute-start | bytes 786440 | tf_op jit(solution)/shard_map/ppermute | solution.py:85
  28.9 16.8 %collective-permute-start.6 = (bf16[256,1024]{1,0:T(8,128)(2,1)S(1)}, bf16[256,1024]{1,0:T(8,128)(2,1)S(1)}, u32[]{:S(2)}, u32[]{:S(2)}) collective-permute-start(bf16[256,1024]{1,0:T(8,128)(2,1)S(1)} %collective-permute-done), channel_id=1, source_target_pairs={{0,4},{4,8},{8,12},{12,0},{1,5},{5,9},{9,13},{13,1},{2,6},{6,10},{... | collective-permute-start | bytes 1572872 | tf_op jit(solution)/shard_map/ppermute | solution.py:114
  34.8 14.1 %collective-permute-start.4 = (bf16[256,1024]{0,1:T(8,128)(2,1)S(1)}, bf16[256,1024]{0,1:T(8,128)(2,1)S(1)}, u32[]{:S(2)}, u32[]{:S(2)}) collective-permute-start(bf16[256,1024]{0,1:T(8,128)(2,1)S(1)} %constant_dynamic-update-slice_fusion), channel_id=1, source_target_pairs={{0,2},{1,3},{18,16},{19,17},{4,6},{5,7},{22,20},{23,21},{8,10},{9,... | collective-permute-start | bytes 1572872 | tf_op jit(solution)/shard_map/ppermute | solution.py:89
  45.7 15.3 %collective-permute-start.7 = (bf16[256,1024]{1,0:T(8,128)(2,1)S(1)}, bf16[256,1024]{1,0:T(8,128)(2,1)S(1)}, u32[]{:S(2)}, u32[]{:S(2)}) collective-permute-start(bf16[256,1024]{1,0:T(8,128)(2,1)S(1)} %collective-permute-done.6), channel_id=1, source_target_pairs={{0,4},{4,8},{8,12},{12,0},{1,5},{5,9},{9,13},{13,1},{2,6},{6,10},{... | collective-permute-start | bytes 1572872 | tf_op jit(solution)/shard_map/ppermute | solution.py:114
  48.9 12.5 %collective-permute-start.5 = (bf16[256,1024]{0,1:T(8,128)(2,1)S(1)}, bf16[256,1024]{0,1:T(8,128)(2,1)S(1)}, u32[]{:S(2)}, u32[]{:S(2)}) collective-permute-start(bf16[256,1024]{0,1:T(8,128)(2,1)S(1)} %broadcast_select_fusion), channel_id=1, source_target_pairs={{0,1},{1,0},{2,3},{3,2},{4,5},{5,4},{6,7},{7,6},{8,9},{9,8},{10,11... | collective-permute-start | bytes 1572872 | tf_op jit(solution)/shard_map/ppermute | solution.py:102
  62.4 12.4 %collective-permute-start.8 = (bf16[256,1024]{1,0:T(8,128)(2,1)S(1)}, bf16[256,1024]{1,0:T(8,128)(2,1)S(1)}, u32[]{:S(2)}, u32[]{:S(2)}) collective-permute-start(bf16[256,1024]{1,0:T(8,128)(2,1)S(1)} %convolution_convert_fusion), channel_id=1, source_target_pairs={{0,16},{16,0},{1,17},{17,1},{2,18},{18,2},{3,19},{19,3},{4,20},{20... | collective-permute-start | bytes 1572872 | tf_op jit(solution)/shard_map/ppermute | solution.py:85

commit v20 on v18

--- a/solution.py
+++ b/solution.py
@@ -23,7 +23,7 @@
     return lax.ppermute(block, axis, route)
 
 
-def attention(queries, keyvals, documents):
+def attention(queries, keyvals, documents, anchor):
     length = queries.shape[1]
     pair_width = keyvals.shape[3]
     pair_heads = pair_width // HEAD_DIM
@@ -46,6 +46,7 @@
         label_blocks.append(arrived[:, 2, 0].astype(jnp.int32))
         place_blocks.append((position - hop) * length + offsets)
     pairs = jnp.concatenate(pair_blocks, axis=0)
+    pairs, anchor = lax.optimization_barrier((pairs, anchor))
     key_labels = jnp.concatenate(label_blocks, axis=0)
     key_place = jnp.concatenate(place_blocks, axis=0)
     key_count = pairs.shape[0]
@@ -76,9 +77,8 @@
         preferred_element_type=jnp.float32,
     )
     head_values = summed / jnp.transpose(total, (2, 0, 1))[..., None]
-    return head_values.reshape(length, pair_heads * query_group_size * HEAD_DIM).astype(
-        jnp.bfloat16
-    )
+    head_values = head_values.reshape(length, pair_heads * query_group_size * HEAD_DIM)
+    return head_values.astype(jnp.bfloat16), anchor
 
 
 def swapped(block, axis):
@@ -153,13 +153,12 @@
     fits = lax.axis_size("tensor") == 4
     if lax.axis_size("dp") == 2 and side_width == 2 * width and fits:
         first = ring_step(output_weight, "ctx")
-        head_values = attention(queries, keyvals, documents)
-        first, head_values = lax.optimization_barrier((first, head_values))
+        head_values, first = attention(queries, keyvals, documents, first)
         side_rows = line_rows(output_weight, first, "ctx")
         result = split_projection(head_values, side_rows)
         return result.astype(jnp.bfloat16)[None]
     all_rows = lax.all_gather(output_weight, ("dp", "ctx"), axis=0, tiled=True)
-    head_values = attention(queries, keyvals, documents)
+    head_values, _ = attention(queries, keyvals, documents, ())
     group = lax.axis_size("tensor")
     me = lax.axis_index("tensor")
     result = None

time: 75.6 us -> 79.4 us (1.050)
  waiting for transfers between devices: 37.6 us -> 39.8 us
  starting transfers between devices: 26.7 us -> 28.2 us
    ppermute x3, waiting for transfers between devices: 10.3 us -> 12.2 us  [ring_step(): lax.ppermute(block, axis, [(i, (i + 1) % count) for i in range(count)])]
    ppermute x2, waiting for transfers between devices: 16.9 us -> 17.9 us  [swapped(): return lax.ppermute(block, axis, [(0, 1), (1, 0)])]
    ppermute x2, starting transfers between devices: 3.05 us -> 3.85 us  [swapped(): return lax.ppermute(block, axis, [(0, 1), (1, 0)])]
where the time goes in v20:
time: 79.4 us; the launch traced here: 79.1 us
  waiting for transfers between devices  39.8 us (50%)
  starting transfers between devices  28.2 us (36%)
  other arithmetic  5.72 us (7%)
  matrix products  3.04 us (4%)
  local copies, waits for them, and re-layouts  2.13 us (3%)
    ppermute x2, waiting for transfers between devices, swapped(): return lax.ppermute(block, axis, [(0, 1), (1, 0)])  17.9 us
    ppermute x3, waiting for transfers between devices, ring_step(): lax.ppermute(block, axis, [(i, (i + 1) % count) for i in range(count)])  12.2 us
    ppermute x2, starting transfers between devices, shifted(): return lax.ppermute(block, axis, route)  9.44 us
    ppermute x3, starting transfers between devices, ring_step(): lax.ppermute(block, axis, [(i, (i + 1) % count) for i in range(count)])  8.11 us
    ppermute x3, starting transfers between devices, sent(): return lax.ppermute(block, ('dp', 'tensor'), route)  6.81 us
    ppermute x3, waiting for transfers between devices, sent(): return lax.ppermute(block, ('dp', 'tensor'), route)  5.12 us
    ppermute x2, waiting for transfers between devices, shifted(): return lax.ppermute(block, axis, route)  4.56 us
    ppermute x2, starting transfers between devices, swapped(): return lax.ppermute(block, axis, [(0, 1), (1, 0)])  3.85 us
  transfers between devices with their start and end apart: 10, of which 7 were waited for; matrix products, arithmetic and copies ran while one was open for 9% of the time, Pallas kernels for 0%

profile of v20, /device:TPU:0, one launch (start us, length us, event | category | flops | bytes accessed | tf_op | source)
XLA Modules:
  0.0 79.1 jit_solution(17800931290555472687)
XLA Ops:
  0.0 0.7 convert_element_type.37
  0.7 0.9 %copy.21 = bf16[1,256,2,128]{3,1,2,0:T(8,128)(2,1)S(1)} copy(bf16[1,256,2,128]{3,2,1,0:T(2,128)(2,1)} %param.5) | data formatting | bytes 262144 | tf_op args[1]
  1.6 0.1 broadcast_in_dim.27
  1.7 6.0 %collective-permute-start.1 = (bf16[256,3,128]{2,0,1:T(8,128)(2,1)S(1)}, bf16[256,3,128]{2,0,1:T(8,128)(2,1)S(1)}, u32[]{:S(2)}, u32[]{:S(2)}) collective-permute-start(bf16[256,3,128]{2,0,1:T(8,128)(2,1)S(1)} %pad_maximum_fusion.4), channel_id=1, source_target_pairs={{0,8},{4,12},{1,9},{5,13},{2,10},{6,14},{3,11},{7,15},{16,24},{20,... | collective-permute-start | bytes 589832 | tf_op jit(solution)/shard_map/ppermute | solution.py:17
  7.7 3.5 %collective-permute-start = (bf16[256,3,128]{2,0,1:T(8,128)(2,1)S(1)}, bf16[256,3,128]{2,0,1:T(8,128)(2,1)S(1)}, u32[]{:S(2)}, u32[]{:S(2)}) collective-permute-start(bf16[256,3,128]{2,0,1:T(8,128)(2,1)S(1)} %pad_maximum_fusion.4), channel_id=1, source_target_pairs={{0,4},{4,8},{8,12},{1,5},{5,9},{9,13},{2,6},{6,10},{10,14},{3,7},{... | collective-permute-start | bytes 589832 | tf_op jit(solution)/shard_map/ppermute | solution.py:17
  11.2 0.1 collective-permute-start.2
  11.3 1.0 %reshape.68 = bf16[256,4,128]{2,1,0:T(4,128)(2,1)S(1)} reshape(bf16[1,256,512]{2,1,0:T(8,128)(2,1)} %param.4) | data formatting | bytes 524288 | tf_op jit(solution)/shard_map/reshape.3
  12.4 0.5 collective-permute-done.1
  12.9 0.1 convert_reduce_fusion
  13.0 4.1 %collective-permute-done = bf16[256,3,128]{2,0,1:T(8,128)(2,1)S(1)} collective-permute-done((bf16[256,3,128]{2,0,1:T(8,128)(2,1)S(1)}, bf16[256,3,128]{2,0,1:T(8,128)(2,1)S(1)}, u32[]{:S(2)}, u32[]{:S(2)}) %collective-permute-start) | collective-permute-done | bytes 196640 | tf_op jit(solution)/shard_map/ppermute | solution.py:17
  17.1 0.1 convert_reduce_fusion.1
  17.2 0.7 pad_add_fusion
  17.9 1.4 %and_and_fusion = pred[256,768]{0,1:T(8,128)(4,1)S(1)} fusion(s32[256]{0:T(256)S(1)} %iota_add_fusion.2, s32[256]{0:T(256)} %bitcast.72, s32[768]{0:T(1024)S(1)} %pad_add_fusion.1, s32[768]{0:T(1024)S(1)} %pad_add_fusion, pred[768]{0:T(1024)(128)(4,1)S(1)} %broadcast_compare_fusion), kind=kLoop, calls=%fused_computation.14 | loop fusion | flops 786432 | bytes 205568 | tf_op jit(solution)/shard_map/and | solution.py:65
  19.3 8.1 %collective-permute-done.2 = bf16[256,1024]{1,0:T(8,128)(2,1)S(1)} collective-permute-done((bf16[256,1024]{1,0:T(8,128)(2,1)}, bf16[256,1024]{1,0:T(8,128)(2,1)S(1)}, u32[]{:S(2)}, u32[]{:S(2)}) %collective-permute-start.2) | collective-permute-done | bytes 524320 | tf_op jit(solution)/shard_map/ppermute | solution.py:118
  27.4 5.7 %collective-permute-start.7 = (bf16[256,1024]{1,0:T(8,128)(2,1)S(1)}, bf16[256,1024]{1,0:T(8,128)(2,1)S(1)}, u32[]{:S(2)}, u32[]{:S(2)}) collective-permute-start(bf16[256,1024]{1,0:T(8,128)(2,1)S(1)} %collective-permute-done.2), channel_id=1, source_target_pairs={{0,4},{4,8},{8,12},{12,0},{1,5},{5,9},{9,13},{13,1},{2,6},{6,10},{... | collective-permute-start | bytes 1572872 | tf_op jit(solution)/shard_map/ppermute | solution.py:118
  33.1 0.6 fusion
  33.8 0.8 %fusion.1 = f32[4,256]{1,0:T(4,128)S(1)} fusion(f32[768,256,4]{1,0,2:T(8,128)S(1)} %get-tuple-element.23, f32[4,256]{1,0:T(4,128)S(1)} %get-tuple-element.22, pred[256,768]{0,1:T(8,128)(4,1)S(1)} %and_and_fusion), kind=kLoop, calls=%fused_computation.3 | loop fusion | flops 3931136 | bytes 3350528 | tf_op jit(solution)/shard_map/reduce_sum | solution.py:72
  34.6 0.0 copy-start
  34.6 0.9 %fusion.13 = bf16[256,1,4,128]{0,3,2,1:T(8,128)(2,1)S(1)} fusion(f32[768,256,4]{1,0,2:T(8,128)S(1)} %get-tuple-element.23, f32[4,256]{1,0:T(4,128)S(1)} %get-tuple-element.22, pred[256,768]{0,1:T(8,128)(4,1)S(1)} %and_and_fusion, f32[256,4]{0,1:T(4,128)S(1)} %bitcast.69, bf16[768,2,128]{2,0,1:T(8,128)(2,1)S(1)} %pad_maximum_fusion.3), kind=kOutput, calls=%fused_computation.13 | convolution fusion | flops 205520896 | bytes 3809280 | tf_op jit(solution)/shard_map/hgqk,khd->qhgd/dot_general | solution.py:73
  35.5 1.6 %collective-permute-start.3 = (bf16[256,512]{0,1:T(8,128)(2,1)S(1)}, bf16[256,512]{0,1:T(8,128)(2,1)S(1)}, u32[]{:S(2)}, u32[]{:S(2)}) collective-permute-start(bf16[256,512]{0,1:T(8,128)(2,1)S(1)} %bitcast.66), channel_id=1, source_target_pairs={{0,16},{16,0},{1,17},{17,1},{2,18},{18,2},{3,19},{19,3},{4,20},{20... | collective-permute-start | bytes 786440 | tf_op jit(solution)/shard_map/ppermute | solution.py:85
  37.1 6.5 %collective-permute-done.3 = bf16[256,512]{0,1:T(8,128)(2,1)S(1)} collective-permute-done((bf16[256,512]{0,1:T(8,128)(2,1)S(1)}, bf16[256,512]{0,1:T(8,128)(2,1)S(1)}, u32[]{:S(2)}, u32[]{:S(2)}) %collective-permute-start.3) | collective-permute-done | bytes 262176 | tf_op jit(solution)/shard_map/ppermute | solution.py:85
  43.6 4.2 %collective-permute-start.4 = (bf16[256,1024]{0,1:T(8,128)(2,1)S(1)}, bf16[256,1024]{0,1:T(8,128)(2,1)}, u32[]{:S(2)}, u32[]{:S(2)}) collective-permute-start(bf16[256,1024]{0,1:T(8,128)(2,1)S(1)} %pad_maximum_fusion.1), channel_id=1, source_target_pairs={{0,2},{1,3},{18,16},{19,17},{4,6},{5,7},{22,20},{23,21},{8,10},{9,... | collective-permute-start | bytes 1572872 | tf_op jit(solution)/shard_map/ppermute | solution.py:89
  47.8 0.0 collective-permute-done.7
  47.8 2.4 %collective-permute-start.8 = (bf16[256,1024]{1,0:T(8,128)(2,1)S(1)}, bf16[256,1024]{1,0:T(8,128)(2,1)S(1)}, u32[]{:S(2)}, u32[]{:S(2)}) collective-permute-start(bf16[256,1024]{1,0:T(8,128)(2,1)S(1)} %collective-permute-done.7), channel_id=1, source_target_pairs={{0,4},{4,8},{8,12},{12,0},{1,5},{5,9},{9,13},{13,1},{2,6},{6,10},{... | collective-permute-start | bytes 1572872 | tf_op jit(solution)/shard_map/ppermute | solution.py:118
  50.2 1.9 %collective-permute-start.5 = (bf16[256,1024]{0,1:T(8,128)(2,1)S(1)}, bf16[256,1024]{0,1:T(8,128)(2,1)S(1)}, u32[]{:S(2)}, u32[]{:S(2)}) collective-permute-start(bf16[256,1024]{0,1:T(8,128)(2,1)S(1)} %pad_maximum_fusion.1), channel_id=1, source_target_pairs={{0,1},{1,0},{18,19},{19,18},{4,5},{5,4},{22,23},{23,22},{8,9},{9,8... | collective-permute-start | bytes 1572872 | tf_op jit(solution)/shard_map/ppermute | solution.py:89
  52.1 5.1 %collective-permute-done.4 = bf16[256,1024]{0,1:T(8,128)(2,1)} collective-permute-done((bf16[256,1024]{0,1:T(8,128)(2,1)S(1)}, bf16[256,1024]{0,1:T(8,128)(2,1)}, u32[]{:S(2)}, u32[]{:S(2)}) %collective-permute-start.4) | collective-permute-done | bytes 524320 | tf_op jit(solution)/shard_map/ppermute | solution.py:89
  57.2 0.7 collective-permute-start.6
  57.9 4.1 %collective-permute-done.8 = bf16[256,1024]{1,0:T(8,128)(2,1)S(1)} collective-permute-done((bf16[256,1024]{1,0:T(8,128)(2,1)S(1)}, bf16[256,1024]{1,0:T(8,128)(2,1)S(1)}, u32[]{:S(2)}, u32[]{:S(2)}) %collective-permute-start.8) | collective-permute-done | bytes 524320 | tf_op jit(solution)/shard_map/ppermute | solution.py:118
  62.0 0.0 copy-done
  62.0 0.1 select_select_fusion.2
  62.1 0.2 select_select_fusion.3
  62.3 0.2 pad_maximum_fusion
  62.5 0.0 collective-permute-done.5
  62.5 0.0 collective-permute-done.6
  62.5 0.3 broadcast_select_fusion.3
  63.0 0.7 convolution_convert_fusion
  63.7 2.3 %collective-permute-start.9 = (bf16[256,1024]{1,0:T(8,128)(2,1)S(1)}, bf16[256,1024]{1,0:T(8,128)(2,1)S(1)}, u32[]{:S(2)}, u32[]{:S(2)}) collective-permute-start(bf16[256,1024]{1,0:T(8,128)(2,1)S(1)} %convolution_convert_fusion), channel_id=1, source_target_pairs={{0,16},{16,0},{1,17},{17,1},{2,18},{18,2},{3,19},{19,3},{4,20},{20... | collective-permute-start | bytes 1572872 | tf_op jit(solution)/shard_map/ppermute | solution.py:85
  66.0 0.7 fusion.32
  66.7 11.5 %collective-permute-done.9 = bf16[256,1024]{1,0:T(8,128)(2,1)S(1)} collective-permute-done((bf16[256,1024]{1,0:T(8,128)(2,1)S(1)}, bf16[256,1024]{1,0:T(8,128)(2,1)S(1)}, u32[]{:S(2)}, u32[]{:S(2)}) %collective-permute-start.9) | collective-permute-done | bytes 524320 | tf_op jit(solution)/shard_map/ppermute | solution.py:85
  78.2 0.9 %fusion.16 = bf16[1,256,1024]{2,1,0:T(8,128)(2,1)} fusion(f32[256,1024]{1,0:T(8,128)S(1)} %fusion.32, bf16[256,1024]{1,0:T(8,128)(2,1)S(1)} %collective-permute-done.9), kind=kLoop, calls=%fused_computation.15 | loop fusion | flops 786432 | bytes 2097152 | tf_op jit(solution)/shard_map/broadcast_in_dim | solution.py:159
  (12 shorter events, 0.2 us)
Async XLA Ops:
  1.7 11.1 %collective-permute-start.1 = (bf16[256,3,128]{2,0,1:T(8,128)(2,1)S(1)}, bf16[256,3,128]{2,0,1:T(8,128)(2,1)S(1)}, u32[]{:S(2)}, u32[]{:S(2)}) collective-permute-start(bf16[256,3,128]{2,0,1:T(8,128)(2,1)S(1)} %pad_maximum_fusion.4), channel_id=1, source_target_pairs={{0,8},{4,12},{1,9},{5,13},{2,10},{6,14},{3,11},{7,15},{16,24},{20,... | collective-permute-start | bytes 589832 | tf_op jit(solution)/shard_map/ppermute | solution.py:17
  7.7 9.4 %collective-permute-start = (bf16[256,3,128]{2,0,1:T(8,128)(2,1)S(1)}, bf16[256,3,128]{2,0,1:T(8,128)(2,1)S(1)}, u32[]{:S(2)}, u32[]{:S(2)}) collective-permute-start(bf16[256,3,128]{2,0,1:T(8,128)(2,1)S(1)} %pad_maximum_fusion.4), channel_id=1, source_target_pairs={{0,4},{4,8},{8,12},{1,5},{5,9},{9,13},{2,6},{6,10},{10,14},{3,7},{... | collective-permute-start | bytes 589832 | tf_op jit(solution)/shard_map/ppermute | solution.py:17
  11.2 16.2 %collective-permute-start.2 = (bf16[256,1024]{1,0:T(8,128)(2,1)}, bf16[256,1024]{1,0:T(8,128)(2,1)S(1)}, u32[]{:S(2)}, u32[]{:S(2)}) collective-permute-start(bf16[256,1024]{1,0:T(8,128)(2,1)} %param.7), channel_id=1, source_target_pairs={{0,4},{4,8},{8,12},{12,0},{1,5},{5,9},{9,13},{13,1},{2,6},{6,10},{... | collective-permute-start | bytes 1572872 | tf_op jit(solution)/shard_map/ppermute | solution.py:118
  27.4 20.4 %collective-permute-start.7 = (bf16[256,1024]{1,0:T(8,128)(2,1)S(1)}, bf16[256,1024]{1,0:T(8,128)(2,1)S(1)}, u32[]{:S(2)}, u32[]{:S(2)}) collective-permute-start(bf16[256,1024]{1,0:T(8,128)(2,1)S(1)} %collective-permute-done.2), channel_id=1, source_target_pairs={{0,4},{4,8},{8,12},{12,0},{1,5},{5,9},{9,13},{13,1},{2,6},{6,10},{... | collective-permute-start | bytes 1572872 | tf_op jit(solution)/shard_map/ppermute | solution.py:118
  34.6 27.5 %copy-start = (bf16[256,1024]{1,0:T(8,128)(2,1)S(1)}, bf16[256,1024]{1,0:T(8,128)(2,1)}, u32[]{:S(2)}) copy-start(bf16[256,1024]{1,0:T(8,128)(2,1)} %param.7) | copy-start | bytes 1572868
  35.5 8.0 %collective-permute-start.3 = (bf16[256,512]{0,1:T(8,128)(2,1)S(1)}, bf16[256,512]{0,1:T(8,128)(2,1)S(1)}, u32[]{:S(2)}, u32[]{:S(2)}) collective-permute-start(bf16[256,512]{0,1:T(8,128)(2,1)S(1)} %bitcast.66), channel_id=1, source_target_pairs={{0,16},{16,0},{1,17},{17,1},{2,18},{18,2},{3,19},{19,3},{4,20},{20... | collective-permute-start | bytes 786440 | tf_op jit(solution)/shard_map/ppermute | solution.py:85
  43.6 13.6 %collective-permute-start.4 = (bf16[256,1024]{0,1:T(8,128)(2,1)S(1)}, bf16[256,1024]{0,1:T(8,128)(2,1)}, u32[]{:S(2)}, u32[]{:S(2)}) collective-permute-start(bf16[256,1024]{0,1:T(8,128)(2,1)S(1)} %pad_maximum_fusion.1), channel_id=1, source_target_pairs={{0,2},{1,3},{18,16},{19,17},{4,6},{5,7},{22,20},{23,21},{8,10},{9,... | collective-permute-start | bytes 1572872 | tf_op jit(solution)/shard_map/ppermute | solution.py:89
  47.8 14.2 %collective-permute-start.8 = (bf16[256,1024]{1,0:T(8,128)(2,1)S(1)}, bf16[256,1024]{1,0:T(8,128)(2,1)S(1)}, u32[]{:S(2)}, u32[]{:S(2)}) collective-permute-start(bf16[256,1024]{1,0:T(8,128)(2,1)S(1)} %collective-permute-done.7), channel_id=1, source_target_pairs={{0,4},{4,8},{8,12},{12,0},{1,5},{5,9},{9,13},{13,1},{2,6},{6,10},{... | collective-permute-start | bytes 1572872 | tf_op jit(solution)/shard_map/ppermute | solution.py:118
  50.2 12.3 %collective-permute-start.5 = (bf16[256,1024]{0,1:T(8,128)(2,1)S(1)}, bf16[256,1024]{0,1:T(8,128)(2,1)S(1)}, u32[]{:S(2)}, u32[]{:S(2)}) collective-permute-start(bf16[256,1024]{0,1:T(8,128)(2,1)S(1)} %pad_maximum_fusion.1), channel_id=1, source_target_pairs={{0,1},{1,0},{18,19},{19,18},{4,5},{5,4},{22,23},{23,22},{8,9},{9,8... | collective-permute-start | bytes 1572872 | tf_op jit(solution)/shard_map/ppermute | solution.py:89
  57.2 5.3 %collective-permute-start.6 = (bf16[256,1024]{0,1:T(8,128)(2,1)}, bf16[256,1024]{0,1:T(8,128)(2,1)S(1)}, u32[]{:S(2)}, u32[]{:S(2)}) collective-permute-start(bf16[256,1024]{0,1:T(8,128)(2,1)} %collective-permute-done.4), channel_id=1, source_target_pairs={{2,3},{3,2},{16,17},{17,16},{6,7},{7,6},{20,21},{21,20},{10,11},{1... | collective-permute-start | bytes 1572872 | tf_op jit(solution)/shard_map/ppermute | solution.py:89
  63.7 14.5 %collective-permute-start.9 = (bf16[256,1024]{1,0:T(8,128)(2,1)S(1)}, bf16[256,1024]{1,0:T(8,128)(2,1)S(1)}, u32[]{:S(2)}, u32[]{:S(2)}) collective-permute-start(bf16[256,1024]{1,0:T(8,128)(2,1)S(1)} %convolution_convert_fusion), channel_id=1, source_target_pairs={{0,16},{16,0},{1,17},{17,1},{2,18},{18,2},{3,19},{19,3},{4,20},{20... | collective-permute-start | bytes 1572872 | tf_op jit(solution)/shard_map/ppermute | solution.py:85

commit v21 on v19

--- a/solution.py
+++ b/solution.py
@@ -93,15 +93,18 @@
     group = lax.axis_size("tensor")
     me = lax.axis_index("tensor")
     side = lax.axis_index("dp")
+    width = head_values.shape[1]
     foreign = swapped(head_values, "dp")
-    mine = jnp.concatenate([head_values, foreign], axis=1)
     owners = [(s, 2 * s + k) for s in range(2) for k in range(2)]
-    over_y = sent(mine, [(s * group + p, s * group + (p ^ 2)) for s, p in owners])
+    own_over = sent(head_values, [(s * group + p, s * group + (p ^ 2)) for s, p in owners])
+    diagonal = [((1 - s) * group + p, s * group + (p ^ 2)) for s, p in owners]
+    foreign_over = sent(head_values, diagonal)
     on_owner = me // 2 == side
-    same_core = jnp.where(on_owner, mine, over_y)
+    own_same = jnp.where(on_owner, head_values, own_over)
+    foreign_same = jnp.where(on_owner, foreign, foreign_over)
+    same_core = jnp.concatenate([own_same, foreign_same], axis=1)
     other_core = lax.ppermute(same_core, "tensor", [(t, t ^ 1) for t in range(group)])
     first_core = me % 2 == 0
-    width = head_values.shape[1]
     lower = jnp.where(first_core, same_core, other_core)
     upper = jnp.where(first_core, other_core, same_core)
     own_full = jnp.concatenate([lower[:, :width], upper[:, :width]], axis=1)

time: 76 us -> 79.7 us (1.049)
  starting transfers between devices: 23.3 us -> 25.5 us
  waiting for transfers between devices: 41.5 us -> 42.7 us
    ppermute x2, starting transfers between devices: 2.09 us -> 3.61 us  [swapped(): return lax.ppermute(block, axis, [(0, 1), (1, 0)])]
    ppermute x3, waiting for transfers between devices: 25 us -> 26.2 us  [ring_step(): lax.ppermute(block, axis, [(i, (i + 1) % count) for i in range(count)])]
    ppermute x1 -> x2, starting transfers between devices: 3.46 us -> 4.1 us  [sent(): return lax.ppermute(block, ('dp', 'tensor'), route)]
  transfers between devices with their start and end apart: 9 -> 10, of which waited for: 8 -> 7; matrix products, arithmetic and copies ran while one was open for 9% -> 9% of each run, Pallas kernels for 0% -> 0%
where the time goes in v21:
time: 79.7 us; the launch traced here: 79.4 us
  waiting for transfers between devices  42.7 us (54%)
  starting transfers between devices  25.5 us (32%)
  other arithmetic  5.64 us (7%)
  matrix products  3.06 us (4%)
  local copies, waits for them, and re-layouts  2.13 us (3%)
    ppermute x3, waiting for transfers between devices, ring_step(): lax.ppermute(block, axis, [(i, (i + 1) % count) for i in range(count)])  26.2 us
    ppermute x2, waiting for transfers between devices, swapped(): return lax.ppermute(block, axis, [(0, 1), (1, 0)])  12 us
    ppermute x2, starting transfers between devices, shifted(): return lax.ppermute(block, axis, route)  9.44 us
    ppermute x3, starting transfers between devices, ring_step(): lax.ppermute(block, axis, [(i, (i + 1) % count) for i in range(count)])  8.27 us
    ppermute x2, waiting for transfers between devices, shifted(): return lax.ppermute(block, axis, route)  4.58 us
    ppermute x2, starting transfers between devices, sent(): return lax.ppermute(block, ('dp', 'tensor'), route)  4.1 us
    ppermute x2, starting transfers between devices, swapped(): return lax.ppermute(block, axis, [(0, 1), (1, 0)])  3.61 us
  transfers between devices with their start and end apart: 10, of which 7 were waited for; matrix products, arithmetic and copies ran while one was open for 9% of the time, Pallas kernels for 0%

profile of v21, /device:TPU:0, one launch (start us, length us, event | category | flops | bytes accessed | tf_op | source)
XLA Modules:
  0.0 79.4 jit_solution(14326973025370230314)
XLA Ops:
  0.0 0.7 convert_element_type.37
  0.7 0.9 %copy.21 = bf16[1,256,2,128]{3,1,2,0:T(8,128)(2,1)S(1)} copy(bf16[1,256,2,128]{3,2,1,0:T(2,128)(2,1)} %param.5) | data formatting | bytes 262144 | tf_op args[1]
  1.6 0.1 broadcast_in_dim.27
  1.7 6.0 %collective-permute-start.2 = (bf16[256,3,128]{2,0,1:T(8,128)(2,1)S(1)}, bf16[256,3,128]{2,0,1:T(8,128)(2,1)S(1)}, u32[]{:S(2)}, u32[]{:S(2)}) collective-permute-start(bf16[256,3,128]{2,0,1:T(8,128)(2,1)S(1)} %pad_maximum_fusion.4), channel_id=1, source_target_pairs={{0,8},{4,12},{1,9},{5,13},{2,10},{6,14},{3,11},{7,15},{16,24},{20,... | collective-permute-start | bytes 589832 | tf_op jit(solution)/shard_map/ppermute | solution.py:17
  7.7 3.5 %collective-permute-start.1 = (bf16[256,3,128]{2,0,1:T(8,128)(2,1)S(1)}, bf16[256,3,128]{2,0,1:T(8,128)(2,1)S(1)}, u32[]{:S(2)}, u32[]{:S(2)}) collective-permute-start(bf16[256,3,128]{2,0,1:T(8,128)(2,1)S(1)} %pad_maximum_fusion.4), channel_id=1, source_target_pairs={{0,4},{4,8},{8,12},{1,5},{5,9},{9,13},{2,6},{6,10},{10,14},{3,7},{... | collective-permute-start | bytes 589832 | tf_op jit(solution)/shard_map/ppermute | solution.py:17
  11.2 0.1 collective-permute-start
  11.3 1.0 %reshape.68 = bf16[256,4,128]{2,1,0:T(4,128)(2,1)S(1)} reshape(bf16[1,256,512]{2,1,0:T(8,128)(2,1)} %param.4) | data formatting | bytes 524288 | tf_op jit(solution)/shard_map/reshape.3
  12.4 0.5 collective-permute-done.2
  12.8 0.1 convert_reduce_fusion
  13.0 4.1 %collective-permute-done.1 = bf16[256,3,128]{2,0,1:T(8,128)(2,1)S(1)} collective-permute-done((bf16[256,3,128]{2,0,1:T(8,128)(2,1)S(1)}, bf16[256,3,128]{2,0,1:T(8,128)(2,1)S(1)}, u32[]{:S(2)}, u32[]{:S(2)}) %collective-permute-start.1) | collective-permute-done | bytes 196640 | tf_op jit(solution)/shard_map/ppermute | solution.py:17
  17.1 0.1 convert_reduce_fusion.1
  17.2 0.7 pad_add_fusion
  17.9 1.4 %and_and_fusion = pred[256,768]{0,1:T(8,128)(4,1)S(1)} fusion(s32[256]{0:T(256)S(1)} %iota_add_fusion.2, s32[256]{0:T(256)} %bitcast.73, s32[768]{0:T(1024)S(1)} %pad_add_fusion.1, s32[768]{0:T(1024)S(1)} %pad_add_fusion, pred[768]{0:T(1024)(128)(4,1)S(1)} %broadcast_compare_fusion), kind=kLoop, calls=%fused_computation.14 | loop fusion | flops 786432 | bytes 205568 | tf_op jit(solution)/shard_map/and | solution.py:64
  19.4 0.7 fusion
  20.0 0.8 fusion.1
  20.8 1.0 %fusion.13 = bf16[256,1,4,128]{0,3,2,1:T(8,128)(2,1)S(1)} fusion(f32[768,256,4]{1,0,2:T(8,128)S(1)} %get-tuple-element.23, f32[4,256]{1,0:T(4,128)S(1)} %get-tuple-element.22, pred[256,768]{0,1:T(8,128)(4,1)S(1)} %and_and_fusion, f32[256,4]{0,1:T(4,128)S(1)} %bitcast.70, bf16[768,2,128]{2,0,1:T(8,128)(2,1)S(1)} %pad_maximum_fusion.3), kind=kOutput, calls=%fused_computation.13 | convolution fusion | flops 205520896 | bytes 3809280 | tf_op jit(solution)/shard_map/hgqk,khd->qhgd/dot_general | solution.py:72
  21.8 5.7 %collective-permute-done = bf16[256,1024]{1,0:T(8,128)(2,1)S(1)} collective-permute-done((bf16[256,1024]{1,0:T(8,128)(2,1)}, bf16[256,1024]{1,0:T(8,128)(2,1)S(1)}, u32[]{:S(2)}, u32[]{:S(2)}) %collective-permute-start) | collective-permute-done | bytes 524320 | tf_op jit(solution)/shard_map/ppermute | solution.py:117
  27.4 3.4 %collective-permute-start.3 = (bf16[256,512]{0,1:T(8,128)(2,1)S(1)}, bf16[256,512]{0,1:T(8,128)(2,1)S(1)}, u32[]{:S(2)}, u32[]{:S(2)}) collective-permute-start(bf16[256,512]{0,1:T(8,128)(2,1)S(1)} %bitcast.66), channel_id=1, source_target_pairs={{0,2},{1,3},{18,16},{19,17},{4,6},{5,7},{22,20},{23,21},{8,10},{9,... | collective-permute-start | bytes 786440 | tf_op jit(solution)/shard_map/ppermute | solution.py:89
  30.9 0.1 collective-permute-start.4
  30.9 0.7 collective-permute-start.5
  31.6 5.7 %collective-permute-start.7 = (bf16[256,1024]{1,0:T(8,128)(2,1)S(1)}, bf16[256,1024]{1,0:T(8,128)(2,1)S(1)}, u32[]{:S(2)}, u32[]{:S(2)}) collective-permute-start(bf16[256,1024]{1,0:T(8,128)(2,1)S(1)} %collective-permute-done), channel_id=1, source_target_pairs={{0,4},{4,8},{8,12},{12,0},{1,5},{5,9},{9,13},{13,1},{2,6},{6,10},{... | collective-permute-start | bytes 1572872 | tf_op jit(solution)/shard_map/ppermute | solution.py:117
  37.4 0.0 collective-permute-done.3
  37.4 0.0 copy-start
  37.4 2.7 %collective-permute-done.4 = bf16[256,512]{0,1:T(8,128)(2,1)S(1)} collective-permute-done((bf16[256,512]{0,1:T(8,128)(2,1)S(1)}, bf16[256,512]{0,1:T(8,128)(2,1)S(1)}, u32[]{:S(2)}, u32[]{:S(2)}) %collective-permute-start.4) | collective-permute-done | bytes 262176 | tf_op jit(solution)/shard_map/ppermute | solution.py:85
  40.2 0.0 collective-permute-done.5
  40.3 0.1 collective-permute-start.6
  40.4 8.0 %collective-permute-done.7 = bf16[256,1024]{1,0:T(8,128)(2,1)S(1)} collective-permute-done((bf16[256,1024]{1,0:T(8,128)(2,1)S(1)}, bf16[256,1024]{1,0:T(8,128)(2,1)S(1)}, u32[]{:S(2)}, u32[]{:S(2)}) %collective-permute-start.7) | collective-permute-done | bytes 524320 | tf_op jit(solution)/shard_map/ppermute | solution.py:117
  48.5 2.5 %collective-permute-start.8 = (bf16[256,1024]{1,0:T(8,128)(2,1)S(1)}, bf16[256,1024]{1,0:T(8,128)(2,1)S(1)}, u32[]{:S(2)}, u32[]{:S(2)}) collective-permute-start(bf16[256,1024]{1,0:T(8,128)(2,1)S(1)} %collective-permute-done.7), channel_id=1, source_target_pairs={{0,4},{4,8},{8,12},{12,0},{1,5},{5,9},{9,13},{13,1},{2,6},{6,10},{... | collective-permute-start | bytes 1572872 | tf_op jit(solution)/shard_map/ppermute | solution.py:117
  50.9 0.0 collective-permute-done.6
  50.9 0.2 broadcast_select_fusion.1
  51.2 12.5 %collective-permute-done.8 = bf16[256,1024]{1,0:T(8,128)(2,1)S(1)} collective-permute-done((bf16[256,1024]{1,0:T(8,128)(2,1)S(1)}, bf16[256,1024]{1,0:T(8,128)(2,1)S(1)}, u32[]{:S(2)}, u32[]{:S(2)}) %collective-permute-start.8) | collective-permute-done | bytes 524320 | tf_op jit(solution)/shard_map/ppermute | solution.py:117
  63.7 0.0 copy-done
  63.7 0.1 select_select_fusion.2
  63.8 0.2 select_select_fusion.3
  64.1 0.2 pad_maximum_fusion
  64.2 0.7 convolution_convert_fusion
  65.0 3.5 %collective-permute-start.9 = (bf16[256,1024]{1,0:T(8,128)(2,1)S(1)}, bf16[256,1024]{1,0:T(8,128)(2,1)S(1)}, u32[]{:S(2)}, u32[]{:S(2)}) collective-permute-start(bf16[256,1024]{1,0:T(8,128)(2,1)S(1)} %convolution_convert_fusion), channel_id=1, source_target_pairs={{0,16},{16,0},{1,17},{17,1},{2,18},{18,2},{3,19},{19,3},{4,20},{20... | collective-permute-start | bytes 1572872 | tf_op jit(solution)/shard_map/ppermute | solution.py:85
  68.5 0.7 fusion.28
  69.3 9.2 %collective-permute-done.9 = bf16[256,1024]{1,0:T(8,128)(2,1)S(1)} collective-permute-done((bf16[256,1024]{1,0:T(8,128)(2,1)S(1)}, bf16[256,1024]{1,0:T(8,128)(2,1)S(1)}, u32[]{:S(2)}, u32[]{:S(2)}) %collective-permute-start.9) | collective-permute-done | bytes 524320 | tf_op jit(solution)/shard_map/ppermute | solution.py:85
  78.5 0.9 %fusion.16 = bf16[1,256,1024]{2,1,0:T(8,128)(2,1)} fusion(f32[256,1024]{1,0:T(8,128)S(1)} %fusion.28, bf16[256,1024]{1,0:T(8,128)(2,1)S(1)} %collective-permute-done.9), kind=kLoop, calls=%fused_computation.15 | loop fusion | flops 786432 | bytes 2097152 | tf_op jit(solution)/shard_map/broadcast_in_dim | solution.py:159
  (14 shorter events, 0.3 us)
Async XLA Ops:
  1.7 11.1 %collective-permute-start.2 = (bf16[256,3,128]{2,0,1:T(8,128)(2,1)S(1)}, bf16[256,3,128]{2,0,1:T(8,128)(2,1)S(1)}, u32[]{:S(2)}, u32[]{:S(2)}) collective-permute-start(bf16[256,3,128]{2,0,1:T(8,128)(2,1)S(1)} %pad_maximum_fusion.4), channel_id=1, source_target_pairs={{0,8},{4,12},{1,9},{5,13},{2,10},{6,14},{3,11},{7,15},{16,24},{20,... | collective-permute-start | bytes 589832 | tf_op jit(solution)/shard_map/ppermute | solution.py:17
  7.7 9.4 %collective-permute-start.1 = (bf16[256,3,128]{2,0,1:T(8,128)(2,1)S(1)}, bf16[256,3,128]{2,0,1:T(8,128)(2,1)S(1)}, u32[]{:S(2)}, u32[]{:S(2)}) collective-permute-start(bf16[256,3,128]{2,0,1:T(8,128)(2,1)S(1)} %pad_maximum_fusion.4), channel_id=1, source_target_pairs={{0,4},{4,8},{8,12},{1,5},{5,9},{9,13},{2,6},{6,10},{10,14},{3,7},{... | collective-permute-start | bytes 589832 | tf_op jit(solution)/shard_map/ppermute | solution.py:17
  11.2 16.2 %collective-permute-start = (bf16[256,1024]{1,0:T(8,128)(2,1)}, bf16[256,1024]{1,0:T(8,128)(2,1)S(1)}, u32[]{:S(2)}, u32[]{:S(2)}) collective-permute-start(bf16[256,1024]{1,0:T(8,128)(2,1)} %param.7), channel_id=1, source_target_pairs={{0,4},{4,8},{8,12},{12,0},{1,5},{5,9},{9,13},{13,1},{2,6},{6,10},{... | collective-permute-start | bytes 1572872 | tf_op jit(solution)/shard_map/ppermute | solution.py:117
  27.4 10.0 %collective-permute-start.3 = (bf16[256,512]{0,1:T(8,128)(2,1)S(1)}, bf16[256,512]{0,1:T(8,128)(2,1)S(1)}, u32[]{:S(2)}, u32[]{:S(2)}) collective-permute-start(bf16[256,512]{0,1:T(8,128)(2,1)S(1)} %bitcast.66), channel_id=1, source_target_pairs={{0,2},{1,3},{18,16},{19,17},{4,6},{5,7},{22,20},{23,21},{8,10},{9,... | collective-permute-start | bytes 786440 | tf_op jit(solution)/shard_map/ppermute | solution.py:89
  30.9 9.3 %collective-permute-start.4 = (bf16[256,512]{0,1:T(8,128)(2,1)S(1)}, bf16[256,512]{0,1:T(8,128)(2,1)S(1)}, u32[]{:S(2)}, u32[]{:S(2)}) collective-permute-start(bf16[256,512]{0,1:T(8,128)(2,1)S(1)} %bitcast.67), channel_id=1, source_target_pairs={{0,16},{16,0},{1,17},{17,1},{2,18},{18,2},{3,19},{19,3},{4,20},{20... | collective-permute-start | bytes 786440 | tf_op jit(solution)/shard_map/ppermute | solution.py:85
  30.9 9.2 %collective-permute-start.5 = (bf16[256,512]{0,1:T(8,128)(2,1)S(1)}, bf16[256,512]{0,1:T(8,128)(2,1)S(1)}, u32[]{:S(2)}, u32[]{:S(2)}) collective-permute-start(bf16[256,512]{0,1:T(8,128)(2,1)S(1)} %bitcast.68), channel_id=1, source_target_pairs={{16,2},{17,3},{2,16},{3,17},{20,6},{21,7},{6,20},{7,21},{24,10},{2... | collective-permute-start | bytes 786440 | tf_op jit(solution)/shard_map/ppermute | solution.py:89
  31.6 16.8 %collective-permute-start.7 = (bf16[256,1024]{1,0:T(8,128)(2,1)S(1)}, bf16[256,1024]{1,0:T(8,128)(2,1)S(1)}, u32[]{:S(2)}, u32[]{:S(2)}) collective-permute-start(bf16[256,1024]{1,0:T(8,128)(2,1)S(1)} %collective-permute-done), channel_id=1, source_target_pairs={{0,4},{4,8},{8,12},{12,0},{1,5},{5,9},{9,13},{13,1},{2,6},{6,10},{... | collective-permute-start | bytes 1572872 | tf_op jit(solution)/shard_map/ppermute | solution.py:117
  37.4 26.3 %copy-start = (bf16[256,1024]{1,0:T(8,128)(2,1)S(1)}, bf16[256,1024]{1,0:T(8,128)(2,1)}, u32[]{:S(2)}) copy-start(bf16[256,1024]{1,0:T(8,128)(2,1)} %param.7) | copy-start | bytes 1572868
  40.3 10.7 %collective-permute-start.6 = (bf16[256,1024]{0,1:T(8,128)(2,1)S(1)}, bf16[256,1024]{0,1:T(8,128)(2,1)S(1)}, u32[]{:S(2)}, u32[]{:S(2)}) collective-permute-start(bf16[256,1024]{0,1:T(8,128)(2,1)S(1)} %pad_maximum_fusion.1), channel_id=1, source_target_pairs={{0,1},{1,0},{2,3},{3,2},{4,5},{5,4},{6,7},{7,6},{8,9},{9,8},{10,11... | collective-permute-start | bytes 1572872 | tf_op jit(solution)/shard_map/ppermute | solution.py:106
  48.5 15.3 %collective-permute-start.8 = (bf16[256,1024]{1,0:T(8,128)(2,1)S(1)}, bf16[256,1024]{1,0:T(8,128)(2,1)S(1)}, u32[]{:S(2)}, u32[]{:S(2)}) collective-permute-start(bf16[256,1024]{1,0:T(8,128)(2,1)S(1)} %collective-permute-done.7), channel_id=1, source_target_pairs={{0,4},{4,8},{8,12},{12,0},{1,5},{5,9},{9,13},{13,1},{2,6},{6,10},{... | collective-permute-start | bytes 1572872 | tf_op jit(solution)/shard_map/ppermute | solution.py:117
  65.0 13.5 %collective-permute-start.9 = (bf16[256,1024]{1,0:T(8,128)(2,1)S(1)}, bf16[256,1024]{1,0:T(8,128)(2,1)S(1)}, u32[]{:S(2)}, u32[]{:S(2)}) collective-permute-start(bf16[256,1024]{1,0:T(8,128)(2,1)S(1)} %convolution_convert_fusion), channel_id=1, source_target_pairs={{0,16},{16,0},{1,17},{17,1},{2,18},{18,2},{3,19},{19,3},{4,20},{20... | collective-permute-start | bytes 1572872 | tf_op jit(solution)/shard_map/ppermute | solution.py:85

commit v22 on v18

--- a/solution.py
+++ b/solution.py
@@ -115,7 +115,7 @@
 
 def ring_step(block, axis):
     count = lax.axis_size(axis)
-    return lax.ppermute(block, axis, [(i, (i + 1) % count) for i in range(count)])
+    return lax.ppermute(block, axis, [(i, (i - 1) % count) for i in range(count)])
 
 
 def line_rows(block, first, axis):
@@ -130,7 +130,7 @@
     for place in range(count):
         chosen = jnp.zeros_like(block)
         for arrived, back in arrivals:
-            chosen = jnp.where((here - back) % count == place, arrived, chosen)
+            chosen = jnp.where((here + back) % count == place, arrived, chosen)
         ordered.append(chosen)
     return jnp.concatenate(ordered, axis=0)
 

time: 75.6 us -> 85.1 us (1.13)
  waiting for transfers between devices: 37.6 us -> 43 us
  starting transfers between devices: 26.7 us -> 30.9 us
    ppermute x3, waiting for transfers between devices: 10.3 us -> 23 us  [ring_step(): lax.ppermute(block, axis, [(i, (i - 1) % count) for i in range(count)])]
    ppermute x3, waiting for transfers between devices: 5.8 us -> 0.01 us  [sent(): return lax.ppermute(block, ('dp', 'tensor'), route)]
    ppermute x3, starting transfers between devices: 8.17 us -> 12.4 us  [ring_step(): lax.ppermute(block, axis, [(i, (i - 1) % count) for i in range(count)])]
    ppermute x2, waiting for transfers between devices: 16.9 us -> 15.3 us  [swapped(): return lax.ppermute(block, axis, [(0, 1), (1, 0)])]
  transfers between devices with their start and end apart: 10 -> 10, of which waited for: 7 -> 7; matrix products, arithmetic and copies ran while one was open for 9% -> 8% of each run, Pallas kernels for 0% -> 0%
where the time goes in v22:
time: 85.1 us; the launch traced here: 84.8 us
  waiting for transfers between devices  43 us (51%)
  starting transfers between devices  30.9 us (36%)
  other arithmetic  5.44 us (6%)
  matrix products  3.04 us (4%)
  local copies, waits for them, and re-layouts  2.17 us (3%)
    ppermute x3, waiting for transfers between devices, ring_step(): lax.ppermute(block, axis, [(i, (i - 1) % count) for i in range(count)])  23 us
    ppermute x2, waiting for transfers between devices, swapped(): return lax.ppermute(block, axis, [(0, 1), (1, 0)])  15.3 us
    ppermute x3, starting transfers between devices, ring_step(): lax.ppermute(block, axis, [(i, (i - 1) % count) for i in range(count)])  12.4 us
    ppermute x2, starting transfers between devices, shifted(): return lax.ppermute(block, axis, route)  9.44 us
    ppermute x3, starting transfers between devices, sent(): return lax.ppermute(block, ('dp', 'tensor'), route)  6.07 us
    ppermute x2, waiting for transfers between devices, shifted(): return lax.ppermute(block, axis, route)  4.68 us
    ppermute x2, starting transfers between devices, swapped(): return lax.ppermute(block, axis, [(0, 1), (1, 0)])  3.04 us
  transfers between devices with their start and end apart: 10, of which 7 were waited for; matrix products, arithmetic and copies ran while one was open for 8% of the time, Pallas kernels for 0%

profile of v22, /device:TPU:0, one launch (start us, length us, event | category | flops | bytes accessed | tf_op | source)
XLA Modules:
  0.0 84.8 jit_solution(10440245628812132963)
XLA Ops:
  0.0 0.7 convert_element_type.37
  0.7 0.9 %copy.21 = bf16[1,256,2,128]{3,1,2,0:T(8,128)(2,1)S(1)} copy(bf16[1,256,2,128]{3,2,1,0:T(2,128)(2,1)} %param.5) | data formatting | bytes 262144 | tf_op args[1]
  1.6 0.1 broadcast_in_dim.27
  1.7 6.0 %collective-permute-start.2 = (bf16[256,3,128]{2,0,1:T(8,128)(2,1)S(1)}, bf16[256,3,128]{2,0,1:T(8,128)(2,1)S(1)}, u32[]{:S(2)}, u32[]{:S(2)}) collective-permute-start(bf16[256,3,128]{2,0,1:T(8,128)(2,1)S(1)} %pad_maximum_fusion.3), channel_id=1, source_target_pairs={{0,8},{4,12},{1,9},{5,13},{2,10},{6,14},{3,11},{7,15},{16,24},{20,... | collective-permute-start | bytes 589832 | tf_op jit(solution)/shard_map/ppermute | solution.py:17
  7.7 3.5 %collective-permute-start.1 = (bf16[256,3,128]{2,0,1:T(8,128)(2,1)S(1)}, bf16[256,3,128]{2,0,1:T(8,128)(2,1)S(1)}, u32[]{:S(2)}, u32[]{:S(2)}) collective-permute-start(bf16[256,3,128]{2,0,1:T(8,128)(2,1)S(1)} %pad_maximum_fusion.3), channel_id=1, source_target_pairs={{0,4},{4,8},{8,12},{1,5},{5,9},{9,13},{2,6},{6,10},{10,14},{3,7},{... | collective-permute-start | bytes 589832 | tf_op jit(solution)/shard_map/ppermute | solution.py:17
  11.2 0.1 collective-permute-start
  11.3 1.0 %reshape.68 = bf16[256,4,128]{2,1,0:T(4,128)(2,1)S(1)} reshape(bf16[1,256,512]{2,1,0:T(8,128)(2,1)} %param.4) | data formatting | bytes 524288 | tf_op jit(solution)/shard_map/reshape.3
  12.4 0.5 collective-permute-done.2
  12.9 4.2 %collective-permute-done.1 = bf16[256,3,128]{2,0,1:T(8,128)(2,1)S(1)} collective-permute-done((bf16[256,3,128]{2,0,1:T(8,128)(2,1)S(1)}, bf16[256,3,128]{2,0,1:T(8,128)(2,1)S(1)}, u32[]{:S(2)}, u32[]{:S(2)}) %collective-permute-start.1) | collective-permute-done | bytes 196640 | tf_op jit(solution)/shard_map/ppermute | solution.py:17
  17.1 0.1 convert_reduce_fusion
  17.2 0.1 convert_reduce_fusion.1
  17.3 0.7 pad_add_fusion
  18.0 1.4 %and_and_fusion = pred[256,768]{0,1:T(8,128)(4,1)S(1)} fusion(s32[256]{0:T(256)S(1)} %iota_add_fusion.2, s32[256]{0:T(256)} %bitcast.71, s32[768]{0:T(1024)S(1)} %pad_add_fusion.1, s32[768]{0:T(1024)S(1)} %pad_add_fusion, pred[768]{0:T(1024)(128)(4,1)S(1)} %broadcast_compare_fusion), kind=kLoop, calls=%fused_computation.14 | loop fusion | flops 786432 | bytes 205568 | tf_op jit(solution)/shard_map/and | solution.py:64
  19.4 0.6 fusion
  20.1 0.8 fusion.1
  20.9 0.0 copy-start
  20.9 0.9 %fusion.13 = bf16[256,1,4,128]{0,3,2,1:T(8,128)(2,1)S(1)} fusion(f32[768,256,4]{1,0,2:T(8,128)S(1)} %get-tuple-element.23, f32[4,256]{1,0:T(4,128)S(1)} %get-tuple-element.22, pred[256,768]{0,1:T(8,128)(4,1)S(1)} %and_and_fusion, f32[256,4]{0,1:T(4,128)S(1)} %bitcast.68, bf16[768,2,128]{2,0,1:T(8,128)(2,1)S(1)} %pad_maximum_fusion.2), kind=kOutput, calls=%fused_computation.13 | convolution fusion | flops 205520896 | bytes 3809280 | tf_op jit(solution)/shard_map/hgqk,khd->qhgd/dot_general | solution.py:72
  21.8 5.6 %collective-permute-done = bf16[256,1024]{1,0:T(8,128)(2,1)S(1)} collective-permute-done((bf16[256,1024]{1,0:T(8,128)(2,1)}, bf16[256,1024]{1,0:T(8,128)(2,1)S(1)}, u32[]{:S(2)}, u32[]{:S(2)}) %collective-permute-start) | collective-permute-done | bytes 524320 | tf_op jit(solution)/shard_map/ppermute | solution.py:118
  27.5 9.4 %collective-permute-start.7 = (bf16[256,1024]{1,0:T(8,128)(2,1)S(1)}, bf16[256,1024]{1,0:T(8,128)(2,1)S(1)}, u32[]{:S(2)}, u32[]{:S(2)}) collective-permute-start(bf16[256,1024]{1,0:T(8,128)(2,1)S(1)} %collective-permute-done), channel_id=1, source_target_pairs={{0,12},{4,0},{8,4},{12,8},{1,13},{5,1},{9,5},{13,9},{2,14},{6,2},{... | collective-permute-start | bytes 1572872 | tf_op jit(solution)/shard_map/ppermute | solution.py:118
  36.9 1.5 %collective-permute-start.3 = (bf16[256,512]{0,1:T(8,128)(2,1)S(1)}, bf16[256,512]{0,1:T(8,128)(2,1)S(1)}, u32[]{:S(2)}, u32[]{:S(2)}) collective-permute-start(bf16[256,512]{0,1:T(8,128)(2,1)S(1)} %bitcast.66), channel_id=1, source_target_pairs={{0,16},{16,0},{1,17},{17,1},{2,18},{18,2},{3,19},{19,3},{4,20},{20... | collective-permute-start | bytes 786440 | tf_op jit(solution)/shard_map/ppermute | solution.py:85
  38.4 4.9 %collective-permute-done.3 = bf16[256,512]{0,1:T(8,128)(2,1)S(1)} collective-permute-done((bf16[256,512]{0,1:T(8,128)(2,1)S(1)}, bf16[256,512]{0,1:T(8,128)(2,1)S(1)}, u32[]{:S(2)}, u32[]{:S(2)}) %collective-permute-start.3) | collective-permute-done | bytes 262176 | tf_op jit(solution)/shard_map/ppermute | solution.py:85
  43.3 3.5 %collective-permute-start.4 = (bf16[256,1024]{0,1:T(8,128)(2,1)S(1)}, bf16[256,1024]{0,1:T(8,128)(2,1)S(1)}, u32[]{:S(2)}, u32[]{:S(2)}) collective-permute-start(bf16[256,1024]{0,1:T(8,128)(2,1)S(1)} %constant_dynamic-update-slice_fusion), channel_id=1, source_target_pairs={{0,2},{1,3},{18,16},{19,17},{4,6},{5,7},{22,20},{23,21},{8,10},{9,... | collective-permute-start | bytes 1572872 | tf_op jit(solution)/shard_map/ppermute | solution.py:89
  46.7 8.7 %collective-permute-done.7 = bf16[256,1024]{1,0:T(8,128)(2,1)S(1)} collective-permute-done((bf16[256,1024]{1,0:T(8,128)(2,1)S(1)}, bf16[256,1024]{1,0:T(8,128)(2,1)S(1)}, u32[]{:S(2)}, u32[]{:S(2)}) %collective-permute-start.7) | collective-permute-done | bytes 524320 | tf_op jit(solution)/shard_map/ppermute | solution.py:118
  55.4 2.9 %collective-permute-start.8 = (bf16[256,1024]{1,0:T(8,128)(2,1)S(1)}, bf16[256,1024]{1,0:T(8,128)(2,1)S(1)}, u32[]{:S(2)}, u32[]{:S(2)}) collective-permute-start(bf16[256,1024]{1,0:T(8,128)(2,1)S(1)} %collective-permute-done.7), channel_id=1, source_target_pairs={{0,12},{4,0},{8,4},{12,8},{1,13},{5,1},{9,5},{13,9},{2,14},{6,2},{... | collective-permute-start | bytes 1572872 | tf_op jit(solution)/shard_map/ppermute | solution.py:118
  58.3 1.9 %collective-permute-start.5 = (bf16[256,1024]{0,1:T(8,128)(2,1)S(1)}, bf16[256,1024]{0,1:T(8,128)(2,1)S(1)}, u32[]{:S(2)}, u32[]{:S(2)}) collective-permute-start(bf16[256,1024]{0,1:T(8,128)(2,1)S(1)} %constant_dynamic-update-slice_fusion), channel_id=1, source_target_pairs={{0,1},{1,0},{18,19},{19,18},{4,5},{5,4},{22,23},{23,22},{8,9},{9,8... | collective-permute-start | bytes 1572872 | tf_op jit(solution)/shard_map/ppermute | solution.py:89
  60.3 0.0 collective-permute-done.4
  60.3 0.7 collective-permute-start.6
  61.0 8.7 %collective-permute-done.8 = bf16[256,1024]{1,0:T(8,128)(2,1)S(1)} collective-permute-done((bf16[256,1024]{1,0:T(8,128)(2,1)S(1)}, bf16[256,1024]{1,0:T(8,128)(2,1)S(1)}, u32[]{:S(2)}, u32[]{:S(2)}) %collective-permute-start.8) | collective-permute-done | bytes 524320 | tf_op jit(solution)/shard_map/ppermute | solution.py:118
  69.6 0.0 copy-done
  69.6 0.1 select_select_fusion.2
  69.7 0.2 select_select_fusion.3
  70.0 0.2 pad_maximum_fusion
  70.1 0.0 collective-permute-done.5
  70.2 0.0 collective-permute-done.6
  70.2 0.1 broadcast_select_fusion.3
  70.4 0.7 convolution_convert_fusion
  71.1 1.5 %collective-permute-start.9 = (bf16[256,1024]{1,0:T(8,128)(2,1)S(1)}, bf16[256,1024]{1,0:T(8,128)(2,1)S(1)}, u32[]{:S(2)}, u32[]{:S(2)}) collective-permute-start(bf16[256,1024]{1,0:T(8,128)(2,1)S(1)} %convolution_convert_fusion), channel_id=1, source_target_pairs={{0,16},{16,0},{1,17},{17,1},{2,18},{18,2},{3,19},{19,3},{4,20},{20... | collective-permute-start | bytes 1572872 | tf_op jit(solution)/shard_map/ppermute | solution.py:85
  72.7 0.7 fusion.28
  73.4 10.5 %collective-permute-done.9 = bf16[256,1024]{1,0:T(8,128)(2,1)S(1)} collective-permute-done((bf16[256,1024]{1,0:T(8,128)(2,1)S(1)}, bf16[256,1024]{1,0:T(8,128)(2,1)S(1)}, u32[]{:S(2)}, u32[]{:S(2)}) %collective-permute-start.9) | collective-permute-done | bytes 524320 | tf_op jit(solution)/shard_map/ppermute | solution.py:85
  83.9 0.9 %fusion.16 = bf16[1,256,1024]{2,1,0:T(8,128)(2,1)} fusion(f32[256,1024]{1,0:T(8,128)S(1)} %fusion.28, bf16[256,1024]{1,0:T(8,128)(2,1)S(1)} %collective-permute-done.9), kind=kLoop, calls=%fused_computation.15 | loop fusion | flops 786432 | bytes 2097152 | tf_op jit(solution)/shard_map/broadcast_in_dim | solution.py:160
  (13 shorter events, 0.2 us)
Async XLA Ops:
  1.7 11.1 %collective-permute-start.2 = (bf16[256,3,128]{2,0,1:T(8,128)(2,1)S(1)}, bf16[256,3,128]{2,0,1:T(8,128)(2,1)S(1)}, u32[]{:S(2)}, u32[]{:S(2)}) collective-permute-start(bf16[256,3,128]{2,0,1:T(8,128)(2,1)S(1)} %pad_maximum_fusion.3), channel_id=1, source_target_pairs={{0,8},{4,12},{1,9},{5,13},{2,10},{6,14},{3,11},{7,15},{16,24},{20,... | collective-permute-start | bytes 589832 | tf_op jit(solution)/shard_map/ppermute | solution.py:17
  7.7 9.4 %collective-permute-start.1 = (bf16[256,3,128]{2,0,1:T(8,128)(2,1)S(1)}, bf16[256,3,128]{2,0,1:T(8,128)(2,1)S(1)}, u32[]{:S(2)}, u32[]{:S(2)}) collective-permute-start(bf16[256,3,128]{2,0,1:T(8,128)(2,1)S(1)} %pad_maximum_fusion.3), channel_id=1, source_target_pairs={{0,4},{4,8},{8,12},{1,5},{5,9},{9,13},{2,6},{6,10},{10,14},{3,7},{... | collective-permute-start | bytes 589832 | tf_op jit(solution)/shard_map/ppermute | solution.py:17
  11.2 16.3 %collective-permute-start = (bf16[256,1024]{1,0:T(8,128)(2,1)}, bf16[256,1024]{1,0:T(8,128)(2,1)S(1)}, u32[]{:S(2)}, u32[]{:S(2)}) collective-permute-start(bf16[256,1024]{1,0:T(8,128)(2,1)} %param.7), channel_id=1, source_target_pairs={{0,12},{4,0},{8,4},{12,8},{1,13},{5,1},{9,5},{13,9},{2,14},{6,2},{... | collective-permute-start | bytes 1572872 | tf_op jit(solution)/shard_map/ppermute | solution.py:118
  20.9 48.8 %copy-start = (bf16[256,1024]{1,0:T(8,128)(2,1)S(1)}, bf16[256,1024]{1,0:T(8,128)(2,1)}, u32[]{:S(2)}) copy-start(bf16[256,1024]{1,0:T(8,128)(2,1)} %param.7) | copy-start | bytes 1572868
  27.5 28.0 %collective-permute-start.7 = (bf16[256,1024]{1,0:T(8,128)(2,1)S(1)}, bf16[256,1024]{1,0:T(8,128)(2,1)S(1)}, u32[]{:S(2)}, u32[]{:S(2)}) collective-permute-start(bf16[256,1024]{1,0:T(8,128)(2,1)S(1)} %collective-permute-done), channel_id=1, source_target_pairs={{0,12},{4,0},{8,4},{12,8},{1,13},{5,1},{9,5},{13,9},{2,14},{6,2},{... | collective-permute-start | bytes 1572872 | tf_op jit(solution)/shard_map/ppermute | solution.py:118
  36.9 6.4 %collective-permute-start.3 = (bf16[256,512]{0,1:T(8,128)(2,1)S(1)}, bf16[256,512]{0,1:T(8,128)(2,1)S(1)}, u32[]{:S(2)}, u32[]{:S(2)}) collective-permute-start(bf16[256,512]{0,1:T(8,128)(2,1)S(1)} %bitcast.66), channel_id=1, source_target_pairs={{0,16},{16,0},{1,17},{17,1},{2,18},{18,2},{3,19},{19,3},{4,20},{20... | collective-permute-start | bytes 786440 | tf_op jit(solution)/shard_map/ppermute | solution.py:85
  43.3 17.0 %collective-permute-start.4 = (bf16[256,1024]{0,1:T(8,128)(2,1)S(1)}, bf16[256,1024]{0,1:T(8,128)(2,1)S(1)}, u32[]{:S(2)}, u32[]{:S(2)}) collective-permute-start(bf16[256,1024]{0,1:T(8,128)(2,1)S(1)} %constant_dynamic-update-slice_fusion), channel_id=1, source_target_pairs={{0,2},{1,3},{18,16},{19,17},{4,6},{5,7},{22,20},{23,21},{8,10},{9,... | collective-permute-start | bytes 1572872 | tf_op jit(solution)/shard_map/ppermute | solution.py:89
  55.4 14.2 %collective-permute-start.8 = (bf16[256,1024]{1,0:T(8,128)(2,1)S(1)}, bf16[256,1024]{1,0:T(8,128)(2,1)S(1)}, u32[]{:S(2)}, u32[]{:S(2)}) collective-permute-start(bf16[256,1024]{1,0:T(8,128)(2,1)S(1)} %collective-permute-done.7), channel_id=1, source_target_pairs={{0,12},{4,0},{8,4},{12,8},{1,13},{5,1},{9,5},{13,9},{2,14},{6,2},{... | collective-permute-start | bytes 1572872 | tf_op jit(solution)/shard_map/ppermute | solution.py:118
  58.3 11.8 %collective-permute-start.5 = (bf16[256,1024]{0,1:T(8,128)(2,1)S(1)}, bf16[256,1024]{0,1:T(8,128)(2,1)S(1)}, u32[]{:S(2)}, u32[]{:S(2)}) collective-permute-start(bf16[256,1024]{0,1:T(8,128)(2,1)S(1)} %constant_dynamic-update-slice_fusion), channel_id=1, source_target_pairs={{0,1},{1,0},{18,19},{19,18},{4,5},{5,4},{22,23},{23,22},{8,9},{9,8... | collective-permute-start | bytes 1572872 | tf_op jit(solution)/shard_map/ppermute | solution.py:89
  60.3 9.9 %collective-permute-start.6 = (bf16[256,1024]{0,1:T(8,128)(2,1)S(1)}, bf16[256,1024]{0,1:T(8,128)(2,1)S(1)}, u32[]{:S(2)}, u32[]{:S(2)}) collective-permute-start(bf16[256,1024]{0,1:T(8,128)(2,1)S(1)} %collective-permute-done.4), channel_id=1, source_target_pairs={{2,3},{3,2},{16,17},{17,16},{6,7},{7,6},{20,21},{21,20},{10,11},{1... | collective-permute-start | bytes 1572872 | tf_op jit(solution)/shard_map/ppermute | solution.py:89
  71.1 12.8 %collective-permute-start.9 = (bf16[256,1024]{1,0:T(8,128)(2,1)S(1)}, bf16[256,1024]{1,0:T(8,128)(2,1)S(1)}, u32[]{:S(2)}, u32[]{:S(2)}) collective-permute-start(bf16[256,1024]{1,0:T(8,128)(2,1)S(1)} %convolution_convert_fusion), channel_id=1, source_target_pairs={{0,16},{16,0},{1,17},{17,1},{2,18},{18,2},{3,19},{19,3},{4,20},{20... | collective-permute-start | bytes 1572872 | tf_op jit(solution)/shard_map/ppermute | solution.py:85

commit v23 on v18

--- a/solution.py
+++ b/solution.py
@@ -36,14 +36,22 @@
     pair_blocks = [keyvals[0]]
     label_blocks = [documents[0]]
     place_blocks = [position * length + offsets]
-    label_slab = jnp.broadcast_to(
-        documents[0].astype(jnp.bfloat16)[:, None, None], (length, 1, pair_width)
-    )
-    packed = jnp.concatenate([keyvals[0], label_slab], axis=1)
+    if length % pair_width == 0:
+        label_rows = documents[0].astype(jnp.bfloat16).reshape(length // pair_width, pair_width)
+        packed = jnp.concatenate([keyvals[0].reshape(2 * length, pair_width), label_rows], axis=0)
+    else:
+        label_slab = jnp.broadcast_to(
+            documents[0].astype(jnp.bfloat16)[:, None, None], (length, 1, pair_width)
+        )
+        packed = jnp.concatenate([keyvals[0], label_slab], axis=1)
     for hop in range(1, reach_hops + 1):
         arrived = shifted(packed, "ctx", hop)
-        pair_blocks.append(arrived[:, :2])
-        label_blocks.append(arrived[:, 2, 0].astype(jnp.int32))
+        if length % pair_width == 0:
+            pair_blocks.append(arrived[: 2 * length].reshape(length, 2, pair_width))
+            label_blocks.append(arrived[2 * length:].reshape(length).astype(jnp.int32))
+        else:
+            pair_blocks.append(arrived[:, :2])
+            label_blocks.append(arrived[:, 2, 0].astype(jnp.int32))
         place_blocks.append((position - hop) * length + offsets)
     pairs = jnp.concatenate(pair_blocks, axis=0)
     key_labels = jnp.concatenate(label_blocks, axis=0)

time: 75.6 us -> 71.4 us (0.944)
  starting transfers between devices: 26.7 us -> 23.7 us
  waiting for transfers between devices: 37.6 us -> 35.8 us
    ppermute x3, starting transfers between devices: 8.17 us -> 5.16 us  [ring_step(): lax.ppermute(block, axis, [(i, (i + 1) % count) for i in range(count)])]
    ppermute x2, waiting for transfers between devices: 4.68 us -> 1.82 us  [shifted(): return lax.ppermute(block, axis, route)]
    ppermute x3, waiting for transfers between devices: 10.3 us -> 11.3 us  [ring_step(): lax.ppermute(block, axis, [(i, (i + 1) % count) for i in range(count)])]
    concatenate x1, other arithmetic: 0.02 us -> 0.91 us  [attention(): jnp.concatenate([keyvals[0].reshape(2 * length, pair_width), label_rows],...]
  transfers between devices with their start and end apart: 10 -> 10, of which waited for: 7 -> 6; matrix products, arithmetic and copies ran while one was open for 9% -> 11% of each run, Pallas kernels for 0% -> 0%
where the time goes in v23:
time: 71.4 us; the launch traced here: 71 us
  waiting for transfers between devices  35.8 us (50%)
  starting transfers between devices  23.7 us (33%)
  other arithmetic  6.14 us (9%)
  matrix products  3.04 us (4%)
  local copies, waits for them, and re-layouts  2.11 us (3%)
    ppermute x2, waiting for transfers between devices, swapped(): return lax.ppermute(block, axis, [(0, 1), (1, 0)])  16.9 us
    ppermute x3, waiting for transfers between devices, ring_step(): lax.ppermute(block, axis, [(i, (i + 1) % count) for i in range(count)])  11.3 us
    ppermute x2, starting transfers between devices, shifted(): return lax.ppermute(block, axis, route)  9.44 us
    ppermute x3, starting transfers between devices, sent(): return lax.ppermute(block, ('dp', 'tensor'), route)  6.05 us
    ppermute x3, waiting for transfers between devices, sent(): return lax.ppermute(block, ('dp', 'tensor'), route)  5.8 us
    ppermute x3, starting transfers between devices, ring_step(): lax.ppermute(block, axis, [(i, (i + 1) % count) for i in range(count)])  5.16 us
    ppermute x2, starting transfers between devices, swapped(): return lax.ppermute(block, axis, [(0, 1), (1, 0)])  3.05 us
    ppermute x2, waiting for transfers between devices, shifted(): return lax.ppermute(block, axis, route)  1.82 us
  transfers between devices with their start and end apart: 10, of which 6 were waited for; matrix products, arithmetic and copies ran while one was open for 11% of the time, Pallas kernels for 0%

profile of v23, /device:TPU:0, one launch (start us, length us, event | category | flops | bytes accessed | tf_op | source)
XLA Modules:
  0.0 71.0 jit_solution(2277581754698645376)
XLA Ops:
  0.0 0.7 convert_reduce_fusion
  0.7 0.9 %pad_maximum_fusion.3 = bf16[514,128]{1,0:T(8,128)(2,1)S(1)} fusion(bf16[2,128]{1,0:T(2,128)(2,1)S(1)} %bitcast.87, bf16[512,128]{1,0:T(8,128)(2,1)} %bitcast.78), kind=kLoop, calls=%fused_computation.33 | loop fusion | flops 263168 | bytes 263168 | tf_op jit(solution)/shard_map/concatenate | solution.py:41
  1.6 5.9 %collective-permute-start.2 = (bf16[514,128]{1,0:T(8,128)(2,1)S(1)}, bf16[514,128]{1,0:T(8,128)(2,1)S(1)}, u32[]{:S(2)}, u32[]{:S(2)}) collective-permute-start(bf16[514,128]{1,0:T(8,128)(2,1)S(1)} %pad_maximum_fusion.3), channel_id=1, source_target_pairs={{0,8},{4,12},{1,9},{5,13},{2,10},{6,14},{3,11},{7,15},{16,24},{20,... | collective-permute-start | bytes 394760 | tf_op jit(solution)/shard_map/ppermute | solution.py:17
  7.6 3.5 %collective-permute-start.1 = (bf16[514,128]{1,0:T(8,128)(2,1)S(1)}, bf16[514,128]{1,0:T(8,128)(2,1)S(1)}, u32[]{:S(2)}, u32[]{:S(2)}) collective-permute-start(bf16[514,128]{1,0:T(8,128)(2,1)S(1)} %pad_maximum_fusion.3), channel_id=1, source_target_pairs={{0,4},{4,8},{8,12},{1,5},{5,9},{9,13},{2,6},{6,10},{10,14},{3,7},{... | collective-permute-start | bytes 394760 | tf_op jit(solution)/shard_map/ppermute | solution.py:17
  11.1 0.1 collective-permute-start
  11.2 0.9 %copy.23 = bf16[1,256,2,128]{3,1,2,0:T(8,128)(2,1)S(1)} copy(bf16[1,256,2,128]{3,2,1,0:T(2,128)(2,1)} %param.5) | data formatting | bytes 262144 | tf_op args[1]
  12.1 1.0 %reshape.74 = bf16[256,4,128]{2,1,0:T(4,128)(2,1)S(1)} reshape(bf16[1,256,512]{2,1,0:T(8,128)(2,1)} %param.4) | data formatting | bytes 524288 | tf_op jit(solution)/shard_map/reshape.1
  13.2 0.0 collective-permute-done.2
  13.2 1.8 %collective-permute-done.1 = bf16[514,128]{1,0:T(8,128)(2,1)S(1)} collective-permute-done((bf16[514,128]{1,0:T(8,128)(2,1)S(1)}, bf16[514,128]{1,0:T(8,128)(2,1)S(1)}, u32[]{:S(2)}, u32[]{:S(2)}) %collective-permute-start.1) | collective-permute-done | bytes 131616 | tf_op jit(solution)/shard_map/ppermute | solution.py:17
  15.1 0.7 pad_add_fusion
  15.8 1.4 %and_and_fusion = pred[256,768]{0,1:T(8,128)(4,1)S(1)} fusion(s32[256]{0:T(256)S(1)} %iota_add_fusion.2, s32[256]{0:T(256)} %bitcast.86, s32[768]{0:T(1024)S(1)} %pad_add_fusion.1, s32[768]{0:T(1024)S(1)} %pad_add_fusion, pred[768]{0:T(1024)(128)(4,1)S(1)} %broadcast_compare_fusion), kind=kLoop, calls=%fused_computation.14 | loop fusion | flops 786432 | bytes 205568 | tf_op jit(solution)/shard_map/and | solution.py:72
  17.2 0.7 fusion
  17.9 0.8 %fusion.1 = f32[4,256]{1,0:T(4,128)S(1)} fusion(f32[768,256,4]{1,0,2:T(8,128)S(1)} %get-tuple-element.23, f32[4,256]{1,0:T(4,128)S(1)} %get-tuple-element.22, pred[256,768]{0,1:T(8,128)(4,1)S(1)} %and_and_fusion), kind=kLoop, calls=%fused_computation.3 | loop fusion | flops 3931136 | bytes 3350528 | tf_op jit(solution)/shard_map/reduce_sum | solution.py:79
  18.7 0.0 copy-start
  18.7 0.9 %fusion.13 = bf16[256,1,4,128]{0,3,2,1:T(8,128)(2,1)S(1)} fusion(f32[768,256,4]{1,0,2:T(8,128)S(1)} %get-tuple-element.23, f32[4,256]{1,0:T(4,128)S(1)} %get-tuple-element.22, pred[256,768]{0,1:T(8,128)(4,1)S(1)} %and_and_fusion, f32[256,4]{0,1:T(4,128)S(1)} %bitcast.84, bf16[768,2,128]{2,0,1:T(8,128)(2,1)S(1)} %pad_maximum_fusion.2), kind=kOutput, calls=%fused_computation.13 | convolution fusion | flops 205520896 | bytes 3809280 | tf_op jit(solution)/shard_map/hgqk,khd->qhgd/dot_general | solution.py:80
  19.6 6.6 %collective-permute-done = bf16[256,1024]{1,0:T(8,128)(2,1)S(1)} collective-permute-done((bf16[256,1024]{1,0:T(8,128)(2,1)}, bf16[256,1024]{1,0:T(8,128)(2,1)S(1)}, u32[]{:S(2)}, u32[]{:S(2)}) %collective-permute-start) | collective-permute-done | bytes 524320 | tf_op jit(solution)/shard_map/ppermute | solution.py:126
  26.2 2.7 %collective-permute-start.7 = (bf16[256,1024]{1,0:T(8,128)(2,1)S(1)}, bf16[256,1024]{1,0:T(8,128)(2,1)S(1)}, u32[]{:S(2)}, u32[]{:S(2)}) collective-permute-start(bf16[256,1024]{1,0:T(8,128)(2,1)S(1)} %collective-permute-done), channel_id=1, source_target_pairs={{0,4},{4,8},{8,12},{12,0},{1,5},{5,9},{9,13},{13,1},{2,6},{6,10},{... | collective-permute-start | bytes 1572872 | tf_op jit(solution)/shard_map/ppermute | solution.py:126
  28.9 1.5 %collective-permute-start.3 = (bf16[256,512]{0,1:T(8,128)(2,1)S(1)}, bf16[256,512]{0,1:T(8,128)(2,1)S(1)}, u32[]{:S(2)}, u32[]{:S(2)}) collective-permute-start(bf16[256,512]{0,1:T(8,128)(2,1)S(1)} %bitcast.82), channel_id=1, source_target_pairs={{0,16},{16,0},{1,17},{17,1},{2,18},{18,2},{3,19},{19,3},{4,20},{20... | collective-permute-start | bytes 786440 | tf_op jit(solution)/shard_map/ppermute | solution.py:93
  30.4 6.4 %collective-permute-done.3 = bf16[256,512]{0,1:T(8,128)(2,1)S(1)} collective-permute-done((bf16[256,512]{0,1:T(8,128)(2,1)S(1)}, bf16[256,512]{0,1:T(8,128)(2,1)S(1)}, u32[]{:S(2)}, u32[]{:S(2)}) %collective-permute-start.3) | collective-permute-done | bytes 262176 | tf_op jit(solution)/shard_map/ppermute | solution.py:93
  36.9 3.5 %collective-permute-start.4 = (bf16[256,1024]{0,1:T(8,128)(2,1)S(1)}, bf16[256,1024]{0,1:T(8,128)(2,1)S(1)}, u32[]{:S(2)}, u32[]{:S(2)}) collective-permute-start(bf16[256,1024]{0,1:T(8,128)(2,1)S(1)} %constant_dynamic-update-slice_fusion), channel_id=1, source_target_pairs={{0,2},{1,3},{18,16},{19,17},{4,6},{5,7},{22,20},{23,21},{8,10},{9,... | collective-permute-start | bytes 1572872 | tf_op jit(solution)/shard_map/ppermute | solution.py:97
  40.3 0.0 collective-permute-done.7
  40.3 2.4 %collective-permute-start.8 = (bf16[256,1024]{1,0:T(8,128)(2,1)S(1)}, bf16[256,1024]{1,0:T(8,128)(2,1)S(1)}, u32[]{:S(2)}, u32[]{:S(2)}) collective-permute-start(bf16[256,1024]{1,0:T(8,128)(2,1)S(1)} %collective-permute-done.7), channel_id=1, source_target_pairs={{0,4},{4,8},{8,12},{12,0},{1,5},{5,9},{9,13},{13,1},{2,6},{6,10},{... | collective-permute-start | bytes 1572872 | tf_op jit(solution)/shard_map/ppermute | solution.py:126
  42.8 1.9 %collective-permute-start.5 = (bf16[256,1024]{0,1:T(8,128)(2,1)S(1)}, bf16[256,1024]{0,1:T(8,128)(2,1)S(1)}, u32[]{:S(2)}, u32[]{:S(2)}) collective-permute-start(bf16[256,1024]{0,1:T(8,128)(2,1)S(1)} %constant_dynamic-update-slice_fusion), channel_id=1, source_target_pairs={{0,1},{1,0},{18,19},{19,18},{4,5},{5,4},{22,23},{23,22},{8,9},{9,8... | collective-permute-start | bytes 1572872 | tf_op jit(solution)/shard_map/ppermute | solution.py:97
  44.7 5.8 %collective-permute-done.4 = bf16[256,1024]{0,1:T(8,128)(2,1)S(1)} collective-permute-done((bf16[256,1024]{0,1:T(8,128)(2,1)S(1)}, bf16[256,1024]{0,1:T(8,128)(2,1)S(1)}, u32[]{:S(2)}, u32[]{:S(2)}) %collective-permute-start.4) | collective-permute-done | bytes 524320 | tf_op jit(solution)/shard_map/ppermute | solution.py:97
  50.5 0.7 collective-permute-start.6
  51.2 4.7 %collective-permute-done.8 = bf16[256,1024]{1,0:T(8,128)(2,1)S(1)} collective-permute-done((bf16[256,1024]{1,0:T(8,128)(2,1)S(1)}, bf16[256,1024]{1,0:T(8,128)(2,1)S(1)}, u32[]{:S(2)}, u32[]{:S(2)}) %collective-permute-start.8) | collective-permute-done | bytes 524320 | tf_op jit(solution)/shard_map/ppermute | solution.py:126
  55.9 0.0 copy-done
  55.9 0.1 select_select_fusion.2
  56.0 0.2 select_select_fusion.3
  56.2 0.2 pad_maximum_fusion
  56.4 0.0 collective-permute-done.5
  56.4 0.0 collective-permute-done.6
  56.4 0.1 broadcast_select_fusion.3
  56.6 0.7 %convolution_convert_fusion = bf16[256,1024]{1,0:T(8,128)(2,1)S(1)} fusion(bf16[1024,1024]{1,0:T(8,128)(2,1)S(1)} %pad_maximum_fusion, bf16[256,512]{0,1:T(8,128)(2,1)S(1)} %get-tuple-element.21, bf16[256,512]{0,1:T(8,128)(2,1)S(1)} %get-tuple-element.19), kind=kOutput, calls=%fused_computation.9 | convolution fusion | flops 538181632 | bytes 3145728 | tf_op jit(solution)/shard_map/dot_general | solution.py:148
  57.3 1.6 %collective-permute-start.9 = (bf16[256,1024]{1,0:T(8,128)(2,1)S(1)}, bf16[256,1024]{1,0:T(8,128)(2,1)S(1)}, u32[]{:S(2)}, u32[]{:S(2)}) collective-permute-start(bf16[256,1024]{1,0:T(8,128)(2,1)S(1)} %convolution_convert_fusion), channel_id=1, source_target_pairs={{0,16},{16,0},{1,17},{17,1},{2,18},{18,2},{3,19},{19,3},{4,20},{20... | collective-permute-start | bytes 1572872 | tf_op jit(solution)/shard_map/ppermute | solution.py:93
  58.9 0.7 %fusion.30 = f32[256,1024]{1,0:T(8,128)S(1)} fusion(bf16[256,1024]{0,1:T(8,128)(2,1)S(1)} %pad_maximum_fusion.1, bf16[1024,1024]{1,0:T(8,128)(2,1)S(1)} %pad_maximum_fusion), kind=kOutput, calls=%fused_computation.54 | convolution fusion | flops 536870912 | bytes 3670016 | tf_op jit(solution)/shard_map/dot_general | solution.py:152
  59.7 10.5 %collective-permute-done.9 = bf16[256,1024]{1,0:T(8,128)(2,1)S(1)} collective-permute-done((bf16[256,1024]{1,0:T(8,128)(2,1)S(1)}, bf16[256,1024]{1,0:T(8,128)(2,1)S(1)}, u32[]{:S(2)}, u32[]{:S(2)}) %collective-permute-start.9) | collective-permute-done | bytes 524320 | tf_op jit(solution)/shard_map/ppermute | solution.py:93
  70.1 0.9 %fusion.16 = bf16[1,256,1024]{2,1,0:T(8,128)(2,1)} fusion(f32[256,1024]{1,0:T(8,128)S(1)} %fusion.30, bf16[256,1024]{1,0:T(8,128)(2,1)S(1)} %collective-permute-done.9), kind=kLoop, calls=%fused_computation.15 | loop fusion | flops 786432 | bytes 2097152 | tf_op jit(solution)/shard_map/broadcast_in_dim | solution.py:168
  (16 shorter events, 0.3 us)
Async XLA Ops:
  1.6 11.5 %collective-permute-start.2 = (bf16[514,128]{1,0:T(8,128)(2,1)S(1)}, bf16[514,128]{1,0:T(8,128)(2,1)S(1)}, u32[]{:S(2)}, u32[]{:S(2)}) collective-permute-start(bf16[514,128]{1,0:T(8,128)(2,1)S(1)} %pad_maximum_fusion.3), channel_id=1, source_target_pairs={{0,8},{4,12},{1,9},{5,13},{2,10},{6,14},{3,11},{7,15},{16,24},{20,... | collective-permute-start | bytes 394760 | tf_op jit(solution)/shard_map/ppermute | solution.py:17
  7.6 7.5 %collective-permute-start.1 = (bf16[514,128]{1,0:T(8,128)(2,1)S(1)}, bf16[514,128]{1,0:T(8,128)(2,1)S(1)}, u32[]{:S(2)}, u32[]{:S(2)}) collective-permute-start(bf16[514,128]{1,0:T(8,128)(2,1)S(1)} %pad_maximum_fusion.3), channel_id=1, source_target_pairs={{0,4},{4,8},{8,12},{1,5},{5,9},{9,13},{2,6},{6,10},{10,14},{3,7},{... | collective-permute-start | bytes 394760 | tf_op jit(solution)/shard_map/ppermute | solution.py:17
  11.1 15.2 %collective-permute-start = (bf16[256,1024]{1,0:T(8,128)(2,1)}, bf16[256,1024]{1,0:T(8,128)(2,1)S(1)}, u32[]{:S(2)}, u32[]{:S(2)}) collective-permute-start(bf16[256,1024]{1,0:T(8,128)(2,1)} %param.7), channel_id=1, source_target_pairs={{0,4},{4,8},{8,12},{12,0},{1,5},{5,9},{9,13},{13,1},{2,6},{6,10},{... | collective-permute-start | bytes 1572872 | tf_op jit(solution)/shard_map/ppermute | solution.py:126
  18.7 37.2 %copy-start = (bf16[256,1024]{1,0:T(8,128)(2,1)S(1)}, bf16[256,1024]{1,0:T(8,128)(2,1)}, u32[]{:S(2)}) copy-start(bf16[256,1024]{1,0:T(8,128)(2,1)} %param.7) | copy-start | bytes 1572868
  26.2 14.1 %collective-permute-start.7 = (bf16[256,1024]{1,0:T(8,128)(2,1)S(1)}, bf16[256,1024]{1,0:T(8,128)(2,1)S(1)}, u32[]{:S(2)}, u32[]{:S(2)}) collective-permute-start(bf16[256,1024]{1,0:T(8,128)(2,1)S(1)} %collective-permute-done), channel_id=1, source_target_pairs={{0,4},{4,8},{8,12},{12,0},{1,5},{5,9},{9,13},{13,1},{2,6},{6,10},{... | collective-permute-start | bytes 1572872 | tf_op jit(solution)/shard_map/ppermute | solution.py:126
  28.9 7.9 %collective-permute-start.3 = (bf16[256,512]{0,1:T(8,128)(2,1)S(1)}, bf16[256,512]{0,1:T(8,128)(2,1)S(1)}, u32[]{:S(2)}, u32[]{:S(2)}) collective-permute-start(bf16[256,512]{0,1:T(8,128)(2,1)S(1)} %bitcast.82), channel_id=1, source_target_pairs={{0,16},{16,0},{1,17},{17,1},{2,18},{18,2},{3,19},{19,3},{4,20},{20... | collective-permute-start | bytes 786440 | tf_op jit(solution)/shard_map/ppermute | solution.py:93
  36.9 13.6 %collective-permute-start.4 = (bf16[256,1024]{0,1:T(8,128)(2,1)S(1)}, bf16[256,1024]{0,1:T(8,128)(2,1)S(1)}, u32[]{:S(2)}, u32[]{:S(2)}) collective-permute-start(bf16[256,1024]{0,1:T(8,128)(2,1)S(1)} %constant_dynamic-update-slice_fusion), channel_id=1, source_target_pairs={{0,2},{1,3},{18,16},{19,17},{4,6},{5,7},{22,20},{23,21},{8,10},{9,... | collective-permute-start | bytes 1572872 | tf_op jit(solution)/shard_map/ppermute | solution.py:97
  40.3 15.5 %collective-permute-start.8 = (bf16[256,1024]{1,0:T(8,128)(2,1)S(1)}, bf16[256,1024]{1,0:T(8,128)(2,1)S(1)}, u32[]{:S(2)}, u32[]{:S(2)}) collective-permute-start(bf16[256,1024]{1,0:T(8,128)(2,1)S(1)} %collective-permute-done.7), channel_id=1, source_target_pairs={{0,4},{4,8},{8,12},{12,0},{1,5},{5,9},{9,13},{13,1},{2,6},{6,10},{... | collective-permute-start | bytes 1572872 | tf_op jit(solution)/shard_map/ppermute | solution.py:126
  42.8 13.6 %collective-permute-start.5 = (bf16[256,1024]{0,1:T(8,128)(2,1)S(1)}, bf16[256,1024]{0,1:T(8,128)(2,1)S(1)}, u32[]{:S(2)}, u32[]{:S(2)}) collective-permute-start(bf16[256,1024]{0,1:T(8,128)(2,1)S(1)} %constant_dynamic-update-slice_fusion), channel_id=1, source_target_pairs={{0,1},{1,0},{18,19},{19,18},{4,5},{5,4},{22,23},{23,22},{8,9},{9,8... | collective-permute-start | bytes 1572872 | tf_op jit(solution)/shard_map/ppermute | solution.py:97
  50.5 5.9 %collective-permute-start.6 = (bf16[256,1024]{0,1:T(8,128)(2,1)S(1)}, bf16[256,1024]{0,1:T(8,128)(2,1)S(1)}, u32[]{:S(2)}, u32[]{:S(2)}) collective-permute-start(bf16[256,1024]{0,1:T(8,128)(2,1)S(1)} %collective-permute-done.4), channel_id=1, source_target_pairs={{2,3},{3,2},{16,17},{17,16},{6,7},{7,6},{20,21},{21,20},{10,11},{1... | collective-permute-start | bytes 1572872 | tf_op jit(solution)/shard_map/ppermute | solution.py:97
  57.3 12.8 %collective-permute-start.9 = (bf16[256,1024]{1,0:T(8,128)(2,1)S(1)}, bf16[256,1024]{1,0:T(8,128)(2,1)S(1)}, u32[]{:S(2)}, u32[]{:S(2)}) collective-permute-start(bf16[256,1024]{1,0:T(8,128)(2,1)S(1)} %convolution_convert_fusion), channel_id=1, source_target_pairs={{0,16},{16,0},{1,17},{17,1},{2,18},{18,2},{3,19},{19,3},{4,20},{20... | collective-permute-start | bytes 1572872 | tf_op jit(solution)/shard_map/ppermute | solution.py:93

commit v24 on v23

--- a/solution.py
+++ b/solution.py
@@ -105,13 +105,9 @@
     mine = jnp.concatenate([head_values, foreign], axis=1)
     owners = [(s, 2 * s + k) for s in range(2) for k in range(2)]
     over_y = sent(mine, [(s * group + p, s * group + (p ^ 2)) for s, p in owners])
-    beside = sent(mine, [(s * group + p, s * group + (p ^ 1)) for s, p in owners])
-    relayed = sent(
-        over_y, [(s * group + (p ^ 2), s * group + (p ^ 3)) for s, p in owners]
-    )
     on_owner = me // 2 == side
     same_core = jnp.where(on_owner, mine, over_y)
-    other_core = jnp.where(on_owner, beside, relayed)
+    other_core = lax.ppermute(same_core, "tensor", [(t, t ^ 1) for t in range(group)])
     first_core = me % 2 == 0
     width = head_values.shape[1]
     lower = jnp.where(first_core, same_core, other_core)

time: 71.4 us -> 71.8 us (level)
  waiting for transfers between devices: 35.8 us -> 39.7 us
  starting transfers between devices: 23.7 us -> 20.2 us
    ppermute x3, waiting for transfers between devices: 11.3 us -> 23.4 us  [ring_step(): lax.ppermute(block, axis, [(i, (i + 1) % count) for i in range(count)])]
    ppermute x3 -> x1, waiting for transfers between devices: 5.8 us -> 1.04 us  [sent(): return lax.ppermute(block, ('dp', 'tensor'), route)]
    ppermute x2, waiting for transfers between devices: 16.9 us -> 13.4 us  [swapped(): return lax.ppermute(block, axis, [(0, 1), (1, 0)])]
    ppermute x3 -> x1, starting transfers between devices: 6.05 us -> 3.46 us  [sent(): return lax.ppermute(block, ('dp', 'tensor'), route)]
    ppermute x2, starting transfers between devices: 3.05 us -> 2.09 us  [swapped(): return lax.ppermute(block, axis, [(0, 1), (1, 0)])]
  transfers between devices with their start and end apart: 10 -> 9, of which waited for: 6 -> 7; matrix products, arithmetic and copies ran while one was open for 11% -> 11% of each run, Pallas kernels for 0% -> 0%
where the time goes in v24:
time: 71.8 us; the launch traced here: 71.5 us
  waiting for transfers between devices  39.7 us (55%)
  starting transfers between devices  20.2 us (28%)
  other arithmetic  6.15 us (9%)
  matrix products  3.04 us (4%)
  local copies, waits for them, and re-layouts  2.12 us (3%)
    ppermute x3, waiting for transfers between devices, ring_step(): lax.ppermute(block, axis, [(i, (i + 1) % count) for i in range(count)])  23.4 us
    ppermute x2, waiting for transfers between devices, swapped(): return lax.ppermute(block, axis, [(0, 1), (1, 0)])  13.4 us
    ppermute x2, starting transfers between devices, shifted(): return lax.ppermute(block, axis, route)  9.44 us
    ppermute x3, starting transfers between devices, ring_step(): lax.ppermute(block, axis, [(i, (i + 1) % count) for i in range(count)])  5.18 us
    ppermute x1, starting transfers between devices, sent(): return lax.ppermute(block, ('dp', 'tensor'), route)  3.46 us
    ppermute x2, starting transfers between devices, swapped(): return lax.ppermute(block, axis, [(0, 1), (1, 0)])  2.09 us
    ppermute x2, waiting for transfers between devices, shifted(): return lax.ppermute(block, axis, route)  1.82 us
  transfers between devices with their start and end apart: 9, of which 7 were waited for; matrix products, arithmetic and copies ran while one was open for 11% of the time, Pallas kernels for 0%

profile of v24, /device:TPU:0, one launch (start us, length us, event | category | flops | bytes accessed | tf_op | source)
XLA Modules:
  0.0 71.5 jit_solution(13052765933070688806)
XLA Ops:
  0.0 0.7 convert_reduce_fusion
  0.7 0.9 %pad_maximum_fusion.3 = bf16[514,128]{1,0:T(8,128)(2,1)S(1)} fusion(bf16[2,128]{1,0:T(2,128)(2,1)S(1)} %bitcast.87, bf16[512,128]{1,0:T(8,128)(2,1)} %bitcast.78), kind=kLoop, calls=%fused_computation.32 | loop fusion | flops 263168 | bytes 263168 | tf_op jit(solution)/shard_map/concatenate | solution.py:41
  1.6 5.9 %collective-permute-start.2 = (bf16[514,128]{1,0:T(8,128)(2,1)S(1)}, bf16[514,128]{1,0:T(8,128)(2,1)S(1)}, u32[]{:S(2)}, u32[]{:S(2)}) collective-permute-start(bf16[514,128]{1,0:T(8,128)(2,1)S(1)} %pad_maximum_fusion.3), channel_id=1, source_target_pairs={{0,8},{4,12},{1,9},{5,13},{2,10},{6,14},{3,11},{7,15},{16,24},{20,... | collective-permute-start | bytes 394760 | tf_op jit(solution)/shard_map/ppermute | solution.py:17
  7.6 3.5 %collective-permute-start.1 = (bf16[514,128]{1,0:T(8,128)(2,1)S(1)}, bf16[514,128]{1,0:T(8,128)(2,1)S(1)}, u32[]{:S(2)}, u32[]{:S(2)}) collective-permute-start(bf16[514,128]{1,0:T(8,128)(2,1)S(1)} %pad_maximum_fusion.3), channel_id=1, source_target_pairs={{0,4},{4,8},{8,12},{1,5},{5,9},{9,13},{2,6},{6,10},{10,14},{3,7},{... | collective-permute-start | bytes 394760 | tf_op jit(solution)/shard_map/ppermute | solution.py:17
  11.1 0.1 collective-permute-start
  11.2 0.9 %copy.23 = bf16[1,256,2,128]{3,1,2,0:T(8,128)(2,1)S(1)} copy(bf16[1,256,2,128]{3,2,1,0:T(2,128)(2,1)} %param.5) | data formatting | bytes 262144 | tf_op args[1]
  12.1 1.0 %reshape.74 = bf16[256,4,128]{2,1,0:T(4,128)(2,1)S(1)} reshape(bf16[1,256,512]{2,1,0:T(8,128)(2,1)} %param.4) | data formatting | bytes 524288 | tf_op jit(solution)/shard_map/reshape.1
  13.2 0.0 collective-permute-done.2
  13.2 1.8 %collective-permute-done.1 = bf16[514,128]{1,0:T(8,128)(2,1)S(1)} collective-permute-done((bf16[514,128]{1,0:T(8,128)(2,1)S(1)}, bf16[514,128]{1,0:T(8,128)(2,1)S(1)}, u32[]{:S(2)}, u32[]{:S(2)}) %collective-permute-start.1) | collective-permute-done | bytes 131616 | tf_op jit(solution)/shard_map/ppermute | solution.py:17
  15.1 0.7 pad_add_fusion
  15.8 1.4 %and_and_fusion = pred[256,768]{0,1:T(8,128)(4,1)S(1)} fusion(s32[256]{0:T(256)S(1)} %iota_add_fusion.2, s32[256]{0:T(256)} %bitcast.86, s32[768]{0:T(1024)S(1)} %pad_add_fusion.1, s32[768]{0:T(1024)S(1)} %pad_add_fusion, pred[768]{0:T(1024)(128)(4,1)S(1)} %broadcast_compare_fusion), kind=kLoop, calls=%fused_computation.14 | loop fusion | flops 786432 | bytes 205568 | tf_op jit(solution)/shard_map/and | solution.py:72
  17.2 0.7 fusion
  17.9 0.8 %fusion.1 = f32[4,256]{1,0:T(4,128)S(1)} fusion(f32[768,256,4]{1,0,2:T(8,128)S(1)} %get-tuple-element.23, f32[4,256]{1,0:T(4,128)S(1)} %get-tuple-element.22, pred[256,768]{0,1:T(8,128)(4,1)S(1)} %and_and_fusion), kind=kLoop, calls=%fused_computation.3 | loop fusion | flops 3931136 | bytes 3350528 | tf_op jit(solution)/shard_map/reduce_sum | solution.py:79
  18.7 0.9 %fusion.13 = bf16[256,1,4,128]{0,3,2,1:T(8,128)(2,1)S(1)} fusion(f32[768,256,4]{1,0,2:T(8,128)S(1)} %get-tuple-element.23, f32[4,256]{1,0:T(4,128)S(1)} %get-tuple-element.22, pred[256,768]{0,1:T(8,128)(4,1)S(1)} %and_and_fusion, f32[256,4]{0,1:T(4,128)S(1)} %bitcast.84, bf16[768,2,128]{2,0,1:T(8,128)(2,1)S(1)} %pad_maximum_fusion.2), kind=kOutput, calls=%fused_computation.13 | convolution fusion | flops 205520896 | bytes 3809280 | tf_op jit(solution)/shard_map/hgqk,khd->qhgd/dot_general | solution.py:80
  19.6 0.0 copy-start
  19.6 6.6 %collective-permute-done = bf16[256,1024]{1,0:T(8,128)(2,1)S(1)} collective-permute-done((bf16[256,1024]{1,0:T(8,128)(2,1)}, bf16[256,1024]{1,0:T(8,128)(2,1)S(1)}, u32[]{:S(2)}, u32[]{:S(2)}) %collective-permute-start) | collective-permute-done | bytes 524320 | tf_op jit(solution)/shard_map/ppermute | solution.py:122
  26.2 1.5 %collective-permute-start.3 = (bf16[256,512]{0,1:T(8,128)(2,1)S(1)}, bf16[256,512]{0,1:T(8,128)(2,1)S(1)}, u32[]{:S(2)}, u32[]{:S(2)}) collective-permute-start(bf16[256,512]{0,1:T(8,128)(2,1)S(1)} %bitcast.82), channel_id=1, source_target_pairs={{0,16},{16,0},{1,17},{17,1},{2,18},{18,2},{3,19},{19,3},{4,20},{20... | collective-permute-start | bytes 786440 | tf_op jit(solution)/shard_map/ppermute | solution.py:93
  27.7 2.7 %collective-permute-start.6 = (bf16[256,1024]{1,0:T(8,128)(2,1)S(1)}, bf16[256,1024]{1,0:T(8,128)(2,1)S(1)}, u32[]{:S(2)}, u32[]{:S(2)}) collective-permute-start(bf16[256,1024]{1,0:T(8,128)(2,1)S(1)} %collective-permute-done), channel_id=1, source_target_pairs={{0,4},{4,8},{8,12},{12,0},{1,5},{5,9},{9,13},{13,1},{2,6},{6,10},{... | collective-permute-start | bytes 1572872 | tf_op jit(solution)/shard_map/ppermute | solution.py:122
  30.4 2.4 %collective-permute-done.3 = bf16[256,512]{0,1:T(8,128)(2,1)S(1)} collective-permute-done((bf16[256,512]{0,1:T(8,128)(2,1)S(1)}, bf16[256,512]{0,1:T(8,128)(2,1)S(1)}, u32[]{:S(2)}, u32[]{:S(2)}) %collective-permute-start.3) | collective-permute-done | bytes 262176 | tf_op jit(solution)/shard_map/ppermute | solution.py:93
  32.8 3.5 %collective-permute-start.4 = (bf16[256,1024]{0,1:T(8,128)(2,1)S(1)}, bf16[256,1024]{0,1:T(8,128)(2,1)S(1)}, u32[]{:S(2)}, u32[]{:S(2)}) collective-permute-start(bf16[256,1024]{0,1:T(8,128)(2,1)S(1)} %constant_dynamic-update-slice_fusion), channel_id=1, source_target_pairs={{0,2},{1,3},{18,16},{19,17},{4,6},{5,7},{22,20},{23,21},{8,10},{9,... | collective-permute-start | bytes 1572872 | tf_op jit(solution)/shard_map/ppermute | solution.py:97
  36.3 5.2 %collective-permute-done.6 = bf16[256,1024]{1,0:T(8,128)(2,1)S(1)} collective-permute-done((bf16[256,1024]{1,0:T(8,128)(2,1)S(1)}, bf16[256,1024]{1,0:T(8,128)(2,1)S(1)}, u32[]{:S(2)}, u32[]{:S(2)}) %collective-permute-start.6) | collective-permute-done | bytes 524320 | tf_op jit(solution)/shard_map/ppermute | solution.py:122
  41.5 2.5 %collective-permute-start.7 = (bf16[256,1024]{1,0:T(8,128)(2,1)S(1)}, bf16[256,1024]{1,0:T(8,128)(2,1)S(1)}, u32[]{:S(2)}, u32[]{:S(2)}) collective-permute-start(bf16[256,1024]{1,0:T(8,128)(2,1)S(1)} %collective-permute-done.6), channel_id=1, source_target_pairs={{0,4},{4,8},{8,12},{12,0},{1,5},{5,9},{9,13},{13,1},{2,6},{6,10},{... | collective-permute-start | bytes 1572872 | tf_op jit(solution)/shard_map/ppermute | solution.py:122
  44.0 1.0 %collective-permute-done.4 = bf16[256,1024]{0,1:T(8,128)(2,1)S(1)} collective-permute-done((bf16[256,1024]{0,1:T(8,128)(2,1)S(1)}, bf16[256,1024]{0,1:T(8,128)(2,1)S(1)}, u32[]{:S(2)}, u32[]{:S(2)}) %collective-permute-start.4) | collective-permute-done | bytes 524320 | tf_op jit(solution)/shard_map/ppermute | solution.py:97
  45.0 0.1 broadcast_select_fusion
  45.1 0.1 collective-permute-start.5
  45.1 11.6 %collective-permute-done.7 = bf16[256,1024]{1,0:T(8,128)(2,1)S(1)} collective-permute-done((bf16[256,1024]{1,0:T(8,128)(2,1)S(1)}, bf16[256,1024]{1,0:T(8,128)(2,1)S(1)}, u32[]{:S(2)}, u32[]{:S(2)}) %collective-permute-start.7) | collective-permute-done | bytes 524320 | tf_op jit(solution)/shard_map/ppermute | solution.py:122
  56.7 0.0 copy-done
  56.8 0.1 select_select_fusion.2
  56.8 0.2 select_select_fusion.3
  57.1 0.2 pad_maximum_fusion
  57.3 0.0 collective-permute-done.5
  57.3 0.1 broadcast_select_fusion.2
  57.4 0.7 %convolution_convert_fusion = bf16[256,1024]{1,0:T(8,128)(2,1)S(1)} fusion(bf16[1024,1024]{1,0:T(8,128)(2,1)S(1)} %pad_maximum_fusion, bf16[256,512]{0,1:T(8,128)(2,1)S(1)} %get-tuple-element.21, bf16[256,512]{0,1:T(8,128)(2,1)S(1)} %get-tuple-element.19), kind=kOutput, calls=%fused_computation.9 | convolution fusion | flops 538181632 | bytes 3145728 | tf_op jit(solution)/shard_map/dot_general | solution.py:144
  58.2 0.6 collective-permute-start.8
  58.8 0.7 %fusion.30 = f32[256,1024]{1,0:T(8,128)S(1)} fusion(bf16[256,1024]{0,1:T(8,128)(2,1)S(1)} %pad_maximum_fusion.1, bf16[1024,1024]{1,0:T(8,128)(2,1)S(1)} %pad_maximum_fusion), kind=kOutput, calls=%fused_computation.53 | convolution fusion | flops 536870912 | bytes 3670016 | tf_op jit(solution)/shard_map/dot_general | solution.py:148
  59.5 11.1 %collective-permute-done.8 = bf16[256,1024]{1,0:T(8,128)(2,1)S(1)} collective-permute-done((bf16[256,1024]{1,0:T(8,128)(2,1)S(1)}, bf16[256,1024]{1,0:T(8,128)(2,1)S(1)}, u32[]{:S(2)}, u32[]{:S(2)}) %collective-permute-start.8) | collective-permute-done | bytes 524320 | tf_op jit(solution)/shard_map/ppermute | solution.py:93
  70.6 0.9 %fusion.16 = bf16[1,256,1024]{2,1,0:T(8,128)(2,1)} fusion(f32[256,1024]{1,0:T(8,128)S(1)} %fusion.30, bf16[256,1024]{1,0:T(8,128)(2,1)S(1)} %collective-permute-done.8), kind=kLoop, calls=%fused_computation.15 | loop fusion | flops 786432 | bytes 2097152 | tf_op jit(solution)/shard_map/broadcast_in_dim | solution.py:164
  (16 shorter events, 0.3 us)
Async XLA Ops:
  1.6 11.5 %collective-permute-start.2 = (bf16[514,128]{1,0:T(8,128)(2,1)S(1)}, bf16[514,128]{1,0:T(8,128)(2,1)S(1)}, u32[]{:S(2)}, u32[]{:S(2)}) collective-permute-start(bf16[514,128]{1,0:T(8,128)(2,1)S(1)} %pad_maximum_fusion.3), channel_id=1, source_target_pairs={{0,8},{4,12},{1,9},{5,13},{2,10},{6,14},{3,11},{7,15},{16,24},{20,... | collective-permute-start | bytes 394760 | tf_op jit(solution)/shard_map/ppermute | solution.py:17
  7.6 7.5 %collective-permute-start.1 = (bf16[514,128]{1,0:T(8,128)(2,1)S(1)}, bf16[514,128]{1,0:T(8,128)(2,1)S(1)}, u32[]{:S(2)}, u32[]{:S(2)}) collective-permute-start(bf16[514,128]{1,0:T(8,128)(2,1)S(1)} %pad_maximum_fusion.3), channel_id=1, source_target_pairs={{0,4},{4,8},{8,12},{1,5},{5,9},{9,13},{2,6},{6,10},{10,14},{3,7},{... | collective-permute-start | bytes 394760 | tf_op jit(solution)/shard_map/ppermute | solution.py:17
  11.1 15.2 %collective-permute-start = (bf16[256,1024]{1,0:T(8,128)(2,1)}, bf16[256,1024]{1,0:T(8,128)(2,1)S(1)}, u32[]{:S(2)}, u32[]{:S(2)}) collective-permute-start(bf16[256,1024]{1,0:T(8,128)(2,1)} %param.7), channel_id=1, source_target_pairs={{0,4},{4,8},{8,12},{12,0},{1,5},{5,9},{9,13},{13,1},{2,6},{6,10},{... | collective-permute-start | bytes 1572872 | tf_op jit(solution)/shard_map/ppermute | solution.py:122
  19.6 37.1 %copy-start = (bf16[256,1024]{1,0:T(8,128)(2,1)S(1)}, bf16[256,1024]{1,0:T(8,128)(2,1)}, u32[]{:S(2)}) copy-start(bf16[256,1024]{1,0:T(8,128)(2,1)} %param.7) | copy-start | bytes 1572868
  26.2 6.6 %collective-permute-start.3 = (bf16[256,512]{0,1:T(8,128)(2,1)S(1)}, bf16[256,512]{0,1:T(8,128)(2,1)S(1)}, u32[]{:S(2)}, u32[]{:S(2)}) collective-permute-start(bf16[256,512]{0,1:T(8,128)(2,1)S(1)} %bitcast.82), channel_id=1, source_target_pairs={{0,16},{16,0},{1,17},{17,1},{2,18},{18,2},{3,19},{19,3},{4,20},{20... | collective-permute-start | bytes 786440 | tf_op jit(solution)/shard_map/ppermute | solution.py:93
  27.7 13.8 %collective-permute-start.6 = (bf16[256,1024]{1,0:T(8,128)(2,1)S(1)}, bf16[256,1024]{1,0:T(8,128)(2,1)S(1)}, u32[]{:S(2)}, u32[]{:S(2)}) collective-permute-start(bf16[256,1024]{1,0:T(8,128)(2,1)S(1)} %collective-permute-done), channel_id=1, source_target_pairs={{0,4},{4,8},{8,12},{12,0},{1,5},{5,9},{9,13},{13,1},{2,6},{6,10},{... | collective-permute-start | bytes 1572872 | tf_op jit(solution)/shard_map/ppermute | solution.py:122
  32.8 12.2 %collective-permute-start.4 = (bf16[256,1024]{0,1:T(8,128)(2,1)S(1)}, bf16[256,1024]{0,1:T(8,128)(2,1)S(1)}, u32[]{:S(2)}, u32[]{:S(2)}) collective-permute-start(bf16[256,1024]{0,1:T(8,128)(2,1)S(1)} %constant_dynamic-update-slice_fusion), channel_id=1, source_target_pairs={{0,2},{1,3},{18,16},{19,17},{4,6},{5,7},{22,20},{23,21},{8,10},{9,... | collective-permute-start | bytes 1572872 | tf_op jit(solution)/shard_map/ppermute | solution.py:97
  41.5 15.2 %collective-permute-start.7 = (bf16[256,1024]{1,0:T(8,128)(2,1)S(1)}, bf16[256,1024]{1,0:T(8,128)(2,1)S(1)}, u32[]{:S(2)}, u32[]{:S(2)}) collective-permute-start(bf16[256,1024]{1,0:T(8,128)(2,1)S(1)} %collective-permute-done.6), channel_id=1, source_target_pairs={{0,4},{4,8},{8,12},{12,0},{1,5},{5,9},{9,13},{13,1},{2,6},{6,10},{... | collective-permute-start | bytes 1572872 | tf_op jit(solution)/shard_map/ppermute | solution.py:122
  45.1 12.2 %collective-permute-start.5 = (bf16[256,1024]{0,1:T(8,128)(2,1)S(1)}, bf16[256,1024]{0,1:T(8,128)(2,1)S(1)}, u32[]{:S(2)}, u32[]{:S(2)}) collective-permute-start(bf16[256,1024]{0,1:T(8,128)(2,1)S(1)} %broadcast_select_fusion), channel_id=1, source_target_pairs={{0,1},{1,0},{2,3},{3,2},{4,5},{5,4},{6,7},{7,6},{8,9},{9,8},{10,11... | collective-permute-start | bytes 1572872 | tf_op jit(solution)/shard_map/ppermute | solution.py:110
  58.2 12.4 %collective-permute-start.8 = (bf16[256,1024]{1,0:T(8,128)(2,1)S(1)}, bf16[256,1024]{1,0:T(8,128)(2,1)S(1)}, u32[]{:S(2)}, u32[]{:S(2)}) collective-permute-start(bf16[256,1024]{1,0:T(8,128)(2,1)S(1)} %convolution_convert_fusion), channel_id=1, source_target_pairs={{0,16},{16,0},{1,17},{17,1},{2,18},{18,2},{3,19},{19,3},{4,20},{20... | collective-permute-start | bytes 1572872 | tf_op jit(solution)/shard_map/ppermute | solution.py:93
